TPU v7x, 256 devices: a whole 4x4x8 slice. The times are simulated.
256 devices in a mesh: pipe: 32 (over x, z), dp: 8 (over y, core).
Axes of the slice: x: 4, y: 4, z: 8, core: 2. Of those that a mesh axis runs over, the one named last changes fastest.
Arguments:
- query_acts: bfloat16 [32, 8, 256, 3584], P('pipe', 'dp'), may hold values from -5.5 to 5.5
- key_acts: bfloat16 [32, 8, 256, 3584], P('pipe', 'dp'), may hold values from -5.5 to 5.5
- layer_inputs: bfloat16 [32, 8, 256, 3584], P('pipe', 'dp'), may hold values from -6 to 6
- grad_out: bfloat16 [8, 256, 3584], P('dp'), may hold values from -6 to 6
- norm_gains: float32 [32, 3584], P('pipe'), may hold values from -0.4 to 0.4
- window_flags: int32 [32], replicated, may hold values from 0 to 1
Outputs:
- grad_inputs: bfloat16 [32, 8, 256, 3584], P('pipe', 'dp')
- grad_queries: bfloat16 [32, 8, 256, 3584], P('pipe', 'dp')
- grad_keys: bfloat16 [32, 8, 256, 3584], P('pipe', 'dp')
- grad_gains: float32 [32, 3584], P('pipe', 'dp')
All inputs are finite; a program needn't handle non-finite values.
Results may differ from a plain program's by a relative error of at most 0.012.
The roundings to bfloat16 on the way count: a program that leaves them out, or rounds other values in their place, can miss the bound.
Values may be sent and summed in bfloat16 or wider, within the bound.
No kernel may reach another device: no remote copies, remote signals or barrier semaphores. Data moves between devices by JAX's collectives and lax.ppermute only.
A program may use at most 64 MiB of HBM per device.

v0:
```python
import jax
import jax.numpy as jnp
from jax import lax
from jax.sharding import PartitionSpec as P

GROUPS = 8
WINDOW = 32


EPSILON = 1e-05
NEGATIVE = -1e30


def passed_along(value, axis, steps):
    count = lax.axis_size(axis)
    leading, last = (max(0, -steps), min(count, count - steps))
    return lax.ppermute(value, axis, [(source, source + steps) for source in range(leading, last)])


def rows_of(source, first_index, row_count):
    return lax.dynamic_slice_in_dim(source, first_index, row_count, 0)


def write_rows(buffer, first_index, new_rows):
    return lax.dynamic_update_slice_in_dim(buffer, new_rows, first_index, 0)


def on_device(query_acts, key_acts, layer_inputs, grad_out, norm_gains, window_flags):
    section_count = lax.axis_size("pipe")
    section_index = lax.axis_index("pipe")
    seq_rows = query_acts.shape[2]
    feature_count = query_acts.shape[3]
    head_count = window_flags.shape[0]
    head_size = feature_count // head_count
    score_scale = head_size ** (-0.5)
    slopes = jnp.exp2(-(jnp.arange(head_count, dtype=jnp.float32) + 1.0) * 8.0 / head_count)
    open_heads = (window_flags == 0)[:, None, None]
    query_rows = query_acts[0, 0]
    key_rows = key_acts[0, 0]
    from_loss = grad_out[0]
    input_rows = layer_inputs[0, 0].astype(jnp.float32)
    inverse = lax.rsqrt(jnp.mean(input_rows * input_rows, axis=-1, keepdims=True) + EPSILON)
    normed = input_rows * inverse
    gain_row = norm_gains[0]
    value_rows = (normed * gain_row).astype(jnp.bfloat16)
    places = jnp.arange(seq_rows, dtype=jnp.int32)
    all_queries = query_rows.reshape(seq_rows, head_count, head_size)
    all_keys = key_rows.reshape(seq_rows, head_count, head_size)
    all_values = value_rows.reshape(seq_rows, head_count, head_size)

    def mask_of(distance):
        allowed = (distance >= 0)[None, :, :] & (open_heads | (distance < WINDOW)[None, :, :])
        return (allowed, distance.astype(jnp.float32))

    def compute(carried_state, first_row, message, rows_here):
        grad_buffer, total_buffer, delta_buffer, query_grads, key_grads, input_grads, gain_sum = (
            carried_state
        )
        incoming = jnp.where(
            section_index == section_count - 1, rows_of(from_loss, first_row, rows_here), message
        )
        grad_buffer = write_rows(grad_buffer, first_row, incoming)
        own_places = first_row + jnp.arange(rows_here, dtype=jnp.int32)
        grad_heads = incoming.reshape(rows_here, head_count, head_size)
        query_heads = rows_of(query_rows, first_row, rows_here).reshape(
            rows_here, head_count, head_size
        )
        allowed, distance = mask_of(own_places[:, None] - places[None, :])
        logits = (
            jnp.einsum("ihd,jhd->hij", query_heads, all_keys, preferred_element_type=jnp.float32)
            * score_scale
        )
        logits = logits - slopes[:, None, None] * distance[None, :, :]
        masked = jnp.where(allowed, logits, NEGATIVE)
        row_top = jnp.max(masked, axis=-1, keepdims=True)
        log_total = row_top + jnp.log(jnp.sum(jnp.exp(masked - row_top), axis=-1, keepdims=True))
        weights = jnp.where(allowed, jnp.exp(masked - log_total), 0.0)
        weights_low = weights.astype(jnp.bfloat16)
        attended = jnp.einsum(
            "hij,jhd->ihd", weights_low, all_values, preferred_element_type=jnp.float32
        )
        delta_rows = jnp.einsum("ihd,ihd->hi", grad_heads.astype(jnp.float32), attended)
        grad_weights = jnp.einsum(
            "ihd,jhd->hij", grad_heads, all_values, preferred_element_type=jnp.float32
        )
        grad_logits = (weights * (grad_weights - delta_rows[:, :, None])).astype(jnp.bfloat16)
        grad_query = (
            jnp.einsum("hij,jhd->ihd", grad_logits, all_keys, preferred_element_type=jnp.float32)
            * score_scale
        )
        grad_query = grad_query.astype(jnp.bfloat16).reshape(rows_here, feature_count)
        total_buffer = write_rows(total_buffer, first_row, log_total[:, :, 0].T)
        delta_buffer = write_rows(delta_buffer, first_row, delta_rows.T)
        query_grads = write_rows(query_grads, first_row, grad_query)
        late_grads = grad_buffer.reshape(seq_rows, head_count, head_size)
        late_totals = total_buffer.T
        late_deltas = delta_buffer.T
        own_keys = rows_of(key_rows, first_row, rows_here).reshape(rows_here, head_count, head_size)
        own_values = rows_of(value_rows, first_row, rows_here).reshape(
            rows_here, head_count, head_size
        )
        allowed, distance = mask_of(places[:, None] - own_places[None, :])
        logits = (
            jnp.einsum("ihd,jhd->hij", all_queries, own_keys, preferred_element_type=jnp.float32)
            * score_scale
        )
        logits = logits - slopes[:, None, None] * distance[None, :, :]
        masked = jnp.where(allowed, logits, NEGATIVE)
        weights = jnp.where(allowed, jnp.exp(masked - late_totals[:, :, None]), 0.0)
        weights_low = weights.astype(jnp.bfloat16)
        grad_weights = jnp.einsum(
            "ihd,jhd->hij", late_grads, own_values, preferred_element_type=jnp.float32
        )
        grad_logits = (weights * (grad_weights - late_deltas[:, :, None])).astype(jnp.bfloat16)
        grad_key = (
            jnp.einsum("hij,ihd->jhd", grad_logits, all_queries, preferred_element_type=jnp.float32)
            * score_scale
        )
        grad_key = grad_key.astype(jnp.bfloat16).reshape(rows_here, feature_count)
        grad_value = jnp.einsum(
            "hij,ihd->jhd", weights_low, late_grads, preferred_element_type=jnp.float32
        )
        grad_value = grad_value.reshape(rows_here, feature_count)
        own_normed = rows_of(normed, first_row, rows_here)
        own_inverse = rows_of(inverse, first_row, rows_here)
        gain_sum = gain_sum + jnp.sum(grad_value * own_normed, axis=0)
        grad_normed = grad_value * gain_row
        grad_input = incoming.astype(jnp.float32) + own_inverse * (
            grad_normed - own_normed * jnp.mean(grad_normed * own_normed, axis=-1, keepdims=True)
        )
        grad_input = grad_input.astype(jnp.bfloat16)
        key_grads = write_rows(key_grads, first_row, grad_key)
        input_grads = write_rows(input_grads, first_row, grad_input)
        return (
            (
                grad_buffer,
                total_buffer,
                delta_buffer,
                query_grads,
                key_grads,
                input_grads,
                gain_sum,
            ),
            grad_input,
        )

    unit_count = GROUPS

    def send_back(outgoing):
        return passed_along(outgoing, "pipe", -1)

    rows_here = seq_rows // unit_count

    def one_turn(turn_index, carried):
        message = carried[0]
        carried_state = carried[1:]
        unit_index = turn_index - (section_count - 1 - section_index)
        active = (unit_index >= 0) & (unit_index < unit_count)
        chosen = jnp.clip(unit_count - 1 - unit_index, 0, unit_count - 1)
        first_row = chosen * rows_here

        def run_step(current):
            return compute(current, first_row, message, rows_here)

        def skip_step(current):
            return (current, jnp.zeros((rows_here, feature_count), jnp.bfloat16))

        carried_state, outgoing = lax.cond(active, run_step, skip_step, carried_state)
        return (send_back(outgoing),) + carried_state

    initial = (
        jnp.zeros((rows_here, feature_count), jnp.bfloat16),
        jnp.zeros((seq_rows, feature_count), jnp.bfloat16),
        jnp.zeros((seq_rows, head_count), jnp.float32),
        jnp.zeros((seq_rows, head_count), jnp.float32),
        jnp.zeros((seq_rows, feature_count), jnp.bfloat16),
        jnp.zeros((seq_rows, feature_count), jnp.bfloat16),
        jnp.zeros((seq_rows, feature_count), jnp.bfloat16),
        jnp.zeros((feature_count,), jnp.float32),
    )
    finished = lax.fori_loop(0, unit_count + section_count - 1, one_turn, initial)
    grad_queries = finished[4].reshape(1, 1, seq_rows, feature_count)
    grad_keys = finished[5].reshape(1, 1, seq_rows, feature_count)
    grad_inputs = finished[6].reshape(1, 1, seq_rows, feature_count)
    grad_gains = lax.psum_scatter(finished[7][None, :], "dp", scatter_dimension=1, tiled=True)
    return (grad_inputs, grad_queries, grad_keys, grad_gains)


def solution(mesh):
    return jax.shard_map(
        on_device,
        mesh=mesh,
        in_specs=(
            P("pipe", "dp", None, None),
            P("pipe", "dp", None, None),
            P("pipe", "dp", None, None),
            P("dp", None, None),
            P("pipe", None),
            P(),
        ),
        out_specs=(
            P("pipe", "dp", None, None),
            P("pipe", "dp", None, None),
            P("pipe", "dp", None, None),
            P("pipe", "dp"),
        ),
        check_vma=False,
    )
```

profile of v0, /device:TPU:15, one launch (start us, length us, event | category | flops | bytes accessed | tf_op | source)
XLA Modules:
  0.0 2073.3 jit_solution(722385523272385222)
XLA Ops:
  24.6 5.2 copy.84
  40.1 1446.6 %while.30 = (s32[]{:T(128)}, bf16[32,3584]{1,0:T(8,128)(2,1)S(1)}, bf16[256,3584]{0,1:T(8,128)(2,1)S(1)}, f32[256,32]{0,1:T(8,128)S(1)}, f32[256,32]{0,1:T(8,128...) while((s32[]{:T(128)}, bf16[32,3584]{1,0:T(8,128)(2,1)S(1)}, ...), condition=%wide.region_8.9_spmd.clone.clone, body=%wide.region_1.8_spmd.clone.clone.sunk | while | flops 480786560 | bytes 46909160 | solution.py:181
  41.0 7.7 collective-permute-start
  48.8 4.6 collective-permute-done
  54.1 6.1 collective-permute-start
  64.6 6.1 collective-permute-start
  74.6 5.8 collective-permute-start
  84.4 5.8 collective-permute-start
  94.2 5.8 collective-permute-start
  104.0 5.8 collective-permute-start
  109.9 283.7 %collective-permute-done = bf16[32,3584]{1,0:T(8,128)(2,1)S(1)} collective-permute-done((bf16[32,3584]{1,0:T(8,128)(2,1)}, bf16[32,3584]{1,0:T(8,128)(2,1)S(1)}, u32[]{:S(2)}, u32[]{:S(2)}) %collective-permute-start) | collective-permute-done | bytes 229408 | tf_op jit(solution)/shard_map/while/body/eval_jaxpr/ppermute | solution.py:17
  393.5 43.1 %conditional.4 = (bf16[256,3584]{0,1:T(8,128)(2,1)S(1)}, f32[256,32]{0,1:T(8,128)S(1)}, f32[256,32]{0,1:T(8,128)S(1)}, bf16[256,3584]{1,0:T(8,128)(2,1)}, bf16[2...) conditional(s32[]{:T(128)} %convert_element_type.152, ...), branch_computations={%region_2.2_spmd, %region_3.7_spmd.clone} | conditional | flops 480786560 | bytes 45989960 | solution.py:168
  406.6 4.0 fusion.23
  417.7 9.8 dynamic_update_slice.30
  438.5 6.3 collective-permute-done
  444.8 43.1 %conditional.4 = (bf16[256,3584]{0,1:T(8,128)(2,1)S(1)}, f32[256,32]{0,1:T(8,128)S(1)}, f32[256,32]{0,1:T(8,128)S(1)}, bf16[256,3584]{1,0:T(8,128)(2,1)}, bf16[2...) conditional(s32[]{:T(128)} %convert_element_type.152, ...), branch_computations={%region_2.2_spmd, %region_3.7_spmd.clone} | conditional | flops 480786560 | bytes 45989960 | solution.py:168
  469.0 9.8 dynamic_update_slice.30
  490.6 5.3 collective-permute-done
  496.0 43.1 %conditional.4 = (bf16[256,3584]{0,1:T(8,128)(2,1)S(1)}, f32[256,32]{0,1:T(8,128)S(1)}, f32[256,32]{0,1:T(8,128)S(1)}, bf16[256,3584]{1,0:T(8,128)(2,1)}, bf16[2...) conditional(s32[]{:T(128)} %convert_element_type.152, ...), branch_computations={%region_2.2_spmd, %region_3.7_spmd.clone} | conditional | flops 480786560 | bytes 45989960 | solution.py:168
  520.2 9.8 dynamic_update_slice.30
  546.0 41.2 %conditional.4 = (bf16[256,3584]{0,1:T(8,128)(2,1)S(1)}, f32[256,32]{0,1:T(8,128)S(1)}, f32[256,32]{0,1:T(8,128)S(1)}, bf16[256,3584]{1,0:T(8,128)(2,1)}, bf16[2...) conditional(s32[]{:T(128)} %convert_element_type.152, ...), branch_computations={%region_2.2_spmd, %region_3.7_spmd.clone} | conditional | flops 480786560 | bytes 45989960 | solution.py:168
  559.1 4.0 fusion.23
  570.0 8.1 dynamic_update_slice.30
  587.2 7.7 collective-permute-start
  598.2 43.4 %conditional.4 = (bf16[256,3584]{0,1:T(8,128)(2,1)S(1)}, f32[256,32]{0,1:T(8,128)S(1)}, f32[256,32]{0,1:T(8,128)S(1)}, bf16[256,3584]{1,0:T(8,128)(2,1)}, bf16[2...) conditional(s32[]{:T(128)} %convert_element_type.152, ...), branch_computations={%region_2.2_spmd, %region_3.7_spmd.clone} | conditional | flops 480786560 | bytes 45989960 | solution.py:168
  611.2 4.0 fusion.23
  622.5 10.0 dynamic_update_slice.30
  645.2 4.1 collective-permute-done
  649.3 43.4 %conditional.4 = (bf16[256,3584]{0,1:T(8,128)(2,1)S(1)}, f32[256,32]{0,1:T(8,128)S(1)}, f32[256,32]{0,1:T(8,128)S(1)}, bf16[256,3584]{1,0:T(8,128)(2,1)}, bf16[2...) conditional(s32[]{:T(128)} %convert_element_type.152, ...), branch_computations={%region_2.2_spmd, %region_3.7_spmd.clone} | conditional | flops 480786560 | bytes 45989960 | solution.py:168
  673.6 10.0 dynamic_update_slice.30
  692.7 5.0 collective-permute-start
  700.9 43.4 %conditional.4 = (bf16[256,3584]{0,1:T(8,128)(2,1)S(1)}, f32[256,32]{0,1:T(8,128)S(1)}, f32[256,32]{0,1:T(8,128)S(1)}, bf16[256,3584]{1,0:T(8,128)(2,1)}, bf16[2...) conditional(s32[]{:T(128)} %convert_element_type.152, ...), branch_computations={%region_2.2_spmd, %region_3.7_spmd.clone} | conditional | flops 480786560 | bytes 45989960 | solution.py:168
  714.0 4.0 fusion.23
  725.3 10.0 dynamic_update_slice.30
  744.4 5.8 collective-permute-start
  753.4 41.5 %conditional.4 = (bf16[256,3584]{0,1:T(8,128)(2,1)S(1)}, f32[256,32]{0,1:T(8,128)S(1)}, f32[256,32]{0,1:T(8,128)S(1)}, bf16[256,3584]{1,0:T(8,128)(2,1)}, bf16[2...) conditional(s32[]{:T(128)} %convert_element_type.152, ...), branch_computations={%region_2.2_spmd, %region_3.7_spmd.clone} | conditional | flops 480786560 | bytes 45989960 | solution.py:168
  766.5 4.0 fusion.23
  777.6 8.3 dynamic_update_slice.30
  794.9 7.7 collective-permute-start
  806.6 46.6 %collective-permute-start = (bf16[32,3584]{1,0:T(8,128)(2,1)}, bf16[32,3584]{1,0:T(8,128)(2,1)S(1)}, u32[]{:S(2)}, u32[]{:S(2)}) collective-permute-start(bf16[32,3584]{1,0:T(8,128)(2,1)} %get-tuple-element.1294), channel_id=1, source_target_pairs={{8,0},{16,8},{24,16},{32,24},{40,32},{48,40},{56,48},{64,56},{72,6... | collective-permute-start | bytes 688136 | tf_op jit(solution)/shard_map/while/body/eval_jaxpr/ppermute | solution.py:17
  857.2 5.8 collective-permute-start
  867.0 40.6 %collective-permute-start = (bf16[32,3584]{1,0:T(8,128)(2,1)}, bf16[32,3584]{1,0:T(8,128)(2,1)S(1)}, u32[]{:S(2)}, u32[]{:S(2)}) collective-permute-start(bf16[32,3584]{1,0:T(8,128)(2,1)} %get-tuple-element.1294), channel_id=1, source_target_pairs={{8,0},{16,8},{24,16},{32,24},{40,32},{48,40},{56,48},{64,56},{72,6... | collective-permute-start | bytes 688136 | tf_op jit(solution)/shard_map/while/body/eval_jaxpr/ppermute | solution.py:17
  911.6 5.8 collective-permute-start
  921.4 42.3 %collective-permute-start = (bf16[32,3584]{1,0:T(8,128)(2,1)}, bf16[32,3584]{1,0:T(8,128)(2,1)S(1)}, u32[]{:S(2)}, u32[]{:S(2)}) collective-permute-start(bf16[32,3584]{1,0:T(8,128)(2,1)} %get-tuple-element.1294), channel_id=1, source_target_pairs={{8,0},{16,8},{24,16},{32,24},{40,32},{48,40},{56,48},{64,56},{72,6... | collective-permute-start | bytes 688136 | tf_op jit(solution)/shard_map/while/body/eval_jaxpr/ppermute | solution.py:17
  967.7 5.8 collective-permute-start
  977.5 42.5 %collective-permute-start = (bf16[32,3584]{1,0:T(8,128)(2,1)}, bf16[32,3584]{1,0:T(8,128)(2,1)S(1)}, u32[]{:S(2)}, u32[]{:S(2)}) collective-permute-start(bf16[32,3584]{1,0:T(8,128)(2,1)} %get-tuple-element.1294), channel_id=1, source_target_pairs={{8,0},{16,8},{24,16},{32,24},{40,32},{48,40},{56,48},{64,56},{72,6... | collective-permute-start | bytes 688136 | tf_op jit(solution)/shard_map/while/body/eval_jaxpr/ppermute | solution.py:17
  1024.0 5.8 collective-permute-start
  1033.8 44.9 %collective-permute-start = (bf16[32,3584]{1,0:T(8,128)(2,1)}, bf16[32,3584]{1,0:T(8,128)(2,1)S(1)}, u32[]{:S(2)}, u32[]{:S(2)}) collective-permute-start(bf16[32,3584]{1,0:T(8,128)(2,1)} %get-tuple-element.1294), channel_id=1, source_target_pairs={{8,0},{16,8},{24,16},{32,24},{40,32},{48,40},{56,48},{64,56},{72,6... | collective-permute-start | bytes 688136 | tf_op jit(solution)/shard_map/while/body/eval_jaxpr/ppermute | solution.py:17
  1082.7 5.8 collective-permute-start
  1092.5 41.3 %collective-permute-start = (bf16[32,3584]{1,0:T(8,128)(2,1)}, bf16[32,3584]{1,0:T(8,128)(2,1)S(1)}, u32[]{:S(2)}, u32[]{:S(2)}) collective-permute-start(bf16[32,3584]{1,0:T(8,128)(2,1)} %get-tuple-element.1294), channel_id=1, source_target_pairs={{8,0},{16,8},{24,16},{32,24},{40,32},{48,40},{56,48},{64,56},{72,6... | collective-permute-start | bytes 688136 | tf_op jit(solution)/shard_map/while/body/eval_jaxpr/ppermute | solution.py:17
  1137.8 5.8 collective-permute-start
  1147.6 42.5 %collective-permute-start = (bf16[32,3584]{1,0:T(8,128)(2,1)}, bf16[32,3584]{1,0:T(8,128)(2,1)S(1)}, u32[]{:S(2)}, u32[]{:S(2)}) collective-permute-start(bf16[32,3584]{1,0:T(8,128)(2,1)} %get-tuple-element.1294), channel_id=1, source_target_pairs={{8,0},{16,8},{24,16},{32,24},{40,32},{48,40},{56,48},{64,56},{72,6... | collective-permute-start | bytes 688136 | tf_op jit(solution)/shard_map/while/body/eval_jaxpr/ppermute | solution.py:17
  1194.1 5.8 collective-permute-start
  1203.9 42.5 %collective-permute-start = (bf16[32,3584]{1,0:T(8,128)(2,1)}, bf16[32,3584]{1,0:T(8,128)(2,1)S(1)}, u32[]{:S(2)}, u32[]{:S(2)}) collective-permute-start(bf16[32,3584]{1,0:T(8,128)(2,1)} %get-tuple-element.1294), channel_id=1, source_target_pairs={{8,0},{16,8},{24,16},{32,24},{40,32},{48,40},{56,48},{64,56},{72,6... | collective-permute-start | bytes 688136 | tf_op jit(solution)/shard_map/while/body/eval_jaxpr/ppermute | solution.py:17
  1250.4 5.9 collective-permute-start
  1260.3 46.6 %collective-permute-start = (bf16[32,3584]{1,0:T(8,128)(2,1)}, bf16[32,3584]{1,0:T(8,128)(2,1)S(1)}, u32[]{:S(2)}, u32[]{:S(2)}) collective-permute-start(bf16[32,3584]{1,0:T(8,128)(2,1)} %get-tuple-element.1294), channel_id=1, source_target_pairs={{8,0},{16,8},{24,16},{32,24},{40,32},{48,40},{56,48},{64,56},{72,6... | collective-permute-start | bytes 688136 | tf_op jit(solution)/shard_map/while/body/eval_jaxpr/ppermute | solution.py:17
  1310.9 5.8 collective-permute-start
  1320.7 40.6 %collective-permute-start = (bf16[32,3584]{1,0:T(8,128)(2,1)}, bf16[32,3584]{1,0:T(8,128)(2,1)S(1)}, u32[]{:S(2)}, u32[]{:S(2)}) collective-permute-start(bf16[32,3584]{1,0:T(8,128)(2,1)} %get-tuple-element.1294), channel_id=1, source_target_pairs={{8,0},{16,8},{24,16},{32,24},{40,32},{48,40},{56,48},{64,56},{72,6... | collective-permute-start | bytes 688136 | tf_op jit(solution)/shard_map/while/body/eval_jaxpr/ppermute | solution.py:17
  1365.2 5.8 collective-permute-start
  1375.0 42.3 %collective-permute-start = (bf16[32,3584]{1,0:T(8,128)(2,1)}, bf16[32,3584]{1,0:T(8,128)(2,1)S(1)}, u32[]{:S(2)}, u32[]{:S(2)}) collective-permute-start(bf16[32,3584]{1,0:T(8,128)(2,1)} %get-tuple-element.1294), channel_id=1, source_target_pairs={{8,0},{16,8},{24,16},{32,24},{40,32},{48,40},{56,48},{64,56},{72,6... | collective-permute-start | bytes 688136 | tf_op jit(solution)/shard_map/while/body/eval_jaxpr/ppermute | solution.py:17
  1421.3 5.8 collective-permute-start
  1431.1 42.5 %collective-permute-start = (bf16[32,3584]{1,0:T(8,128)(2,1)}, bf16[32,3584]{1,0:T(8,128)(2,1)S(1)}, u32[]{:S(2)}, u32[]{:S(2)}) collective-permute-start(bf16[32,3584]{1,0:T(8,128)(2,1)} %get-tuple-element.1294), channel_id=1, source_target_pairs={{8,0},{16,8},{24,16},{32,24},{40,32},{48,40},{56,48},{64,56},{72,6... | collective-permute-start | bytes 688136 | tf_op jit(solution)/shard_map/while/body/eval_jaxpr/ppermute | solution.py:17
  1477.6 5.8 collective-permute-start
  1488.5 576.3 %reduce-scatter.4.cloned.1.call-done = f32[448,1]{1,0:T(8,128)} async-done(((f32[3584,1]{1,0:T(8,128)}), f32[448,1]{1,0:T(8,128)}) %reduce-scatter.4.cloned.1.call-update) | async-done | bytes 1808
  (644 shorter events, 443.1 us)
Async XLA Ops:
  7.2 2057.7 %reduce-scatter.4.cloned.1.call-start = ((), (), s32[]{:S(2)}) async-start(), calls=%async_computation.1 | async-start | bytes 2064384
  41.0 12.3 collective-permute-start
  54.1 9.8 collective-permute-start
  64.6 9.4 collective-permute-start
  74.6 9.1 collective-permute-start
  84.4 9.1 collective-permute-start
  94.2 9.1 collective-permute-start
  104.0 289.5 %collective-permute-start = (bf16[32,3584]{1,0:T(8,128)(2,1)}, bf16[32,3584]{1,0:T(8,128)(2,1)S(1)}, u32[]{:S(2)}, u32[]{:S(2)}) collective-permute-start(bf16[32,3584]{1,0:T(8,128)(2,1)} %get-tuple-element.1294), channel_id=1, source_target_pairs={{8,0},{16,8},{24,16},{32,24},{40,32},{48,40},{56,48},{64,56},{72,6... | collective-permute-start | bytes 688136 | tf_op jit(solution)/shard_map/while/body/eval_jaxpr/ppermute | solution.py:17
  393.6 8.7 copy-start.7
  406.5 7.8 copy-start.3
  406.5 7.8 copy-start.8
  436.6 8.2 collective-permute-start
  444.8 8.7 copy-start.7
  457.8 7.8 copy-start.2
  457.8 7.8 copy-start.3
  457.8 7.8 copy-start.8
  487.8 8.2 collective-permute-start
  496.0 8.7 copy-start.7
  509.0 7.8 copy-start.3
  509.0 7.8 copy-start.8
  539.0 7.0 collective-permute-start
  546.1 8.7 copy-start.7
  587.2 10.9 collective-permute-start
  598.2 8.7 copy-start.7
  611.2 7.9 copy-start.2
  611.2 7.9 copy-start.3
  611.2 7.9 copy-start.8
  641.6 7.7 collective-permute-start
  649.3 8.7 copy-start.7
  662.3 7.9 copy-start.2
  662.3 7.9 copy-start.3
  662.3 7.9 copy-start.8
  692.7 8.2 collective-permute-start
  701.0 8.7 copy-start.7
  713.9 7.9 copy-start.2
  714.0 7.9 copy-start.3
  714.0 7.9 copy-start.8
  744.4 9.1 collective-permute-start
  753.5 8.7 copy-start.7
  794.9 11.0 collective-permute-start
  806.6 49.9 %collective-permute-start = (bf16[32,3584]{1,0:T(8,128)(2,1)}, bf16[32,3584]{1,0:T(8,128)(2,1)S(1)}, u32[]{:S(2)}, u32[]{:S(2)}) collective-permute-start(bf16[32,3584]{1,0:T(8,128)(2,1)} %get-tuple-element.1294), channel_id=1, source_target_pairs={{8,0},{16,8},{24,16},{32,24},{40,32},{48,40},{56,48},{64,56},{72,6... | collective-permute-start | bytes 688136 | tf_op jit(solution)/shard_map/while/body/eval_jaxpr/ppermute | solution.py:17
  857.2 9.1 collective-permute-start
  867.0 43.9 %collective-permute-start = (bf16[32,3584]{1,0:T(8,128)(2,1)}, bf16[32,3584]{1,0:T(8,128)(2,1)S(1)}, u32[]{:S(2)}, u32[]{:S(2)}) collective-permute-start(bf16[32,3584]{1,0:T(8,128)(2,1)} %get-tuple-element.1294), channel_id=1, source_target_pairs={{8,0},{16,8},{24,16},{32,24},{40,32},{48,40},{56,48},{64,56},{72,6... | collective-permute-start | bytes 688136 | tf_op jit(solution)/shard_map/while/body/eval_jaxpr/ppermute | solution.py:17
  911.6 9.1 collective-permute-start
  921.4 45.6 %collective-permute-start = (bf16[32,3584]{1,0:T(8,128)(2,1)}, bf16[32,3584]{1,0:T(8,128)(2,1)S(1)}, u32[]{:S(2)}, u32[]{:S(2)}) collective-permute-start(bf16[32,3584]{1,0:T(8,128)(2,1)} %get-tuple-element.1294), channel_id=1, source_target_pairs={{8,0},{16,8},{24,16},{32,24},{40,32},{48,40},{56,48},{64,56},{72,6... | collective-permute-start | bytes 688136 | tf_op jit(solution)/shard_map/while/body/eval_jaxpr/ppermute | solution.py:17
  967.7 9.1 collective-permute-start
  977.5 45.8 %collective-permute-start = (bf16[32,3584]{1,0:T(8,128)(2,1)}, bf16[32,3584]{1,0:T(8,128)(2,1)S(1)}, u32[]{:S(2)}, u32[]{:S(2)}) collective-permute-start(bf16[32,3584]{1,0:T(8,128)(2,1)} %get-tuple-element.1294), channel_id=1, source_target_pairs={{8,0},{16,8},{24,16},{32,24},{40,32},{48,40},{56,48},{64,56},{72,6... | collective-permute-start | bytes 688136 | tf_op jit(solution)/shard_map/while/body/eval_jaxpr/ppermute | solution.py:17
  1024.0 9.1 collective-permute-start
  1033.8 48.2 %collective-permute-start = (bf16[32,3584]{1,0:T(8,128)(2,1)}, bf16[32,3584]{1,0:T(8,128)(2,1)S(1)}, u32[]{:S(2)}, u32[]{:S(2)}) collective-permute-start(bf16[32,3584]{1,0:T(8,128)(2,1)} %get-tuple-element.1294), channel_id=1, source_target_pairs={{8,0},{16,8},{24,16},{32,24},{40,32},{48,40},{56,48},{64,56},{72,6... | collective-permute-start | bytes 688136 | tf_op jit(solution)/shard_map/while/body/eval_jaxpr/ppermute | solution.py:17
  1082.7 9.1 collective-permute-start
  1092.5 44.6 %collective-permute-start = (bf16[32,3584]{1,0:T(8,128)(2,1)}, bf16[32,3584]{1,0:T(8,128)(2,1)S(1)}, u32[]{:S(2)}, u32[]{:S(2)}) collective-permute-start(bf16[32,3584]{1,0:T(8,128)(2,1)} %get-tuple-element.1294), channel_id=1, source_target_pairs={{8,0},{16,8},{24,16},{32,24},{40,32},{48,40},{56,48},{64,56},{72,6... | collective-permute-start | bytes 688136 | tf_op jit(solution)/shard_map/while/body/eval_jaxpr/ppermute | solution.py:17
  1137.8 9.1 collective-permute-start
  1147.6 45.8 %collective-permute-start = (bf16[32,3584]{1,0:T(8,128)(2,1)}, bf16[32,3584]{1,0:T(8,128)(2,1)S(1)}, u32[]{:S(2)}, u32[]{:S(2)}) collective-permute-start(bf16[32,3584]{1,0:T(8,128)(2,1)} %get-tuple-element.1294), channel_id=1, source_target_pairs={{8,0},{16,8},{24,16},{32,24},{40,32},{48,40},{56,48},{64,56},{72,6... | collective-permute-start | bytes 688136 | tf_op jit(solution)/shard_map/while/body/eval_jaxpr/ppermute | solution.py:17
  1194.1 9.1 collective-permute-start
  1203.9 45.8 %collective-permute-start = (bf16[32,3584]{1,0:T(8,128)(2,1)}, bf16[32,3584]{1,0:T(8,128)(2,1)S(1)}, u32[]{:S(2)}, u32[]{:S(2)}) collective-permute-start(bf16[32,3584]{1,0:T(8,128)(2,1)} %get-tuple-element.1294), channel_id=1, source_target_pairs={{8,0},{16,8},{24,16},{32,24},{40,32},{48,40},{56,48},{64,56},{72,6... | collective-permute-start | bytes 688136 | tf_op jit(solution)/shard_map/while/body/eval_jaxpr/ppermute | solution.py:17
  1250.4 9.2 collective-permute-start
  1260.3 49.9 %collective-permute-start = (bf16[32,3584]{1,0:T(8,128)(2,1)}, bf16[32,3584]{1,0:T(8,128)(2,1)S(1)}, u32[]{:S(2)}, u32[]{:S(2)}) collective-permute-start(bf16[32,3584]{1,0:T(8,128)(2,1)} %get-tuple-element.1294), channel_id=1, source_target_pairs={{8,0},{16,8},{24,16},{32,24},{40,32},{48,40},{56,48},{64,56},{72,6... | collective-permute-start | bytes 688136 | tf_op jit(solution)/shard_map/while/body/eval_jaxpr/ppermute | solution.py:17
  1310.9 9.1 collective-permute-start
  1320.7 43.9 %collective-permute-start = (bf16[32,3584]{1,0:T(8,128)(2,1)}, bf16[32,3584]{1,0:T(8,128)(2,1)S(1)}, u32[]{:S(2)}, u32[]{:S(2)}) collective-permute-start(bf16[32,3584]{1,0:T(8,128)(2,1)} %get-tuple-element.1294), channel_id=1, source_target_pairs={{8,0},{16,8},{24,16},{32,24},{40,32},{48,40},{56,48},{64,56},{72,6... | collective-permute-start | bytes 688136 | tf_op jit(solution)/shard_map/while/body/eval_jaxpr/ppermute | solution.py:17
  1365.2 9.1 collective-permute-start
  1375.0 45.6 %collective-permute-start = (bf16[32,3584]{1,0:T(8,128)(2,1)}, bf16[32,3584]{1,0:T(8,128)(2,1)S(1)}, u32[]{:S(2)}, u32[]{:S(2)}) collective-permute-start(bf16[32,3584]{1,0:T(8,128)(2,1)} %get-tuple-element.1294), channel_id=1, source_target_pairs={{8,0},{16,8},{24,16},{32,24},{40,32},{48,40},{56,48},{64,56},{72,6... | collective-permute-start | bytes 688136 | tf_op jit(solution)/shard_map/while/body/eval_jaxpr/ppermute | solution.py:17
  1421.3 9.1 collective-permute-start
  1431.1 45.8 %collective-permute-start = (bf16[32,3584]{1,0:T(8,128)(2,1)}, bf16[32,3584]{1,0:T(8,128)(2,1)S(1)}, u32[]{:S(2)}, u32[]{:S(2)}) collective-permute-start(bf16[32,3584]{1,0:T(8,128)(2,1)} %get-tuple-element.1294), channel_id=1, source_target_pairs={{8,0},{16,8},{24,16},{32,24},{40,32},{48,40},{56,48},{64,56},{72,6... | collective-permute-start | bytes 688136 | tf_op jit(solution)/shard_map/while/body/eval_jaxpr/ppermute | solution.py:17
  1477.6 9.1 collective-permute-start
  (48 other events, 195.4 us)
Sparse Core Ops, SparseCore 0:
  1488.6 576.1 reduce-scatter.3
where the time goes:
time: 2080 us; the launch traced here: 2070 us
  waiting for transfers between devices  991 us (48%)
  starting transfers between devices  666 us (32%)
  local copies, waits for them, and re-layouts  233 us (11%)
  matrix products  105 us (5%)
  other arithmetic  60.4 us (3%)
    ppermute x39, starting transfers between devices, passed_along(): lax.ppermute(value, axis, [(source, source + steps) for source in range(l...  666 us
    unnamed x2, waiting for transfers between devices  576 us
    ppermute x39, waiting for transfers between devices, passed_along(): lax.ppermute(value, axis, [(source, source + steps) for source in range(l...  415 us
    dynamic_update_slice x40, local copies, waits for them, and re-layouts, write_rows(): return lax.dynamic_update_slice_in_dim(buffer, new_rows, first_index, 0)  101 us
  transfers between devices with their start and end apart: 40, of which 40 were waited for; matrix products, arithmetic and copies ran while one was open for 0% of the time, Pallas kernels for 0%

commit v1 on v0

v1 whole, which is shorter than its diff:
```python
import jax
import jax.numpy as jnp
from jax import lax
from jax.sharding import PartitionSpec as P

GROUPS = 8
WINDOW = 32


EPSILON = 1e-05
NEGATIVE = -1e30


def passed_along(value, axis, steps):
    count = lax.axis_size(axis)
    leading, last = (max(0, -steps), min(count, count - steps))
    return lax.ppermute(value, axis, [(source, source + steps) for source in range(leading, last)])


def rows_of(source, first_index, row_count):
    return lax.dynamic_slice_in_dim(source, first_index, row_count, 0)


def write_rows(buffer, first_index, new_rows):
    return lax.dynamic_update_slice_in_dim(buffer, new_rows, first_index, 0)


def on_device(query_acts, key_acts, layer_inputs, grad_out, norm_gains, window_flags):
    section_count = lax.axis_size("pipe")
    section_index = lax.axis_index("pipe")
    seq_rows = query_acts.shape[2]
    feature_count = query_acts.shape[3]
    head_count = window_flags.shape[0]
    head_size = feature_count // head_count
    score_scale = head_size ** (-0.5)
    slopes = jnp.exp2(-(jnp.arange(head_count, dtype=jnp.float32) + 1.0) * 8.0 / head_count)
    open_heads = (window_flags == 0)[:, None, None]
    query_rows = query_acts[0, 0]
    key_rows = key_acts[0, 0]
    from_loss = grad_out[0]
    input_rows = layer_inputs[0, 0].astype(jnp.float32)
    inverse = lax.rsqrt(jnp.mean(input_rows * input_rows, axis=-1, keepdims=True) + EPSILON)
    normed = input_rows * inverse
    gain_row = norm_gains[0]
    value_rows = (normed * gain_row).astype(jnp.bfloat16)
    places = jnp.arange(seq_rows, dtype=jnp.int32)
    all_queries = query_rows.reshape(seq_rows, head_count, head_size)
    all_keys = key_rows.reshape(seq_rows, head_count, head_size)
    all_values = value_rows.reshape(seq_rows, head_count, head_size)

    distance = places[:, None] - places[None, :]
    allowed = (distance >= 0)[None, :, :] & (open_heads | (distance < WINDOW)[None, :, :])
    logits = (
        jnp.einsum("ihd,jhd->hij", all_queries, all_keys, preferred_element_type=jnp.float32)
        * score_scale
    )
    logits = logits - slopes[:, None, None] * distance.astype(jnp.float32)[None, :, :]
    masked = jnp.where(allowed, logits, NEGATIVE)
    row_top = jnp.max(masked, axis=-1, keepdims=True)
    log_total = row_top + jnp.log(jnp.sum(jnp.exp(masked - row_top), axis=-1, keepdims=True))
    weights = jnp.where(allowed, jnp.exp(masked - log_total), 0.0)
    weights_low = weights.astype(jnp.bfloat16)
    attended = jnp.einsum(
        "hij,jhd->ihd", weights_low, all_values, preferred_element_type=jnp.float32
    )

    unit_count = GROUPS
    rows_here = seq_rows // unit_count
    column_blocks = jnp.pad(weights_low, ((0, 0), (0, rows_here), (0, 0)))
    column_blocks = column_blocks.reshape(
        head_count, seq_rows + rows_here, unit_count, rows_here
    ).transpose(2, 0, 1, 3)

    def one_turn(turn_index, carried):
        message, grad_buffer, input_grads = carried
        unit_index = turn_index - (section_count - 1 - section_index)
        active = (unit_index >= 0) & (unit_index < unit_count)
        chosen = jnp.clip(unit_count - 1 - unit_index, 0, unit_count - 1)
        first_row = chosen * rows_here
        slot = jnp.where(active, first_row, seq_rows)
        incoming = jnp.where(
            section_index == section_count - 1, rows_of(from_loss, first_row, rows_here), message
        )
        incoming = jnp.where(active, incoming, jnp.zeros_like(incoming))
        grad_buffer = write_rows(grad_buffer, slot, incoming)
        block = column_blocks[chosen]
        grad_value = jnp.einsum(
            "hij,ihd->jhd",
            block,
            grad_buffer.reshape(seq_rows + rows_here, head_count, head_size),
            preferred_element_type=jnp.float32,
        ).reshape(rows_here, feature_count)
        own_normed = rows_of(normed, first_row, rows_here)
        own_inverse = rows_of(inverse, first_row, rows_here)
        grad_normed = grad_value * gain_row
        grad_input = incoming.astype(jnp.float32) + own_inverse * (
            grad_normed - own_normed * jnp.mean(grad_normed * own_normed, axis=-1, keepdims=True)
        )
        grad_input = grad_input.astype(jnp.bfloat16)
        input_grads = write_rows(input_grads, slot, grad_input)
        return (passed_along(grad_input, "pipe", -1), grad_buffer, input_grads)

    initial = (
        jnp.zeros((rows_here, feature_count), jnp.bfloat16),
        jnp.zeros((seq_rows + rows_here, feature_count), jnp.bfloat16),
        jnp.zeros((seq_rows + rows_here, feature_count), jnp.bfloat16),
    )
    _, grad_buffer, input_grads = lax.fori_loop(
        0, unit_count + section_count - 1, one_turn, initial
    )
    grad_rows = grad_buffer[:seq_rows]
    grad_heads = grad_rows.reshape(seq_rows, head_count, head_size)

    delta_rows = jnp.einsum("ihd,ihd->hi", grad_heads.astype(jnp.float32), attended)
    grad_weights = jnp.einsum(
        "ihd,jhd->hij", grad_heads, all_values, preferred_element_type=jnp.float32
    )
    grad_logits = (weights * (grad_weights - delta_rows[:, :, None])).astype(jnp.bfloat16)
    grad_query = (
        jnp.einsum("hij,jhd->ihd", grad_logits, all_keys, preferred_element_type=jnp.float32)
        * score_scale
    )
    grad_query = grad_query.astype(jnp.bfloat16).reshape(seq_rows, feature_count)
    grad_key = (
        jnp.einsum("hij,ihd->jhd", grad_logits, all_queries, preferred_element_type=jnp.float32)
        * score_scale
    )
    grad_key = grad_key.astype(jnp.bfloat16).reshape(seq_rows, feature_count)
    grad_value = jnp.einsum(
        "hij,ihd->jhd", weights_low, grad_heads, preferred_element_type=jnp.float32
    ).reshape(seq_rows, feature_count)
    gain_sum = jnp.sum(grad_value * normed, axis=0)

    grad_queries = grad_query.reshape(1, 1, seq_rows, feature_count)
    grad_keys = grad_key.reshape(1, 1, seq_rows, feature_count)
    grad_inputs = input_grads[:seq_rows].reshape(1, 1, seq_rows, feature_count)
    grad_gains = lax.psum_scatter(gain_sum[None, :], "dp", scatter_dimension=1, tiled=True)
    return (grad_inputs, grad_queries, grad_keys, grad_gains)


def solution(mesh):
    return jax.shard_map(
        on_device,
        mesh=mesh,
        in_specs=(
            P("pipe", "dp", None, None),
            P("pipe", "dp", None, None),
            P("pipe", "dp", None, None),
            P("dp", None, None),
            P("pipe", None),
            P(),
        ),
        out_specs=(
            P("pipe", "dp", None, None),
            P("pipe", "dp", None, None),
            P("pipe", "dp", None, None),
            P("pipe", "dp"),
        ),
        check_vma=False,
    )
```

time: 2080 us -> 1010 us (0.49)
  waiting for transfers between devices: 991 us -> 173 us
  starting transfers between devices: 666 us -> 234 us
  other arithmetic: 60.4 us -> 200 us
  matrix products: 105 us -> 128 us
    unnamed x2, waiting for transfers between devices: 576 us -> 49.9 us
    ppermute x39, starting transfers between devices: 666 us -> 234 us  [passed_along(): lax.ppermute(value, axis, [(source, source + steps) for source in range(l...]
    ppermute x39, waiting for transfers between devices: 415 us -> 123 us  [passed_along(): lax.ppermute(value, axis, [(source, source + steps) for source in range(l...]
    reshape x56 -> x79, local copies, waits for them, and re-layouts: 41.8 us -> 188 us  [the longest x39 175 us: one_turn(): grad_buffer.reshape(seq_rows + rows_here, head_count, head_size)]
    dynamic_update_slice x8 -> x78, other arithmetic: 15.6 us -> 141 us  [write_rows(): return lax.dynamic_update_slice_in_dim(buffer, new_rows, first_index, 0)]
    dynamic_update_slice x40 -> x0, local copies, waits for them, and re-layouts: 101 us -> none  [write_rows(): return lax.dynamic_update_slice_in_dim(buffer, new_rows, first_index, 0)]
    reduce_sum x16 -> x40, other arithmetic: 13 us -> 48.5 us  [the longest x39 46 us: one_turn(): jnp.mean(grad_normed * own_normed, axis=-1, keepdims=True)]
    another operation x38 -> x3, local copies, waits for them, and re-layouts: 26.3 us -> 2.91 us
  transfers between devices with their start and end apart: 40 -> 40, of which waited for: 40 -> 40; matrix products, arithmetic and copies ran while one was open for 0% -> 2% of each run, Pallas kernels for 0% -> 0%
where the time goes in v1:
time: 1010 us; the launch traced here: 997 us
  local copies, waits for them, and re-layouts  247 us (24%)
  starting transfers between devices  234 us (23%)
  other arithmetic  200 us (20%)
  waiting for transfers between devices  173 us (17%)
  matrix products  128 us (13%)
  between operations  14.2 us (1%)
    ppermute x39, starting transfers between devices, passed_along(): lax.ppermute(value, axis, [(source, source + steps) for source in range(l...  234 us
    reshape x39, local copies, waits for them, and re-layouts, one_turn(): grad_buffer.reshape(seq_rows + rows_here, head_count, head_size)  175 us
    dynamic_update_slice x78, other arithmetic, write_rows(): return lax.dynamic_update_slice_in_dim(buffer, new_rows, first_index, 0)  141 us
    ppermute x39, waiting for transfers between devices, passed_along(): lax.ppermute(value, axis, [(source, source + steps) for source in range(l...  123 us
    dot_general x39, matrix products, one_turn(): jnp.einsum('hij,ihd->jhd', block, grad_buffer.reshape(seq_rows + rows_her...  102 us
    unnamed x2, waiting for transfers between devices  49.9 us
    reduce_sum x39, other arithmetic, one_turn(): jnp.mean(grad_normed * own_normed, axis=-1, keepdims=True)  46 us
    unnamed x24, local copies, waits for them, and re-layouts  23.3 us
  transfers between devices with their start and end apart: 40, of which 40 were waited for; matrix products, arithmetic and copies ran while one was open for 2% of the time, Pallas kernels for 0%

profile of v1, /device:TPU:15, one launch (start us, length us, event | category | flops | bytes accessed | tf_op | source)
XLA Modules:
  0.0 997.1 jit_solution(15116755699030791563)
XLA Ops:
  20.5 4.7 fusion.17
  32.3 6.6 copy.52
  41.3 5.8 pad.4.clone
  50.0 850.8 %while.19 = (s32[]{:T(128)}, bf16[32,3584]{1,0:T(8,128)(2,1)S(1)}, bf16[288,3584]{1,0:T(8,128)(2,1)}, bf16[288,3584]{1,0:T(8,128)(2,1)}, s32[]{:T(128)}, /*index...) while((s32[]{:T(128)}, bf16[32,3584]{1,0:T(8,128)(2,1)S(1)}, ...), condition=%wide.region_5.6_spmd, body=%wide.region_3.5_spmd.sunk | while | flops 67665936 | bytes 13691161 | solution.py:108
  51.7 4.5 reshape.153
  62.7 7.7 collective-permute-start
  76.4 4.5 reshape.153
  87.3 6.2 collective-permute-start
  98.6 4.5 reshape.153
  109.5 6.2 collective-permute-start
  120.4 4.5 reshape.153
  131.4 5.9 collective-permute-start
  141.9 4.5 reshape.153
  152.9 5.9 collective-permute-start
  163.4 4.5 reshape.153
  174.4 5.9 collective-permute-start
  185.0 4.5 reshape.153
  195.9 5.9 collective-permute-start
  206.5 4.5 reshape.153
  217.5 5.9 collective-permute-start
  228.0 4.5 reshape.153
  239.0 5.9 collective-permute-start
  249.6 4.5 reshape.153
  260.5 5.9 collective-permute-start
  271.1 4.5 reshape.153
  282.1 5.9 collective-permute-start
  303.6 5.9 collective-permute-start
  314.2 4.5 reshape.153
  325.1 5.9 collective-permute-start
  335.7 4.5 reshape.153
  346.7 5.9 collective-permute-start
  357.2 4.5 reshape.153
  368.2 5.9 collective-permute-start
  378.8 4.5 reshape.153
  389.7 5.9 collective-permute-start
  400.3 4.5 reshape.153
  411.3 5.9 collective-permute-start
  432.8 5.9 collective-permute-start
  454.3 5.9 collective-permute-start
  476.9 5.9 collective-permute-start
  482.9 5.1 collective-permute-done
  500.7 5.9 collective-permute-start
  506.6 4.6 collective-permute-done
  523.9 6.2 collective-permute-start
  546.4 6.2 collective-permute-start
  568.2 5.9 collective-permute-start
  589.7 5.9 collective-permute-start
  611.3 5.9 collective-permute-start
  632.8 5.9 collective-permute-start
  654.3 5.9 collective-permute-start
  675.8 5.9 collective-permute-start
  697.4 5.9 collective-permute-start
  718.9 5.9 collective-permute-start
  740.4 5.9 collective-permute-start
  762.0 5.9 collective-permute-start
  783.5 5.9 collective-permute-start
  805.0 5.9 collective-permute-start
  826.5 5.9 collective-permute-start
  848.1 5.9 collective-permute-start
  869.6 5.9 collective-permute-start
  891.1 5.9 collective-permute-start
  913.3 4.9 fusion.12
  918.3 8.4 multiply_convert_fusion
  938.7 49.9 %reduce-scatter.4.cloned.1.call-done = f32[448,1]{1,0:T(8,128)} async-done(((f32[3584,1]{1,0:T(8,128)}), f32[448,1]{1,0:T(8,128)}) %reduce-scatter.4.cloned.1.call-update) | async-done | bytes 1808
  (459 shorter events, 585.8 us)
Async XLA Ops:
  7.2 981.4 %reduce-scatter.4.cloned.1.call-start = ((), (), s32[]{:S(2)}) async-start(), calls=%async_computation.1 | async-start | bytes 2064384
  7.3 6.0 copy-start.8
  16.2 9.0 copy-start.4
  25.2 3.2 copy-start
  32.3 6.6 copy-start.2
  47.0 2.9 copy-start.7
  62.7 12.0 %collective-permute-start = (bf16[32,3584]{1,0:T(8,128)(2,1)S(1)}, bf16[32,3584]{1,0:T(8,128)(2,1)S(1)}, u32[]{:S(2)}, u32[]{:S(2)}) collective-permute-start(bf16[32,3584]{1,0:T(8,128)(2,1)S(1)} %get-tuple-element.376), channel_id=1, source_target_pairs={{8,0},{16,8},{24,16},{32,24},{40,32},{48,40},{56,48},{64,56},{72,6... | collective-permute-start | bytes 688136 | tf_op jit(solution)/shard_map/while/body/eval_jaxpr/ppermute | solution.py:17
  87.3 9.5 collective-permute-start
  109.5 9.2 collective-permute-start
  131.4 8.9 collective-permute-start
  152.9 8.9 collective-permute-start
  174.4 8.9 collective-permute-start
  195.9 8.9 collective-permute-start
  217.5 8.8 collective-permute-start
  239.0 8.9 collective-permute-start
  260.5 8.9 collective-permute-start
  282.1 8.8 collective-permute-start
  303.6 8.9 collective-permute-start
  325.1 8.9 collective-permute-start
  346.7 8.9 collective-permute-start
  368.2 8.9 collective-permute-start
  389.7 8.9 collective-permute-start
  411.3 8.9 collective-permute-start
  432.8 8.9 collective-permute-start
  454.3 10.0 collective-permute-start
  476.9 11.1 %collective-permute-start = (bf16[32,3584]{1,0:T(8,128)(2,1)S(1)}, bf16[32,3584]{1,0:T(8,128)(2,1)S(1)}, u32[]{:S(2)}, u32[]{:S(2)}) collective-permute-start(bf16[32,3584]{1,0:T(8,128)(2,1)S(1)} %get-tuple-element.376), channel_id=1, source_target_pairs={{8,0},{16,8},{24,16},{32,24},{40,32},{48,40},{56,48},{64,56},{72,6... | collective-permute-start | bytes 688136 | tf_op jit(solution)/shard_map/while/body/eval_jaxpr/ppermute | solution.py:17
  500.7 10.5 %collective-permute-start = (bf16[32,3584]{1,0:T(8,128)(2,1)S(1)}, bf16[32,3584]{1,0:T(8,128)(2,1)S(1)}, u32[]{:S(2)}, u32[]{:S(2)}) collective-permute-start(bf16[32,3584]{1,0:T(8,128)(2,1)S(1)} %get-tuple-element.376), channel_id=1, source_target_pairs={{8,0},{16,8},{24,16},{32,24},{40,32},{48,40},{56,48},{64,56},{72,6... | collective-permute-start | bytes 688136 | tf_op jit(solution)/shard_map/while/body/eval_jaxpr/ppermute | solution.py:17
  523.9 9.9 collective-permute-start
  546.4 9.2 collective-permute-start
  568.2 8.9 collective-permute-start
  589.7 8.9 collective-permute-start
  611.3 8.9 collective-permute-start
  632.8 8.9 collective-permute-start
  654.3 8.9 collective-permute-start
  675.8 8.9 collective-permute-start
  697.4 8.9 collective-permute-start
  718.9 8.9 collective-permute-start
  740.4 8.9 collective-permute-start
  762.0 8.9 collective-permute-start
  783.5 8.9 collective-permute-start
  805.0 8.9 collective-permute-start
  826.5 8.9 collective-permute-start
  848.1 8.9 collective-permute-start
  869.6 8.9 collective-permute-start
  891.1 9.6 collective-permute-start
  913.3 4.9 copy-start.1
  918.3 8.4 copy-start.6
  926.7 1.6 copy-start.3
  928.2 2.2 copy-start.5
Sparse Core Ops, SparseCore 0:
  913.3 75.2 reduce-scatter.3

commit v2 on v1

--- a/solution.py
+++ b/solution.py
@@ -70,6 +70,7 @@
     column_blocks = column_blocks.reshape(
         head_count, seq_rows + rows_here, unit_count, rows_here
     ).transpose(2, 0, 1, 3)
+    spare_rows = seq_rows + rows_here
 
     def one_turn(turn_index, carried):
         message, grad_buffer, input_grads = carried
@@ -82,13 +83,11 @@
             section_index == section_count - 1, rows_of(from_loss, first_row, rows_here), message
         )
         incoming = jnp.where(active, incoming, jnp.zeros_like(incoming))
-        grad_buffer = write_rows(grad_buffer, slot, incoming)
+        incoming_heads = incoming.reshape(rows_here, head_count, head_size).transpose(1, 0, 2)
+        grad_buffer = lax.dynamic_update_slice_in_dim(grad_buffer, incoming_heads, slot, 1)
         block = column_blocks[chosen]
         grad_value = jnp.einsum(
-            "hij,ihd->jhd",
-            block,
-            grad_buffer.reshape(seq_rows + rows_here, head_count, head_size),
-            preferred_element_type=jnp.float32,
+            "hij,hid->jhd", block, grad_buffer, preferred_element_type=jnp.float32
         ).reshape(rows_here, feature_count)
         own_normed = rows_of(normed, first_row, rows_here)
         own_inverse = rows_of(inverse, first_row, rows_here)
@@ -102,14 +101,13 @@
 
     initial = (
         jnp.zeros((rows_here, feature_count), jnp.bfloat16),
-        jnp.zeros((seq_rows + rows_here, feature_count), jnp.bfloat16),
-        jnp.zeros((seq_rows + rows_here, feature_count), jnp.bfloat16),
+        jnp.zeros((head_count, spare_rows, head_size), jnp.bfloat16),
+        jnp.zeros((spare_rows, feature_count), jnp.bfloat16),
     )
     _, grad_buffer, input_grads = lax.fori_loop(
         0, unit_count + section_count - 1, one_turn, initial
     )
-    grad_rows = grad_buffer[:seq_rows]
-    grad_heads = grad_rows.reshape(seq_rows, head_count, head_size)
+    grad_heads = grad_buffer[:, :seq_rows].transpose(1, 0, 2)
 
     delta_rows = jnp.einsum("ihd,ihd->hi", grad_heads.astype(jnp.float32), attended)
     grad_weights = jnp.einsum(
@@ -134,7 +132,11 @@
     grad_queries = grad_query.reshape(1, 1, seq_rows, feature_count)
     grad_keys = grad_key.reshape(1, 1, seq_rows, feature_count)
     grad_inputs = input_grads[:seq_rows].reshape(1, 1, seq_rows, feature_count)
-    grad_gains = lax.psum_scatter(gain_sum[None, :], "dp", scatter_dimension=1, tiled=True)
+    group_count = lax.axis_size("dp")
+    gain_parts = lax.all_to_all(
+        gain_sum.reshape(group_count, feature_count // group_count), "dp", 0, 0, tiled=True
+    )
+    grad_gains = jnp.sum(gain_parts, axis=0, keepdims=True)
     return (grad_inputs, grad_queries, grad_keys, grad_gains)
 
 

time: 1010 us -> 771 us (0.76)
  local copies, waits for them, and re-layouts: 247 us -> 82 us
  starting transfers between devices: 234 us -> 282 us
  waiting for transfers between devices: 173 us -> 127 us
  matrix products: 128 us -> 95.1 us
  other arithmetic: 200 us -> 174 us
  between operations: 14.2 us -> 0.82 us
    reshape x78, local copies, waits for them, and re-layouts: 187 us -> 25.6 us  [the longest x39 13.8 us: one_turn(): incoming.reshape(rows_here, head_count, head_size).transpose(1, 0, 2)]
    dynamic_update_slice x78 -> x39, other arithmetic: 141 us -> 75 us  [write_rows(): return lax.dynamic_update_slice_in_dim(buffer, new_rows, first_index, 0)]
    unnamed x2 -> x0, waiting for transfers between devices: 49.9 us -> none
    all_to_all x0 -> x1, starting transfers between devices: none -> 48 us  [on_device(): lax.all_to_all(gain_sum.reshape(group_count, feature_count // group_count...]
    select_n x0 -> x39, other arithmetic: none -> 39.3 us  [one_turn(): incoming = jnp.where(active, incoming, jnp.zeros_like(incoming))]
    dot_general x39, matrix products: 102 us -> 66.3 us  [one_turn(): jnp.einsum('hij,hid->jhd', block, grad_buffer, preferred_element_type=jnp...]
    unnamed x24 -> x29, local copies, waits for them, and re-layouts: 23.3 us -> 20 us
  transfers between devices with their start and end apart: 40 -> 40, of which waited for: 40 -> 39; matrix products, arithmetic and copies ran while one was open for 2% -> 3% of each run, Pallas kernels for 0% -> 0%
where the time goes in v2:
time: 771 us; the launch traced here: 764 us
  starting transfers between devices  282 us (37%)
  other arithmetic  174 us (23%)
  waiting for transfers between devices  127 us (16%)
  matrix products  95.1 us (12%)
  local copies, waits for them, and re-layouts  82 us (11%)
    ppermute x39, starting transfers between devices, passed_along(): lax.ppermute(value, axis, [(source, source + steps) for source in range(l...  234 us
    ppermute x39, waiting for transfers between devices, passed_along(): lax.ppermute(value, axis, [(source, source + steps) for source in range(l...  127 us
    dynamic_update_slice x39, other arithmetic, write_rows(): return lax.dynamic_update_slice_in_dim(buffer, new_rows, first_index, 0)  75 us
    dot_general x39, matrix products, one_turn(): jnp.einsum('hij,hid->jhd', block, grad_buffer, preferred_element_type=jnp...  66.3 us
    all_to_all x1, starting transfers between devices, on_device(): lax.all_to_all(gain_sum.reshape(group_count, feature_count // group_count...  48 us
    reduce_sum x39, other arithmetic, one_turn(): jnp.mean(grad_normed * own_normed, axis=-1, keepdims=True)  46 us
    select_n x39, other arithmetic, one_turn(): incoming = jnp.where(active, incoming, jnp.zeros_like(incoming))  39.3 us
    unnamed x29, local copies, waits for them, and re-layouts  20 us
  transfers between devices with their start and end apart: 40, of which 39 were waited for; matrix products, arithmetic and copies ran while one was open for 3% of the time, Pallas kernels for 0%

profile of v2, /device:TPU:15, one launch (start us, length us, event | category | flops | bytes accessed | tf_op | source)
XLA Modules:
  0.0 764.3 jit_solution(6668786661843744549)
XLA Ops:
  2.8 4.0 copy.37
  12.1 5.4 fusion.15
  20.7 3.8 fusion.4
  24.5 6.6 copy.48
  33.5 5.8 pad.4.clone
  41.0 638.8 %while.19 = (s32[]{:T(128)}, bf16[32,3584]{1,0:T(8,128)(2,1)S(1)}, bf16[32,288,112]{2,1,0:T(8,128)(2,1)S(1)}, bf16[288,3584]{1,0:T(8,128)(2,1)}, s32[]{:T(128)},...) while((s32[]{:T(128)}, bf16[32,3584]{1,0:T(8,128)(2,1)S(1)}, ...), condition=%wide.region_5.6_spmd, body=%wide.region_3.5_spmd.sunk | while | flops 67436560 | bytes 11232565 | solution.py:107
  48.2 7.7 %collective-permute-start = (bf16[32,3584]{1,0:T(8,128)(2,1)S(1)}, bf16[32,3584]{1,0:T(8,128)(2,1)S(1)}, u32[]{:S(2)}, u32[]{:S(2)}) collective-permute-start(bf16[32,3584]{1,0:T(8,128)(2,1)S(1)} %get-tuple-element.376), channel_id=1, source_target_pairs={{8,0},{16,8},{24,16},{32,24},{40,32},{48,40},{56,48},{64,56},{72,6... | collective-permute-start | bytes 688136 | tf_op jit(solution)/shard_map/while/body/eval_jaxpr/ppermute | solution.py:17
  55.9 4.2 collective-permute-done
  67.2 6.2 collective-permute-start
  73.4 3.3 collective-permute-done
  83.8 6.2 collective-permute-start
  90.0 2.9 collective-permute-done
  100.0 5.9 collective-permute-start
  106.0 2.9 collective-permute-done
  116.0 5.9 collective-permute-start
  121.9 2.9 collective-permute-done
  132.0 5.9 collective-permute-start
  147.9 5.9 collective-permute-start
  163.9 5.9 collective-permute-start
  179.8 5.9 collective-permute-start
  195.8 5.9 collective-permute-start
  211.7 5.9 collective-permute-start
  227.6 5.9 collective-permute-start
  243.6 5.9 collective-permute-start
  259.5 5.9 collective-permute-start
  265.5 3.9 collective-permute-done
  276.4 5.9 collective-permute-start
  282.3 5.0 collective-permute-done
  294.4 5.9 collective-permute-start
  300.3 4.6 collective-permute-done
  312.0 6.2 collective-permute-start
  318.2 3.7 collective-permute-done
  329.0 6.2 collective-permute-start
  345.2 5.9 collective-permute-start
  361.2 5.9 collective-permute-start
  377.1 5.9 collective-permute-start
  393.1 5.9 collective-permute-start
  409.1 5.9 collective-permute-start
  425.0 5.9 collective-permute-start
  440.9 5.9 collective-permute-start
  456.9 5.9 collective-permute-start
  472.8 5.9 collective-permute-start
  488.8 5.9 collective-permute-start
  504.8 5.9 collective-permute-start
  510.7 3.6 collective-permute-done
  521.4 5.9 collective-permute-start
  527.3 4.6 collective-permute-done
  539.0 5.9 collective-permute-start
  544.9 5.0 collective-permute-done
  557.0 6.2 collective-permute-start
  563.2 4.1 collective-permute-done
  574.4 6.2 collective-permute-start
  580.6 3.2 collective-permute-done
  590.9 6.2 collective-permute-start
  607.2 5.9 collective-permute-start
  623.1 5.9 collective-permute-start
  639.1 5.9 collective-permute-start
  655.1 5.9 collective-permute-start
  671.0 5.9 collective-permute-start
  682.5 4.9 fusion.5
  688.1 48.0 %all-to-all-start = ((f32[8,1,448]{2,1,0:T(1,128)}), f32[8,1,448]{2,1,0:T(1,128)S(1)}, u32[]{:S(2)}, u32[]{:S(2)}) async-start(f32[8,1,448]{2,1,0:T(1,128)} %all_to_all.6), calls=%async_computation | async-start | bytes 32768 | tf_op jit(solution)/shard_map/all_to_all | solution.py:136
  736.2 5.4 fusion.6
  741.9 8.4 %multiply_convert_fusion = bf16[32,256,256]{2,1,0:T(8,128)(2,1)S(1)} fusion(f32[32,256,256]{2,1,0:T(8,128)} %copy-done.1, f32[32,256]{1,0:T(8,128)S(1)} %fusion.6, f32[32,256]{1,0:T(8,128)S(1)} %log_add_fusion, pred[256,256]{1,0:T(8,128)(4,1)S(1)} %get-tuple-element.305, pred[256,256]{1,0:T(8,128)(4,1)S(1)} %get-tuple-element.306, ...), kind=kOutput, calls=%fused_computation.12 | convolution fusion | flops 487194624 | bytes 18302464 | tf_op jit(solution)/shard_map/ihd,jhd->hij/dot_general | solution.py:113
  757.2 3.9 copy.39
  (580 shorter events, 376.0 us)
Async XLA Ops:
  0.7 6.1 copy-start.12
  0.8 6.1 copy-start.10
  12.1 5.4 copy-start.6
  17.5 3.2 copy-start.1
  24.5 6.6 copy-start.3
  42.1 2.2 copy-start
  48.2 12.0 %collective-permute-start = (bf16[32,3584]{1,0:T(8,128)(2,1)S(1)}, bf16[32,3584]{1,0:T(8,128)(2,1)S(1)}, u32[]{:S(2)}, u32[]{:S(2)}) collective-permute-start(bf16[32,3584]{1,0:T(8,128)(2,1)S(1)} %get-tuple-element.376), channel_id=1, source_target_pairs={{8,0},{16,8},{24,16},{32,24},{40,32},{48,40},{56,48},{64,56},{72,6... | collective-permute-start | bytes 688136 | tf_op jit(solution)/shard_map/while/body/eval_jaxpr/ppermute | solution.py:17
  67.2 9.5 %collective-permute-start = (bf16[32,3584]{1,0:T(8,128)(2,1)S(1)}, bf16[32,3584]{1,0:T(8,128)(2,1)S(1)}, u32[]{:S(2)}, u32[]{:S(2)}) collective-permute-start(bf16[32,3584]{1,0:T(8,128)(2,1)S(1)} %get-tuple-element.376), channel_id=1, source_target_pairs={{8,0},{16,8},{24,16},{32,24},{40,32},{48,40},{56,48},{64,56},{72,6... | collective-permute-start | bytes 688136 | tf_op jit(solution)/shard_map/while/body/eval_jaxpr/ppermute | solution.py:17
  77.7 2.2 copy-start
  83.8 9.2 %collective-permute-start = (bf16[32,3584]{1,0:T(8,128)(2,1)S(1)}, bf16[32,3584]{1,0:T(8,128)(2,1)S(1)}, u32[]{:S(2)}, u32[]{:S(2)}) collective-permute-start(bf16[32,3584]{1,0:T(8,128)(2,1)S(1)} %get-tuple-element.376), channel_id=1, source_target_pairs={{8,0},{16,8},{24,16},{32,24},{40,32},{48,40},{56,48},{64,56},{72,6... | collective-permute-start | bytes 688136 | tf_op jit(solution)/shard_map/while/body/eval_jaxpr/ppermute | solution.py:17
  100.0 8.9 %collective-permute-start = (bf16[32,3584]{1,0:T(8,128)(2,1)S(1)}, bf16[32,3584]{1,0:T(8,128)(2,1)S(1)}, u32[]{:S(2)}, u32[]{:S(2)}) collective-permute-start(bf16[32,3584]{1,0:T(8,128)(2,1)S(1)} %get-tuple-element.376), channel_id=1, source_target_pairs={{8,0},{16,8},{24,16},{32,24},{40,32},{48,40},{56,48},{64,56},{72,6... | collective-permute-start | bytes 688136 | tf_op jit(solution)/shard_map/while/body/eval_jaxpr/ppermute | solution.py:17
  109.9 2.2 copy-start
  116.0 8.9 %collective-permute-start = (bf16[32,3584]{1,0:T(8,128)(2,1)S(1)}, bf16[32,3584]{1,0:T(8,128)(2,1)S(1)}, u32[]{:S(2)}, u32[]{:S(2)}) collective-permute-start(bf16[32,3584]{1,0:T(8,128)(2,1)S(1)} %get-tuple-element.376), channel_id=1, source_target_pairs={{8,0},{16,8},{24,16},{32,24},{40,32},{48,40},{56,48},{64,56},{72,6... | collective-permute-start | bytes 688136 | tf_op jit(solution)/shard_map/while/body/eval_jaxpr/ppermute | solution.py:17
  132.0 8.9 %collective-permute-start = (bf16[32,3584]{1,0:T(8,128)(2,1)S(1)}, bf16[32,3584]{1,0:T(8,128)(2,1)S(1)}, u32[]{:S(2)}, u32[]{:S(2)}) collective-permute-start(bf16[32,3584]{1,0:T(8,128)(2,1)S(1)} %get-tuple-element.376), channel_id=1, source_target_pairs={{8,0},{16,8},{24,16},{32,24},{40,32},{48,40},{56,48},{64,56},{72,6... | collective-permute-start | bytes 688136 | tf_op jit(solution)/shard_map/while/body/eval_jaxpr/ppermute | solution.py:17
  147.9 8.9 %collective-permute-start = (bf16[32,3584]{1,0:T(8,128)(2,1)S(1)}, bf16[32,3584]{1,0:T(8,128)(2,1)S(1)}, u32[]{:S(2)}, u32[]{:S(2)}) collective-permute-start(bf16[32,3584]{1,0:T(8,128)(2,1)S(1)} %get-tuple-element.376), channel_id=1, source_target_pairs={{8,0},{16,8},{24,16},{32,24},{40,32},{48,40},{56,48},{64,56},{72,6... | collective-permute-start | bytes 688136 | tf_op jit(solution)/shard_map/while/body/eval_jaxpr/ppermute | solution.py:17
  157.8 2.2 copy-start
  163.9 8.9 %collective-permute-start = (bf16[32,3584]{1,0:T(8,128)(2,1)S(1)}, bf16[32,3584]{1,0:T(8,128)(2,1)S(1)}, u32[]{:S(2)}, u32[]{:S(2)}) collective-permute-start(bf16[32,3584]{1,0:T(8,128)(2,1)S(1)} %get-tuple-element.376), channel_id=1, source_target_pairs={{8,0},{16,8},{24,16},{32,24},{40,32},{48,40},{56,48},{64,56},{72,6... | collective-permute-start | bytes 688136 | tf_op jit(solution)/shard_map/while/body/eval_jaxpr/ppermute | solution.py:17
  179.8 8.9 %collective-permute-start = (bf16[32,3584]{1,0:T(8,128)(2,1)S(1)}, bf16[32,3584]{1,0:T(8,128)(2,1)S(1)}, u32[]{:S(2)}, u32[]{:S(2)}) collective-permute-start(bf16[32,3584]{1,0:T(8,128)(2,1)S(1)} %get-tuple-element.376), channel_id=1, source_target_pairs={{8,0},{16,8},{24,16},{32,24},{40,32},{48,40},{56,48},{64,56},{72,6... | collective-permute-start | bytes 688136 | tf_op jit(solution)/shard_map/while/body/eval_jaxpr/ppermute | solution.py:17
  189.7 2.2 copy-start
  195.8 8.9 %collective-permute-start = (bf16[32,3584]{1,0:T(8,128)(2,1)S(1)}, bf16[32,3584]{1,0:T(8,128)(2,1)S(1)}, u32[]{:S(2)}, u32[]{:S(2)}) collective-permute-start(bf16[32,3584]{1,0:T(8,128)(2,1)S(1)} %get-tuple-element.376), channel_id=1, source_target_pairs={{8,0},{16,8},{24,16},{32,24},{40,32},{48,40},{56,48},{64,56},{72,6... | collective-permute-start | bytes 688136 | tf_op jit(solution)/shard_map/while/body/eval_jaxpr/ppermute | solution.py:17
  211.7 8.9 %collective-permute-start = (bf16[32,3584]{1,0:T(8,128)(2,1)S(1)}, bf16[32,3584]{1,0:T(8,128)(2,1)S(1)}, u32[]{:S(2)}, u32[]{:S(2)}) collective-permute-start(bf16[32,3584]{1,0:T(8,128)(2,1)S(1)} %get-tuple-element.376), channel_id=1, source_target_pairs={{8,0},{16,8},{24,16},{32,24},{40,32},{48,40},{56,48},{64,56},{72,6... | collective-permute-start | bytes 688136 | tf_op jit(solution)/shard_map/while/body/eval_jaxpr/ppermute | solution.py:17
  227.6 8.9 %collective-permute-start = (bf16[32,3584]{1,0:T(8,128)(2,1)S(1)}, bf16[32,3584]{1,0:T(8,128)(2,1)S(1)}, u32[]{:S(2)}, u32[]{:S(2)}) collective-permute-start(bf16[32,3584]{1,0:T(8,128)(2,1)S(1)} %get-tuple-element.376), channel_id=1, source_target_pairs={{8,0},{16,8},{24,16},{32,24},{40,32},{48,40},{56,48},{64,56},{72,6... | collective-permute-start | bytes 688136 | tf_op jit(solution)/shard_map/while/body/eval_jaxpr/ppermute | solution.py:17
  237.5 2.2 copy-start
  243.6 8.8 %collective-permute-start = (bf16[32,3584]{1,0:T(8,128)(2,1)S(1)}, bf16[32,3584]{1,0:T(8,128)(2,1)S(1)}, u32[]{:S(2)}, u32[]{:S(2)}) collective-permute-start(bf16[32,3584]{1,0:T(8,128)(2,1)S(1)} %get-tuple-element.376), channel_id=1, source_target_pairs={{8,0},{16,8},{24,16},{32,24},{40,32},{48,40},{56,48},{64,56},{72,6... | collective-permute-start | bytes 688136 | tf_op jit(solution)/shard_map/while/body/eval_jaxpr/ppermute | solution.py:17
  253.5 2.2 copy-start
  259.5 9.8 %collective-permute-start = (bf16[32,3584]{1,0:T(8,128)(2,1)S(1)}, bf16[32,3584]{1,0:T(8,128)(2,1)S(1)}, u32[]{:S(2)}, u32[]{:S(2)}) collective-permute-start(bf16[32,3584]{1,0:T(8,128)(2,1)S(1)} %get-tuple-element.376), channel_id=1, source_target_pairs={{8,0},{16,8},{24,16},{32,24},{40,32},{48,40},{56,48},{64,56},{72,6... | collective-permute-start | bytes 688136 | tf_op jit(solution)/shard_map/while/body/eval_jaxpr/ppermute | solution.py:17
  276.4 10.9 %collective-permute-start = (bf16[32,3584]{1,0:T(8,128)(2,1)S(1)}, bf16[32,3584]{1,0:T(8,128)(2,1)S(1)}, u32[]{:S(2)}, u32[]{:S(2)}) collective-permute-start(bf16[32,3584]{1,0:T(8,128)(2,1)S(1)} %get-tuple-element.376), channel_id=1, source_target_pairs={{8,0},{16,8},{24,16},{32,24},{40,32},{48,40},{56,48},{64,56},{72,6... | collective-permute-start | bytes 688136 | tf_op jit(solution)/shard_map/while/body/eval_jaxpr/ppermute | solution.py:17
  294.4 10.5 %collective-permute-start = (bf16[32,3584]{1,0:T(8,128)(2,1)S(1)}, bf16[32,3584]{1,0:T(8,128)(2,1)S(1)}, u32[]{:S(2)}, u32[]{:S(2)}) collective-permute-start(bf16[32,3584]{1,0:T(8,128)(2,1)S(1)} %get-tuple-element.376), channel_id=1, source_target_pairs={{8,0},{16,8},{24,16},{32,24},{40,32},{48,40},{56,48},{64,56},{72,6... | collective-permute-start | bytes 688136 | tf_op jit(solution)/shard_map/while/body/eval_jaxpr/ppermute | solution.py:17
  312.0 9.9 %collective-permute-start = (bf16[32,3584]{1,0:T(8,128)(2,1)S(1)}, bf16[32,3584]{1,0:T(8,128)(2,1)S(1)}, u32[]{:S(2)}, u32[]{:S(2)}) collective-permute-start(bf16[32,3584]{1,0:T(8,128)(2,1)S(1)} %get-tuple-element.376), channel_id=1, source_target_pairs={{8,0},{16,8},{24,16},{32,24},{40,32},{48,40},{56,48},{64,56},{72,6... | collective-permute-start | bytes 688136 | tf_op jit(solution)/shard_map/while/body/eval_jaxpr/ppermute | solution.py:17
  329.0 9.2 %collective-permute-start = (bf16[32,3584]{1,0:T(8,128)(2,1)S(1)}, bf16[32,3584]{1,0:T(8,128)(2,1)S(1)}, u32[]{:S(2)}, u32[]{:S(2)}) collective-permute-start(bf16[32,3584]{1,0:T(8,128)(2,1)S(1)} %get-tuple-element.376), channel_id=1, source_target_pairs={{8,0},{16,8},{24,16},{32,24},{40,32},{48,40},{56,48},{64,56},{72,6... | collective-permute-start | bytes 688136 | tf_op jit(solution)/shard_map/while/body/eval_jaxpr/ppermute | solution.py:17
  339.1 2.2 copy-start
  345.2 8.9 %collective-permute-start = (bf16[32,3584]{1,0:T(8,128)(2,1)S(1)}, bf16[32,3584]{1,0:T(8,128)(2,1)S(1)}, u32[]{:S(2)}, u32[]{:S(2)}) collective-permute-start(bf16[32,3584]{1,0:T(8,128)(2,1)S(1)} %get-tuple-element.376), channel_id=1, source_target_pairs={{8,0},{16,8},{24,16},{32,24},{40,32},{48,40},{56,48},{64,56},{72,6... | collective-permute-start | bytes 688136 | tf_op jit(solution)/shard_map/while/body/eval_jaxpr/ppermute | solution.py:17
  361.2 8.9 %collective-permute-start = (bf16[32,3584]{1,0:T(8,128)(2,1)S(1)}, bf16[32,3584]{1,0:T(8,128)(2,1)S(1)}, u32[]{:S(2)}, u32[]{:S(2)}) collective-permute-start(bf16[32,3584]{1,0:T(8,128)(2,1)S(1)} %get-tuple-element.376), channel_id=1, source_target_pairs={{8,0},{16,8},{24,16},{32,24},{40,32},{48,40},{56,48},{64,56},{72,6... | collective-permute-start | bytes 688136 | tf_op jit(solution)/shard_map/while/body/eval_jaxpr/ppermute | solution.py:17
  377.1 8.9 %collective-permute-start = (bf16[32,3584]{1,0:T(8,128)(2,1)S(1)}, bf16[32,3584]{1,0:T(8,128)(2,1)S(1)}, u32[]{:S(2)}, u32[]{:S(2)}) collective-permute-start(bf16[32,3584]{1,0:T(8,128)(2,1)S(1)} %get-tuple-element.376), channel_id=1, source_target_pairs={{8,0},{16,8},{24,16},{32,24},{40,32},{48,40},{56,48},{64,56},{72,6... | collective-permute-start | bytes 688136 | tf_op jit(solution)/shard_map/while/body/eval_jaxpr/ppermute | solution.py:17
  387.0 2.2 copy-start
  393.1 8.9 %collective-permute-start = (bf16[32,3584]{1,0:T(8,128)(2,1)S(1)}, bf16[32,3584]{1,0:T(8,128)(2,1)S(1)}, u32[]{:S(2)}, u32[]{:S(2)}) collective-permute-start(bf16[32,3584]{1,0:T(8,128)(2,1)S(1)} %get-tuple-element.376), channel_id=1, source_target_pairs={{8,0},{16,8},{24,16},{32,24},{40,32},{48,40},{56,48},{64,56},{72,6... | collective-permute-start | bytes 688136 | tf_op jit(solution)/shard_map/while/body/eval_jaxpr/ppermute | solution.py:17
  409.1 8.9 %collective-permute-start = (bf16[32,3584]{1,0:T(8,128)(2,1)S(1)}, bf16[32,3584]{1,0:T(8,128)(2,1)S(1)}, u32[]{:S(2)}, u32[]{:S(2)}) collective-permute-start(bf16[32,3584]{1,0:T(8,128)(2,1)S(1)} %get-tuple-element.376), channel_id=1, source_target_pairs={{8,0},{16,8},{24,16},{32,24},{40,32},{48,40},{56,48},{64,56},{72,6... | collective-permute-start | bytes 688136 | tf_op jit(solution)/shard_map/while/body/eval_jaxpr/ppermute | solution.py:17
  425.0 8.9 %collective-permute-start = (bf16[32,3584]{1,0:T(8,128)(2,1)S(1)}, bf16[32,3584]{1,0:T(8,128)(2,1)S(1)}, u32[]{:S(2)}, u32[]{:S(2)}) collective-permute-start(bf16[32,3584]{1,0:T(8,128)(2,1)S(1)} %get-tuple-element.376), channel_id=1, source_target_pairs={{8,0},{16,8},{24,16},{32,24},{40,32},{48,40},{56,48},{64,56},{72,6... | collective-permute-start | bytes 688136 | tf_op jit(solution)/shard_map/while/body/eval_jaxpr/ppermute | solution.py:17
  434.8 2.2 copy-start
  440.9 8.9 %collective-permute-start = (bf16[32,3584]{1,0:T(8,128)(2,1)S(1)}, bf16[32,3584]{1,0:T(8,128)(2,1)S(1)}, u32[]{:S(2)}, u32[]{:S(2)}) collective-permute-start(bf16[32,3584]{1,0:T(8,128)(2,1)S(1)} %get-tuple-element.376), channel_id=1, source_target_pairs={{8,0},{16,8},{24,16},{32,24},{40,32},{48,40},{56,48},{64,56},{72,6... | collective-permute-start | bytes 688136 | tf_op jit(solution)/shard_map/while/body/eval_jaxpr/ppermute | solution.py:17
  456.9 8.9 %collective-permute-start = (bf16[32,3584]{1,0:T(8,128)(2,1)S(1)}, bf16[32,3584]{1,0:T(8,128)(2,1)S(1)}, u32[]{:S(2)}, u32[]{:S(2)}) collective-permute-start(bf16[32,3584]{1,0:T(8,128)(2,1)S(1)} %get-tuple-element.376), channel_id=1, source_target_pairs={{8,0},{16,8},{24,16},{32,24},{40,32},{48,40},{56,48},{64,56},{72,6... | collective-permute-start | bytes 688136 | tf_op jit(solution)/shard_map/while/body/eval_jaxpr/ppermute | solution.py:17
  472.8 8.9 %collective-permute-start = (bf16[32,3584]{1,0:T(8,128)(2,1)S(1)}, bf16[32,3584]{1,0:T(8,128)(2,1)S(1)}, u32[]{:S(2)}, u32[]{:S(2)}) collective-permute-start(bf16[32,3584]{1,0:T(8,128)(2,1)S(1)} %get-tuple-element.376), channel_id=1, source_target_pairs={{8,0},{16,8},{24,16},{32,24},{40,32},{48,40},{56,48},{64,56},{72,6... | collective-permute-start | bytes 688136 | tf_op jit(solution)/shard_map/while/body/eval_jaxpr/ppermute | solution.py:17
  482.7 2.2 copy-start
  488.8 8.9 %collective-permute-start = (bf16[32,3584]{1,0:T(8,128)(2,1)S(1)}, bf16[32,3584]{1,0:T(8,128)(2,1)S(1)}, u32[]{:S(2)}, u32[]{:S(2)}) collective-permute-start(bf16[32,3584]{1,0:T(8,128)(2,1)S(1)} %get-tuple-element.376), channel_id=1, source_target_pairs={{8,0},{16,8},{24,16},{32,24},{40,32},{48,40},{56,48},{64,56},{72,6... | collective-permute-start | bytes 688136 | tf_op jit(solution)/shard_map/while/body/eval_jaxpr/ppermute | solution.py:17
  504.8 9.5 %collective-permute-start = (bf16[32,3584]{1,0:T(8,128)(2,1)S(1)}, bf16[32,3584]{1,0:T(8,128)(2,1)S(1)}, u32[]{:S(2)}, u32[]{:S(2)}) collective-permute-start(bf16[32,3584]{1,0:T(8,128)(2,1)S(1)} %get-tuple-element.376), channel_id=1, source_target_pairs={{8,0},{16,8},{24,16},{32,24},{40,32},{48,40},{56,48},{64,56},{72,6... | collective-permute-start | bytes 688136 | tf_op jit(solution)/shard_map/while/body/eval_jaxpr/ppermute | solution.py:17
  521.4 10.6 %collective-permute-start = (bf16[32,3584]{1,0:T(8,128)(2,1)S(1)}, bf16[32,3584]{1,0:T(8,128)(2,1)S(1)}, u32[]{:S(2)}, u32[]{:S(2)}) collective-permute-start(bf16[32,3584]{1,0:T(8,128)(2,1)S(1)} %get-tuple-element.376), channel_id=1, source_target_pairs={{8,0},{16,8},{24,16},{32,24},{40,32},{48,40},{56,48},{64,56},{72,6... | collective-permute-start | bytes 688136 | tf_op jit(solution)/shard_map/while/body/eval_jaxpr/ppermute | solution.py:17
  539.0 10.9 %collective-permute-start = (bf16[32,3584]{1,0:T(8,128)(2,1)S(1)}, bf16[32,3584]{1,0:T(8,128)(2,1)S(1)}, u32[]{:S(2)}, u32[]{:S(2)}) collective-permute-start(bf16[32,3584]{1,0:T(8,128)(2,1)S(1)} %get-tuple-element.376), channel_id=1, source_target_pairs={{8,0},{16,8},{24,16},{32,24},{40,32},{48,40},{56,48},{64,56},{72,6... | collective-permute-start | bytes 688136 | tf_op jit(solution)/shard_map/while/body/eval_jaxpr/ppermute | solution.py:17
  557.0 10.3 %collective-permute-start = (bf16[32,3584]{1,0:T(8,128)(2,1)S(1)}, bf16[32,3584]{1,0:T(8,128)(2,1)S(1)}, u32[]{:S(2)}, u32[]{:S(2)}) collective-permute-start(bf16[32,3584]{1,0:T(8,128)(2,1)S(1)} %get-tuple-element.376), channel_id=1, source_target_pairs={{8,0},{16,8},{24,16},{32,24},{40,32},{48,40},{56,48},{64,56},{72,6... | collective-permute-start | bytes 688136 | tf_op jit(solution)/shard_map/while/body/eval_jaxpr/ppermute | solution.py:17
  568.3 2.2 copy-start
  574.4 9.4 %collective-permute-start = (bf16[32,3584]{1,0:T(8,128)(2,1)S(1)}, bf16[32,3584]{1,0:T(8,128)(2,1)S(1)}, u32[]{:S(2)}, u32[]{:S(2)}) collective-permute-start(bf16[32,3584]{1,0:T(8,128)(2,1)S(1)} %get-tuple-element.376), channel_id=1, source_target_pairs={{8,0},{16,8},{24,16},{32,24},{40,32},{48,40},{56,48},{64,56},{72,6... | collective-permute-start | bytes 688136 | tf_op jit(solution)/shard_map/while/body/eval_jaxpr/ppermute | solution.py:17
  584.8 2.2 copy-start
  590.9 9.2 %collective-permute-start = (bf16[32,3584]{1,0:T(8,128)(2,1)S(1)}, bf16[32,3584]{1,0:T(8,128)(2,1)S(1)}, u32[]{:S(2)}, u32[]{:S(2)}) collective-permute-start(bf16[32,3584]{1,0:T(8,128)(2,1)S(1)} %get-tuple-element.376), channel_id=1, source_target_pairs={{8,0},{16,8},{24,16},{32,24},{40,32},{48,40},{56,48},{64,56},{72,6... | collective-permute-start | bytes 688136 | tf_op jit(solution)/shard_map/while/body/eval_jaxpr/ppermute | solution.py:17
  607.2 8.9 %collective-permute-start = (bf16[32,3584]{1,0:T(8,128)(2,1)S(1)}, bf16[32,3584]{1,0:T(8,128)(2,1)S(1)}, u32[]{:S(2)}, u32[]{:S(2)}) collective-permute-start(bf16[32,3584]{1,0:T(8,128)(2,1)S(1)} %get-tuple-element.376), channel_id=1, source_target_pairs={{8,0},{16,8},{24,16},{32,24},{40,32},{48,40},{56,48},{64,56},{72,6... | collective-permute-start | bytes 688136 | tf_op jit(solution)/shard_map/while/body/eval_jaxpr/ppermute | solution.py:17
  623.1 8.9 %collective-permute-start = (bf16[32,3584]{1,0:T(8,128)(2,1)S(1)}, bf16[32,3584]{1,0:T(8,128)(2,1)S(1)}, u32[]{:S(2)}, u32[]{:S(2)}) collective-permute-start(bf16[32,3584]{1,0:T(8,128)(2,1)S(1)} %get-tuple-element.376), channel_id=1, source_target_pairs={{8,0},{16,8},{24,16},{32,24},{40,32},{48,40},{56,48},{64,56},{72,6... | collective-permute-start | bytes 688136 | tf_op jit(solution)/shard_map/while/body/eval_jaxpr/ppermute | solution.py:17
  633.0 2.2 copy-start
  639.1 8.9 %collective-permute-start = (bf16[32,3584]{1,0:T(8,128)(2,1)S(1)}, bf16[32,3584]{1,0:T(8,128)(2,1)S(1)}, u32[]{:S(2)}, u32[]{:S(2)}) collective-permute-start(bf16[32,3584]{1,0:T(8,128)(2,1)S(1)} %get-tuple-element.376), channel_id=1, source_target_pairs={{8,0},{16,8},{24,16},{32,24},{40,32},{48,40},{56,48},{64,56},{72,6... | collective-permute-start | bytes 688136 | tf_op jit(solution)/shard_map/while/body/eval_jaxpr/ppermute | solution.py:17
  655.1 8.9 %collective-permute-start = (bf16[32,3584]{1,0:T(8,128)(2,1)S(1)}, bf16[32,3584]{1,0:T(8,128)(2,1)S(1)}, u32[]{:S(2)}, u32[]{:S(2)}) collective-permute-start(bf16[32,3584]{1,0:T(8,128)(2,1)S(1)} %get-tuple-element.376), channel_id=1, source_target_pairs={{8,0},{16,8},{24,16},{32,24},{40,32},{48,40},{56,48},{64,56},{72,6... | collective-permute-start | bytes 688136 | tf_op jit(solution)/shard_map/while/body/eval_jaxpr/ppermute | solution.py:17
  671.0 8.9 %collective-permute-start = (bf16[32,3584]{1,0:T(8,128)(2,1)S(1)}, bf16[32,3584]{1,0:T(8,128)(2,1)S(1)}, u32[]{:S(2)}, u32[]{:S(2)}) collective-permute-start(bf16[32,3584]{1,0:T(8,128)(2,1)S(1)} %get-tuple-element.376), channel_id=1, source_target_pairs={{8,0},{16,8},{24,16},{32,24},{40,32},{48,40},{56,48},{64,56},{72,6... | collective-permute-start | bytes 688136 | tf_op jit(solution)/shard_map/while/body/eval_jaxpr/ppermute | solution.py:17
  688.1 75.6 %all-to-all-start = ((f32[8,1,448]{2,1,0:T(1,128)}), f32[8,1,448]{2,1,0:T(1,128)S(1)}, u32[]{:S(2)}, u32[]{:S(2)}) async-start(f32[8,1,448]{2,1,0:T(1,128)} %all_to_all.6), calls=%async_computation | async-start | bytes 32768 | tf_op jit(solution)/shard_map/all_to_all | solution.py:136
  736.2 5.5 copy-start.2
  736.2 5.7 copy-start.4
  741.9 8.4 %copy-start.8 = (bf16[1,1,256,3584]{2,3,1,0:T(8,128)(2,1)S(1)}, bf16[1,1,256,3584]{2,3,1,0:T(8,128)(2,1)}, u32[]{:S(2)}) copy-start(bf16[1,1,256,3584]{2,3,1,0:T(8,128)(2,1)} %copy.33) | copy-start | bytes 5505028
  750.3 2.7 copy-start.5
  757.2 3.9 copy-start.9
  (27 other events, 59.1 us)

commit v3 on v2

--- a/solution.py
+++ b/solution.py
@@ -1,6 +1,11 @@
+import functools
+import math
+
 import jax
 import jax.numpy as jnp
 from jax import lax
+from jax.experimental import pallas as pl
+from jax.experimental.pallas import tpu as pltpu
 from jax.sharding import PartitionSpec as P
 
 GROUPS = 8
@@ -23,6 +28,92 @@
 
 def write_rows(buffer, first_index, new_rows):
     return lax.dynamic_update_slice_in_dim(buffer, new_rows, first_index, 0)
+
+
+def turn_kernel(
+    flags_ref,
+    w_ref, wd_ref, g_ref, msg_ref, loss_ref, normed_ref, inv_ref, gain_ref,
+    out_ref, inc_ref,
+    gn_s, acc_s,
+    *, group_lanes, head_size, rows_here, groups, feature_count,
+):
+    g = pl.program_id(0)
+    from_loss = flags_ref[1] == 1
+    active = flags_ref[2] == 1
+
+    @pl.when(g == 0)
+    def _():
+        inc = jnp.where(from_loss, loss_ref[...], msg_ref[...])
+        inc = jnp.where(active, inc, jnp.zeros_like(inc))
+        inc_ref[...] = inc
+        acc_s[...] = jnp.zeros_like(acc_s)
+
+    lanes = pl.ds(pl.multiple_of(g * group_lanes, 128), group_lanes)
+    inc_g = inc_ref[:, lanes]
+    stacked = jnp.dot(w_ref[0, 0], g_ref[...], preferred_element_type=jnp.float32)
+    stacked = stacked + jnp.dot(wd_ref[0, 0], inc_g, preferred_element_type=jnp.float32)
+    lane_head = lax.broadcasted_iota(jnp.int32, (rows_here, group_lanes), 1) // head_size
+    value = jnp.zeros((rows_here, group_lanes), jnp.float32)
+    for k in range(group_lanes // head_size):
+        value = value + jnp.where(
+            lane_head == k, stacked[k * rows_here:(k + 1) * rows_here, :], 0.0
+        )
+    grad_normed = value * gain_ref[:, lanes]
+    gn_s[g] = grad_normed
+    acc_s[...] += jnp.sum(grad_normed * normed_ref[:, lanes], axis=1, keepdims=True)
+
+    @pl.when(g == groups - 1)
+    def _():
+        mean = acc_s[...] * (1.0 / feature_count)
+        inv = inv_ref[...]
+        for k in range(groups):
+            cols = slice(k * group_lanes, (k + 1) * group_lanes)
+            out_ref[:, cols] = (
+                inc_ref[:, cols].astype(jnp.float32)
+                + inv * (gn_s[k] - normed_ref[:, cols] * mean)
+            ).astype(out_ref.dtype)
+
+
+def turn_call(flags, w_blocks, w_diag, grad_buffer, message, from_loss, normed, inverse, gain,
+              *, head_size, rows_here):
+    unit_count, groups, stack_rows, spare_rows = w_blocks.shape
+    feature_count = grad_buffer.shape[1]
+    group_lanes = feature_count // groups
+    kernel = functools.partial(
+        turn_kernel, group_lanes=group_lanes, head_size=head_size, rows_here=rows_here,
+        groups=groups, feature_count=feature_count,
+    )
+    grid_spec = pltpu.PrefetchScalarGridSpec(
+        num_scalar_prefetch=1,
+        grid=(groups,),
+        in_specs=[
+            pl.BlockSpec((1, 1, stack_rows, spare_rows), lambda g, f: (f[0], g, 0, 0)),
+            pl.BlockSpec((1, 1, stack_rows, rows_here), lambda g, f: (f[0], g, 0, 0)),
+            pl.BlockSpec((spare_rows, group_lanes), lambda g, f: (0, g)),
+            pl.BlockSpec((rows_here, feature_count), lambda g, f: (0, 0)),
+            pl.BlockSpec((rows_here, feature_count), lambda g, f: (f[0], 0)),
+            pl.BlockSpec((rows_here, feature_count), lambda g, f: (f[0], 0)),
+            pl.BlockSpec((rows_here, 1), lambda g, f: (f[0], 0)),
+            pl.BlockSpec((1, feature_count), lambda g, f: (0, 0)),
+        ],
+        out_specs=[
+            pl.BlockSpec((rows_here, feature_count), lambda g, f: (0, 0)),
+            pl.BlockSpec((rows_here, feature_count), lambda g, f: (0, 0)),
+        ],
+        scratch_shapes=[
+            pltpu.VMEM((groups, rows_here, group_lanes), jnp.float32),
+            pltpu.VMEM((rows_here, 1), jnp.float32),
+        ],
+    )
+    return pl.pallas_call(
+        kernel,
+        grid_spec=grid_spec,
+        out_shape=[
+            jax.ShapeDtypeStruct((rows_here, feature_count), jnp.bfloat16),
+            jax.ShapeDtypeStruct((rows_here, feature_count), jnp.bfloat16),
+        ],
+        compiler_params=pltpu.CompilerParams(dimension_semantics=("arbitrary",)),
+    )(flags, w_blocks, w_diag, grad_buffer, message, from_loss, normed, inverse, gain)
 
 
 def on_device(query_acts, key_acts, layer_inputs, grad_out, norm_gains, window_flags):
@@ -66,48 +157,46 @@
 
     unit_count = GROUPS
     rows_here = seq_rows // unit_count
-    column_blocks = jnp.pad(weights_low, ((0, 0), (0, rows_here), (0, 0)))
-    column_blocks = column_blocks.reshape(
-        head_count, seq_rows + rows_here, unit_count, rows_here
-    ).transpose(2, 0, 1, 3)
+    group_lanes = math.lcm(head_size, 128)
+    groups = feature_count // group_lanes
+    group_heads = group_lanes // head_size
     spare_rows = seq_rows + rows_here
+    transposed = weights_low.transpose(0, 2, 1)
+    w_blocks = jnp.pad(transposed, ((0, 0), (0, 0), (0, rows_here)))
+    w_blocks = w_blocks.reshape(groups, group_heads, unit_count, rows_here, spare_rows)
+    w_blocks = w_blocks.transpose(2, 0, 1, 3, 4).reshape(
+        unit_count, groups, group_heads * rows_here, spare_rows
+    )
+    split = transposed.reshape(head_count, unit_count, rows_here, unit_count, rows_here)
+    w_diag = jnp.stack([split[:, c, :, c, :] for c in range(unit_count)])
+    w_diag = w_diag.reshape(unit_count, groups, group_heads * rows_here, rows_here)
+    last_stage = (section_index == section_count - 1).astype(jnp.int32)
+    gain_line = gain_row[None, :]
 
     def one_turn(turn_index, carried):
         message, grad_buffer, input_grads = carried
         unit_index = turn_index - (section_count - 1 - section_index)
         active = (unit_index >= 0) & (unit_index < unit_count)
         chosen = jnp.clip(unit_count - 1 - unit_index, 0, unit_count - 1)
-        first_row = chosen * rows_here
-        slot = jnp.where(active, first_row, seq_rows)
-        incoming = jnp.where(
-            section_index == section_count - 1, rows_of(from_loss, first_row, rows_here), message
+        slot = jnp.where(active, chosen * rows_here, seq_rows)
+        flags = jnp.stack([chosen, last_stage, active.astype(jnp.int32)])
+        grad_input, incoming = turn_call(
+            flags, w_blocks, w_diag, grad_buffer, message, from_loss, normed, inverse, gain_line,
+            head_size=head_size, rows_here=rows_here,
         )
-        incoming = jnp.where(active, incoming, jnp.zeros_like(incoming))
-        incoming_heads = incoming.reshape(rows_here, head_count, head_size).transpose(1, 0, 2)
-        grad_buffer = lax.dynamic_update_slice_in_dim(grad_buffer, incoming_heads, slot, 1)
-        block = column_blocks[chosen]
-        grad_value = jnp.einsum(
-            "hij,hid->jhd", block, grad_buffer, preferred_element_type=jnp.float32
-        ).reshape(rows_here, feature_count)
-        own_normed = rows_of(normed, first_row, rows_here)
-        own_inverse = rows_of(inverse, first_row, rows_here)
-        grad_normed = grad_value * gain_row
-        grad_input = incoming.astype(jnp.float32) + own_inverse * (
-            grad_normed - own_normed * jnp.mean(grad_normed * own_normed, axis=-1, keepdims=True)
-        )
-        grad_input = grad_input.astype(jnp.bfloat16)
+        grad_buffer = write_rows(grad_buffer, slot, incoming)
         input_grads = write_rows(input_grads, slot, grad_input)
         return (passed_along(grad_input, "pipe", -1), grad_buffer, input_grads)
 
     initial = (
         jnp.zeros((rows_here, feature_count), jnp.bfloat16),
-        jnp.zeros((head_count, spare_rows, head_size), jnp.bfloat16),
+        jnp.zeros((spare_rows, feature_count), jnp.bfloat16),
         jnp.zeros((spare_rows, feature_count), jnp.bfloat16),
     )
     _, grad_buffer, input_grads = lax.fori_loop(
         0, unit_count + section_count - 1, one_turn, initial
     )
-    grad_heads = grad_buffer[:, :seq_rows].transpose(1, 0, 2)
+    grad_heads = grad_buffer[:seq_rows].reshape(seq_rows, head_count, head_size)
 
     delta_rows = jnp.einsum("ihd,ihd->hi", grad_heads.astype(jnp.float32), attended)
     grad_weights = jnp.einsum(

time: 771 us -> 825 us (1.070)
  Pallas kernels: 0 us -> 224 us
  other arithmetic: 174 us -> 40.3 us
  local copies, waits for them, and re-layouts: 82 us -> 170 us
  matrix products: 95.1 us -> 34.2 us
  waiting for transfers between devices: 127 us -> 70.1 us
    pallas_call x0 -> x39, Pallas kernels: none -> 224 us  [turn_call(): pl.pallas_call(kernel, grid_spec=grid_spec, out_shape=[jax.ShapeDtypeStru...]
    dynamic_update_slice x39 -> x0, other arithmetic: 75 us -> none  [write_rows(): return lax.dynamic_update_slice_in_dim(buffer, new_rows, first_index, 0)]
    dot_general x39 -> x0, matrix products: 66.3 us -> none  [one_turn(): jnp.einsum('hij,hid->jhd', block, grad_buffer, preferred_element_type=jnp...]
    dynamic_update_slice x39, local copies, waits for them, and re-layouts: 4.72 us -> 69.6 us  [write_rows(): return lax.dynamic_update_slice_in_dim(buffer, new_rows, first_index, 0)]
    ppermute x39, waiting for transfers between devices: 127 us -> 70.1 us  [passed_along(): lax.ppermute(value, axis, [(source, source + steps) for source in range(l...]
    reduce_sum x39 -> x0, other arithmetic: 46 us -> none  [one_turn(): jnp.mean(grad_normed * own_normed, axis=-1, keepdims=True)]
    select_n x39 -> x0, other arithmetic: 39.3 us -> none  [one_turn(): incoming = jnp.where(active, incoming, jnp.zeros_like(incoming))]
    another operation x39, other arithmetic: 1.46 us -> 23.3 us  [one_turn(): flags = jnp.stack([chosen, last_stage, active.astype(jnp.int32)])]
  transfers between devices with their start and end apart: 40 -> 40, of which waited for: 39 -> 39; matrix products, arithmetic and copies ran while one was open for 3% -> 12% of each run, Pallas kernels for 0% -> 0%
where the time goes in v3:
time: 825 us; the launch traced here: 819 us
  starting transfers between devices  278 us (34%)
  Pallas kernels  224 us (27%)
  local copies, waits for them, and re-layouts  170 us (21%)
  waiting for transfers between devices  70.1 us (8%)
  other arithmetic  40.3 us (5%)
  matrix products  34.2 us (4%)
    ppermute x39, starting transfers between devices, passed_along(): lax.ppermute(value, axis, [(source, source + steps) for source in range(l...  230 us
    pallas_call x39, Pallas kernels, turn_call(): pl.pallas_call(kernel, grid_spec=grid_spec, out_shape=[jax.ShapeDtypeStru...  224 us
    ppermute x39, waiting for transfers between devices, passed_along(): lax.ppermute(value, axis, [(source, source + steps) for source in range(l...  70.1 us
    dynamic_update_slice x39, local copies, waits for them, and re-layouts, write_rows(): return lax.dynamic_update_slice_in_dim(buffer, new_rows, first_index, 0)  69.6 us
    all_to_all x1, starting transfers between devices, on_device(): lax.all_to_all(gain_sum.reshape(group_count, feature_count // group_count...  47.8 us
    unnamed x43, local copies, waits for them, and re-layouts  32.1 us
    another operation x39, other arithmetic, one_turn(): flags = jnp.stack([chosen, last_stage, active.astype(jnp.int32)])  23.3 us
    reshape x1, local copies, waits for them, and re-layouts, on_device(): transposed.reshape(head_count, unit_count, rows_here, unit_count, rows_here)  18.7 us
  transfers between devices with their start and end apart: 40, of which 39 were waited for; matrix products, arithmetic and copies ran while one was open for 12% of the time, Pallas kernels for 0%

profile of v3, /device:TPU:15, one launch (start us, length us, event | category | flops | bytes accessed | tf_op | source)
XLA Modules:
  0.0 818.7 jit_solution(18308053119994078069)
XLA Ops:
  13.4 8.6 %fusion.17 = (f32[32,256]{1,0:T(8,128)S(1)}, f32[32,256,256]{2,1,0:T(8,128)}) fusion(f32[256,256]{1,0:T(8,128)S(1)} %fusion.9, f32[32]{0:T(128)S(1)} %multiply_exponential_fusion, pred[256,256]{1,0:T(8,128)(4,1)S(1)} %get-tuple-element.338, pred[32]{0:T(512)(128)(4,1)S(1)} %broadcast_compare_fusion, pred[256,256]{1,0:T(8,128)(4,1)S(1)} %get-tuple-element.339, ...), kind=kOutput, calls=%fused_computation.47 | convolution fusion | flops 484433920 | bytes 12484768 | tf_op jit(solution)/shard_map/ihd,jhd->hij/dot_general | solution.py:145
  21.9 9.0 %copy.40 = f32[32,256,256]{1,2,0:T(8,128)} copy(f32[32,256,256]{2,1,0:T(8,128)} %get-tuple-element.337) | data formatting | bytes 16777216 | tf_op jit(solution)/shard_map/mul | solution.py:145
  30.9 7.2 exponential_reduce_fusion
  42.7 18.7 %reshape.143 = bf16[32,8,32,8,32]{4,3,2,1,0:T(8,128)(2,1)} reshape(bf16[32,256,256]{2,1,0:T(8,128)(2,1)} %fusion.4) | data formatting | bytes 8388608 | tf_op jit(solution)/shard_map/reshape | solution.py:170
  61.4 9.3 %fusion.18 = (bf16[32,1,32,1,32]{4,3,2,1,0:T(2,128)(2,1)S(1)}, bf16[32,1,32,1,32]{4,3,2,1,0:T(2,128)(2,1)S(1)}, bf16[32,1,32,1,32]{4,3,2,1,0:T(2,128)(2,1)S(1)},...) fusion(bf16[32,8,32,8,32]{4,3,2,1,0:T(8,128)(2,1)} %reshape.143), kind=kLoop, calls=%fused_computation.48 | loop fusion | bytes 1048576 | tf_op jit(solution)/shard_map/slice | solution.py:171
  112.3 618.8 %while.19 = (s32[]{:T(128)}, bf16[32,3584]{1,0:T(8,128)(2,1)S(1)}, bf16[288,3584]{1,0:T(8,128)(2,1)S(1)}, bf16[288,3584]{1,0:T(8,128)(2,1)}, s32[]{:T(128)}, /*i...) while((s32[]{:T(128)}, bf16[32,3584]{1,0:T(8,128)(2,1)S(1)}, ...), condition=%wide.region_4.5_spmd, body=%wide.region_3.4_spmd.sunk | while | flops 21 | bytes 1835382 | solution.py:196
  118.7 7.7 collective-permute-start
  137.3 6.1 collective-permute-start
  153.4 6.1 collective-permute-start
  163.4 5.8 eval_jaxpr.7
  169.1 5.8 collective-permute-start
  184.5 5.8 collective-permute-start
  194.2 5.8 eval_jaxpr.7
  200.0 5.8 collective-permute-start
  215.4 5.8 collective-permute-start
  225.1 5.8 eval_jaxpr.7
  230.9 5.8 collective-permute-start
  246.3 5.8 collective-permute-start
  256.0 5.8 eval_jaxpr.7
  261.7 5.8 collective-permute-start
  277.1 5.8 collective-permute-start
  286.8 5.8 eval_jaxpr.7
  292.6 5.8 collective-permute-start
  308.0 5.8 collective-permute-start
  323.6 5.8 collective-permute-start
  334.4 5.8 eval_jaxpr.7
  357.9 6.0 collective-permute-start
  369.4 5.8 eval_jaxpr.7
  375.2 6.1 collective-permute-start
  391.6 6.1 collective-permute-start
  407.3 5.8 collective-permute-start
  422.7 5.8 collective-permute-start
  432.4 5.8 eval_jaxpr.7
  438.2 5.8 collective-permute-start
  453.6 5.8 collective-permute-start
  463.3 5.8 eval_jaxpr.7
  469.0 5.8 collective-permute-start
  484.4 5.8 collective-permute-start
  494.1 5.8 eval_jaxpr.7
  499.9 5.8 collective-permute-start
  515.3 5.8 collective-permute-start
  525.0 5.8 eval_jaxpr.7
  530.8 5.8 collective-permute-start
  546.1 5.8 collective-permute-start
  555.9 5.8 eval_jaxpr.7
  561.6 5.8 collective-permute-start
  578.1 5.8 collective-permute-start
  595.6 5.8 collective-permute-start
  612.7 6.1 collective-permute-start
  623.3 5.8 eval_jaxpr.7
  629.1 6.1 collective-permute-start
  644.8 5.8 collective-permute-start
  654.5 5.8 eval_jaxpr.7
  660.3 5.8 collective-permute-start
  675.7 5.8 collective-permute-start
  685.4 5.8 eval_jaxpr.7
  691.1 5.8 collective-permute-start
  706.5 5.8 collective-permute-start
  716.2 5.8 eval_jaxpr.7
  722.0 5.8 collective-permute-start
  735.3 6.4 fusion.6
  742.4 47.8 %all-to-all-start = ((f32[8,1,448]{2,1,0:T(1,128)}), f32[8,1,448]{2,1,0:T(1,128)S(1)}, u32[]{:S(2)}, u32[]{:S(2)}) async-start(f32[8,1,448]{2,1,0:T(1,128)} %all_to_all.6), calls=%async_computation | async-start | bytes 32768 | tf_op jit(solution)/shard_map/all_to_all | solution.py:225
  790.3 6.8 fusion.7
  797.1 8.9 %multiply_convert_fusion = bf16[32,256,256]{2,1,0:T(8,128)(2,1)S(1)} fusion(f32[32,256]{1,0:T(8,128)S(1)} %fusion.7, f32[32,256]{1,0:T(8,128)S(1)} %copy-done.10, pred[256,256]{1,0:T(8,128)(4,1)S(1)} %get-tuple-element.338, pred[256,256]{1,0:T(8,128)(4,1)S(1)} %get-tuple-element.339, pred[32]{0:T(512)(128)(4,1)S(1)} %broadcast_compare_fusion, ...), kind=kOutput, calls=%fused_computation.9 | convolution fusion | flops 493486080 | bytes 18562208 | tf_op jit(solution)/shard_map/ihd,jhd->hij/dot_general | solution.py:202
  (222 shorter events, 377.2 us)
Async XLA Ops:
  0.6 2.4 copy-start.1
  0.7 30.2 %copy-start.6 = (f32[256,256]{1,0:T(8,128)}, f32[256,256]{1,0:T(8,128)S(1)}, u32[]{:S(2)}) copy-start(f32[256,256]{1,0:T(8,128)S(1)} %fusion.9) | copy-start | bytes 786436
  0.9 4.9 copy-start.11
  30.9 7.3 copy-start
  38.2 4.5 copy-start.9
  108.1 4.1 copy-start.8
  118.7 12.3 %collective-permute-start = (bf16[32,3584]{1,0:T(8,128)(2,1)}, bf16[32,3584]{1,0:T(8,128)(2,1)S(1)}, u32[]{:S(2)}, u32[]{:S(2)}) collective-permute-start(bf16[32,3584]{1,0:T(8,128)(2,1)} %get-tuple-element.419), channel_id=1, source_target_pairs={{8,0},{16,8},{24,16},{32,24},{40,32},{48,40},{56,48},{64,56},{72,6... | collective-permute-start | bytes 688136 | tf_op jit(solution)/shard_map/while/body/eval_jaxpr/ppermute | solution.py:22
  137.3 9.8 %collective-permute-start = (bf16[32,3584]{1,0:T(8,128)(2,1)}, bf16[32,3584]{1,0:T(8,128)(2,1)S(1)}, u32[]{:S(2)}, u32[]{:S(2)}) collective-permute-start(bf16[32,3584]{1,0:T(8,128)(2,1)} %get-tuple-element.419), channel_id=1, source_target_pairs={{8,0},{16,8},{24,16},{32,24},{40,32},{48,40},{56,48},{64,56},{72,6... | collective-permute-start | bytes 688136 | tf_op jit(solution)/shard_map/while/body/eval_jaxpr/ppermute | solution.py:22
  153.4 9.4 %collective-permute-start = (bf16[32,3584]{1,0:T(8,128)(2,1)}, bf16[32,3584]{1,0:T(8,128)(2,1)S(1)}, u32[]{:S(2)}, u32[]{:S(2)}) collective-permute-start(bf16[32,3584]{1,0:T(8,128)(2,1)} %get-tuple-element.419), channel_id=1, source_target_pairs={{8,0},{16,8},{24,16},{32,24},{40,32},{48,40},{56,48},{64,56},{72,6... | collective-permute-start | bytes 688136 | tf_op jit(solution)/shard_map/while/body/eval_jaxpr/ppermute | solution.py:22
  169.1 9.1 %collective-permute-start = (bf16[32,3584]{1,0:T(8,128)(2,1)}, bf16[32,3584]{1,0:T(8,128)(2,1)S(1)}, u32[]{:S(2)}, u32[]{:S(2)}) collective-permute-start(bf16[32,3584]{1,0:T(8,128)(2,1)} %get-tuple-element.419), channel_id=1, source_target_pairs={{8,0},{16,8},{24,16},{32,24},{40,32},{48,40},{56,48},{64,56},{72,6... | collective-permute-start | bytes 688136 | tf_op jit(solution)/shard_map/while/body/eval_jaxpr/ppermute | solution.py:22
  184.5 9.1 %collective-permute-start = (bf16[32,3584]{1,0:T(8,128)(2,1)}, bf16[32,3584]{1,0:T(8,128)(2,1)S(1)}, u32[]{:S(2)}, u32[]{:S(2)}) collective-permute-start(bf16[32,3584]{1,0:T(8,128)(2,1)} %get-tuple-element.419), channel_id=1, source_target_pairs={{8,0},{16,8},{24,16},{32,24},{40,32},{48,40},{56,48},{64,56},{72,6... | collective-permute-start | bytes 688136 | tf_op jit(solution)/shard_map/while/body/eval_jaxpr/ppermute | solution.py:22
  200.0 9.1 %collective-permute-start = (bf16[32,3584]{1,0:T(8,128)(2,1)}, bf16[32,3584]{1,0:T(8,128)(2,1)S(1)}, u32[]{:S(2)}, u32[]{:S(2)}) collective-permute-start(bf16[32,3584]{1,0:T(8,128)(2,1)} %get-tuple-element.419), channel_id=1, source_target_pairs={{8,0},{16,8},{24,16},{32,24},{40,32},{48,40},{56,48},{64,56},{72,6... | collective-permute-start | bytes 688136 | tf_op jit(solution)/shard_map/while/body/eval_jaxpr/ppermute | solution.py:22
  215.4 9.1 %collective-permute-start = (bf16[32,3584]{1,0:T(8,128)(2,1)}, bf16[32,3584]{1,0:T(8,128)(2,1)S(1)}, u32[]{:S(2)}, u32[]{:S(2)}) collective-permute-start(bf16[32,3584]{1,0:T(8,128)(2,1)} %get-tuple-element.419), channel_id=1, source_target_pairs={{8,0},{16,8},{24,16},{32,24},{40,32},{48,40},{56,48},{64,56},{72,6... | collective-permute-start | bytes 688136 | tf_op jit(solution)/shard_map/while/body/eval_jaxpr/ppermute | solution.py:22
  230.9 9.1 %collective-permute-start = (bf16[32,3584]{1,0:T(8,128)(2,1)}, bf16[32,3584]{1,0:T(8,128)(2,1)S(1)}, u32[]{:S(2)}, u32[]{:S(2)}) collective-permute-start(bf16[32,3584]{1,0:T(8,128)(2,1)} %get-tuple-element.419), channel_id=1, source_target_pairs={{8,0},{16,8},{24,16},{32,24},{40,32},{48,40},{56,48},{64,56},{72,6... | collective-permute-start | bytes 688136 | tf_op jit(solution)/shard_map/while/body/eval_jaxpr/ppermute | solution.py:22
  246.3 9.1 %collective-permute-start = (bf16[32,3584]{1,0:T(8,128)(2,1)}, bf16[32,3584]{1,0:T(8,128)(2,1)S(1)}, u32[]{:S(2)}, u32[]{:S(2)}) collective-permute-start(bf16[32,3584]{1,0:T(8,128)(2,1)} %get-tuple-element.419), channel_id=1, source_target_pairs={{8,0},{16,8},{24,16},{32,24},{40,32},{48,40},{56,48},{64,56},{72,6... | collective-permute-start | bytes 688136 | tf_op jit(solution)/shard_map/while/body/eval_jaxpr/ppermute | solution.py:22
  261.7 9.1 %collective-permute-start = (bf16[32,3584]{1,0:T(8,128)(2,1)}, bf16[32,3584]{1,0:T(8,128)(2,1)S(1)}, u32[]{:S(2)}, u32[]{:S(2)}) collective-permute-start(bf16[32,3584]{1,0:T(8,128)(2,1)} %get-tuple-element.419), channel_id=1, source_target_pairs={{8,0},{16,8},{24,16},{32,24},{40,32},{48,40},{56,48},{64,56},{72,6... | collective-permute-start | bytes 688136 | tf_op jit(solution)/shard_map/while/body/eval_jaxpr/ppermute | solution.py:22
  277.1 9.1 %collective-permute-start = (bf16[32,3584]{1,0:T(8,128)(2,1)}, bf16[32,3584]{1,0:T(8,128)(2,1)S(1)}, u32[]{:S(2)}, u32[]{:S(2)}) collective-permute-start(bf16[32,3584]{1,0:T(8,128)(2,1)} %get-tuple-element.419), channel_id=1, source_target_pairs={{8,0},{16,8},{24,16},{32,24},{40,32},{48,40},{56,48},{64,56},{72,6... | collective-permute-start | bytes 688136 | tf_op jit(solution)/shard_map/while/body/eval_jaxpr/ppermute | solution.py:22
  292.6 9.1 %collective-permute-start = (bf16[32,3584]{1,0:T(8,128)(2,1)}, bf16[32,3584]{1,0:T(8,128)(2,1)S(1)}, u32[]{:S(2)}, u32[]{:S(2)}) collective-permute-start(bf16[32,3584]{1,0:T(8,128)(2,1)} %get-tuple-element.419), channel_id=1, source_target_pairs={{8,0},{16,8},{24,16},{32,24},{40,32},{48,40},{56,48},{64,56},{72,6... | collective-permute-start | bytes 688136 | tf_op jit(solution)/shard_map/while/body/eval_jaxpr/ppermute | solution.py:22
  308.0 9.2 %collective-permute-start = (bf16[32,3584]{1,0:T(8,128)(2,1)}, bf16[32,3584]{1,0:T(8,128)(2,1)S(1)}, u32[]{:S(2)}, u32[]{:S(2)}) collective-permute-start(bf16[32,3584]{1,0:T(8,128)(2,1)} %get-tuple-element.419), channel_id=1, source_target_pairs={{8,0},{16,8},{24,16},{32,24},{40,32},{48,40},{56,48},{64,56},{72,6... | collective-permute-start | bytes 688136 | tf_op jit(solution)/shard_map/while/body/eval_jaxpr/ppermute | solution.py:22
  323.6 10.3 %collective-permute-start = (bf16[32,3584]{1,0:T(8,128)(2,1)}, bf16[32,3584]{1,0:T(8,128)(2,1)S(1)}, u32[]{:S(2)}, u32[]{:S(2)}) collective-permute-start(bf16[32,3584]{1,0:T(8,128)(2,1)} %get-tuple-element.419), channel_id=1, source_target_pairs={{8,0},{16,8},{24,16},{32,24},{40,32},{48,40},{56,48},{64,56},{72,6... | collective-permute-start | bytes 688136 | tf_op jit(solution)/shard_map/while/body/eval_jaxpr/ppermute | solution.py:22
  340.2 11.4 %collective-permute-start = (bf16[32,3584]{1,0:T(8,128)(2,1)}, bf16[32,3584]{1,0:T(8,128)(2,1)S(1)}, u32[]{:S(2)}, u32[]{:S(2)}) collective-permute-start(bf16[32,3584]{1,0:T(8,128)(2,1)} %get-tuple-element.419), channel_id=1, source_target_pairs={{8,0},{16,8},{24,16},{32,24},{40,32},{48,40},{56,48},{64,56},{72,6... | collective-permute-start | bytes 688136 | tf_op jit(solution)/shard_map/while/body/eval_jaxpr/ppermute | solution.py:22
  357.9 10.9 %collective-permute-start = (bf16[32,3584]{1,0:T(8,128)(2,1)}, bf16[32,3584]{1,0:T(8,128)(2,1)S(1)}, u32[]{:S(2)}, u32[]{:S(2)}) collective-permute-start(bf16[32,3584]{1,0:T(8,128)(2,1)} %get-tuple-element.419), channel_id=1, source_target_pairs={{8,0},{16,8},{24,16},{32,24},{40,32},{48,40},{56,48},{64,56},{72,6... | collective-permute-start | bytes 688136 | tf_op jit(solution)/shard_map/while/body/eval_jaxpr/ppermute | solution.py:22
  375.2 10.0 %collective-permute-start = (bf16[32,3584]{1,0:T(8,128)(2,1)}, bf16[32,3584]{1,0:T(8,128)(2,1)S(1)}, u32[]{:S(2)}, u32[]{:S(2)}) collective-permute-start(bf16[32,3584]{1,0:T(8,128)(2,1)} %get-tuple-element.419), channel_id=1, source_target_pairs={{8,0},{16,8},{24,16},{32,24},{40,32},{48,40},{56,48},{64,56},{72,6... | collective-permute-start | bytes 688136 | tf_op jit(solution)/shard_map/while/body/eval_jaxpr/ppermute | solution.py:22
  391.6 9.4 %collective-permute-start = (bf16[32,3584]{1,0:T(8,128)(2,1)}, bf16[32,3584]{1,0:T(8,128)(2,1)S(1)}, u32[]{:S(2)}, u32[]{:S(2)}) collective-permute-start(bf16[32,3584]{1,0:T(8,128)(2,1)} %get-tuple-element.419), channel_id=1, source_target_pairs={{8,0},{16,8},{24,16},{32,24},{40,32},{48,40},{56,48},{64,56},{72,6... | collective-permute-start | bytes 688136 | tf_op jit(solution)/shard_map/while/body/eval_jaxpr/ppermute | solution.py:22
  407.3 9.1 %collective-permute-start = (bf16[32,3584]{1,0:T(8,128)(2,1)}, bf16[32,3584]{1,0:T(8,128)(2,1)S(1)}, u32[]{:S(2)}, u32[]{:S(2)}) collective-permute-start(bf16[32,3584]{1,0:T(8,128)(2,1)} %get-tuple-element.419), channel_id=1, source_target_pairs={{8,0},{16,8},{24,16},{32,24},{40,32},{48,40},{56,48},{64,56},{72,6... | collective-permute-start | bytes 688136 | tf_op jit(solution)/shard_map/while/body/eval_jaxpr/ppermute | solution.py:22
  422.7 9.1 %collective-permute-start = (bf16[32,3584]{1,0:T(8,128)(2,1)}, bf16[32,3584]{1,0:T(8,128)(2,1)S(1)}, u32[]{:S(2)}, u32[]{:S(2)}) collective-permute-start(bf16[32,3584]{1,0:T(8,128)(2,1)} %get-tuple-element.419), channel_id=1, source_target_pairs={{8,0},{16,8},{24,16},{32,24},{40,32},{48,40},{56,48},{64,56},{72,6... | collective-permute-start | bytes 688136 | tf_op jit(solution)/shard_map/while/body/eval_jaxpr/ppermute | solution.py:22
  438.2 9.1 %collective-permute-start = (bf16[32,3584]{1,0:T(8,128)(2,1)}, bf16[32,3584]{1,0:T(8,128)(2,1)S(1)}, u32[]{:S(2)}, u32[]{:S(2)}) collective-permute-start(bf16[32,3584]{1,0:T(8,128)(2,1)} %get-tuple-element.419), channel_id=1, source_target_pairs={{8,0},{16,8},{24,16},{32,24},{40,32},{48,40},{56,48},{64,56},{72,6... | collective-permute-start | bytes 688136 | tf_op jit(solution)/shard_map/while/body/eval_jaxpr/ppermute | solution.py:22
  453.6 9.1 %collective-permute-start = (bf16[32,3584]{1,0:T(8,128)(2,1)}, bf16[32,3584]{1,0:T(8,128)(2,1)S(1)}, u32[]{:S(2)}, u32[]{:S(2)}) collective-permute-start(bf16[32,3584]{1,0:T(8,128)(2,1)} %get-tuple-element.419), channel_id=1, source_target_pairs={{8,0},{16,8},{24,16},{32,24},{40,32},{48,40},{56,48},{64,56},{72,6... | collective-permute-start | bytes 688136 | tf_op jit(solution)/shard_map/while/body/eval_jaxpr/ppermute | solution.py:22
  469.0 9.1 %collective-permute-start = (bf16[32,3584]{1,0:T(8,128)(2,1)}, bf16[32,3584]{1,0:T(8,128)(2,1)S(1)}, u32[]{:S(2)}, u32[]{:S(2)}) collective-permute-start(bf16[32,3584]{1,0:T(8,128)(2,1)} %get-tuple-element.419), channel_id=1, source_target_pairs={{8,0},{16,8},{24,16},{32,24},{40,32},{48,40},{56,48},{64,56},{72,6... | collective-permute-start | bytes 688136 | tf_op jit(solution)/shard_map/while/body/eval_jaxpr/ppermute | solution.py:22
  484.4 9.1 %collective-permute-start = (bf16[32,3584]{1,0:T(8,128)(2,1)}, bf16[32,3584]{1,0:T(8,128)(2,1)S(1)}, u32[]{:S(2)}, u32[]{:S(2)}) collective-permute-start(bf16[32,3584]{1,0:T(8,128)(2,1)} %get-tuple-element.419), channel_id=1, source_target_pairs={{8,0},{16,8},{24,16},{32,24},{40,32},{48,40},{56,48},{64,56},{72,6... | collective-permute-start | bytes 688136 | tf_op jit(solution)/shard_map/while/body/eval_jaxpr/ppermute | solution.py:22
  499.9 9.1 %collective-permute-start = (bf16[32,3584]{1,0:T(8,128)(2,1)}, bf16[32,3584]{1,0:T(8,128)(2,1)S(1)}, u32[]{:S(2)}, u32[]{:S(2)}) collective-permute-start(bf16[32,3584]{1,0:T(8,128)(2,1)} %get-tuple-element.419), channel_id=1, source_target_pairs={{8,0},{16,8},{24,16},{32,24},{40,32},{48,40},{56,48},{64,56},{72,6... | collective-permute-start | bytes 688136 | tf_op jit(solution)/shard_map/while/body/eval_jaxpr/ppermute | solution.py:22
  515.3 9.1 %collective-permute-start = (bf16[32,3584]{1,0:T(8,128)(2,1)}, bf16[32,3584]{1,0:T(8,128)(2,1)S(1)}, u32[]{:S(2)}, u32[]{:S(2)}) collective-permute-start(bf16[32,3584]{1,0:T(8,128)(2,1)} %get-tuple-element.419), channel_id=1, source_target_pairs={{8,0},{16,8},{24,16},{32,24},{40,32},{48,40},{56,48},{64,56},{72,6... | collective-permute-start | bytes 688136 | tf_op jit(solution)/shard_map/while/body/eval_jaxpr/ppermute | solution.py:22
  530.8 9.1 %collective-permute-start = (bf16[32,3584]{1,0:T(8,128)(2,1)}, bf16[32,3584]{1,0:T(8,128)(2,1)S(1)}, u32[]{:S(2)}, u32[]{:S(2)}) collective-permute-start(bf16[32,3584]{1,0:T(8,128)(2,1)} %get-tuple-element.419), channel_id=1, source_target_pairs={{8,0},{16,8},{24,16},{32,24},{40,32},{48,40},{56,48},{64,56},{72,6... | collective-permute-start | bytes 688136 | tf_op jit(solution)/shard_map/while/body/eval_jaxpr/ppermute | solution.py:22
  546.1 9.1 %collective-permute-start = (bf16[32,3584]{1,0:T(8,128)(2,1)}, bf16[32,3584]{1,0:T(8,128)(2,1)S(1)}, u32[]{:S(2)}, u32[]{:S(2)}) collective-permute-start(bf16[32,3584]{1,0:T(8,128)(2,1)} %get-tuple-element.419), channel_id=1, source_target_pairs={{8,0},{16,8},{24,16},{32,24},{40,32},{48,40},{56,48},{64,56},{72,6... | collective-permute-start | bytes 688136 | tf_op jit(solution)/shard_map/while/body/eval_jaxpr/ppermute | solution.py:22
  561.6 10.1 %collective-permute-start = (bf16[32,3584]{1,0:T(8,128)(2,1)}, bf16[32,3584]{1,0:T(8,128)(2,1)S(1)}, u32[]{:S(2)}, u32[]{:S(2)}) collective-permute-start(bf16[32,3584]{1,0:T(8,128)(2,1)} %get-tuple-element.419), channel_id=1, source_target_pairs={{8,0},{16,8},{24,16},{32,24},{40,32},{48,40},{56,48},{64,56},{72,6... | collective-permute-start | bytes 688136 | tf_op jit(solution)/shard_map/while/body/eval_jaxpr/ppermute | solution.py:22
  578.1 11.2 %collective-permute-start = (bf16[32,3584]{1,0:T(8,128)(2,1)}, bf16[32,3584]{1,0:T(8,128)(2,1)S(1)}, u32[]{:S(2)}, u32[]{:S(2)}) collective-permute-start(bf16[32,3584]{1,0:T(8,128)(2,1)} %get-tuple-element.419), channel_id=1, source_target_pairs={{8,0},{16,8},{24,16},{32,24},{40,32},{48,40},{56,48},{64,56},{72,6... | collective-permute-start | bytes 688136 | tf_op jit(solution)/shard_map/while/body/eval_jaxpr/ppermute | solution.py:22
  595.6 10.7 %collective-permute-start = (bf16[32,3584]{1,0:T(8,128)(2,1)}, bf16[32,3584]{1,0:T(8,128)(2,1)S(1)}, u32[]{:S(2)}, u32[]{:S(2)}) collective-permute-start(bf16[32,3584]{1,0:T(8,128)(2,1)} %get-tuple-element.419), channel_id=1, source_target_pairs={{8,0},{16,8},{24,16},{32,24},{40,32},{48,40},{56,48},{64,56},{72,6... | collective-permute-start | bytes 688136 | tf_op jit(solution)/shard_map/while/body/eval_jaxpr/ppermute | solution.py:22
  612.7 10.1 %collective-permute-start = (bf16[32,3584]{1,0:T(8,128)(2,1)}, bf16[32,3584]{1,0:T(8,128)(2,1)S(1)}, u32[]{:S(2)}, u32[]{:S(2)}) collective-permute-start(bf16[32,3584]{1,0:T(8,128)(2,1)} %get-tuple-element.419), channel_id=1, source_target_pairs={{8,0},{16,8},{24,16},{32,24},{40,32},{48,40},{56,48},{64,56},{72,6... | collective-permute-start | bytes 688136 | tf_op jit(solution)/shard_map/while/body/eval_jaxpr/ppermute | solution.py:22
  629.1 9.3 %collective-permute-start = (bf16[32,3584]{1,0:T(8,128)(2,1)}, bf16[32,3584]{1,0:T(8,128)(2,1)S(1)}, u32[]{:S(2)}, u32[]{:S(2)}) collective-permute-start(bf16[32,3584]{1,0:T(8,128)(2,1)} %get-tuple-element.419), channel_id=1, source_target_pairs={{8,0},{16,8},{24,16},{32,24},{40,32},{48,40},{56,48},{64,56},{72,6... | collective-permute-start | bytes 688136 | tf_op jit(solution)/shard_map/while/body/eval_jaxpr/ppermute | solution.py:22
  644.8 9.1 %collective-permute-start = (bf16[32,3584]{1,0:T(8,128)(2,1)}, bf16[32,3584]{1,0:T(8,128)(2,1)S(1)}, u32[]{:S(2)}, u32[]{:S(2)}) collective-permute-start(bf16[32,3584]{1,0:T(8,128)(2,1)} %get-tuple-element.419), channel_id=1, source_target_pairs={{8,0},{16,8},{24,16},{32,24},{40,32},{48,40},{56,48},{64,56},{72,6... | collective-permute-start | bytes 688136 | tf_op jit(solution)/shard_map/while/body/eval_jaxpr/ppermute | solution.py:22
  660.3 9.1 %collective-permute-start = (bf16[32,3584]{1,0:T(8,128)(2,1)}, bf16[32,3584]{1,0:T(8,128)(2,1)S(1)}, u32[]{:S(2)}, u32[]{:S(2)}) collective-permute-start(bf16[32,3584]{1,0:T(8,128)(2,1)} %get-tuple-element.419), channel_id=1, source_target_pairs={{8,0},{16,8},{24,16},{32,24},{40,32},{48,40},{56,48},{64,56},{72,6... | collective-permute-start | bytes 688136 | tf_op jit(solution)/shard_map/while/body/eval_jaxpr/ppermute | solution.py:22
  675.7 9.1 %collective-permute-start = (bf16[32,3584]{1,0:T(8,128)(2,1)}, bf16[32,3584]{1,0:T(8,128)(2,1)S(1)}, u32[]{:S(2)}, u32[]{:S(2)}) collective-permute-start(bf16[32,3584]{1,0:T(8,128)(2,1)} %get-tuple-element.419), channel_id=1, source_target_pairs={{8,0},{16,8},{24,16},{32,24},{40,32},{48,40},{56,48},{64,56},{72,6... | collective-permute-start | bytes 688136 | tf_op jit(solution)/shard_map/while/body/eval_jaxpr/ppermute | solution.py:22
  691.1 9.1 %collective-permute-start = (bf16[32,3584]{1,0:T(8,128)(2,1)}, bf16[32,3584]{1,0:T(8,128)(2,1)S(1)}, u32[]{:S(2)}, u32[]{:S(2)}) collective-permute-start(bf16[32,3584]{1,0:T(8,128)(2,1)} %get-tuple-element.419), channel_id=1, source_target_pairs={{8,0},{16,8},{24,16},{32,24},{40,32},{48,40},{56,48},{64,56},{72,6... | collective-permute-start | bytes 688136 | tf_op jit(solution)/shard_map/while/body/eval_jaxpr/ppermute | solution.py:22
  706.5 9.1 %collective-permute-start = (bf16[32,3584]{1,0:T(8,128)(2,1)}, bf16[32,3584]{1,0:T(8,128)(2,1)S(1)}, u32[]{:S(2)}, u32[]{:S(2)}) collective-permute-start(bf16[32,3584]{1,0:T(8,128)(2,1)} %get-tuple-element.419), channel_id=1, source_target_pairs={{8,0},{16,8},{24,16},{32,24},{40,32},{48,40},{56,48},{64,56},{72,6... | collective-permute-start | bytes 688136 | tf_op jit(solution)/shard_map/while/body/eval_jaxpr/ppermute | solution.py:22
  722.0 9.1 %collective-permute-start = (bf16[32,3584]{1,0:T(8,128)(2,1)}, bf16[32,3584]{1,0:T(8,128)(2,1)S(1)}, u32[]{:S(2)}, u32[]{:S(2)}) collective-permute-start(bf16[32,3584]{1,0:T(8,128)(2,1)} %get-tuple-element.419), channel_id=1, source_target_pairs={{8,0},{16,8},{24,16},{32,24},{40,32},{48,40},{56,48},{64,56},{72,6... | collective-permute-start | bytes 688136 | tf_op jit(solution)/shard_map/while/body/eval_jaxpr/ppermute | solution.py:22
  731.1 4.2 copy-start.7
  731.1 4.3 copy-start.10
  742.4 75.7 %all-to-all-start = ((f32[8,1,448]{2,1,0:T(1,128)}), f32[8,1,448]{2,1,0:T(1,128)S(1)}, u32[]{:S(2)}, u32[]{:S(2)}) async-start(f32[8,1,448]{2,1,0:T(1,128)} %all_to_all.6), calls=%async_computation | async-start | bytes 32768 | tf_op jit(solution)/shard_map/all_to_all | solution.py:225
  790.3 6.8 copy-start.5
  797.1 8.9 %copy-start.4 = (bf16[1,1,256,3584]{2,3,1,0:T(8,128)(2,1)S(1)}, bf16[1,1,256,3584]{2,3,1,0:T(8,128)(2,1)}, u32[]{:S(2)}) copy-start(bf16[1,1,256,3584]{2,3,1,0:T(8,128)(2,1)} %copy.39) | copy-start | bytes 5505028
  806.0 1.6 copy-start.2
  807.5 2.2 copy-start.3

commit v4 on v3

v4 whole, which is shorter than its diff:
```python
import functools
import math

import jax
import jax.numpy as jnp
from jax import lax
from jax.experimental import pallas as pl
from jax.experimental.pallas import tpu as pltpu
from jax.sharding import PartitionSpec as P

GROUPS = 8
WINDOW = 32


EPSILON = 1e-05
NEGATIVE = -1e30


def passed_along(value, axis, steps):
    count = lax.axis_size(axis)
    leading, last = (max(0, -steps), min(count, count - steps))
    return lax.ppermute(value, axis, [(source, source + steps) for source in range(leading, last)])


def rows_of(source, first_index, row_count):
    return lax.dynamic_slice_in_dim(source, first_index, row_count, 0)


def write_rows(buffer, first_index, new_rows):
    return lax.dynamic_update_slice_in_dim(buffer, new_rows, first_index, 0)


def turn_kernel(
    flags_ref,
    w_hbm, g_hbm, ig_hbm, msg_ref, loss_ref, normed_ref, inv_ref, gain_ref,
    out_ref, g_out, ig_out,
    w_v, g_v, inc_v, gn_v, sems,
    *, group_lanes, head_size, rows_here, groups, seq_rows, feature_count,
):
    chosen = flags_ref[0]
    from_loss = flags_ref[1] == 1
    active = flags_ref[2] == 1
    slot = pl.multiple_of(flags_ref[3], rows_here)
    group_heads = group_lanes // head_size
    reads = []
    for g in range(groups):
        w_copy = pltpu.make_async_copy(w_hbm.at[g, :, chosen], w_v.at[g], sems.at[0, g])
        g_copy = pltpu.make_async_copy(
            g_hbm.at[pl.ds(0, seq_rows), pl.ds(g * group_lanes, group_lanes)],
            g_v.at[g],
            sems.at[1, g],
        )
        w_copy.start()
        g_copy.start()
        reads.append((w_copy, g_copy))
    inc = jnp.where(from_loss, loss_ref[...], msg_ref[...])
    inc = jnp.where(active, inc, jnp.zeros_like(inc))
    inc_v[...] = inc
    first_row = pl.multiple_of(chosen * rows_here, rows_here)
    lane_head = lax.broadcasted_iota(jnp.int32, (rows_here, group_lanes), 1) // head_size
    total = jnp.zeros((rows_here, 1), jnp.float32)
    for g in range(groups):
        cols = slice(g * group_lanes, (g + 1) * group_lanes)
        w_copy, g_copy = reads[g]
        w_copy.wait()
        g_copy.wait()
        g_v[g, pl.ds(first_row, rows_here), :] = inc_v[:, cols]
        stacked = jnp.dot(
            w_v[g].reshape(group_heads * rows_here, seq_rows),
            g_v[g],
            preferred_element_type=jnp.float32,
        )
        value = jnp.zeros((rows_here, group_lanes), jnp.float32)
        for k in range(group_heads):
            value = value + jnp.where(
                lane_head == k, stacked[k * rows_here:(k + 1) * rows_here, :], 0.0
            )
        grad_normed = value * gain_ref[:, cols]
        gn_v[g] = grad_normed
        total = total + jnp.sum(grad_normed * normed_ref[:, cols], axis=1, keepdims=True)
    g_write = pltpu.make_async_copy(inc_v, g_out.at[pl.ds(slot, rows_here)], sems.at[2, 0])
    g_write.start()
    mean = total * (1.0 / feature_count)
    inv = inv_ref[...]
    for g in range(groups):
        cols = slice(g * group_lanes, (g + 1) * group_lanes)
        out_ref[:, cols] = (
            inc_v[:, cols].astype(jnp.float32) + inv * (gn_v[g] - normed_ref[:, cols] * mean)
        ).astype(out_ref.dtype)
    ig_write = pltpu.make_async_copy(out_ref, ig_out.at[pl.ds(slot, rows_here)], sems.at[2, 1])
    ig_write.start()
    g_write.wait()
    ig_write.wait()


def turn_call(flags, w_split, grad_buffer, input_grads, message, from_loss, normed, inverse, gain,
              *, head_size, rows_here):
    groups, group_heads, unit_count, _, seq_rows = w_split.shape
    feature_count = grad_buffer.shape[1]
    group_lanes = feature_count // groups
    kernel = functools.partial(
        turn_kernel, group_lanes=group_lanes, head_size=head_size, rows_here=rows_here,
        groups=groups, seq_rows=seq_rows, feature_count=feature_count,
    )
    grid_spec = pltpu.PrefetchScalarGridSpec(
        num_scalar_prefetch=1,
        grid=(1,),
        in_specs=[
            pl.BlockSpec(memory_space=pl.ANY),
            pl.BlockSpec(memory_space=pl.ANY),
            pl.BlockSpec(memory_space=pl.ANY),
            pl.BlockSpec((rows_here, feature_count), lambda i, f: (0, 0)),
            pl.BlockSpec((rows_here, feature_count), lambda i, f: (f[0], 0)),
            pl.BlockSpec((rows_here, feature_count), lambda i, f: (f[0], 0)),
            pl.BlockSpec((rows_here, 1), lambda i, f: (f[0], 0)),
            pl.BlockSpec((1, feature_count), lambda i, f: (0, 0)),
        ],
        out_specs=[
            pl.BlockSpec((rows_here, feature_count), lambda i, f: (0, 0)),
            pl.BlockSpec(memory_space=pl.ANY),
            pl.BlockSpec(memory_space=pl.ANY),
        ],
        scratch_shapes=[
            pltpu.VMEM((groups, group_heads, rows_here, seq_rows), jnp.bfloat16),
            pltpu.VMEM((groups, seq_rows, group_lanes), jnp.bfloat16),
            pltpu.VMEM((rows_here, feature_count), jnp.bfloat16),
            pltpu.VMEM((groups, rows_here, group_lanes), jnp.float32),
            pltpu.SemaphoreType.DMA((3, groups)),
        ],
    )
    return pl.pallas_call(
        kernel,
        grid_spec=grid_spec,
        out_shape=[
            jax.ShapeDtypeStruct((rows_here, feature_count), jnp.bfloat16),
            jax.ShapeDtypeStruct(grad_buffer.shape, grad_buffer.dtype),
            jax.ShapeDtypeStruct(input_grads.shape, input_grads.dtype),
        ],
        input_output_aliases={2: 1, 3: 2},
        compiler_params=pltpu.CompilerParams(dimension_semantics=("arbitrary",)),
    )(flags, w_split, grad_buffer, input_grads, message, from_loss, normed, inverse, gain)


def on_device(query_acts, key_acts, layer_inputs, grad_out, norm_gains, window_flags):
    section_count = lax.axis_size("pipe")
    section_index = lax.axis_index("pipe")
    seq_rows = query_acts.shape[2]
    feature_count = query_acts.shape[3]
    head_count = window_flags.shape[0]
    head_size = feature_count // head_count
    score_scale = head_size ** (-0.5)
    slopes = jnp.exp2(-(jnp.arange(head_count, dtype=jnp.float32) + 1.0) * 8.0 / head_count)
    open_heads = (window_flags == 0)[:, None, None]
    query_rows = query_acts[0, 0]
    key_rows = key_acts[0, 0]
    from_loss = grad_out[0]
    input_rows = layer_inputs[0, 0].astype(jnp.float32)
    inverse = lax.rsqrt(jnp.mean(input_rows * input_rows, axis=-1, keepdims=True) + EPSILON)
    normed = input_rows * inverse
    gain_row = norm_gains[0]
    value_rows = (normed * gain_row).astype(jnp.bfloat16)
    places = jnp.arange(seq_rows, dtype=jnp.int32)
    all_queries = query_rows.reshape(seq_rows, head_count, head_size)
    all_keys = key_rows.reshape(seq_rows, head_count, head_size)
    all_values = value_rows.reshape(seq_rows, head_count, head_size)

    distance = places[None, :] - places[:, None]
    allowed = (distance >= 0)[None, :, :] & (open_heads | (distance < WINDOW)[None, :, :])
    logits = (
        jnp.einsum("jhd,ihd->hji", all_keys, all_queries, preferred_element_type=jnp.float32)
        * score_scale
    )
    logits = logits - slopes[:, None, None] * distance.astype(jnp.float32)[None, :, :]
    masked = jnp.where(allowed, logits, NEGATIVE)
    row_top = jnp.max(masked, axis=1, keepdims=True)
    log_total = row_top + jnp.log(jnp.sum(jnp.exp(masked - row_top), axis=1, keepdims=True))
    weights = jnp.where(allowed, jnp.exp(masked - log_total), 0.0)
    weights_low = weights.astype(jnp.bfloat16)
    attended = jnp.einsum(
        "hji,jhd->ihd", weights_low, all_values, preferred_element_type=jnp.float32
    )

    unit_count = GROUPS
    rows_here = seq_rows // unit_count
    group_lanes = math.lcm(head_size, 128)
    groups = feature_count // group_lanes
    spare_rows = seq_rows + rows_here
    w_split = weights_low.reshape(
        groups, group_lanes // head_size, unit_count, rows_here, seq_rows
    )
    last_stage = (section_index == section_count - 1).astype(jnp.int32)
    gain_line = gain_row[None, :]

    def one_turn(turn_index, carried):
        message, grad_buffer, input_grads = carried
        unit_index = turn_index - (section_count - 1 - section_index)
        active = (unit_index >= 0) & (unit_index < unit_count)
        chosen = jnp.clip(unit_count - 1 - unit_index, 0, unit_count - 1)
        slot = jnp.where(active, chosen * rows_here, seq_rows)
        flags = jnp.stack([chosen, last_stage, active.astype(jnp.int32), slot])
        grad_input, grad_buffer, input_grads = turn_call(
            flags, w_split, grad_buffer, input_grads, message, from_loss, normed, inverse,
            gain_line, head_size=head_size, rows_here=rows_here,
        )
        return (passed_along(grad_input, "pipe", -1), grad_buffer, input_grads)

    initial = (
        jnp.zeros((rows_here, feature_count), jnp.bfloat16),
        jnp.zeros((spare_rows, feature_count), jnp.bfloat16),
        jnp.zeros((spare_rows, feature_count), jnp.bfloat16),
    )
    _, grad_buffer, input_grads = lax.fori_loop(
        0, unit_count + section_count - 1, one_turn, initial
    )
    grad_heads = grad_buffer[:seq_rows].reshape(seq_rows, head_count, head_size)

    delta_rows = jnp.einsum("ihd,ihd->hi", grad_heads.astype(jnp.float32), attended)
    grad_weights = jnp.einsum(
        "jhd,ihd->hji", all_values, grad_heads, preferred_element_type=jnp.float32
    )
    grad_logits = (weights * (grad_weights - delta_rows[:, None, :])).astype(jnp.bfloat16)
    grad_query = (
        jnp.einsum("hji,jhd->ihd", grad_logits, all_keys, preferred_element_type=jnp.float32)
        * score_scale
    )
    grad_query = grad_query.astype(jnp.bfloat16).reshape(seq_rows, feature_count)
    grad_key = (
        jnp.einsum("hji,ihd->jhd", grad_logits, all_queries, preferred_element_type=jnp.float32)
        * score_scale
    )
    grad_key = grad_key.astype(jnp.bfloat16).reshape(seq_rows, feature_count)
    grad_value = jnp.einsum(
        "hji,ihd->jhd", weights_low, grad_heads, preferred_element_type=jnp.float32
    ).reshape(seq_rows, feature_count)
    gain_sum = jnp.sum(grad_value * normed, axis=0)

    grad_queries = grad_query.reshape(1, 1, seq_rows, feature_count)
    grad_keys = grad_key.reshape(1, 1, seq_rows, feature_count)
    grad_inputs = input_grads[:seq_rows].reshape(1, 1, seq_rows, feature_count)
    group_count = lax.axis_size("dp")
    gain_parts = lax.all_to_all(
        gain_sum.reshape(group_count, feature_count // group_count), "dp", 0, 0, tiled=True
    )
    grad_gains = jnp.sum(gain_parts, axis=0, keepdims=True)
    return (grad_inputs, grad_queries, grad_keys, grad_gains)


def solution(mesh):
    return jax.shard_map(
        on_device,
        mesh=mesh,
        in_specs=(
            P("pipe", "dp", None, None),
            P("pipe", "dp", None, None),
            P("pipe", "dp", None, None),
            P("dp", None, None),
            P("pipe", None),
            P(),
        ),
        out_specs=(
            P("pipe", "dp", None, None),
            P("pipe", "dp", None, None),
            P("pipe", "dp", None, None),
            P("pipe", "dp"),
        ),
        check_vma=False,
    )
```

time: 825 us -> 752 us (0.912)
  local copies, waits for them, and re-layouts: 170 us -> 28 us
  waiting for transfers between devices: 70.1 us -> 140 us
  Pallas kernels: 224 us -> 241 us
  matrix products: 34.2 us -> 23 us
    ppermute x39, waiting for transfers between devices: 70.1 us -> 140 us  [passed_along(): lax.ppermute(value, axis, [(source, source + steps) for source in range(l...]
    dynamic_update_slice x39 -> x0, local copies, waits for them, and re-layouts: 69.6 us -> none  [write_rows(): return lax.dynamic_update_slice_in_dim(buffer, new_rows, first_index, 0)]
    reshape x1 -> x0, local copies, waits for them, and re-layouts: 18.7 us -> none  [on_device(): transposed.reshape(head_count, unit_count, rows_here, unit_count, rows_here)]
    pallas_call x39, Pallas kernels: 224 us -> 241 us  [turn_call(): pl.pallas_call(kernel, grid_spec=grid_spec, out_shape=[jax.ShapeDtypeStru...]
    unnamed x43 -> x22, local copies, waits for them, and re-layouts: 32.1 us -> 15.9 us
    dot_general x6, matrix products: 34.2 us -> 23 us  [the longest x1 6.07 us: on_device(): jnp.einsum('jhd,ihd->hji', all_values, grad_heads, preferred_element_type...]
    another operation x11 -> x2, local copies, waits for them, and re-layouts: 12.1 us -> 1.63 us  [the longest x9 10.5 us: on_device(): w_diag = jnp.stack([split[:, c, :, c, :] for c in range(unit_count)])]
    slice x1 -> x0, local copies, waits for them, and re-layouts: 9.32 us -> none  [on_device(): w_diag = jnp.stack([split[:, c, :, c, :] for c in range(unit_count)])]
  transfers between devices with their start and end apart: 40 -> 40, of which waited for: 39 -> 39; matrix products, arithmetic and copies ran while one was open for 12% -> 3% of each run, Pallas kernels for 0% -> 0%
where the time goes in v4:
time: 752 us; the launch traced here: 749 us
  starting transfers between devices  279 us (37%)
  Pallas kernels  241 us (32%)
  waiting for transfers between devices  140 us (19%)
  other arithmetic  35.8 us (5%)
  local copies, waits for them, and re-layouts  28 us (4%)
  matrix products  23 us (3%)
    pallas_call x39, Pallas kernels, turn_call(): pl.pallas_call(kernel, grid_spec=grid_spec, out_shape=[jax.ShapeDtypeStru...  241 us
    ppermute x39, starting transfers between devices, passed_along(): lax.ppermute(value, axis, [(source, source + steps) for source in range(l...  231 us
    ppermute x39, waiting for transfers between devices, passed_along(): lax.ppermute(value, axis, [(source, source + steps) for source in range(l...  140 us
    all_to_all x1, starting transfers between devices, on_device(): lax.all_to_all(gain_sum.reshape(group_count, feature_count // group_count...  47.6 us
    another operation x39, other arithmetic, one_turn(): flags = jnp.stack([chosen, last_stage, active.astype(jnp.int32), slot])  25.6 us
    unnamed x22, local copies, waits for them, and re-layouts  15.9 us
  transfers between devices with their start and end apart: 40, of which 39 were waited for; matrix products, arithmetic and copies ran while one was open for 3% of the time, Pallas kernels for 0%

profile of v4, /device:TPU:15, one launch (start us, length us, event | category | flops | bytes accessed | tf_op | source)
XLA Modules:
  0.0 748.5 jit_solution(7726002857914124226)
XLA Ops:
  29.0 638.8 %while.19 = (s32[]{:T(128)}, bf16[32,3584]{1,0:T(8,128)(2,1)S(1)}, bf16[288,3584]{1,0:T(8,128)(2,1)S(1)}, bf16[288,3584]{1,0:T(8,128)(2,1)}, s32[]{:T(128)}, /*i...) while((s32[]{:T(128)}, bf16[32,3584]{1,0:T(8,128)(2,1)S(1)}, ...), condition=%wide.region_4.5_spmd, body=%wide.region_3.4_spmd.sunk | while | flops 24 | bytes 917832 | solution.py:212
  29.7 6.2 eval_jaxpr.7
  35.9 7.8 %collective-permute-start = (bf16[32,3584]{1,0:T(8,128)(2,1)}, bf16[32,3584]{1,0:T(8,128)(2,1)S(1)}, u32[]{:S(2)}, u32[]{:S(2)}) collective-permute-start(bf16[32,3584]{1,0:T(8,128)(2,1)} %get-tuple-element.383), channel_id=1, source_target_pairs={{8,0},{16,8},{24,16},{32,24},{40,32},{48,40},{56,48},{64,56},{72,6... | collective-permute-start | bytes 688136 | tf_op jit(solution)/shard_map/while/body/eval_jaxpr/ppermute | solution.py:22
  48.9 6.2 eval_jaxpr.7
  55.0 6.1 collective-permute-start
  65.5 6.2 eval_jaxpr.7
  71.6 6.1 collective-permute-start
  81.7 6.2 eval_jaxpr.7
  97.6 6.2 eval_jaxpr.7
  103.8 5.8 collective-permute-start
  113.5 6.2 eval_jaxpr.7
  119.7 5.8 collective-permute-start
  129.5 6.2 eval_jaxpr.7
  135.7 5.8 collective-permute-start
  145.4 6.2 eval_jaxpr.7
  151.6 5.8 collective-permute-start
  161.3 6.2 eval_jaxpr.7
  167.5 5.8 collective-permute-start
  177.2 6.2 eval_jaxpr.7
  183.4 5.8 collective-permute-start
  193.2 6.2 eval_jaxpr.7
  199.3 5.8 collective-permute-start
  209.1 6.2 eval_jaxpr.7
  225.0 6.2 eval_jaxpr.7
  240.9 6.2 eval_jaxpr.7
  257.8 6.2 eval_jaxpr.7
  275.7 6.2 eval_jaxpr.7
  293.4 6.2 eval_jaxpr.7
  299.6 6.1 collective-permute-start
  310.4 6.2 eval_jaxpr.7
  316.6 6.1 collective-permute-start
  326.6 6.2 eval_jaxpr.7
  342.6 6.2 eval_jaxpr.7
  348.8 5.8 collective-permute-start
  358.5 6.2 eval_jaxpr.7
  374.5 6.2 eval_jaxpr.7
  390.4 6.2 eval_jaxpr.7
  396.6 5.8 collective-permute-start
  406.4 6.2 eval_jaxpr.7
  422.3 6.2 eval_jaxpr.7
  438.2 6.2 eval_jaxpr.7
  444.4 5.8 collective-permute-start
  454.2 6.2 eval_jaxpr.7
  470.1 6.2 eval_jaxpr.7
  486.1 6.2 eval_jaxpr.7
  492.3 5.8 collective-permute-start
  502.6 6.2 eval_jaxpr.7
  508.8 5.8 collective-permute-start
  520.2 6.2 eval_jaxpr.7
  526.4 5.8 collective-permute-start
  538.3 6.2 eval_jaxpr.7
  544.5 6.1 collective-permute-start
  555.8 6.2 eval_jaxpr.7
  562.0 6.1 collective-permute-start
  572.5 6.2 eval_jaxpr.7
  578.7 6.1 collective-permute-start
  588.7 6.2 eval_jaxpr.7
  604.7 6.2 eval_jaxpr.7
  620.6 6.2 eval_jaxpr.7
  626.8 5.8 collective-permute-start
  636.5 6.2 eval_jaxpr.7
  652.5 6.2 eval_jaxpr.7
  677.6 47.6 %all-to-all-start = ((f32[8,1,448]{2,1,0:T(1,128)}), f32[8,1,448]{2,1,0:T(1,128)S(1)}, u32[]{:S(2)}, u32[]{:S(2)}) async-start(f32[8,1,448]{2,1,0:T(1,128)} %all_to_all.6), calls=%async_computation | async-start | bytes 32768 | tf_op jit(solution)/shard_map/all_to_all | solution.py:241
  729.7 6.1 multiply_convert_fusion
  (145 shorter events, 319.8 us)
Async XLA Ops:
  0.7 6.0 copy-start.8
  9.6 8.5 %copy-start.4 = (bf16[1,1,256,3584]{2,3,1,0:T(8,128)(2,1)}, bf16[1,1,256,3584]{2,3,1,0:T(8,128)(2,1)S(1)}, u32[]{:S(2)}) copy-start(bf16[1,1,256,3584]{2,3,1,0:T(8,128)(2,1)S(1)} %copy.27) | copy-start | bytes 5505028
  18.1 3.2 copy-start.1
  21.3 3.6 copy-start.3
  24.9 4.1 copy-start.7
  35.9 12.3 %collective-permute-start = (bf16[32,3584]{1,0:T(8,128)(2,1)}, bf16[32,3584]{1,0:T(8,128)(2,1)S(1)}, u32[]{:S(2)}, u32[]{:S(2)}) collective-permute-start(bf16[32,3584]{1,0:T(8,128)(2,1)} %get-tuple-element.383), channel_id=1, source_target_pairs={{8,0},{16,8},{24,16},{32,24},{40,32},{48,40},{56,48},{64,56},{72,6... | collective-permute-start | bytes 688136 | tf_op jit(solution)/shard_map/while/body/eval_jaxpr/ppermute | solution.py:22
  55.0 9.8 %collective-permute-start = (bf16[32,3584]{1,0:T(8,128)(2,1)}, bf16[32,3584]{1,0:T(8,128)(2,1)S(1)}, u32[]{:S(2)}, u32[]{:S(2)}) collective-permute-start(bf16[32,3584]{1,0:T(8,128)(2,1)} %get-tuple-element.383), channel_id=1, source_target_pairs={{8,0},{16,8},{24,16},{32,24},{40,32},{48,40},{56,48},{64,56},{72,6... | collective-permute-start | bytes 688136 | tf_op jit(solution)/shard_map/while/body/eval_jaxpr/ppermute | solution.py:22
  71.6 9.4 %collective-permute-start = (bf16[32,3584]{1,0:T(8,128)(2,1)}, bf16[32,3584]{1,0:T(8,128)(2,1)S(1)}, u32[]{:S(2)}, u32[]{:S(2)}) collective-permute-start(bf16[32,3584]{1,0:T(8,128)(2,1)} %get-tuple-element.383), channel_id=1, source_target_pairs={{8,0},{16,8},{24,16},{32,24},{40,32},{48,40},{56,48},{64,56},{72,6... | collective-permute-start | bytes 688136 | tf_op jit(solution)/shard_map/while/body/eval_jaxpr/ppermute | solution.py:22
  87.9 9.1 %collective-permute-start = (bf16[32,3584]{1,0:T(8,128)(2,1)}, bf16[32,3584]{1,0:T(8,128)(2,1)S(1)}, u32[]{:S(2)}, u32[]{:S(2)}) collective-permute-start(bf16[32,3584]{1,0:T(8,128)(2,1)} %get-tuple-element.383), channel_id=1, source_target_pairs={{8,0},{16,8},{24,16},{32,24},{40,32},{48,40},{56,48},{64,56},{72,6... | collective-permute-start | bytes 688136 | tf_op jit(solution)/shard_map/while/body/eval_jaxpr/ppermute | solution.py:22
  103.8 9.1 %collective-permute-start = (bf16[32,3584]{1,0:T(8,128)(2,1)}, bf16[32,3584]{1,0:T(8,128)(2,1)S(1)}, u32[]{:S(2)}, u32[]{:S(2)}) collective-permute-start(bf16[32,3584]{1,0:T(8,128)(2,1)} %get-tuple-element.383), channel_id=1, source_target_pairs={{8,0},{16,8},{24,16},{32,24},{40,32},{48,40},{56,48},{64,56},{72,6... | collective-permute-start | bytes 688136 | tf_op jit(solution)/shard_map/while/body/eval_jaxpr/ppermute | solution.py:22
  119.7 9.1 %collective-permute-start = (bf16[32,3584]{1,0:T(8,128)(2,1)}, bf16[32,3584]{1,0:T(8,128)(2,1)S(1)}, u32[]{:S(2)}, u32[]{:S(2)}) collective-permute-start(bf16[32,3584]{1,0:T(8,128)(2,1)} %get-tuple-element.383), channel_id=1, source_target_pairs={{8,0},{16,8},{24,16},{32,24},{40,32},{48,40},{56,48},{64,56},{72,6... | collective-permute-start | bytes 688136 | tf_op jit(solution)/shard_map/while/body/eval_jaxpr/ppermute | solution.py:22
  135.7 9.1 %collective-permute-start = (bf16[32,3584]{1,0:T(8,128)(2,1)}, bf16[32,3584]{1,0:T(8,128)(2,1)S(1)}, u32[]{:S(2)}, u32[]{:S(2)}) collective-permute-start(bf16[32,3584]{1,0:T(8,128)(2,1)} %get-tuple-element.383), channel_id=1, source_target_pairs={{8,0},{16,8},{24,16},{32,24},{40,32},{48,40},{56,48},{64,56},{72,6... | collective-permute-start | bytes 688136 | tf_op jit(solution)/shard_map/while/body/eval_jaxpr/ppermute | solution.py:22
  151.6 9.1 %collective-permute-start = (bf16[32,3584]{1,0:T(8,128)(2,1)}, bf16[32,3584]{1,0:T(8,128)(2,1)S(1)}, u32[]{:S(2)}, u32[]{:S(2)}) collective-permute-start(bf16[32,3584]{1,0:T(8,128)(2,1)} %get-tuple-element.383), channel_id=1, source_target_pairs={{8,0},{16,8},{24,16},{32,24},{40,32},{48,40},{56,48},{64,56},{72,6... | collective-permute-start | bytes 688136 | tf_op jit(solution)/shard_map/while/body/eval_jaxpr/ppermute | solution.py:22
  167.5 9.1 %collective-permute-start = (bf16[32,3584]{1,0:T(8,128)(2,1)}, bf16[32,3584]{1,0:T(8,128)(2,1)S(1)}, u32[]{:S(2)}, u32[]{:S(2)}) collective-permute-start(bf16[32,3584]{1,0:T(8,128)(2,1)} %get-tuple-element.383), channel_id=1, source_target_pairs={{8,0},{16,8},{24,16},{32,24},{40,32},{48,40},{56,48},{64,56},{72,6... | collective-permute-start | bytes 688136 | tf_op jit(solution)/shard_map/while/body/eval_jaxpr/ppermute | solution.py:22
  183.4 9.1 %collective-permute-start = (bf16[32,3584]{1,0:T(8,128)(2,1)}, bf16[32,3584]{1,0:T(8,128)(2,1)S(1)}, u32[]{:S(2)}, u32[]{:S(2)}) collective-permute-start(bf16[32,3584]{1,0:T(8,128)(2,1)} %get-tuple-element.383), channel_id=1, source_target_pairs={{8,0},{16,8},{24,16},{32,24},{40,32},{48,40},{56,48},{64,56},{72,6... | collective-permute-start | bytes 688136 | tf_op jit(solution)/shard_map/while/body/eval_jaxpr/ppermute | solution.py:22
  199.3 9.1 %collective-permute-start = (bf16[32,3584]{1,0:T(8,128)(2,1)}, bf16[32,3584]{1,0:T(8,128)(2,1)S(1)}, u32[]{:S(2)}, u32[]{:S(2)}) collective-permute-start(bf16[32,3584]{1,0:T(8,128)(2,1)} %get-tuple-element.383), channel_id=1, source_target_pairs={{8,0},{16,8},{24,16},{32,24},{40,32},{48,40},{56,48},{64,56},{72,6... | collective-permute-start | bytes 688136 | tf_op jit(solution)/shard_map/while/body/eval_jaxpr/ppermute | solution.py:22
  215.2 9.1 %collective-permute-start = (bf16[32,3584]{1,0:T(8,128)(2,1)}, bf16[32,3584]{1,0:T(8,128)(2,1)S(1)}, u32[]{:S(2)}, u32[]{:S(2)}) collective-permute-start(bf16[32,3584]{1,0:T(8,128)(2,1)} %get-tuple-element.383), channel_id=1, source_target_pairs={{8,0},{16,8},{24,16},{32,24},{40,32},{48,40},{56,48},{64,56},{72,6... | collective-permute-start | bytes 688136 | tf_op jit(solution)/shard_map/while/body/eval_jaxpr/ppermute | solution.py:22
  231.2 9.1 %collective-permute-start = (bf16[32,3584]{1,0:T(8,128)(2,1)}, bf16[32,3584]{1,0:T(8,128)(2,1)S(1)}, u32[]{:S(2)}, u32[]{:S(2)}) collective-permute-start(bf16[32,3584]{1,0:T(8,128)(2,1)} %get-tuple-element.383), channel_id=1, source_target_pairs={{8,0},{16,8},{24,16},{32,24},{40,32},{48,40},{56,48},{64,56},{72,6... | collective-permute-start | bytes 688136 | tf_op jit(solution)/shard_map/while/body/eval_jaxpr/ppermute | solution.py:22
  247.1 10.0 %collective-permute-start = (bf16[32,3584]{1,0:T(8,128)(2,1)}, bf16[32,3584]{1,0:T(8,128)(2,1)S(1)}, u32[]{:S(2)}, u32[]{:S(2)}) collective-permute-start(bf16[32,3584]{1,0:T(8,128)(2,1)} %get-tuple-element.383), channel_id=1, source_target_pairs={{8,0},{16,8},{24,16},{32,24},{40,32},{48,40},{56,48},{64,56},{72,6... | collective-permute-start | bytes 688136 | tf_op jit(solution)/shard_map/while/body/eval_jaxpr/ppermute | solution.py:22
  264.0 11.1 %collective-permute-start = (bf16[32,3584]{1,0:T(8,128)(2,1)}, bf16[32,3584]{1,0:T(8,128)(2,1)S(1)}, u32[]{:S(2)}, u32[]{:S(2)}) collective-permute-start(bf16[32,3584]{1,0:T(8,128)(2,1)} %get-tuple-element.383), channel_id=1, source_target_pairs={{8,0},{16,8},{24,16},{32,24},{40,32},{48,40},{56,48},{64,56},{72,6... | collective-permute-start | bytes 688136 | tf_op jit(solution)/shard_map/while/body/eval_jaxpr/ppermute | solution.py:22
  281.9 10.8 %collective-permute-start = (bf16[32,3584]{1,0:T(8,128)(2,1)}, bf16[32,3584]{1,0:T(8,128)(2,1)S(1)}, u32[]{:S(2)}, u32[]{:S(2)}) collective-permute-start(bf16[32,3584]{1,0:T(8,128)(2,1)} %get-tuple-element.383), channel_id=1, source_target_pairs={{8,0},{16,8},{24,16},{32,24},{40,32},{48,40},{56,48},{64,56},{72,6... | collective-permute-start | bytes 688136 | tf_op jit(solution)/shard_map/while/body/eval_jaxpr/ppermute | solution.py:22
  299.6 10.2 %collective-permute-start = (bf16[32,3584]{1,0:T(8,128)(2,1)}, bf16[32,3584]{1,0:T(8,128)(2,1)S(1)}, u32[]{:S(2)}, u32[]{:S(2)}) collective-permute-start(bf16[32,3584]{1,0:T(8,128)(2,1)} %get-tuple-element.383), channel_id=1, source_target_pairs={{8,0},{16,8},{24,16},{32,24},{40,32},{48,40},{56,48},{64,56},{72,6... | collective-permute-start | bytes 688136 | tf_op jit(solution)/shard_map/while/body/eval_jaxpr/ppermute | solution.py:22
  316.6 9.4 %collective-permute-start = (bf16[32,3584]{1,0:T(8,128)(2,1)}, bf16[32,3584]{1,0:T(8,128)(2,1)S(1)}, u32[]{:S(2)}, u32[]{:S(2)}) collective-permute-start(bf16[32,3584]{1,0:T(8,128)(2,1)} %get-tuple-element.383), channel_id=1, source_target_pairs={{8,0},{16,8},{24,16},{32,24},{40,32},{48,40},{56,48},{64,56},{72,6... | collective-permute-start | bytes 688136 | tf_op jit(solution)/shard_map/while/body/eval_jaxpr/ppermute | solution.py:22
  332.8 9.1 %collective-permute-start = (bf16[32,3584]{1,0:T(8,128)(2,1)}, bf16[32,3584]{1,0:T(8,128)(2,1)S(1)}, u32[]{:S(2)}, u32[]{:S(2)}) collective-permute-start(bf16[32,3584]{1,0:T(8,128)(2,1)} %get-tuple-element.383), channel_id=1, source_target_pairs={{8,0},{16,8},{24,16},{32,24},{40,32},{48,40},{56,48},{64,56},{72,6... | collective-permute-start | bytes 688136 | tf_op jit(solution)/shard_map/while/body/eval_jaxpr/ppermute | solution.py:22
  348.8 9.1 %collective-permute-start = (bf16[32,3584]{1,0:T(8,128)(2,1)}, bf16[32,3584]{1,0:T(8,128)(2,1)S(1)}, u32[]{:S(2)}, u32[]{:S(2)}) collective-permute-start(bf16[32,3584]{1,0:T(8,128)(2,1)} %get-tuple-element.383), channel_id=1, source_target_pairs={{8,0},{16,8},{24,16},{32,24},{40,32},{48,40},{56,48},{64,56},{72,6... | collective-permute-start | bytes 688136 | tf_op jit(solution)/shard_map/while/body/eval_jaxpr/ppermute | solution.py:22
  364.7 9.1 %collective-permute-start = (bf16[32,3584]{1,0:T(8,128)(2,1)}, bf16[32,3584]{1,0:T(8,128)(2,1)S(1)}, u32[]{:S(2)}, u32[]{:S(2)}) collective-permute-start(bf16[32,3584]{1,0:T(8,128)(2,1)} %get-tuple-element.383), channel_id=1, source_target_pairs={{8,0},{16,8},{24,16},{32,24},{40,32},{48,40},{56,48},{64,56},{72,6... | collective-permute-start | bytes 688136 | tf_op jit(solution)/shard_map/while/body/eval_jaxpr/ppermute | solution.py:22
  380.7 9.1 %collective-permute-start = (bf16[32,3584]{1,0:T(8,128)(2,1)}, bf16[32,3584]{1,0:T(8,128)(2,1)S(1)}, u32[]{:S(2)}, u32[]{:S(2)}) collective-permute-start(bf16[32,3584]{1,0:T(8,128)(2,1)} %get-tuple-element.383), channel_id=1, source_target_pairs={{8,0},{16,8},{24,16},{32,24},{40,32},{48,40},{56,48},{64,56},{72,6... | collective-permute-start | bytes 688136 | tf_op jit(solution)/shard_map/while/body/eval_jaxpr/ppermute | solution.py:22
  396.6 9.1 %collective-permute-start = (bf16[32,3584]{1,0:T(8,128)(2,1)}, bf16[32,3584]{1,0:T(8,128)(2,1)S(1)}, u32[]{:S(2)}, u32[]{:S(2)}) collective-permute-start(bf16[32,3584]{1,0:T(8,128)(2,1)} %get-tuple-element.383), channel_id=1, source_target_pairs={{8,0},{16,8},{24,16},{32,24},{40,32},{48,40},{56,48},{64,56},{72,6... | collective-permute-start | bytes 688136 | tf_op jit(solution)/shard_map/while/body/eval_jaxpr/ppermute | solution.py:22
  412.6 9.1 %collective-permute-start = (bf16[32,3584]{1,0:T(8,128)(2,1)}, bf16[32,3584]{1,0:T(8,128)(2,1)S(1)}, u32[]{:S(2)}, u32[]{:S(2)}) collective-permute-start(bf16[32,3584]{1,0:T(8,128)(2,1)} %get-tuple-element.383), channel_id=1, source_target_pairs={{8,0},{16,8},{24,16},{32,24},{40,32},{48,40},{56,48},{64,56},{72,6... | collective-permute-start | bytes 688136 | tf_op jit(solution)/shard_map/while/body/eval_jaxpr/ppermute | solution.py:22
  428.5 9.1 %collective-permute-start = (bf16[32,3584]{1,0:T(8,128)(2,1)}, bf16[32,3584]{1,0:T(8,128)(2,1)S(1)}, u32[]{:S(2)}, u32[]{:S(2)}) collective-permute-start(bf16[32,3584]{1,0:T(8,128)(2,1)} %get-tuple-element.383), channel_id=1, source_target_pairs={{8,0},{16,8},{24,16},{32,24},{40,32},{48,40},{56,48},{64,56},{72,6... | collective-permute-start | bytes 688136 | tf_op jit(solution)/shard_map/while/body/eval_jaxpr/ppermute | solution.py:22
  444.4 9.1 %collective-permute-start = (bf16[32,3584]{1,0:T(8,128)(2,1)}, bf16[32,3584]{1,0:T(8,128)(2,1)S(1)}, u32[]{:S(2)}, u32[]{:S(2)}) collective-permute-start(bf16[32,3584]{1,0:T(8,128)(2,1)} %get-tuple-element.383), channel_id=1, source_target_pairs={{8,0},{16,8},{24,16},{32,24},{40,32},{48,40},{56,48},{64,56},{72,6... | collective-permute-start | bytes 688136 | tf_op jit(solution)/shard_map/while/body/eval_jaxpr/ppermute | solution.py:22
  460.4 9.1 %collective-permute-start = (bf16[32,3584]{1,0:T(8,128)(2,1)}, bf16[32,3584]{1,0:T(8,128)(2,1)S(1)}, u32[]{:S(2)}, u32[]{:S(2)}) collective-permute-start(bf16[32,3584]{1,0:T(8,128)(2,1)} %get-tuple-element.383), channel_id=1, source_target_pairs={{8,0},{16,8},{24,16},{32,24},{40,32},{48,40},{56,48},{64,56},{72,6... | collective-permute-start | bytes 688136 | tf_op jit(solution)/shard_map/while/body/eval_jaxpr/ppermute | solution.py:22
  476.3 9.1 %collective-permute-start = (bf16[32,3584]{1,0:T(8,128)(2,1)}, bf16[32,3584]{1,0:T(8,128)(2,1)S(1)}, u32[]{:S(2)}, u32[]{:S(2)}) collective-permute-start(bf16[32,3584]{1,0:T(8,128)(2,1)} %get-tuple-element.383), channel_id=1, source_target_pairs={{8,0},{16,8},{24,16},{32,24},{40,32},{48,40},{56,48},{64,56},{72,6... | collective-permute-start | bytes 688136 | tf_op jit(solution)/shard_map/while/body/eval_jaxpr/ppermute | solution.py:22
  492.3 9.6 %collective-permute-start = (bf16[32,3584]{1,0:T(8,128)(2,1)}, bf16[32,3584]{1,0:T(8,128)(2,1)S(1)}, u32[]{:S(2)}, u32[]{:S(2)}) collective-permute-start(bf16[32,3584]{1,0:T(8,128)(2,1)} %get-tuple-element.383), channel_id=1, source_target_pairs={{8,0},{16,8},{24,16},{32,24},{40,32},{48,40},{56,48},{64,56},{72,6... | collective-permute-start | bytes 688136 | tf_op jit(solution)/shard_map/while/body/eval_jaxpr/ppermute | solution.py:22
  508.8 10.7 %collective-permute-start = (bf16[32,3584]{1,0:T(8,128)(2,1)}, bf16[32,3584]{1,0:T(8,128)(2,1)S(1)}, u32[]{:S(2)}, u32[]{:S(2)}) collective-permute-start(bf16[32,3584]{1,0:T(8,128)(2,1)} %get-tuple-element.383), channel_id=1, source_target_pairs={{8,0},{16,8},{24,16},{32,24},{40,32},{48,40},{56,48},{64,56},{72,6... | collective-permute-start | bytes 688136 | tf_op jit(solution)/shard_map/while/body/eval_jaxpr/ppermute | solution.py:22
  526.4 11.3 %collective-permute-start = (bf16[32,3584]{1,0:T(8,128)(2,1)}, bf16[32,3584]{1,0:T(8,128)(2,1)S(1)}, u32[]{:S(2)}, u32[]{:S(2)}) collective-permute-start(bf16[32,3584]{1,0:T(8,128)(2,1)} %get-tuple-element.383), channel_id=1, source_target_pairs={{8,0},{16,8},{24,16},{32,24},{40,32},{48,40},{56,48},{64,56},{72,6... | collective-permute-start | bytes 688136 | tf_op jit(solution)/shard_map/while/body/eval_jaxpr/ppermute | solution.py:22
  544.5 10.7 %collective-permute-start = (bf16[32,3584]{1,0:T(8,128)(2,1)}, bf16[32,3584]{1,0:T(8,128)(2,1)S(1)}, u32[]{:S(2)}, u32[]{:S(2)}) collective-permute-start(bf16[32,3584]{1,0:T(8,128)(2,1)} %get-tuple-element.383), channel_id=1, source_target_pairs={{8,0},{16,8},{24,16},{32,24},{40,32},{48,40},{56,48},{64,56},{72,6... | collective-permute-start | bytes 688136 | tf_op jit(solution)/shard_map/while/body/eval_jaxpr/ppermute | solution.py:22
  562.0 9.8 %collective-permute-start = (bf16[32,3584]{1,0:T(8,128)(2,1)}, bf16[32,3584]{1,0:T(8,128)(2,1)S(1)}, u32[]{:S(2)}, u32[]{:S(2)}) collective-permute-start(bf16[32,3584]{1,0:T(8,128)(2,1)} %get-tuple-element.383), channel_id=1, source_target_pairs={{8,0},{16,8},{24,16},{32,24},{40,32},{48,40},{56,48},{64,56},{72,6... | collective-permute-start | bytes 688136 | tf_op jit(solution)/shard_map/while/body/eval_jaxpr/ppermute | solution.py:22
  578.7 9.4 %collective-permute-start = (bf16[32,3584]{1,0:T(8,128)(2,1)}, bf16[32,3584]{1,0:T(8,128)(2,1)S(1)}, u32[]{:S(2)}, u32[]{:S(2)}) collective-permute-start(bf16[32,3584]{1,0:T(8,128)(2,1)} %get-tuple-element.383), channel_id=1, source_target_pairs={{8,0},{16,8},{24,16},{32,24},{40,32},{48,40},{56,48},{64,56},{72,6... | collective-permute-start | bytes 688136 | tf_op jit(solution)/shard_map/while/body/eval_jaxpr/ppermute | solution.py:22
  594.9 9.1 %collective-permute-start = (bf16[32,3584]{1,0:T(8,128)(2,1)}, bf16[32,3584]{1,0:T(8,128)(2,1)S(1)}, u32[]{:S(2)}, u32[]{:S(2)}) collective-permute-start(bf16[32,3584]{1,0:T(8,128)(2,1)} %get-tuple-element.383), channel_id=1, source_target_pairs={{8,0},{16,8},{24,16},{32,24},{40,32},{48,40},{56,48},{64,56},{72,6... | collective-permute-start | bytes 688136 | tf_op jit(solution)/shard_map/while/body/eval_jaxpr/ppermute | solution.py:22
  610.9 9.1 %collective-permute-start = (bf16[32,3584]{1,0:T(8,128)(2,1)}, bf16[32,3584]{1,0:T(8,128)(2,1)S(1)}, u32[]{:S(2)}, u32[]{:S(2)}) collective-permute-start(bf16[32,3584]{1,0:T(8,128)(2,1)} %get-tuple-element.383), channel_id=1, source_target_pairs={{8,0},{16,8},{24,16},{32,24},{40,32},{48,40},{56,48},{64,56},{72,6... | collective-permute-start | bytes 688136 | tf_op jit(solution)/shard_map/while/body/eval_jaxpr/ppermute | solution.py:22
  626.8 9.1 %collective-permute-start = (bf16[32,3584]{1,0:T(8,128)(2,1)}, bf16[32,3584]{1,0:T(8,128)(2,1)S(1)}, u32[]{:S(2)}, u32[]{:S(2)}) collective-permute-start(bf16[32,3584]{1,0:T(8,128)(2,1)} %get-tuple-element.383), channel_id=1, source_target_pairs={{8,0},{16,8},{24,16},{32,24},{40,32},{48,40},{56,48},{64,56},{72,6... | collective-permute-start | bytes 688136 | tf_op jit(solution)/shard_map/while/body/eval_jaxpr/ppermute | solution.py:22
  642.7 9.1 %collective-permute-start = (bf16[32,3584]{1,0:T(8,128)(2,1)}, bf16[32,3584]{1,0:T(8,128)(2,1)S(1)}, u32[]{:S(2)}, u32[]{:S(2)}) collective-permute-start(bf16[32,3584]{1,0:T(8,128)(2,1)} %get-tuple-element.383), channel_id=1, source_target_pairs={{8,0},{16,8},{24,16},{32,24},{40,32},{48,40},{56,48},{64,56},{72,6... | collective-permute-start | bytes 688136 | tf_op jit(solution)/shard_map/while/body/eval_jaxpr/ppermute | solution.py:22
  658.7 9.1 %collective-permute-start = (bf16[32,3584]{1,0:T(8,128)(2,1)}, bf16[32,3584]{1,0:T(8,128)(2,1)S(1)}, u32[]{:S(2)}, u32[]{:S(2)}) collective-permute-start(bf16[32,3584]{1,0:T(8,128)(2,1)} %get-tuple-element.383), channel_id=1, source_target_pairs={{8,0},{16,8},{24,16},{32,24},{40,32},{48,40},{56,48},{64,56},{72,6... | collective-permute-start | bytes 688136 | tf_op jit(solution)/shard_map/while/body/eval_jaxpr/ppermute | solution.py:22
  677.6 70.3 %all-to-all-start = ((f32[8,1,448]{2,1,0:T(1,128)}), f32[8,1,448]{2,1,0:T(1,128)S(1)}, u32[]{:S(2)}, u32[]{:S(2)}) async-start(f32[8,1,448]{2,1,0:T(1,128)} %all_to_all.6), calls=%async_computation | async-start | bytes 32768 | tf_op jit(solution)/shard_map/all_to_all | solution.py:241
  725.3 4.4 copy-start.2
  729.7 6.1 copy-start.6
  735.8 1.6 copy-start
  737.3 2.2 copy-start.5

commit v5 on v4

--- a/solution.py
+++ b/solution.py
@@ -8,7 +8,7 @@
 from jax.experimental.pallas import tpu as pltpu
 from jax.sharding import PartitionSpec as P
 
-GROUPS = 8
+GROUPS = 16
 WINDOW = 32
 
 
@@ -31,16 +31,17 @@
 
 
 def turn_kernel(
-    flags_ref,
+    turn_ref, stage_ref,
     w_hbm, g_hbm, ig_hbm, msg_ref, loss_ref, normed_ref, inv_ref, gain_ref,
     out_ref, g_out, ig_out,
     w_v, g_v, inc_v, gn_v, sems,
-    *, group_lanes, head_size, rows_here, groups, seq_rows, feature_count,
+    *, group_lanes, head_size, rows_here, groups, seq_rows, feature_count, stage_count, unit_count,
 ):
-    chosen = flags_ref[0]
-    from_loss = flags_ref[1] == 1
-    active = flags_ref[2] == 1
-    slot = pl.multiple_of(flags_ref[3], rows_here)
+    unit_index = turn_ref[0] - (stage_count - 1 - stage_ref[0])
+    active = (unit_index >= 0) & (unit_index < unit_count)
+    chosen = jnp.clip(unit_count - 1 - unit_index, 0, unit_count - 1)
+    from_loss = stage_ref[0] == stage_count - 1
+    slot = pl.multiple_of(jnp.where(active, chosen * rows_here, seq_rows), rows_here)
     group_heads = group_lanes // head_size
     reads = []
     for g in range(groups):
@@ -93,30 +94,35 @@
     ig_write.wait()
 
 
-def turn_call(flags, w_split, grad_buffer, input_grads, message, from_loss, normed, inverse, gain,
-              *, head_size, rows_here):
+def turn_call(turn, stage, w_split, grad_buffer, input_grads, message, from_loss, normed, inverse,
+              gain, *, head_size, rows_here, stage_count):
     groups, group_heads, unit_count, _, seq_rows = w_split.shape
     feature_count = grad_buffer.shape[1]
     group_lanes = feature_count // groups
     kernel = functools.partial(
         turn_kernel, group_lanes=group_lanes, head_size=head_size, rows_here=rows_here,
-        groups=groups, seq_rows=seq_rows, feature_count=feature_count,
-    )
+        groups=groups, seq_rows=seq_rows, feature_count=feature_count, stage_count=stage_count,
+        unit_count=unit_count,
+    )
+
+    def chunk_of(i, t, s):
+        return jnp.clip(unit_count - 1 - (t[0] - (stage_count - 1 - s[0])), 0, unit_count - 1)
+
     grid_spec = pltpu.PrefetchScalarGridSpec(
-        num_scalar_prefetch=1,
+        num_scalar_prefetch=2,
         grid=(1,),
         in_specs=[
             pl.BlockSpec(memory_space=pl.ANY),
             pl.BlockSpec(memory_space=pl.ANY),
             pl.BlockSpec(memory_space=pl.ANY),
-            pl.BlockSpec((rows_here, feature_count), lambda i, f: (0, 0)),
-            pl.BlockSpec((rows_here, feature_count), lambda i, f: (f[0], 0)),
-            pl.BlockSpec((rows_here, feature_count), lambda i, f: (f[0], 0)),
-            pl.BlockSpec((rows_here, 1), lambda i, f: (f[0], 0)),
-            pl.BlockSpec((1, feature_count), lambda i, f: (0, 0)),
+            pl.BlockSpec((rows_here, feature_count), lambda i, t, s: (0, 0)),
+            pl.BlockSpec((rows_here, feature_count), lambda i, t, s: (chunk_of(i, t, s), 0)),
+            pl.BlockSpec((rows_here, feature_count), lambda i, t, s: (chunk_of(i, t, s), 0)),
+            pl.BlockSpec((rows_here, 1), lambda i, t, s: (chunk_of(i, t, s), 0)),
+            pl.BlockSpec((1, feature_count), lambda i, t, s: (0, 0)),
         ],
         out_specs=[
-            pl.BlockSpec((rows_here, feature_count), lambda i, f: (0, 0)),
+            pl.BlockSpec((rows_here, feature_count), lambda i, t, s: (0, 0)),
             pl.BlockSpec(memory_space=pl.ANY),
             pl.BlockSpec(memory_space=pl.ANY),
         ],
@@ -136,9 +142,9 @@
             jax.ShapeDtypeStruct(grad_buffer.shape, grad_buffer.dtype),
             jax.ShapeDtypeStruct(input_grads.shape, input_grads.dtype),
         ],
-        input_output_aliases={2: 1, 3: 2},
+        input_output_aliases={3: 1, 4: 2},
         compiler_params=pltpu.CompilerParams(dimension_semantics=("arbitrary",)),
-    )(flags, w_split, grad_buffer, input_grads, message, from_loss, normed, inverse, gain)
+    )(turn, stage, w_split, grad_buffer, input_grads, message, from_loss, normed, inverse, gain)
 
 
 def on_device(query_acts, key_acts, layer_inputs, grad_out, norm_gains, window_flags):
@@ -188,19 +194,15 @@
     w_split = weights_low.reshape(
         groups, group_lanes // head_size, unit_count, rows_here, seq_rows
     )
-    last_stage = (section_index == section_count - 1).astype(jnp.int32)
+    stage = section_index.astype(jnp.int32).reshape(1)
     gain_line = gain_row[None, :]
 
     def one_turn(turn_index, carried):
         message, grad_buffer, input_grads = carried
-        unit_index = turn_index - (section_count - 1 - section_index)
-        active = (unit_index >= 0) & (unit_index < unit_count)
-        chosen = jnp.clip(unit_count - 1 - unit_index, 0, unit_count - 1)
-        slot = jnp.where(active, chosen * rows_here, seq_rows)
-        flags = jnp.stack([chosen, last_stage, active.astype(jnp.int32), slot])
         grad_input, grad_buffer, input_grads = turn_call(
-            flags, w_split, grad_buffer, input_grads, message, from_loss, normed, inverse,
-            gain_line, head_size=head_size, rows_here=rows_here,
+            turn_index.astype(jnp.int32).reshape(1), stage, w_split, grad_buffer, input_grads,
+            message, from_loss, normed, inverse, gain_line,
+            head_size=head_size, rows_here=rows_here, stage_count=section_count,
         )
         return (passed_along(grad_input, "pipe", -1), grad_buffer, input_grads)
 

time: 752 us -> 725 us (0.964)
  starting transfers between devices: 279 us -> 332 us
  waiting for transfers between devices: 140 us -> 102 us
  other arithmetic: 35.8 us -> 10.2 us
  Pallas kernels: 241 us -> 223 us
    ppermute x39 -> x47, starting transfers between devices: 231 us -> 275 us  [passed_along(): lax.ppermute(value, axis, [(source, source + steps) for source in range(l...]
    ppermute x39 -> x47, waiting for transfers between devices: 140 us -> 102 us  [passed_along(): lax.ppermute(value, axis, [(source, source + steps) for source in range(l...]
    another operation x39 -> x0, other arithmetic: 25.6 us -> none  [one_turn(): flags = jnp.stack([chosen, last_stage, active.astype(jnp.int32), slot])]
    pallas_call x39 -> x47, Pallas kernels: 241 us -> 223 us  [turn_call(): pl.pallas_call(kernel, grid_spec=grid_spec, out_shape=[jax.ShapeDtypeStru...]
    all_to_all x1, starting transfers between devices: 47.6 us -> 57.5 us  [on_device(): lax.all_to_all(gain_sum.reshape(group_count, feature_count // group_count...]
  transfers between devices with their start and end apart: 40 -> 48, of which waited for: 39 -> 47; matrix products, arithmetic and copies ran while one was open for 3% -> 3% of each run, Pallas kernels for 0% -> 0%
where the time goes in v5:
time: 725 us; the launch traced here: 720 us
  starting transfers between devices  332 us (46%)
  Pallas kernels  223 us (31%)
  waiting for transfers between devices  102 us (14%)
  local copies, waits for them, and re-layouts  27.9 us (4%)
  matrix products  23 us (3%)
  other arithmetic  10.2 us (1%)
    ppermute x47, starting transfers between devices, passed_along(): lax.ppermute(value, axis, [(source, source + steps) for source in range(l...  275 us
    pallas_call x47, Pallas kernels, turn_call(): pl.pallas_call(kernel, grid_spec=grid_spec, out_shape=[jax.ShapeDtypeStru...  223 us
    ppermute x47, waiting for transfers between devices, passed_along(): lax.ppermute(value, axis, [(source, source + steps) for source in range(l...  102 us
    all_to_all x1, starting transfers between devices, on_device(): lax.all_to_all(gain_sum.reshape(group_count, feature_count // group_count...  57.5 us
    unnamed x22, local copies, waits for them, and re-layouts  15.9 us
  transfers between devices with their start and end apart: 48, of which 47 were waited for; matrix products, arithmetic and copies ran while one was open for 3% of the time, Pallas kernels for 0%

profile of v5, /device:TPU:15, one launch (start us, length us, event | category | flops | bytes accessed | tf_op | source)
XLA Modules:
  0.0 719.5 jit_solution(942925606357882523)
XLA Ops:
  28.9 600.0 %while.17 = (s32[]{:T(128)}, bf16[16,3584]{1,0:T(8,128)(2,1)S(1)}, bf16[272,3584]{1,0:T(8,128)(2,1)S(1)}, bf16[272,3584]{1,0:T(8,128)(2,1)}, s32[1]{0:T(128)}, /...) while((s32[]{:T(128)}, bf16[16,3584]{1,0:T(8,128)(2,1)S(1)}, ...), condition=%wide.region_4.5_spmd, body=%wide.region_3.4_spmd.sunk | while | flops 2 | bytes 458901 | solution.py:214
  33.7 7.7 %collective-permute-start = (bf16[16,3584]{1,0:T(8,128)(2,1)}, bf16[16,3584]{1,0:T(8,128)(2,1)S(1)}, u32[]{:S(2)}, u32[]{:S(2)}) collective-permute-start(bf16[16,3584]{1,0:T(8,128)(2,1)} %get-tuple-element.282), channel_id=1, source_target_pairs={{8,0},{16,8},{24,16},{32,24},{40,32},{48,40},{56,48},{64,56},{72,6... | collective-permute-start | bytes 344072 | tf_op jit(solution)/shard_map/while/body/eval_jaxpr/ppermute | solution.py:22
  48.3 6.1 collective-permute-start
  61.2 5.8 collective-permute-start
  73.8 5.8 collective-permute-start
  86.4 5.8 collective-permute-start
  99.0 5.8 collective-permute-start
  111.6 5.8 collective-permute-start
  124.2 5.8 collective-permute-start
  136.8 5.8 collective-permute-start
  149.4 5.8 collective-permute-start
  162.0 5.8 collective-permute-start
  174.6 5.8 collective-permute-start
  188.1 5.9 collective-permute-start
  201.1 6.1 collective-permute-start
  214.1 5.7 collective-permute-start
  226.7 5.8 collective-permute-start
  239.3 5.8 collective-permute-start
  251.8 5.8 collective-permute-start
  264.4 5.8 collective-permute-start
  277.0 5.8 collective-permute-start
  289.6 5.8 collective-permute-start
  302.2 5.8 collective-permute-start
  314.8 5.8 collective-permute-start
  322.7 4.8 eval_jaxpr.5
  327.5 5.8 collective-permute-start
  340.7 5.8 collective-permute-start
  349.2 4.8 eval_jaxpr.5
  353.9 6.1 collective-permute-start
  362.1 4.8 eval_jaxpr.5
  366.9 5.8 collective-permute-start
  374.7 4.8 eval_jaxpr.5
  379.5 5.8 collective-permute-start
  387.4 4.8 eval_jaxpr.5
  392.1 5.8 collective-permute-start
  400.0 4.8 eval_jaxpr.5
  404.7 5.8 collective-permute-start
  412.6 4.8 eval_jaxpr.5
  417.4 5.8 collective-permute-start
  425.2 4.8 eval_jaxpr.5
  430.0 5.8 collective-permute-start
  437.8 4.8 eval_jaxpr.5
  442.6 5.8 collective-permute-start
  450.4 4.8 eval_jaxpr.5
  455.2 5.8 collective-permute-start
  463.1 4.8 eval_jaxpr.5
  467.8 5.8 collective-permute-start
  475.7 4.8 eval_jaxpr.5
  480.4 5.8 collective-permute-start
  493.4 5.8 collective-permute-start
  502.1 4.8 eval_jaxpr.5
  506.9 6.1 collective-permute-start
  519.8 6.1 collective-permute-start
  532.8 5.8 collective-permute-start
  545.4 5.8 collective-permute-start
  558.0 5.8 collective-permute-start
  570.6 5.8 collective-permute-start
  583.3 5.8 collective-permute-start
  595.9 5.8 collective-permute-start
  608.5 5.8 collective-permute-start
  621.1 5.8 collective-permute-start
  633.2 4.9 fusion.1
  638.8 57.5 %all-to-all-start = ((f32[8,1,448]{2,1,0:T(1,128)}), f32[8,1,448]{2,1,0:T(1,128)S(1)}, u32[]{:S(2)}, u32[]{:S(2)}) async-start(f32[8,1,448]{2,1,0:T(1,128)} %all_to_all.6), calls=%async_computation | async-start | bytes 32768 | tf_op jit(solution)/shard_map/all_to_all | solution.py:243
  700.8 6.1 multiply_convert_fusion
  (130 shorter events, 312.9 us)
Async XLA Ops:
  0.7 6.0 copy-start.8
  9.6 8.5 %copy-start.4 = (bf16[1,1,256,3584]{2,3,1,0:T(8,128)(2,1)}, bf16[1,1,256,3584]{2,3,1,0:T(8,128)(2,1)S(1)}, u32[]{:S(2)}) copy-start(bf16[1,1,256,3584]{2,3,1,0:T(8,128)(2,1)S(1)} %copy.27) | copy-start | bytes 5505028
  18.1 3.2 copy-start.1
  21.3 3.6 copy-start.3
  24.9 4.0 copy-start.7
  33.7 9.8 %collective-permute-start = (bf16[16,3584]{1,0:T(8,128)(2,1)}, bf16[16,3584]{1,0:T(8,128)(2,1)S(1)}, u32[]{:S(2)}, u32[]{:S(2)}) collective-permute-start(bf16[16,3584]{1,0:T(8,128)(2,1)} %get-tuple-element.282), channel_id=1, source_target_pairs={{8,0},{16,8},{24,16},{32,24},{40,32},{48,40},{56,48},{64,56},{72,6... | collective-permute-start | bytes 344072 | tf_op jit(solution)/shard_map/while/body/eval_jaxpr/ppermute | solution.py:22
  48.3 8.2 %collective-permute-start = (bf16[16,3584]{1,0:T(8,128)(2,1)}, bf16[16,3584]{1,0:T(8,128)(2,1)S(1)}, u32[]{:S(2)}, u32[]{:S(2)}) collective-permute-start(bf16[16,3584]{1,0:T(8,128)(2,1)} %get-tuple-element.282), channel_id=1, source_target_pairs={{8,0},{16,8},{24,16},{32,24},{40,32},{48,40},{56,48},{64,56},{72,6... | collective-permute-start | bytes 344072 | tf_op jit(solution)/shard_map/while/body/eval_jaxpr/ppermute | solution.py:22
  61.2 7.9 %collective-permute-start = (bf16[16,3584]{1,0:T(8,128)(2,1)}, bf16[16,3584]{1,0:T(8,128)(2,1)S(1)}, u32[]{:S(2)}, u32[]{:S(2)}) collective-permute-start(bf16[16,3584]{1,0:T(8,128)(2,1)} %get-tuple-element.282), channel_id=1, source_target_pairs={{8,0},{16,8},{24,16},{32,24},{40,32},{48,40},{56,48},{64,56},{72,6... | collective-permute-start | bytes 344072 | tf_op jit(solution)/shard_map/while/body/eval_jaxpr/ppermute | solution.py:22
  73.8 7.9 %collective-permute-start = (bf16[16,3584]{1,0:T(8,128)(2,1)}, bf16[16,3584]{1,0:T(8,128)(2,1)S(1)}, u32[]{:S(2)}, u32[]{:S(2)}) collective-permute-start(bf16[16,3584]{1,0:T(8,128)(2,1)} %get-tuple-element.282), channel_id=1, source_target_pairs={{8,0},{16,8},{24,16},{32,24},{40,32},{48,40},{56,48},{64,56},{72,6... | collective-permute-start | bytes 344072 | tf_op jit(solution)/shard_map/while/body/eval_jaxpr/ppermute | solution.py:22
  86.4 7.9 %collective-permute-start = (bf16[16,3584]{1,0:T(8,128)(2,1)}, bf16[16,3584]{1,0:T(8,128)(2,1)S(1)}, u32[]{:S(2)}, u32[]{:S(2)}) collective-permute-start(bf16[16,3584]{1,0:T(8,128)(2,1)} %get-tuple-element.282), channel_id=1, source_target_pairs={{8,0},{16,8},{24,16},{32,24},{40,32},{48,40},{56,48},{64,56},{72,6... | collective-permute-start | bytes 344072 | tf_op jit(solution)/shard_map/while/body/eval_jaxpr/ppermute | solution.py:22
  99.0 7.9 %collective-permute-start = (bf16[16,3584]{1,0:T(8,128)(2,1)}, bf16[16,3584]{1,0:T(8,128)(2,1)S(1)}, u32[]{:S(2)}, u32[]{:S(2)}) collective-permute-start(bf16[16,3584]{1,0:T(8,128)(2,1)} %get-tuple-element.282), channel_id=1, source_target_pairs={{8,0},{16,8},{24,16},{32,24},{40,32},{48,40},{56,48},{64,56},{72,6... | collective-permute-start | bytes 344072 | tf_op jit(solution)/shard_map/while/body/eval_jaxpr/ppermute | solution.py:22
  111.6 7.9 %collective-permute-start = (bf16[16,3584]{1,0:T(8,128)(2,1)}, bf16[16,3584]{1,0:T(8,128)(2,1)S(1)}, u32[]{:S(2)}, u32[]{:S(2)}) collective-permute-start(bf16[16,3584]{1,0:T(8,128)(2,1)} %get-tuple-element.282), channel_id=1, source_target_pairs={{8,0},{16,8},{24,16},{32,24},{40,32},{48,40},{56,48},{64,56},{72,6... | collective-permute-start | bytes 344072 | tf_op jit(solution)/shard_map/while/body/eval_jaxpr/ppermute | solution.py:22
  124.2 7.9 %collective-permute-start = (bf16[16,3584]{1,0:T(8,128)(2,1)}, bf16[16,3584]{1,0:T(8,128)(2,1)S(1)}, u32[]{:S(2)}, u32[]{:S(2)}) collective-permute-start(bf16[16,3584]{1,0:T(8,128)(2,1)} %get-tuple-element.282), channel_id=1, source_target_pairs={{8,0},{16,8},{24,16},{32,24},{40,32},{48,40},{56,48},{64,56},{72,6... | collective-permute-start | bytes 344072 | tf_op jit(solution)/shard_map/while/body/eval_jaxpr/ppermute | solution.py:22
  136.8 7.9 %collective-permute-start = (bf16[16,3584]{1,0:T(8,128)(2,1)}, bf16[16,3584]{1,0:T(8,128)(2,1)S(1)}, u32[]{:S(2)}, u32[]{:S(2)}) collective-permute-start(bf16[16,3584]{1,0:T(8,128)(2,1)} %get-tuple-element.282), channel_id=1, source_target_pairs={{8,0},{16,8},{24,16},{32,24},{40,32},{48,40},{56,48},{64,56},{72,6... | collective-permute-start | bytes 344072 | tf_op jit(solution)/shard_map/while/body/eval_jaxpr/ppermute | solution.py:22
  149.4 7.9 %collective-permute-start = (bf16[16,3584]{1,0:T(8,128)(2,1)}, bf16[16,3584]{1,0:T(8,128)(2,1)S(1)}, u32[]{:S(2)}, u32[]{:S(2)}) collective-permute-start(bf16[16,3584]{1,0:T(8,128)(2,1)} %get-tuple-element.282), channel_id=1, source_target_pairs={{8,0},{16,8},{24,16},{32,24},{40,32},{48,40},{56,48},{64,56},{72,6... | collective-permute-start | bytes 344072 | tf_op jit(solution)/shard_map/while/body/eval_jaxpr/ppermute | solution.py:22
  162.0 7.9 %collective-permute-start = (bf16[16,3584]{1,0:T(8,128)(2,1)}, bf16[16,3584]{1,0:T(8,128)(2,1)S(1)}, u32[]{:S(2)}, u32[]{:S(2)}) collective-permute-start(bf16[16,3584]{1,0:T(8,128)(2,1)} %get-tuple-element.282), channel_id=1, source_target_pairs={{8,0},{16,8},{24,16},{32,24},{40,32},{48,40},{56,48},{64,56},{72,6... | collective-permute-start | bytes 344072 | tf_op jit(solution)/shard_map/while/body/eval_jaxpr/ppermute | solution.py:22
  174.6 8.8 %collective-permute-start = (bf16[16,3584]{1,0:T(8,128)(2,1)}, bf16[16,3584]{1,0:T(8,128)(2,1)S(1)}, u32[]{:S(2)}, u32[]{:S(2)}) collective-permute-start(bf16[16,3584]{1,0:T(8,128)(2,1)} %get-tuple-element.282), channel_id=1, source_target_pairs={{8,0},{16,8},{24,16},{32,24},{40,32},{48,40},{56,48},{64,56},{72,6... | collective-permute-start | bytes 344072 | tf_op jit(solution)/shard_map/while/body/eval_jaxpr/ppermute | solution.py:22
  188.1 8.3 %collective-permute-start = (bf16[16,3584]{1,0:T(8,128)(2,1)}, bf16[16,3584]{1,0:T(8,128)(2,1)S(1)}, u32[]{:S(2)}, u32[]{:S(2)}) collective-permute-start(bf16[16,3584]{1,0:T(8,128)(2,1)} %get-tuple-element.282), channel_id=1, source_target_pairs={{8,0},{16,8},{24,16},{32,24},{40,32},{48,40},{56,48},{64,56},{72,6... | collective-permute-start | bytes 344072 | tf_op jit(solution)/shard_map/while/body/eval_jaxpr/ppermute | solution.py:22
  201.1 8.2 %collective-permute-start = (bf16[16,3584]{1,0:T(8,128)(2,1)}, bf16[16,3584]{1,0:T(8,128)(2,1)S(1)}, u32[]{:S(2)}, u32[]{:S(2)}) collective-permute-start(bf16[16,3584]{1,0:T(8,128)(2,1)} %get-tuple-element.282), channel_id=1, source_target_pairs={{8,0},{16,8},{24,16},{32,24},{40,32},{48,40},{56,48},{64,56},{72,6... | collective-permute-start | bytes 344072 | tf_op jit(solution)/shard_map/while/body/eval_jaxpr/ppermute | solution.py:22
  214.1 7.8 %collective-permute-start = (bf16[16,3584]{1,0:T(8,128)(2,1)}, bf16[16,3584]{1,0:T(8,128)(2,1)S(1)}, u32[]{:S(2)}, u32[]{:S(2)}) collective-permute-start(bf16[16,3584]{1,0:T(8,128)(2,1)} %get-tuple-element.282), channel_id=1, source_target_pairs={{8,0},{16,8},{24,16},{32,24},{40,32},{48,40},{56,48},{64,56},{72,6... | collective-permute-start | bytes 344072 | tf_op jit(solution)/shard_map/while/body/eval_jaxpr/ppermute | solution.py:22
  226.7 7.9 %collective-permute-start = (bf16[16,3584]{1,0:T(8,128)(2,1)}, bf16[16,3584]{1,0:T(8,128)(2,1)S(1)}, u32[]{:S(2)}, u32[]{:S(2)}) collective-permute-start(bf16[16,3584]{1,0:T(8,128)(2,1)} %get-tuple-element.282), channel_id=1, source_target_pairs={{8,0},{16,8},{24,16},{32,24},{40,32},{48,40},{56,48},{64,56},{72,6... | collective-permute-start | bytes 344072 | tf_op jit(solution)/shard_map/while/body/eval_jaxpr/ppermute | solution.py:22
  239.3 7.9 %collective-permute-start = (bf16[16,3584]{1,0:T(8,128)(2,1)}, bf16[16,3584]{1,0:T(8,128)(2,1)S(1)}, u32[]{:S(2)}, u32[]{:S(2)}) collective-permute-start(bf16[16,3584]{1,0:T(8,128)(2,1)} %get-tuple-element.282), channel_id=1, source_target_pairs={{8,0},{16,8},{24,16},{32,24},{40,32},{48,40},{56,48},{64,56},{72,6... | collective-permute-start | bytes 344072 | tf_op jit(solution)/shard_map/while/body/eval_jaxpr/ppermute | solution.py:22
  251.8 7.8 %collective-permute-start = (bf16[16,3584]{1,0:T(8,128)(2,1)}, bf16[16,3584]{1,0:T(8,128)(2,1)S(1)}, u32[]{:S(2)}, u32[]{:S(2)}) collective-permute-start(bf16[16,3584]{1,0:T(8,128)(2,1)} %get-tuple-element.282), channel_id=1, source_target_pairs={{8,0},{16,8},{24,16},{32,24},{40,32},{48,40},{56,48},{64,56},{72,6... | collective-permute-start | bytes 344072 | tf_op jit(solution)/shard_map/while/body/eval_jaxpr/ppermute | solution.py:22
  264.4 7.9 %collective-permute-start = (bf16[16,3584]{1,0:T(8,128)(2,1)}, bf16[16,3584]{1,0:T(8,128)(2,1)S(1)}, u32[]{:S(2)}, u32[]{:S(2)}) collective-permute-start(bf16[16,3584]{1,0:T(8,128)(2,1)} %get-tuple-element.282), channel_id=1, source_target_pairs={{8,0},{16,8},{24,16},{32,24},{40,32},{48,40},{56,48},{64,56},{72,6... | collective-permute-start | bytes 344072 | tf_op jit(solution)/shard_map/while/body/eval_jaxpr/ppermute | solution.py:22
  277.0 7.9 %collective-permute-start = (bf16[16,3584]{1,0:T(8,128)(2,1)}, bf16[16,3584]{1,0:T(8,128)(2,1)S(1)}, u32[]{:S(2)}, u32[]{:S(2)}) collective-permute-start(bf16[16,3584]{1,0:T(8,128)(2,1)} %get-tuple-element.282), channel_id=1, source_target_pairs={{8,0},{16,8},{24,16},{32,24},{40,32},{48,40},{56,48},{64,56},{72,6... | collective-permute-start | bytes 344072 | tf_op jit(solution)/shard_map/while/body/eval_jaxpr/ppermute | solution.py:22
  289.6 7.9 %collective-permute-start = (bf16[16,3584]{1,0:T(8,128)(2,1)}, bf16[16,3584]{1,0:T(8,128)(2,1)S(1)}, u32[]{:S(2)}, u32[]{:S(2)}) collective-permute-start(bf16[16,3584]{1,0:T(8,128)(2,1)} %get-tuple-element.282), channel_id=1, source_target_pairs={{8,0},{16,8},{24,16},{32,24},{40,32},{48,40},{56,48},{64,56},{72,6... | collective-permute-start | bytes 344072 | tf_op jit(solution)/shard_map/while/body/eval_jaxpr/ppermute | solution.py:22
  302.2 7.9 %collective-permute-start = (bf16[16,3584]{1,0:T(8,128)(2,1)}, bf16[16,3584]{1,0:T(8,128)(2,1)S(1)}, u32[]{:S(2)}, u32[]{:S(2)}) collective-permute-start(bf16[16,3584]{1,0:T(8,128)(2,1)} %get-tuple-element.282), channel_id=1, source_target_pairs={{8,0},{16,8},{24,16},{32,24},{40,32},{48,40},{56,48},{64,56},{72,6... | collective-permute-start | bytes 344072 | tf_op jit(solution)/shard_map/while/body/eval_jaxpr/ppermute | solution.py:22
  314.8 7.9 %collective-permute-start = (bf16[16,3584]{1,0:T(8,128)(2,1)}, bf16[16,3584]{1,0:T(8,128)(2,1)S(1)}, u32[]{:S(2)}, u32[]{:S(2)}) collective-permute-start(bf16[16,3584]{1,0:T(8,128)(2,1)} %get-tuple-element.282), channel_id=1, source_target_pairs={{8,0},{16,8},{24,16},{32,24},{40,32},{48,40},{56,48},{64,56},{72,6... | collective-permute-start | bytes 344072 | tf_op jit(solution)/shard_map/while/body/eval_jaxpr/ppermute | solution.py:22
  327.5 8.4 %collective-permute-start = (bf16[16,3584]{1,0:T(8,128)(2,1)}, bf16[16,3584]{1,0:T(8,128)(2,1)S(1)}, u32[]{:S(2)}, u32[]{:S(2)}) collective-permute-start(bf16[16,3584]{1,0:T(8,128)(2,1)} %get-tuple-element.282), channel_id=1, source_target_pairs={{8,0},{16,8},{24,16},{32,24},{40,32},{48,40},{56,48},{64,56},{72,6... | collective-permute-start | bytes 344072 | tf_op jit(solution)/shard_map/while/body/eval_jaxpr/ppermute | solution.py:22
  340.7 8.5 %collective-permute-start = (bf16[16,3584]{1,0:T(8,128)(2,1)}, bf16[16,3584]{1,0:T(8,128)(2,1)S(1)}, u32[]{:S(2)}, u32[]{:S(2)}) collective-permute-start(bf16[16,3584]{1,0:T(8,128)(2,1)} %get-tuple-element.282), channel_id=1, source_target_pairs={{8,0},{16,8},{24,16},{32,24},{40,32},{48,40},{56,48},{64,56},{72,6... | collective-permute-start | bytes 344072 | tf_op jit(solution)/shard_map/while/body/eval_jaxpr/ppermute | solution.py:22
  353.9 8.2 %collective-permute-start = (bf16[16,3584]{1,0:T(8,128)(2,1)}, bf16[16,3584]{1,0:T(8,128)(2,1)S(1)}, u32[]{:S(2)}, u32[]{:S(2)}) collective-permute-start(bf16[16,3584]{1,0:T(8,128)(2,1)} %get-tuple-element.282), channel_id=1, source_target_pairs={{8,0},{16,8},{24,16},{32,24},{40,32},{48,40},{56,48},{64,56},{72,6... | collective-permute-start | bytes 344072 | tf_op jit(solution)/shard_map/while/body/eval_jaxpr/ppermute | solution.py:22
  366.9 7.9 %collective-permute-start = (bf16[16,3584]{1,0:T(8,128)(2,1)}, bf16[16,3584]{1,0:T(8,128)(2,1)S(1)}, u32[]{:S(2)}, u32[]{:S(2)}) collective-permute-start(bf16[16,3584]{1,0:T(8,128)(2,1)} %get-tuple-element.282), channel_id=1, source_target_pairs={{8,0},{16,8},{24,16},{32,24},{40,32},{48,40},{56,48},{64,56},{72,6... | collective-permute-start | bytes 344072 | tf_op jit(solution)/shard_map/while/body/eval_jaxpr/ppermute | solution.py:22
  379.5 7.9 %collective-permute-start = (bf16[16,3584]{1,0:T(8,128)(2,1)}, bf16[16,3584]{1,0:T(8,128)(2,1)S(1)}, u32[]{:S(2)}, u32[]{:S(2)}) collective-permute-start(bf16[16,3584]{1,0:T(8,128)(2,1)} %get-tuple-element.282), channel_id=1, source_target_pairs={{8,0},{16,8},{24,16},{32,24},{40,32},{48,40},{56,48},{64,56},{72,6... | collective-permute-start | bytes 344072 | tf_op jit(solution)/shard_map/while/body/eval_jaxpr/ppermute | solution.py:22
  392.1 7.9 %collective-permute-start = (bf16[16,3584]{1,0:T(8,128)(2,1)}, bf16[16,3584]{1,0:T(8,128)(2,1)S(1)}, u32[]{:S(2)}, u32[]{:S(2)}) collective-permute-start(bf16[16,3584]{1,0:T(8,128)(2,1)} %get-tuple-element.282), channel_id=1, source_target_pairs={{8,0},{16,8},{24,16},{32,24},{40,32},{48,40},{56,48},{64,56},{72,6... | collective-permute-start | bytes 344072 | tf_op jit(solution)/shard_map/while/body/eval_jaxpr/ppermute | solution.py:22
  404.7 7.9 %collective-permute-start = (bf16[16,3584]{1,0:T(8,128)(2,1)}, bf16[16,3584]{1,0:T(8,128)(2,1)S(1)}, u32[]{:S(2)}, u32[]{:S(2)}) collective-permute-start(bf16[16,3584]{1,0:T(8,128)(2,1)} %get-tuple-element.282), channel_id=1, source_target_pairs={{8,0},{16,8},{24,16},{32,24},{40,32},{48,40},{56,48},{64,56},{72,6... | collective-permute-start | bytes 344072 | tf_op jit(solution)/shard_map/while/body/eval_jaxpr/ppermute | solution.py:22
  417.4 7.9 %collective-permute-start = (bf16[16,3584]{1,0:T(8,128)(2,1)}, bf16[16,3584]{1,0:T(8,128)(2,1)S(1)}, u32[]{:S(2)}, u32[]{:S(2)}) collective-permute-start(bf16[16,3584]{1,0:T(8,128)(2,1)} %get-tuple-element.282), channel_id=1, source_target_pairs={{8,0},{16,8},{24,16},{32,24},{40,32},{48,40},{56,48},{64,56},{72,6... | collective-permute-start | bytes 344072 | tf_op jit(solution)/shard_map/while/body/eval_jaxpr/ppermute | solution.py:22
  430.0 7.9 %collective-permute-start = (bf16[16,3584]{1,0:T(8,128)(2,1)}, bf16[16,3584]{1,0:T(8,128)(2,1)S(1)}, u32[]{:S(2)}, u32[]{:S(2)}) collective-permute-start(bf16[16,3584]{1,0:T(8,128)(2,1)} %get-tuple-element.282), channel_id=1, source_target_pairs={{8,0},{16,8},{24,16},{32,24},{40,32},{48,40},{56,48},{64,56},{72,6... | collective-permute-start | bytes 344072 | tf_op jit(solution)/shard_map/while/body/eval_jaxpr/ppermute | solution.py:22
  442.6 7.9 %collective-permute-start = (bf16[16,3584]{1,0:T(8,128)(2,1)}, bf16[16,3584]{1,0:T(8,128)(2,1)S(1)}, u32[]{:S(2)}, u32[]{:S(2)}) collective-permute-start(bf16[16,3584]{1,0:T(8,128)(2,1)} %get-tuple-element.282), channel_id=1, source_target_pairs={{8,0},{16,8},{24,16},{32,24},{40,32},{48,40},{56,48},{64,56},{72,6... | collective-permute-start | bytes 344072 | tf_op jit(solution)/shard_map/while/body/eval_jaxpr/ppermute | solution.py:22
  455.2 7.9 %collective-permute-start = (bf16[16,3584]{1,0:T(8,128)(2,1)}, bf16[16,3584]{1,0:T(8,128)(2,1)S(1)}, u32[]{:S(2)}, u32[]{:S(2)}) collective-permute-start(bf16[16,3584]{1,0:T(8,128)(2,1)} %get-tuple-element.282), channel_id=1, source_target_pairs={{8,0},{16,8},{24,16},{32,24},{40,32},{48,40},{56,48},{64,56},{72,6... | collective-permute-start | bytes 344072 | tf_op jit(solution)/shard_map/while/body/eval_jaxpr/ppermute | solution.py:22
  467.8 7.9 %collective-permute-start = (bf16[16,3584]{1,0:T(8,128)(2,1)}, bf16[16,3584]{1,0:T(8,128)(2,1)S(1)}, u32[]{:S(2)}, u32[]{:S(2)}) collective-permute-start(bf16[16,3584]{1,0:T(8,128)(2,1)} %get-tuple-element.282), channel_id=1, source_target_pairs={{8,0},{16,8},{24,16},{32,24},{40,32},{48,40},{56,48},{64,56},{72,6... | collective-permute-start | bytes 344072 | tf_op jit(solution)/shard_map/while/body/eval_jaxpr/ppermute | solution.py:22
  480.4 8.2 %collective-permute-start = (bf16[16,3584]{1,0:T(8,128)(2,1)}, bf16[16,3584]{1,0:T(8,128)(2,1)S(1)}, u32[]{:S(2)}, u32[]{:S(2)}) collective-permute-start(bf16[16,3584]{1,0:T(8,128)(2,1)} %get-tuple-element.282), channel_id=1, source_target_pairs={{8,0},{16,8},{24,16},{32,24},{40,32},{48,40},{56,48},{64,56},{72,6... | collective-permute-start | bytes 344072 | tf_op jit(solution)/shard_map/while/body/eval_jaxpr/ppermute | solution.py:22
  493.4 8.8 %collective-permute-start = (bf16[16,3584]{1,0:T(8,128)(2,1)}, bf16[16,3584]{1,0:T(8,128)(2,1)S(1)}, u32[]{:S(2)}, u32[]{:S(2)}) collective-permute-start(bf16[16,3584]{1,0:T(8,128)(2,1)} %get-tuple-element.282), channel_id=1, source_target_pairs={{8,0},{16,8},{24,16},{32,24},{40,32},{48,40},{56,48},{64,56},{72,6... | collective-permute-start | bytes 344072 | tf_op jit(solution)/shard_map/while/body/eval_jaxpr/ppermute | solution.py:22
  506.9 8.2 %collective-permute-start = (bf16[16,3584]{1,0:T(8,128)(2,1)}, bf16[16,3584]{1,0:T(8,128)(2,1)S(1)}, u32[]{:S(2)}, u32[]{:S(2)}) collective-permute-start(bf16[16,3584]{1,0:T(8,128)(2,1)} %get-tuple-element.282), channel_id=1, source_target_pairs={{8,0},{16,8},{24,16},{32,24},{40,32},{48,40},{56,48},{64,56},{72,6... | collective-permute-start | bytes 344072 | tf_op jit(solution)/shard_map/while/body/eval_jaxpr/ppermute | solution.py:22
  519.8 8.2 %collective-permute-start = (bf16[16,3584]{1,0:T(8,128)(2,1)}, bf16[16,3584]{1,0:T(8,128)(2,1)S(1)}, u32[]{:S(2)}, u32[]{:S(2)}) collective-permute-start(bf16[16,3584]{1,0:T(8,128)(2,1)} %get-tuple-element.282), channel_id=1, source_target_pairs={{8,0},{16,8},{24,16},{32,24},{40,32},{48,40},{56,48},{64,56},{72,6... | collective-permute-start | bytes 344072 | tf_op jit(solution)/shard_map/while/body/eval_jaxpr/ppermute | solution.py:22
  532.8 7.9 %collective-permute-start = (bf16[16,3584]{1,0:T(8,128)(2,1)}, bf16[16,3584]{1,0:T(8,128)(2,1)S(1)}, u32[]{:S(2)}, u32[]{:S(2)}) collective-permute-start(bf16[16,3584]{1,0:T(8,128)(2,1)} %get-tuple-element.282), channel_id=1, source_target_pairs={{8,0},{16,8},{24,16},{32,24},{40,32},{48,40},{56,48},{64,56},{72,6... | collective-permute-start | bytes 344072 | tf_op jit(solution)/shard_map/while/body/eval_jaxpr/ppermute | solution.py:22
  545.4 7.9 %collective-permute-start = (bf16[16,3584]{1,0:T(8,128)(2,1)}, bf16[16,3584]{1,0:T(8,128)(2,1)S(1)}, u32[]{:S(2)}, u32[]{:S(2)}) collective-permute-start(bf16[16,3584]{1,0:T(8,128)(2,1)} %get-tuple-element.282), channel_id=1, source_target_pairs={{8,0},{16,8},{24,16},{32,24},{40,32},{48,40},{56,48},{64,56},{72,6... | collective-permute-start | bytes 344072 | tf_op jit(solution)/shard_map/while/body/eval_jaxpr/ppermute | solution.py:22
  558.0 7.9 %collective-permute-start = (bf16[16,3584]{1,0:T(8,128)(2,1)}, bf16[16,3584]{1,0:T(8,128)(2,1)S(1)}, u32[]{:S(2)}, u32[]{:S(2)}) collective-permute-start(bf16[16,3584]{1,0:T(8,128)(2,1)} %get-tuple-element.282), channel_id=1, source_target_pairs={{8,0},{16,8},{24,16},{32,24},{40,32},{48,40},{56,48},{64,56},{72,6... | collective-permute-start | bytes 344072 | tf_op jit(solution)/shard_map/while/body/eval_jaxpr/ppermute | solution.py:22
  570.6 7.9 %collective-permute-start = (bf16[16,3584]{1,0:T(8,128)(2,1)}, bf16[16,3584]{1,0:T(8,128)(2,1)S(1)}, u32[]{:S(2)}, u32[]{:S(2)}) collective-permute-start(bf16[16,3584]{1,0:T(8,128)(2,1)} %get-tuple-element.282), channel_id=1, source_target_pairs={{8,0},{16,8},{24,16},{32,24},{40,32},{48,40},{56,48},{64,56},{72,6... | collective-permute-start | bytes 344072 | tf_op jit(solution)/shard_map/while/body/eval_jaxpr/ppermute | solution.py:22
  583.3 7.9 %collective-permute-start = (bf16[16,3584]{1,0:T(8,128)(2,1)}, bf16[16,3584]{1,0:T(8,128)(2,1)S(1)}, u32[]{:S(2)}, u32[]{:S(2)}) collective-permute-start(bf16[16,3584]{1,0:T(8,128)(2,1)} %get-tuple-element.282), channel_id=1, source_target_pairs={{8,0},{16,8},{24,16},{32,24},{40,32},{48,40},{56,48},{64,56},{72,6... | collective-permute-start | bytes 344072 | tf_op jit(solution)/shard_map/while/body/eval_jaxpr/ppermute | solution.py:22
  595.9 7.9 %collective-permute-start = (bf16[16,3584]{1,0:T(8,128)(2,1)}, bf16[16,3584]{1,0:T(8,128)(2,1)S(1)}, u32[]{:S(2)}, u32[]{:S(2)}) collective-permute-start(bf16[16,3584]{1,0:T(8,128)(2,1)} %get-tuple-element.282), channel_id=1, source_target_pairs={{8,0},{16,8},{24,16},{32,24},{40,32},{48,40},{56,48},{64,56},{72,6... | collective-permute-start | bytes 344072 | tf_op jit(solution)/shard_map/while/body/eval_jaxpr/ppermute | solution.py:22
  608.5 7.9 %collective-permute-start = (bf16[16,3584]{1,0:T(8,128)(2,1)}, bf16[16,3584]{1,0:T(8,128)(2,1)S(1)}, u32[]{:S(2)}, u32[]{:S(2)}) collective-permute-start(bf16[16,3584]{1,0:T(8,128)(2,1)} %get-tuple-element.282), channel_id=1, source_target_pairs={{8,0},{16,8},{24,16},{32,24},{40,32},{48,40},{56,48},{64,56},{72,6... | collective-permute-start | bytes 344072 | tf_op jit(solution)/shard_map/while/body/eval_jaxpr/ppermute | solution.py:22
  621.1 7.9 %collective-permute-start = (bf16[16,3584]{1,0:T(8,128)(2,1)}, bf16[16,3584]{1,0:T(8,128)(2,1)S(1)}, u32[]{:S(2)}, u32[]{:S(2)}) collective-permute-start(bf16[16,3584]{1,0:T(8,128)(2,1)} %get-tuple-element.282), channel_id=1, source_target_pairs={{8,0},{16,8},{24,16},{32,24},{40,32},{48,40},{56,48},{64,56},{72,6... | collective-permute-start | bytes 344072 | tf_op jit(solution)/shard_map/while/body/eval_jaxpr/ppermute | solution.py:22
  638.8 80.2 %all-to-all-start = ((f32[8,1,448]{2,1,0:T(1,128)}), f32[8,1,448]{2,1,0:T(1,128)S(1)}, u32[]{:S(2)}, u32[]{:S(2)}) async-start(f32[8,1,448]{2,1,0:T(1,128)} %all_to_all.6), calls=%async_computation | async-start | bytes 32768 | tf_op jit(solution)/shard_map/all_to_all | solution.py:243
  696.4 4.4 copy-start.2
  700.7 6.1 copy-start.6
  706.8 1.5 copy-start
  708.3 2.2 copy-start.5

commit v6 on v5

--- a/solution.py
+++ b/solution.py
@@ -8,7 +8,7 @@
 from jax.experimental.pallas import tpu as pltpu
 from jax.sharding import PartitionSpec as P
 
-GROUPS = 16
+GROUPS = 8
 WINDOW = 32
 
 
@@ -34,7 +34,7 @@
     turn_ref, stage_ref,
     w_hbm, g_hbm, ig_hbm, msg_ref, loss_ref, normed_ref, inv_ref, gain_ref,
     out_ref, g_out, ig_out,
-    w_v, g_v, inc_v, gn_v, sems,
+    w_v, gn_v, normed_v, loss_v, sems,
     *, group_lanes, head_size, rows_here, groups, seq_rows, feature_count, stage_count, unit_count,
 ):
     unit_index = turn_ref[0] - (stage_count - 1 - stage_ref[0])
@@ -43,32 +43,33 @@
     from_loss = stage_ref[0] == stage_count - 1
     slot = pl.multiple_of(jnp.where(active, chosen * rows_here, seq_rows), rows_here)
     group_heads = group_lanes // head_size
-    reads = []
+    w_copies = []
     for g in range(groups):
         w_copy = pltpu.make_async_copy(w_hbm.at[g, :, chosen], w_v.at[g], sems.at[0, g])
-        g_copy = pltpu.make_async_copy(
-            g_hbm.at[pl.ds(0, seq_rows), pl.ds(g * group_lanes, group_lanes)],
-            g_v.at[g],
-            sems.at[1, g],
-        )
         w_copy.start()
-        g_copy.start()
-        reads.append((w_copy, g_copy))
-    inc = jnp.where(from_loss, loss_ref[...], msg_ref[...])
+        w_copies.append(w_copy)
+    first_row = pl.multiple_of(chosen * rows_here, rows_here)
+    normed_copy = pltpu.make_async_copy(
+        normed_ref.at[pl.ds(first_row, rows_here)], normed_v, sems.at[1, 0]
+    )
+    loss_copy = pltpu.make_async_copy(
+        loss_ref.at[pl.ds(first_row, rows_here)], loss_v, sems.at[1, 1]
+    )
+    normed_copy.start()
+    loss_copy.start()
+    loss_copy.wait()
+    inc = jnp.where(from_loss, loss_v[...], msg_ref[...])
     inc = jnp.where(active, inc, jnp.zeros_like(inc))
-    inc_v[...] = inc
-    first_row = pl.multiple_of(chosen * rows_here, rows_here)
+    g_out[pl.ds(slot, rows_here), :] = inc
     lane_head = lax.broadcasted_iota(jnp.int32, (rows_here, group_lanes), 1) // head_size
     total = jnp.zeros((rows_here, 1), jnp.float32)
+    normed_copy.wait()
     for g in range(groups):
         cols = slice(g * group_lanes, (g + 1) * group_lanes)
-        w_copy, g_copy = reads[g]
-        w_copy.wait()
-        g_copy.wait()
-        g_v[g, pl.ds(first_row, rows_here), :] = inc_v[:, cols]
+        w_copies[g].wait()
         stacked = jnp.dot(
             w_v[g].reshape(group_heads * rows_here, seq_rows),
-            g_v[g],
+            g_out[pl.ds(0, seq_rows), cols],
             preferred_element_type=jnp.float32,
         )
         value = jnp.zeros((rows_here, group_lanes), jnp.float32)
@@ -78,19 +79,16 @@
             )
         grad_normed = value * gain_ref[:, cols]
         gn_v[g] = grad_normed
-        total = total + jnp.sum(grad_normed * normed_ref[:, cols], axis=1, keepdims=True)
-    g_write = pltpu.make_async_copy(inc_v, g_out.at[pl.ds(slot, rows_here)], sems.at[2, 0])
-    g_write.start()
+        total = total + jnp.sum(grad_normed * normed_v[:, cols], axis=1, keepdims=True)
     mean = total * (1.0 / feature_count)
     inv = inv_ref[...]
     for g in range(groups):
         cols = slice(g * group_lanes, (g + 1) * group_lanes)
         out_ref[:, cols] = (
-            inc_v[:, cols].astype(jnp.float32) + inv * (gn_v[g] - normed_ref[:, cols] * mean)
+            inc[:, cols].astype(jnp.float32) + inv * (gn_v[g] - normed_v[:, cols] * mean)
         ).astype(out_ref.dtype)
-    ig_write = pltpu.make_async_copy(out_ref, ig_out.at[pl.ds(slot, rows_here)], sems.at[2, 1])
+    ig_write = pltpu.make_async_copy(out_ref, ig_out.at[pl.ds(slot, rows_here)], sems.at[2, 0])
     ig_write.start()
-    g_write.wait()
     ig_write.wait()
 
 
@@ -113,24 +111,24 @@
         grid=(1,),
         in_specs=[
             pl.BlockSpec(memory_space=pl.ANY),
-            pl.BlockSpec(memory_space=pl.ANY),
+            pl.BlockSpec(memory_space=pltpu.VMEM),
             pl.BlockSpec(memory_space=pl.ANY),
             pl.BlockSpec((rows_here, feature_count), lambda i, t, s: (0, 0)),
-            pl.BlockSpec((rows_here, feature_count), lambda i, t, s: (chunk_of(i, t, s), 0)),
-            pl.BlockSpec((rows_here, feature_count), lambda i, t, s: (chunk_of(i, t, s), 0)),
+            pl.BlockSpec(memory_space=pl.ANY),
+            pl.BlockSpec(memory_space=pl.ANY),
             pl.BlockSpec((rows_here, 1), lambda i, t, s: (chunk_of(i, t, s), 0)),
             pl.BlockSpec((1, feature_count), lambda i, t, s: (0, 0)),
         ],
         out_specs=[
             pl.BlockSpec((rows_here, feature_count), lambda i, t, s: (0, 0)),
-            pl.BlockSpec(memory_space=pl.ANY),
+            pl.BlockSpec(memory_space=pltpu.VMEM),
             pl.BlockSpec(memory_space=pl.ANY),
         ],
         scratch_shapes=[
             pltpu.VMEM((groups, group_heads, rows_here, seq_rows), jnp.bfloat16),
-            pltpu.VMEM((groups, seq_rows, group_lanes), jnp.bfloat16),
+            pltpu.VMEM((groups, rows_here, group_lanes), jnp.float32),
+            pltpu.VMEM((rows_here, feature_count), jnp.float32),
             pltpu.VMEM((rows_here, feature_count), jnp.bfloat16),
-            pltpu.VMEM((groups, rows_here, group_lanes), jnp.float32),
             pltpu.SemaphoreType.DMA((3, groups)),
         ],
     )

time: 725 us -> 661 us (0.912)
  starting transfers between devices: 332 us -> 279 us
  Pallas kernels: 223 us -> 175 us
  waiting for transfers between devices: 102 us -> 141 us
    pallas_call x47 -> x39, Pallas kernels: 223 us -> 175 us  [turn_call(): pl.pallas_call(kernel, grid_spec=grid_spec, out_shape=[jax.ShapeDtypeStru...]
    ppermute x47 -> x39, starting transfers between devices: 275 us -> 231 us  [passed_along(): lax.ppermute(value, axis, [(source, source + steps) for source in range(l...]
    ppermute x47 -> x39, waiting for transfers between devices: 102 us -> 141 us  [passed_along(): lax.ppermute(value, axis, [(source, source + steps) for source in range(l...]
    all_to_all x1, starting transfers between devices: 57.5 us -> 47.8 us  [on_device(): lax.all_to_all(gain_sum.reshape(group_count, feature_count // group_count...]
  transfers between devices with their start and end apart: 48 -> 40, of which waited for: 47 -> 39; matrix products, arithmetic and copies ran while one was open for 3% -> 3% of each run, Pallas kernels for 0% -> 0%
where the time goes in v6:
time: 661 us; the launch traced here: 658 us
  starting transfers between devices  279 us (42%)
  Pallas kernels  175 us (26%)
  waiting for transfers between devices  141 us (21%)
  local copies, waits for them, and re-layouts  28 us (4%)
  matrix products  23 us (3%)
  other arithmetic  10.2 us (2%)
    ppermute x39, starting transfers between devices, passed_along(): lax.ppermute(value, axis, [(source, source + steps) for source in range(l...  231 us
    pallas_call x39, Pallas kernels, turn_call(): pl.pallas_call(kernel, grid_spec=grid_spec, out_shape=[jax.ShapeDtypeStru...  175 us
    ppermute x39, waiting for transfers between devices, passed_along(): lax.ppermute(value, axis, [(source, source + steps) for source in range(l...  141 us
    all_to_all x1, starting transfers between devices, on_device(): lax.all_to_all(gain_sum.reshape(group_count, feature_count // group_count...  47.8 us
    unnamed x22, local copies, waits for them, and re-layouts  15.9 us
  transfers between devices with their start and end apart: 40, of which 39 were waited for; matrix products, arithmetic and copies ran while one was open for 3% of the time, Pallas kernels for 0%

profile of v6, /device:TPU:15, one launch (start us, length us, event | category | flops | bytes accessed | tf_op | source)
XLA Modules:
  0.0 657.8 jit_solution(7393545521874951426)
XLA Ops:
  29.0 547.9 %while.17 = (s32[]{:T(128)}, bf16[32,3584]{1,0:T(8,128)(2,1)S(1)}, bf16[288,3584]{1,0:T(8,128)(2,1)S(1)}, bf16[288,3584]{1,0:T(8,128)(2,1)}, s32[1]{0:T(128)}, /...) while((s32[]{:T(128)}, bf16[32,3584]{1,0:T(8,128)(2,1)S(1)}, ...), condition=%wide.region_4.5_spmd, body=%wide.region_3.4_spmd.sunk | while | flops 2 | bytes 917653 | solution.py:212
  29.0 4.5 eval_jaxpr.5
  33.5 7.7 %collective-permute-start = (bf16[32,3584]{1,0:T(8,128)(2,1)}, bf16[32,3584]{1,0:T(8,128)(2,1)S(1)}, u32[]{:S(2)}, u32[]{:S(2)}) collective-permute-start(bf16[32,3584]{1,0:T(8,128)(2,1)} %get-tuple-element.282), channel_id=1, source_target_pairs={{8,0},{16,8},{24,16},{32,24},{40,32},{48,40},{56,48},{64,56},{72,6... | collective-permute-start | bytes 688136 | tf_op jit(solution)/shard_map/while/body/eval_jaxpr/ppermute | solution.py:22
  41.3 4.6 collective-permute-done
  50.3 6.1 collective-permute-start
  60.1 4.5 eval_jaxpr.5
  64.6 6.1 collective-permute-start
  78.5 5.8 collective-permute-start
  92.1 5.8 collective-permute-start
  101.1 4.5 eval_jaxpr.5
  105.6 5.8 collective-permute-start
  114.7 4.5 eval_jaxpr.5
  119.2 5.8 collective-permute-start
  132.8 5.8 collective-permute-start
  146.4 5.8 collective-permute-start
  160.0 5.8 collective-permute-start
  173.5 5.8 collective-permute-start
  187.1 5.8 collective-permute-start
  201.7 5.8 collective-permute-start
  207.5 5.4 collective-permute-done
  217.4 5.9 collective-permute-start
  223.2 4.9 collective-permute-done
  232.6 6.1 collective-permute-start
  242.7 4.5 eval_jaxpr.5
  247.2 6.1 collective-permute-start
  256.6 4.5 eval_jaxpr.5
  261.1 5.8 collective-permute-start
  270.2 4.5 eval_jaxpr.5
  274.7 5.8 collective-permute-start
  288.2 5.8 collective-permute-start
  297.3 4.5 eval_jaxpr.5
  301.8 5.8 collective-permute-start
  315.4 5.8 collective-permute-start
  329.0 5.8 collective-permute-start
  338.1 4.5 eval_jaxpr.5
  342.6 5.8 collective-permute-start
  351.7 4.5 eval_jaxpr.5
  356.2 5.8 collective-permute-start
  365.3 4.5 eval_jaxpr.5
  369.8 5.8 collective-permute-start
  384.0 5.8 collective-permute-start
  389.8 5.0 collective-permute-done
  399.3 5.8 collective-permute-start
  405.2 5.3 collective-permute-done
  410.5 4.5 eval_jaxpr.5
  415.0 6.1 collective-permute-start
  430.0 6.1 collective-permute-start
  439.6 4.5 eval_jaxpr.5
  444.1 6.1 collective-permute-start
  458.0 5.8 collective-permute-start
  471.6 5.8 collective-permute-start
  485.2 5.8 collective-permute-start
  494.3 4.5 eval_jaxpr.5
  498.8 5.8 collective-permute-start
  507.9 4.5 eval_jaxpr.5
  512.4 5.8 collective-permute-start
  526.0 5.8 collective-permute-start
  535.0 4.5 eval_jaxpr.5
  539.5 5.8 collective-permute-start
  553.1 5.8 collective-permute-start
  566.7 5.8 collective-permute-start
  581.2 4.9 fusion.1
  586.7 47.8 %all-to-all-start = ((f32[8,1,448]{2,1,0:T(1,128)}), f32[8,1,448]{2,1,0:T(1,128)S(1)}, u32[]{:S(2)}, u32[]{:S(2)}) async-start(f32[8,1,448]{2,1,0:T(1,128)} %all_to_all.6), calls=%async_computation | async-start | bytes 32768 | tf_op jit(solution)/shard_map/all_to_all | solution.py:241
  639.0 6.1 multiply_convert_fusion
  (106 shorter events, 269.5 us)
Async XLA Ops:
  0.7 6.0 copy-start.8
  9.6 8.5 %copy-start.4 = (bf16[1,1,256,3584]{2,3,1,0:T(8,128)(2,1)}, bf16[1,1,256,3584]{2,3,1,0:T(8,128)(2,1)S(1)}, u32[]{:S(2)}) copy-start(bf16[1,1,256,3584]{2,3,1,0:T(8,128)(2,1)S(1)} %copy.27) | copy-start | bytes 5505028
  18.1 3.2 copy-start.1
  21.3 3.6 copy-start.3
  24.9 4.1 copy-start.7
  33.5 12.3 %collective-permute-start = (bf16[32,3584]{1,0:T(8,128)(2,1)}, bf16[32,3584]{1,0:T(8,128)(2,1)S(1)}, u32[]{:S(2)}, u32[]{:S(2)}) collective-permute-start(bf16[32,3584]{1,0:T(8,128)(2,1)} %get-tuple-element.282), channel_id=1, source_target_pairs={{8,0},{16,8},{24,16},{32,24},{40,32},{48,40},{56,48},{64,56},{72,6... | collective-permute-start | bytes 688136 | tf_op jit(solution)/shard_map/while/body/eval_jaxpr/ppermute | solution.py:22
  50.3 9.8 %collective-permute-start = (bf16[32,3584]{1,0:T(8,128)(2,1)}, bf16[32,3584]{1,0:T(8,128)(2,1)S(1)}, u32[]{:S(2)}, u32[]{:S(2)}) collective-permute-start(bf16[32,3584]{1,0:T(8,128)(2,1)} %get-tuple-element.282), channel_id=1, source_target_pairs={{8,0},{16,8},{24,16},{32,24},{40,32},{48,40},{56,48},{64,56},{72,6... | collective-permute-start | bytes 688136 | tf_op jit(solution)/shard_map/while/body/eval_jaxpr/ppermute | solution.py:22
  64.6 9.4 %collective-permute-start = (bf16[32,3584]{1,0:T(8,128)(2,1)}, bf16[32,3584]{1,0:T(8,128)(2,1)S(1)}, u32[]{:S(2)}, u32[]{:S(2)}) collective-permute-start(bf16[32,3584]{1,0:T(8,128)(2,1)} %get-tuple-element.282), channel_id=1, source_target_pairs={{8,0},{16,8},{24,16},{32,24},{40,32},{48,40},{56,48},{64,56},{72,6... | collective-permute-start | bytes 688136 | tf_op jit(solution)/shard_map/while/body/eval_jaxpr/ppermute | solution.py:22
  78.5 9.1 %collective-permute-start = (bf16[32,3584]{1,0:T(8,128)(2,1)}, bf16[32,3584]{1,0:T(8,128)(2,1)S(1)}, u32[]{:S(2)}, u32[]{:S(2)}) collective-permute-start(bf16[32,3584]{1,0:T(8,128)(2,1)} %get-tuple-element.282), channel_id=1, source_target_pairs={{8,0},{16,8},{24,16},{32,24},{40,32},{48,40},{56,48},{64,56},{72,6... | collective-permute-start | bytes 688136 | tf_op jit(solution)/shard_map/while/body/eval_jaxpr/ppermute | solution.py:22
  92.1 9.1 %collective-permute-start = (bf16[32,3584]{1,0:T(8,128)(2,1)}, bf16[32,3584]{1,0:T(8,128)(2,1)S(1)}, u32[]{:S(2)}, u32[]{:S(2)}) collective-permute-start(bf16[32,3584]{1,0:T(8,128)(2,1)} %get-tuple-element.282), channel_id=1, source_target_pairs={{8,0},{16,8},{24,16},{32,24},{40,32},{48,40},{56,48},{64,56},{72,6... | collective-permute-start | bytes 688136 | tf_op jit(solution)/shard_map/while/body/eval_jaxpr/ppermute | solution.py:22
  105.6 9.1 %collective-permute-start = (bf16[32,3584]{1,0:T(8,128)(2,1)}, bf16[32,3584]{1,0:T(8,128)(2,1)S(1)}, u32[]{:S(2)}, u32[]{:S(2)}) collective-permute-start(bf16[32,3584]{1,0:T(8,128)(2,1)} %get-tuple-element.282), channel_id=1, source_target_pairs={{8,0},{16,8},{24,16},{32,24},{40,32},{48,40},{56,48},{64,56},{72,6... | collective-permute-start | bytes 688136 | tf_op jit(solution)/shard_map/while/body/eval_jaxpr/ppermute | solution.py:22
  119.2 9.1 %collective-permute-start = (bf16[32,3584]{1,0:T(8,128)(2,1)}, bf16[32,3584]{1,0:T(8,128)(2,1)S(1)}, u32[]{:S(2)}, u32[]{:S(2)}) collective-permute-start(bf16[32,3584]{1,0:T(8,128)(2,1)} %get-tuple-element.282), channel_id=1, source_target_pairs={{8,0},{16,8},{24,16},{32,24},{40,32},{48,40},{56,48},{64,56},{72,6... | collective-permute-start | bytes 688136 | tf_op jit(solution)/shard_map/while/body/eval_jaxpr/ppermute | solution.py:22
  132.8 9.1 %collective-permute-start = (bf16[32,3584]{1,0:T(8,128)(2,1)}, bf16[32,3584]{1,0:T(8,128)(2,1)S(1)}, u32[]{:S(2)}, u32[]{:S(2)}) collective-permute-start(bf16[32,3584]{1,0:T(8,128)(2,1)} %get-tuple-element.282), channel_id=1, source_target_pairs={{8,0},{16,8},{24,16},{32,24},{40,32},{48,40},{56,48},{64,56},{72,6... | collective-permute-start | bytes 688136 | tf_op jit(solution)/shard_map/while/body/eval_jaxpr/ppermute | solution.py:22
  146.4 9.1 %collective-permute-start = (bf16[32,3584]{1,0:T(8,128)(2,1)}, bf16[32,3584]{1,0:T(8,128)(2,1)S(1)}, u32[]{:S(2)}, u32[]{:S(2)}) collective-permute-start(bf16[32,3584]{1,0:T(8,128)(2,1)} %get-tuple-element.282), channel_id=1, source_target_pairs={{8,0},{16,8},{24,16},{32,24},{40,32},{48,40},{56,48},{64,56},{72,6... | collective-permute-start | bytes 688136 | tf_op jit(solution)/shard_map/while/body/eval_jaxpr/ppermute | solution.py:22
  160.0 9.1 %collective-permute-start = (bf16[32,3584]{1,0:T(8,128)(2,1)}, bf16[32,3584]{1,0:T(8,128)(2,1)S(1)}, u32[]{:S(2)}, u32[]{:S(2)}) collective-permute-start(bf16[32,3584]{1,0:T(8,128)(2,1)} %get-tuple-element.282), channel_id=1, source_target_pairs={{8,0},{16,8},{24,16},{32,24},{40,32},{48,40},{56,48},{64,56},{72,6... | collective-permute-start | bytes 688136 | tf_op jit(solution)/shard_map/while/body/eval_jaxpr/ppermute | solution.py:22
  173.5 9.1 %collective-permute-start = (bf16[32,3584]{1,0:T(8,128)(2,1)}, bf16[32,3584]{1,0:T(8,128)(2,1)S(1)}, u32[]{:S(2)}, u32[]{:S(2)}) collective-permute-start(bf16[32,3584]{1,0:T(8,128)(2,1)} %get-tuple-element.282), channel_id=1, source_target_pairs={{8,0},{16,8},{24,16},{32,24},{40,32},{48,40},{56,48},{64,56},{72,6... | collective-permute-start | bytes 688136 | tf_op jit(solution)/shard_map/while/body/eval_jaxpr/ppermute | solution.py:22
  187.1 10.1 %collective-permute-start = (bf16[32,3584]{1,0:T(8,128)(2,1)}, bf16[32,3584]{1,0:T(8,128)(2,1)S(1)}, u32[]{:S(2)}, u32[]{:S(2)}) collective-permute-start(bf16[32,3584]{1,0:T(8,128)(2,1)} %get-tuple-element.282), channel_id=1, source_target_pairs={{8,0},{16,8},{24,16},{32,24},{40,32},{48,40},{56,48},{64,56},{72,6... | collective-permute-start | bytes 688136 | tf_op jit(solution)/shard_map/while/body/eval_jaxpr/ppermute | solution.py:22
  201.7 11.2 %collective-permute-start = (bf16[32,3584]{1,0:T(8,128)(2,1)}, bf16[32,3584]{1,0:T(8,128)(2,1)S(1)}, u32[]{:S(2)}, u32[]{:S(2)}) collective-permute-start(bf16[32,3584]{1,0:T(8,128)(2,1)} %get-tuple-element.282), channel_id=1, source_target_pairs={{8,0},{16,8},{24,16},{32,24},{40,32},{48,40},{56,48},{64,56},{72,6... | collective-permute-start | bytes 688136 | tf_op jit(solution)/shard_map/while/body/eval_jaxpr/ppermute | solution.py:22
  217.4 10.8 %collective-permute-start = (bf16[32,3584]{1,0:T(8,128)(2,1)}, bf16[32,3584]{1,0:T(8,128)(2,1)S(1)}, u32[]{:S(2)}, u32[]{:S(2)}) collective-permute-start(bf16[32,3584]{1,0:T(8,128)(2,1)} %get-tuple-element.282), channel_id=1, source_target_pairs={{8,0},{16,8},{24,16},{32,24},{40,32},{48,40},{56,48},{64,56},{72,6... | collective-permute-start | bytes 688136 | tf_op jit(solution)/shard_map/while/body/eval_jaxpr/ppermute | solution.py:22
  232.6 10.1 %collective-permute-start = (bf16[32,3584]{1,0:T(8,128)(2,1)}, bf16[32,3584]{1,0:T(8,128)(2,1)S(1)}, u32[]{:S(2)}, u32[]{:S(2)}) collective-permute-start(bf16[32,3584]{1,0:T(8,128)(2,1)} %get-tuple-element.282), channel_id=1, source_target_pairs={{8,0},{16,8},{24,16},{32,24},{40,32},{48,40},{56,48},{64,56},{72,6... | collective-permute-start | bytes 688136 | tf_op jit(solution)/shard_map/while/body/eval_jaxpr/ppermute | solution.py:22
  247.2 9.4 %collective-permute-start = (bf16[32,3584]{1,0:T(8,128)(2,1)}, bf16[32,3584]{1,0:T(8,128)(2,1)S(1)}, u32[]{:S(2)}, u32[]{:S(2)}) collective-permute-start(bf16[32,3584]{1,0:T(8,128)(2,1)} %get-tuple-element.282), channel_id=1, source_target_pairs={{8,0},{16,8},{24,16},{32,24},{40,32},{48,40},{56,48},{64,56},{72,6... | collective-permute-start | bytes 688136 | tf_op jit(solution)/shard_map/while/body/eval_jaxpr/ppermute | solution.py:22
  261.1 9.1 %collective-permute-start = (bf16[32,3584]{1,0:T(8,128)(2,1)}, bf16[32,3584]{1,0:T(8,128)(2,1)S(1)}, u32[]{:S(2)}, u32[]{:S(2)}) collective-permute-start(bf16[32,3584]{1,0:T(8,128)(2,1)} %get-tuple-element.282), channel_id=1, source_target_pairs={{8,0},{16,8},{24,16},{32,24},{40,32},{48,40},{56,48},{64,56},{72,6... | collective-permute-start | bytes 688136 | tf_op jit(solution)/shard_map/while/body/eval_jaxpr/ppermute | solution.py:22
  274.7 9.1 %collective-permute-start = (bf16[32,3584]{1,0:T(8,128)(2,1)}, bf16[32,3584]{1,0:T(8,128)(2,1)S(1)}, u32[]{:S(2)}, u32[]{:S(2)}) collective-permute-start(bf16[32,3584]{1,0:T(8,128)(2,1)} %get-tuple-element.282), channel_id=1, source_target_pairs={{8,0},{16,8},{24,16},{32,24},{40,32},{48,40},{56,48},{64,56},{72,6... | collective-permute-start | bytes 688136 | tf_op jit(solution)/shard_map/while/body/eval_jaxpr/ppermute | solution.py:22
  288.2 9.1 %collective-permute-start = (bf16[32,3584]{1,0:T(8,128)(2,1)}, bf16[32,3584]{1,0:T(8,128)(2,1)S(1)}, u32[]{:S(2)}, u32[]{:S(2)}) collective-permute-start(bf16[32,3584]{1,0:T(8,128)(2,1)} %get-tuple-element.282), channel_id=1, source_target_pairs={{8,0},{16,8},{24,16},{32,24},{40,32},{48,40},{56,48},{64,56},{72,6... | collective-permute-start | bytes 688136 | tf_op jit(solution)/shard_map/while/body/eval_jaxpr/ppermute | solution.py:22
  301.8 9.1 %collective-permute-start = (bf16[32,3584]{1,0:T(8,128)(2,1)}, bf16[32,3584]{1,0:T(8,128)(2,1)S(1)}, u32[]{:S(2)}, u32[]{:S(2)}) collective-permute-start(bf16[32,3584]{1,0:T(8,128)(2,1)} %get-tuple-element.282), channel_id=1, source_target_pairs={{8,0},{16,8},{24,16},{32,24},{40,32},{48,40},{56,48},{64,56},{72,6... | collective-permute-start | bytes 688136 | tf_op jit(solution)/shard_map/while/body/eval_jaxpr/ppermute | solution.py:22
  315.4 9.1 %collective-permute-start = (bf16[32,3584]{1,0:T(8,128)(2,1)}, bf16[32,3584]{1,0:T(8,128)(2,1)S(1)}, u32[]{:S(2)}, u32[]{:S(2)}) collective-permute-start(bf16[32,3584]{1,0:T(8,128)(2,1)} %get-tuple-element.282), channel_id=1, source_target_pairs={{8,0},{16,8},{24,16},{32,24},{40,32},{48,40},{56,48},{64,56},{72,6... | collective-permute-start | bytes 688136 | tf_op jit(solution)/shard_map/while/body/eval_jaxpr/ppermute | solution.py:22
  329.0 9.1 %collective-permute-start = (bf16[32,3584]{1,0:T(8,128)(2,1)}, bf16[32,3584]{1,0:T(8,128)(2,1)S(1)}, u32[]{:S(2)}, u32[]{:S(2)}) collective-permute-start(bf16[32,3584]{1,0:T(8,128)(2,1)} %get-tuple-element.282), channel_id=1, source_target_pairs={{8,0},{16,8},{24,16},{32,24},{40,32},{48,40},{56,48},{64,56},{72,6... | collective-permute-start | bytes 688136 | tf_op jit(solution)/shard_map/while/body/eval_jaxpr/ppermute | solution.py:22
  342.6 9.1 %collective-permute-start = (bf16[32,3584]{1,0:T(8,128)(2,1)}, bf16[32,3584]{1,0:T(8,128)(2,1)S(1)}, u32[]{:S(2)}, u32[]{:S(2)}) collective-permute-start(bf16[32,3584]{1,0:T(8,128)(2,1)} %get-tuple-element.282), channel_id=1, source_target_pairs={{8,0},{16,8},{24,16},{32,24},{40,32},{48,40},{56,48},{64,56},{72,6... | collective-permute-start | bytes 688136 | tf_op jit(solution)/shard_map/while/body/eval_jaxpr/ppermute | solution.py:22
  356.2 9.1 %collective-permute-start = (bf16[32,3584]{1,0:T(8,128)(2,1)}, bf16[32,3584]{1,0:T(8,128)(2,1)S(1)}, u32[]{:S(2)}, u32[]{:S(2)}) collective-permute-start(bf16[32,3584]{1,0:T(8,128)(2,1)} %get-tuple-element.282), channel_id=1, source_target_pairs={{8,0},{16,8},{24,16},{32,24},{40,32},{48,40},{56,48},{64,56},{72,6... | collective-permute-start | bytes 688136 | tf_op jit(solution)/shard_map/while/body/eval_jaxpr/ppermute | solution.py:22
  369.8 9.7 %collective-permute-start = (bf16[32,3584]{1,0:T(8,128)(2,1)}, bf16[32,3584]{1,0:T(8,128)(2,1)S(1)}, u32[]{:S(2)}, u32[]{:S(2)}) collective-permute-start(bf16[32,3584]{1,0:T(8,128)(2,1)} %get-tuple-element.282), channel_id=1, source_target_pairs={{8,0},{16,8},{24,16},{32,24},{40,32},{48,40},{56,48},{64,56},{72,6... | collective-permute-start | bytes 688136 | tf_op jit(solution)/shard_map/while/body/eval_jaxpr/ppermute | solution.py:22
  384.0 10.8 %collective-permute-start = (bf16[32,3584]{1,0:T(8,128)(2,1)}, bf16[32,3584]{1,0:T(8,128)(2,1)S(1)}, u32[]{:S(2)}, u32[]{:S(2)}) collective-permute-start(bf16[32,3584]{1,0:T(8,128)(2,1)} %get-tuple-element.282), channel_id=1, source_target_pairs={{8,0},{16,8},{24,16},{32,24},{40,32},{48,40},{56,48},{64,56},{72,6... | collective-permute-start | bytes 688136 | tf_op jit(solution)/shard_map/while/body/eval_jaxpr/ppermute | solution.py:22
  399.3 11.1 %collective-permute-start = (bf16[32,3584]{1,0:T(8,128)(2,1)}, bf16[32,3584]{1,0:T(8,128)(2,1)S(1)}, u32[]{:S(2)}, u32[]{:S(2)}) collective-permute-start(bf16[32,3584]{1,0:T(8,128)(2,1)} %get-tuple-element.282), channel_id=1, source_target_pairs={{8,0},{16,8},{24,16},{32,24},{40,32},{48,40},{56,48},{64,56},{72,6... | collective-permute-start | bytes 688136 | tf_op jit(solution)/shard_map/while/body/eval_jaxpr/ppermute | solution.py:22
  415.0 10.5 %collective-permute-start = (bf16[32,3584]{1,0:T(8,128)(2,1)}, bf16[32,3584]{1,0:T(8,128)(2,1)S(1)}, u32[]{:S(2)}, u32[]{:S(2)}) collective-permute-start(bf16[32,3584]{1,0:T(8,128)(2,1)} %get-tuple-element.282), channel_id=1, source_target_pairs={{8,0},{16,8},{24,16},{32,24},{40,32},{48,40},{56,48},{64,56},{72,6... | collective-permute-start | bytes 688136 | tf_op jit(solution)/shard_map/while/body/eval_jaxpr/ppermute | solution.py:22
  430.0 9.6 %collective-permute-start = (bf16[32,3584]{1,0:T(8,128)(2,1)}, bf16[32,3584]{1,0:T(8,128)(2,1)S(1)}, u32[]{:S(2)}, u32[]{:S(2)}) collective-permute-start(bf16[32,3584]{1,0:T(8,128)(2,1)} %get-tuple-element.282), channel_id=1, source_target_pairs={{8,0},{16,8},{24,16},{32,24},{40,32},{48,40},{56,48},{64,56},{72,6... | collective-permute-start | bytes 688136 | tf_op jit(solution)/shard_map/while/body/eval_jaxpr/ppermute | solution.py:22
  444.1 9.4 %collective-permute-start = (bf16[32,3584]{1,0:T(8,128)(2,1)}, bf16[32,3584]{1,0:T(8,128)(2,1)S(1)}, u32[]{:S(2)}, u32[]{:S(2)}) collective-permute-start(bf16[32,3584]{1,0:T(8,128)(2,1)} %get-tuple-element.282), channel_id=1, source_target_pairs={{8,0},{16,8},{24,16},{32,24},{40,32},{48,40},{56,48},{64,56},{72,6... | collective-permute-start | bytes 688136 | tf_op jit(solution)/shard_map/while/body/eval_jaxpr/ppermute | solution.py:22
  458.0 9.1 %collective-permute-start = (bf16[32,3584]{1,0:T(8,128)(2,1)}, bf16[32,3584]{1,0:T(8,128)(2,1)S(1)}, u32[]{:S(2)}, u32[]{:S(2)}) collective-permute-start(bf16[32,3584]{1,0:T(8,128)(2,1)} %get-tuple-element.282), channel_id=1, source_target_pairs={{8,0},{16,8},{24,16},{32,24},{40,32},{48,40},{56,48},{64,56},{72,6... | collective-permute-start | bytes 688136 | tf_op jit(solution)/shard_map/while/body/eval_jaxpr/ppermute | solution.py:22
  471.6 9.1 %collective-permute-start = (bf16[32,3584]{1,0:T(8,128)(2,1)}, bf16[32,3584]{1,0:T(8,128)(2,1)S(1)}, u32[]{:S(2)}, u32[]{:S(2)}) collective-permute-start(bf16[32,3584]{1,0:T(8,128)(2,1)} %get-tuple-element.282), channel_id=1, source_target_pairs={{8,0},{16,8},{24,16},{32,24},{40,32},{48,40},{56,48},{64,56},{72,6... | collective-permute-start | bytes 688136 | tf_op jit(solution)/shard_map/while/body/eval_jaxpr/ppermute | solution.py:22
  485.2 9.1 %collective-permute-start = (bf16[32,3584]{1,0:T(8,128)(2,1)}, bf16[32,3584]{1,0:T(8,128)(2,1)S(1)}, u32[]{:S(2)}, u32[]{:S(2)}) collective-permute-start(bf16[32,3584]{1,0:T(8,128)(2,1)} %get-tuple-element.282), channel_id=1, source_target_pairs={{8,0},{16,8},{24,16},{32,24},{40,32},{48,40},{56,48},{64,56},{72,6... | collective-permute-start | bytes 688136 | tf_op jit(solution)/shard_map/while/body/eval_jaxpr/ppermute | solution.py:22
  498.8 9.1 %collective-permute-start = (bf16[32,3584]{1,0:T(8,128)(2,1)}, bf16[32,3584]{1,0:T(8,128)(2,1)S(1)}, u32[]{:S(2)}, u32[]{:S(2)}) collective-permute-start(bf16[32,3584]{1,0:T(8,128)(2,1)} %get-tuple-element.282), channel_id=1, source_target_pairs={{8,0},{16,8},{24,16},{32,24},{40,32},{48,40},{56,48},{64,56},{72,6... | collective-permute-start | bytes 688136 | tf_op jit(solution)/shard_map/while/body/eval_jaxpr/ppermute | solution.py:22
  512.4 9.1 %collective-permute-start = (bf16[32,3584]{1,0:T(8,128)(2,1)}, bf16[32,3584]{1,0:T(8,128)(2,1)S(1)}, u32[]{:S(2)}, u32[]{:S(2)}) collective-permute-start(bf16[32,3584]{1,0:T(8,128)(2,1)} %get-tuple-element.282), channel_id=1, source_target_pairs={{8,0},{16,8},{24,16},{32,24},{40,32},{48,40},{56,48},{64,56},{72,6... | collective-permute-start | bytes 688136 | tf_op jit(solution)/shard_map/while/body/eval_jaxpr/ppermute | solution.py:22
  526.0 9.1 %collective-permute-start = (bf16[32,3584]{1,0:T(8,128)(2,1)}, bf16[32,3584]{1,0:T(8,128)(2,1)S(1)}, u32[]{:S(2)}, u32[]{:S(2)}) collective-permute-start(bf16[32,3584]{1,0:T(8,128)(2,1)} %get-tuple-element.282), channel_id=1, source_target_pairs={{8,0},{16,8},{24,16},{32,24},{40,32},{48,40},{56,48},{64,56},{72,6... | collective-permute-start | bytes 688136 | tf_op jit(solution)/shard_map/while/body/eval_jaxpr/ppermute | solution.py:22
  539.5 9.1 %collective-permute-start = (bf16[32,3584]{1,0:T(8,128)(2,1)}, bf16[32,3584]{1,0:T(8,128)(2,1)S(1)}, u32[]{:S(2)}, u32[]{:S(2)}) collective-permute-start(bf16[32,3584]{1,0:T(8,128)(2,1)} %get-tuple-element.282), channel_id=1, source_target_pairs={{8,0},{16,8},{24,16},{32,24},{40,32},{48,40},{56,48},{64,56},{72,6... | collective-permute-start | bytes 688136 | tf_op jit(solution)/shard_map/while/body/eval_jaxpr/ppermute | solution.py:22
  553.1 9.1 %collective-permute-start = (bf16[32,3584]{1,0:T(8,128)(2,1)}, bf16[32,3584]{1,0:T(8,128)(2,1)S(1)}, u32[]{:S(2)}, u32[]{:S(2)}) collective-permute-start(bf16[32,3584]{1,0:T(8,128)(2,1)} %get-tuple-element.282), channel_id=1, source_target_pairs={{8,0},{16,8},{24,16},{32,24},{40,32},{48,40},{56,48},{64,56},{72,6... | collective-permute-start | bytes 688136 | tf_op jit(solution)/shard_map/while/body/eval_jaxpr/ppermute | solution.py:22
  566.7 10.2 %collective-permute-start = (bf16[32,3584]{1,0:T(8,128)(2,1)}, bf16[32,3584]{1,0:T(8,128)(2,1)S(1)}, u32[]{:S(2)}, u32[]{:S(2)}) collective-permute-start(bf16[32,3584]{1,0:T(8,128)(2,1)} %get-tuple-element.282), channel_id=1, source_target_pairs={{8,0},{16,8},{24,16},{32,24},{40,32},{48,40},{56,48},{64,56},{72,6... | collective-permute-start | bytes 688136 | tf_op jit(solution)/shard_map/while/body/eval_jaxpr/ppermute | solution.py:22
  586.7 70.5 %all-to-all-start = ((f32[8,1,448]{2,1,0:T(1,128)}), f32[8,1,448]{2,1,0:T(1,128)S(1)}, u32[]{:S(2)}, u32[]{:S(2)}) async-start(f32[8,1,448]{2,1,0:T(1,128)} %all_to_all.6), calls=%async_computation | async-start | bytes 32768 | tf_op jit(solution)/shard_map/all_to_all | solution.py:241
  634.6 4.4 copy-start.2
  639.0 6.1 copy-start.6
  645.1 1.6 copy-start
  646.6 2.2 copy-start.5

commit v7 on v6

--- a/solution.py
+++ b/solution.py
@@ -81,7 +81,7 @@
         gn_v[g] = grad_normed
         total = total + jnp.sum(grad_normed * normed_v[:, cols], axis=1, keepdims=True)
     mean = total * (1.0 / feature_count)
-    inv = inv_ref[...]
+    inv = inv_ref[pl.ds(first_row, rows_here), :]
     for g in range(groups):
         cols = slice(g * group_lanes, (g + 1) * group_lanes)
         out_ref[:, cols] = (
@@ -113,14 +113,14 @@
             pl.BlockSpec(memory_space=pl.ANY),
             pl.BlockSpec(memory_space=pltpu.VMEM),
             pl.BlockSpec(memory_space=pl.ANY),
-            pl.BlockSpec((rows_here, feature_count), lambda i, t, s: (0, 0)),
-            pl.BlockSpec(memory_space=pl.ANY),
-            pl.BlockSpec(memory_space=pl.ANY),
-            pl.BlockSpec((rows_here, 1), lambda i, t, s: (chunk_of(i, t, s), 0)),
-            pl.BlockSpec((1, feature_count), lambda i, t, s: (0, 0)),
+            pl.BlockSpec(memory_space=pltpu.VMEM),
+            pl.BlockSpec(memory_space=pl.ANY),
+            pl.BlockSpec(memory_space=pl.ANY),
+            pl.BlockSpec(memory_space=pltpu.VMEM),
+            pl.BlockSpec(memory_space=pltpu.VMEM),
         ],
         out_specs=[
-            pl.BlockSpec((rows_here, feature_count), lambda i, t, s: (0, 0)),
+            pl.BlockSpec(memory_space=pltpu.VMEM),
             pl.BlockSpec(memory_space=pltpu.VMEM),
             pl.BlockSpec(memory_space=pl.ANY),
         ],

time: 661 us -> 661 us (level)
  no operation moved by 1% of the time
where the time goes in v7:
time: 661 us; the launch traced here: 658 us
  starting transfers between devices  279 us (42%)
  Pallas kernels  175 us (26%)
  waiting for transfers between devices  141 us (21%)
  local copies, waits for them, and re-layouts  28 us (4%)
  matrix products  23 us (3%)
  other arithmetic  10.2 us (2%)
    ppermute x39, starting transfers between devices, passed_along(): lax.ppermute(value, axis, [(source, source + steps) for source in range(l...  231 us
    pallas_call x39, Pallas kernels, turn_call(): pl.pallas_call(kernel, grid_spec=grid_spec, out_shape=[jax.ShapeDtypeStru...  175 us
    ppermute x39, waiting for transfers between devices, passed_along(): lax.ppermute(value, axis, [(source, source + steps) for source in range(l...  141 us
    all_to_all x1, starting transfers between devices, on_device(): lax.all_to_all(gain_sum.reshape(group_count, feature_count // group_count...  47.7 us
    unnamed x22, local copies, waits for them, and re-layouts  15.9 us
  transfers between devices with their start and end apart: 40, of which 39 were waited for; matrix products, arithmetic and copies ran while one was open for 3% of the time, Pallas kernels for 0%

profile of v7, /device:TPU:15, one launch (start us, length us, event | category | flops | bytes accessed | tf_op | source)
XLA Modules:
  0.0 657.8 jit_solution(4293512845997225965)
XLA Ops:
  29.0 548.0 %while.17 = (s32[]{:T(128)}, bf16[32,3584]{1,0:T(8,128)(2,1)S(1)}, bf16[288,3584]{1,0:T(8,128)(2,1)S(1)}, bf16[288,3584]{1,0:T(8,128)(2,1)}, s32[1]{0:T(128)}, /...) while((s32[]{:T(128)}, bf16[32,3584]{1,0:T(8,128)(2,1)S(1)}, ...), condition=%wide.region_4.5_spmd, body=%wide.region_3.4_spmd.sunk | while | flops 2 | bytes 917653 | solution.py:212
  29.0 4.5 eval_jaxpr.5
  33.5 7.7 %collective-permute-start = (bf16[32,3584]{1,0:T(8,128)(2,1)}, bf16[32,3584]{1,0:T(8,128)(2,1)S(1)}, u32[]{:S(2)}, u32[]{:S(2)}) collective-permute-start(bf16[32,3584]{1,0:T(8,128)(2,1)} %get-tuple-element.282), channel_id=1, source_target_pairs={{8,0},{16,8},{24,16},{32,24},{40,32},{48,40},{56,48},{64,56},{72,6... | collective-permute-start | bytes 688136 | tf_op jit(solution)/shard_map/while/body/eval_jaxpr/ppermute | solution.py:22
  41.3 4.6 collective-permute-done
  50.3 6.1 collective-permute-start
  60.1 4.5 eval_jaxpr.5
  64.6 6.1 collective-permute-start
  74.0 4.5 eval_jaxpr.5
  78.5 5.8 collective-permute-start
  87.6 4.5 eval_jaxpr.5
  92.1 5.8 collective-permute-start
  101.1 4.5 eval_jaxpr.5
  105.6 5.8 collective-permute-start
  119.2 5.8 collective-permute-start
  132.8 5.8 collective-permute-start
  146.4 5.8 collective-permute-start
  160.0 5.8 collective-permute-start
  173.5 5.8 collective-permute-start
  187.1 5.8 collective-permute-start
  201.7 5.8 collective-permute-start
  207.5 5.4 collective-permute-done
  217.4 5.8 collective-permute-start
  223.2 4.9 collective-permute-done
  228.1 4.5 eval_jaxpr.5
  232.6 6.1 collective-permute-start
  242.8 4.5 eval_jaxpr.5
  247.3 6.1 collective-permute-start
  256.6 4.5 eval_jaxpr.5
  261.1 5.8 collective-permute-start
  270.2 4.5 eval_jaxpr.5
  274.7 5.8 collective-permute-start
  283.8 4.5 eval_jaxpr.5
  288.3 5.8 collective-permute-start
  301.9 5.8 collective-permute-start
  311.0 4.5 eval_jaxpr.5
  315.5 5.8 collective-permute-start
  324.6 4.5 eval_jaxpr.5
  329.1 5.8 collective-permute-start
  342.6 5.8 collective-permute-start
  356.2 5.8 collective-permute-start
  369.8 5.8 collective-permute-start
  384.0 5.8 collective-permute-start
  389.8 4.9 collective-permute-done
  399.3 5.8 collective-permute-start
  405.1 5.4 collective-permute-done
  410.5 4.5 eval_jaxpr.5
  415.0 6.1 collective-permute-start
  421.1 4.5 collective-permute-done
  430.1 6.1 collective-permute-start
  444.3 6.1 collective-permute-start
  453.7 4.5 eval_jaxpr.5
  458.2 5.8 collective-permute-start
  467.3 4.5 eval_jaxpr.5
  471.8 5.8 collective-permute-start
  485.4 5.8 collective-permute-start
  498.9 5.8 collective-permute-start
  512.5 5.8 collective-permute-start
  526.1 5.8 collective-permute-start
  539.7 5.8 collective-permute-start
  553.3 5.8 collective-permute-start
  566.9 5.8 collective-permute-start
  581.3 4.9 fusion.1
  586.8 47.7 %all-to-all-start = ((f32[8,1,448]{2,1,0:T(1,128)}), f32[8,1,448]{2,1,0:T(1,128)S(1)}, u32[]{:S(2)}, u32[]{:S(2)}) async-start(f32[8,1,448]{2,1,0:T(1,128)} %all_to_all.6), calls=%async_computation | async-start | bytes 32768 | tf_op jit(solution)/shard_map/all_to_all | solution.py:241
  639.0 6.1 multiply_convert_fusion
  (106 shorter events, 269.6 us)
Async XLA Ops:
  0.7 6.0 copy-start.8
  9.6 8.5 %copy-start.4 = (bf16[1,1,256,3584]{2,3,1,0:T(8,128)(2,1)}, bf16[1,1,256,3584]{2,3,1,0:T(8,128)(2,1)S(1)}, u32[]{:S(2)}) copy-start(bf16[1,1,256,3584]{2,3,1,0:T(8,128)(2,1)S(1)} %copy.27) | copy-start | bytes 5505028
  18.1 3.2 copy-start.1
  21.3 3.6 copy-start.3
  24.9 4.1 copy-start.7
  33.5 12.3 %collective-permute-start = (bf16[32,3584]{1,0:T(8,128)(2,1)}, bf16[32,3584]{1,0:T(8,128)(2,1)S(1)}, u32[]{:S(2)}, u32[]{:S(2)}) collective-permute-start(bf16[32,3584]{1,0:T(8,128)(2,1)} %get-tuple-element.282), channel_id=1, source_target_pairs={{8,0},{16,8},{24,16},{32,24},{40,32},{48,40},{56,48},{64,56},{72,6... | collective-permute-start | bytes 688136 | tf_op jit(solution)/shard_map/while/body/eval_jaxpr/ppermute | solution.py:22
  50.3 9.8 %collective-permute-start = (bf16[32,3584]{1,0:T(8,128)(2,1)}, bf16[32,3584]{1,0:T(8,128)(2,1)S(1)}, u32[]{:S(2)}, u32[]{:S(2)}) collective-permute-start(bf16[32,3584]{1,0:T(8,128)(2,1)} %get-tuple-element.282), channel_id=1, source_target_pairs={{8,0},{16,8},{24,16},{32,24},{40,32},{48,40},{56,48},{64,56},{72,6... | collective-permute-start | bytes 688136 | tf_op jit(solution)/shard_map/while/body/eval_jaxpr/ppermute | solution.py:22
  64.6 9.4 %collective-permute-start = (bf16[32,3584]{1,0:T(8,128)(2,1)}, bf16[32,3584]{1,0:T(8,128)(2,1)S(1)}, u32[]{:S(2)}, u32[]{:S(2)}) collective-permute-start(bf16[32,3584]{1,0:T(8,128)(2,1)} %get-tuple-element.282), channel_id=1, source_target_pairs={{8,0},{16,8},{24,16},{32,24},{40,32},{48,40},{56,48},{64,56},{72,6... | collective-permute-start | bytes 688136 | tf_op jit(solution)/shard_map/while/body/eval_jaxpr/ppermute | solution.py:22
  78.5 9.1 %collective-permute-start = (bf16[32,3584]{1,0:T(8,128)(2,1)}, bf16[32,3584]{1,0:T(8,128)(2,1)S(1)}, u32[]{:S(2)}, u32[]{:S(2)}) collective-permute-start(bf16[32,3584]{1,0:T(8,128)(2,1)} %get-tuple-element.282), channel_id=1, source_target_pairs={{8,0},{16,8},{24,16},{32,24},{40,32},{48,40},{56,48},{64,56},{72,6... | collective-permute-start | bytes 688136 | tf_op jit(solution)/shard_map/while/body/eval_jaxpr/ppermute | solution.py:22
  92.1 9.1 %collective-permute-start = (bf16[32,3584]{1,0:T(8,128)(2,1)}, bf16[32,3584]{1,0:T(8,128)(2,1)S(1)}, u32[]{:S(2)}, u32[]{:S(2)}) collective-permute-start(bf16[32,3584]{1,0:T(8,128)(2,1)} %get-tuple-element.282), channel_id=1, source_target_pairs={{8,0},{16,8},{24,16},{32,24},{40,32},{48,40},{56,48},{64,56},{72,6... | collective-permute-start | bytes 688136 | tf_op jit(solution)/shard_map/while/body/eval_jaxpr/ppermute | solution.py:22
  105.6 9.1 %collective-permute-start = (bf16[32,3584]{1,0:T(8,128)(2,1)}, bf16[32,3584]{1,0:T(8,128)(2,1)S(1)}, u32[]{:S(2)}, u32[]{:S(2)}) collective-permute-start(bf16[32,3584]{1,0:T(8,128)(2,1)} %get-tuple-element.282), channel_id=1, source_target_pairs={{8,0},{16,8},{24,16},{32,24},{40,32},{48,40},{56,48},{64,56},{72,6... | collective-permute-start | bytes 688136 | tf_op jit(solution)/shard_map/while/body/eval_jaxpr/ppermute | solution.py:22
  119.2 9.1 %collective-permute-start = (bf16[32,3584]{1,0:T(8,128)(2,1)}, bf16[32,3584]{1,0:T(8,128)(2,1)S(1)}, u32[]{:S(2)}, u32[]{:S(2)}) collective-permute-start(bf16[32,3584]{1,0:T(8,128)(2,1)} %get-tuple-element.282), channel_id=1, source_target_pairs={{8,0},{16,8},{24,16},{32,24},{40,32},{48,40},{56,48},{64,56},{72,6... | collective-permute-start | bytes 688136 | tf_op jit(solution)/shard_map/while/body/eval_jaxpr/ppermute | solution.py:22
  132.8 9.1 %collective-permute-start = (bf16[32,3584]{1,0:T(8,128)(2,1)}, bf16[32,3584]{1,0:T(8,128)(2,1)S(1)}, u32[]{:S(2)}, u32[]{:S(2)}) collective-permute-start(bf16[32,3584]{1,0:T(8,128)(2,1)} %get-tuple-element.282), channel_id=1, source_target_pairs={{8,0},{16,8},{24,16},{32,24},{40,32},{48,40},{56,48},{64,56},{72,6... | collective-permute-start | bytes 688136 | tf_op jit(solution)/shard_map/while/body/eval_jaxpr/ppermute | solution.py:22
  146.4 9.1 %collective-permute-start = (bf16[32,3584]{1,0:T(8,128)(2,1)}, bf16[32,3584]{1,0:T(8,128)(2,1)S(1)}, u32[]{:S(2)}, u32[]{:S(2)}) collective-permute-start(bf16[32,3584]{1,0:T(8,128)(2,1)} %get-tuple-element.282), channel_id=1, source_target_pairs={{8,0},{16,8},{24,16},{32,24},{40,32},{48,40},{56,48},{64,56},{72,6... | collective-permute-start | bytes 688136 | tf_op jit(solution)/shard_map/while/body/eval_jaxpr/ppermute | solution.py:22
  160.0 9.1 %collective-permute-start = (bf16[32,3584]{1,0:T(8,128)(2,1)}, bf16[32,3584]{1,0:T(8,128)(2,1)S(1)}, u32[]{:S(2)}, u32[]{:S(2)}) collective-permute-start(bf16[32,3584]{1,0:T(8,128)(2,1)} %get-tuple-element.282), channel_id=1, source_target_pairs={{8,0},{16,8},{24,16},{32,24},{40,32},{48,40},{56,48},{64,56},{72,6... | collective-permute-start | bytes 688136 | tf_op jit(solution)/shard_map/while/body/eval_jaxpr/ppermute | solution.py:22
  173.5 9.1 %collective-permute-start = (bf16[32,3584]{1,0:T(8,128)(2,1)}, bf16[32,3584]{1,0:T(8,128)(2,1)S(1)}, u32[]{:S(2)}, u32[]{:S(2)}) collective-permute-start(bf16[32,3584]{1,0:T(8,128)(2,1)} %get-tuple-element.282), channel_id=1, source_target_pairs={{8,0},{16,8},{24,16},{32,24},{40,32},{48,40},{56,48},{64,56},{72,6... | collective-permute-start | bytes 688136 | tf_op jit(solution)/shard_map/while/body/eval_jaxpr/ppermute | solution.py:22
  187.1 10.1 %collective-permute-start = (bf16[32,3584]{1,0:T(8,128)(2,1)}, bf16[32,3584]{1,0:T(8,128)(2,1)S(1)}, u32[]{:S(2)}, u32[]{:S(2)}) collective-permute-start(bf16[32,3584]{1,0:T(8,128)(2,1)} %get-tuple-element.282), channel_id=1, source_target_pairs={{8,0},{16,8},{24,16},{32,24},{40,32},{48,40},{56,48},{64,56},{72,6... | collective-permute-start | bytes 688136 | tf_op jit(solution)/shard_map/while/body/eval_jaxpr/ppermute | solution.py:22
  201.7 11.2 %collective-permute-start = (bf16[32,3584]{1,0:T(8,128)(2,1)}, bf16[32,3584]{1,0:T(8,128)(2,1)S(1)}, u32[]{:S(2)}, u32[]{:S(2)}) collective-permute-start(bf16[32,3584]{1,0:T(8,128)(2,1)} %get-tuple-element.282), channel_id=1, source_target_pairs={{8,0},{16,8},{24,16},{32,24},{40,32},{48,40},{56,48},{64,56},{72,6... | collective-permute-start | bytes 688136 | tf_op jit(solution)/shard_map/while/body/eval_jaxpr/ppermute | solution.py:22
  217.4 10.8 %collective-permute-start = (bf16[32,3584]{1,0:T(8,128)(2,1)}, bf16[32,3584]{1,0:T(8,128)(2,1)S(1)}, u32[]{:S(2)}, u32[]{:S(2)}) collective-permute-start(bf16[32,3584]{1,0:T(8,128)(2,1)} %get-tuple-element.282), channel_id=1, source_target_pairs={{8,0},{16,8},{24,16},{32,24},{40,32},{48,40},{56,48},{64,56},{72,6... | collective-permute-start | bytes 688136 | tf_op jit(solution)/shard_map/while/body/eval_jaxpr/ppermute | solution.py:22
  232.6 10.1 %collective-permute-start = (bf16[32,3584]{1,0:T(8,128)(2,1)}, bf16[32,3584]{1,0:T(8,128)(2,1)S(1)}, u32[]{:S(2)}, u32[]{:S(2)}) collective-permute-start(bf16[32,3584]{1,0:T(8,128)(2,1)} %get-tuple-element.282), channel_id=1, source_target_pairs={{8,0},{16,8},{24,16},{32,24},{40,32},{48,40},{56,48},{64,56},{72,6... | collective-permute-start | bytes 688136 | tf_op jit(solution)/shard_map/while/body/eval_jaxpr/ppermute | solution.py:22
  247.3 9.4 %collective-permute-start = (bf16[32,3584]{1,0:T(8,128)(2,1)}, bf16[32,3584]{1,0:T(8,128)(2,1)S(1)}, u32[]{:S(2)}, u32[]{:S(2)}) collective-permute-start(bf16[32,3584]{1,0:T(8,128)(2,1)} %get-tuple-element.282), channel_id=1, source_target_pairs={{8,0},{16,8},{24,16},{32,24},{40,32},{48,40},{56,48},{64,56},{72,6... | collective-permute-start | bytes 688136 | tf_op jit(solution)/shard_map/while/body/eval_jaxpr/ppermute | solution.py:22
  261.1 9.1 %collective-permute-start = (bf16[32,3584]{1,0:T(8,128)(2,1)}, bf16[32,3584]{1,0:T(8,128)(2,1)S(1)}, u32[]{:S(2)}, u32[]{:S(2)}) collective-permute-start(bf16[32,3584]{1,0:T(8,128)(2,1)} %get-tuple-element.282), channel_id=1, source_target_pairs={{8,0},{16,8},{24,16},{32,24},{40,32},{48,40},{56,48},{64,56},{72,6... | collective-permute-start | bytes 688136 | tf_op jit(solution)/shard_map/while/body/eval_jaxpr/ppermute | solution.py:22
  274.7 9.1 %collective-permute-start = (bf16[32,3584]{1,0:T(8,128)(2,1)}, bf16[32,3584]{1,0:T(8,128)(2,1)S(1)}, u32[]{:S(2)}, u32[]{:S(2)}) collective-permute-start(bf16[32,3584]{1,0:T(8,128)(2,1)} %get-tuple-element.282), channel_id=1, source_target_pairs={{8,0},{16,8},{24,16},{32,24},{40,32},{48,40},{56,48},{64,56},{72,6... | collective-permute-start | bytes 688136 | tf_op jit(solution)/shard_map/while/body/eval_jaxpr/ppermute | solution.py:22
  288.3 9.1 %collective-permute-start = (bf16[32,3584]{1,0:T(8,128)(2,1)}, bf16[32,3584]{1,0:T(8,128)(2,1)S(1)}, u32[]{:S(2)}, u32[]{:S(2)}) collective-permute-start(bf16[32,3584]{1,0:T(8,128)(2,1)} %get-tuple-element.282), channel_id=1, source_target_pairs={{8,0},{16,8},{24,16},{32,24},{40,32},{48,40},{56,48},{64,56},{72,6... | collective-permute-start | bytes 688136 | tf_op jit(solution)/shard_map/while/body/eval_jaxpr/ppermute | solution.py:22
  301.9 9.1 %collective-permute-start = (bf16[32,3584]{1,0:T(8,128)(2,1)}, bf16[32,3584]{1,0:T(8,128)(2,1)S(1)}, u32[]{:S(2)}, u32[]{:S(2)}) collective-permute-start(bf16[32,3584]{1,0:T(8,128)(2,1)} %get-tuple-element.282), channel_id=1, source_target_pairs={{8,0},{16,8},{24,16},{32,24},{40,32},{48,40},{56,48},{64,56},{72,6... | collective-permute-start | bytes 688136 | tf_op jit(solution)/shard_map/while/body/eval_jaxpr/ppermute | solution.py:22
  315.5 9.1 %collective-permute-start = (bf16[32,3584]{1,0:T(8,128)(2,1)}, bf16[32,3584]{1,0:T(8,128)(2,1)S(1)}, u32[]{:S(2)}, u32[]{:S(2)}) collective-permute-start(bf16[32,3584]{1,0:T(8,128)(2,1)} %get-tuple-element.282), channel_id=1, source_target_pairs={{8,0},{16,8},{24,16},{32,24},{40,32},{48,40},{56,48},{64,56},{72,6... | collective-permute-start | bytes 688136 | tf_op jit(solution)/shard_map/while/body/eval_jaxpr/ppermute | solution.py:22
  329.1 9.1 %collective-permute-start = (bf16[32,3584]{1,0:T(8,128)(2,1)}, bf16[32,3584]{1,0:T(8,128)(2,1)S(1)}, u32[]{:S(2)}, u32[]{:S(2)}) collective-permute-start(bf16[32,3584]{1,0:T(8,128)(2,1)} %get-tuple-element.282), channel_id=1, source_target_pairs={{8,0},{16,8},{24,16},{32,24},{40,32},{48,40},{56,48},{64,56},{72,6... | collective-permute-start | bytes 688136 | tf_op jit(solution)/shard_map/while/body/eval_jaxpr/ppermute | solution.py:22
  342.6 9.1 %collective-permute-start = (bf16[32,3584]{1,0:T(8,128)(2,1)}, bf16[32,3584]{1,0:T(8,128)(2,1)S(1)}, u32[]{:S(2)}, u32[]{:S(2)}) collective-permute-start(bf16[32,3584]{1,0:T(8,128)(2,1)} %get-tuple-element.282), channel_id=1, source_target_pairs={{8,0},{16,8},{24,16},{32,24},{40,32},{48,40},{56,48},{64,56},{72,6... | collective-permute-start | bytes 688136 | tf_op jit(solution)/shard_map/while/body/eval_jaxpr/ppermute | solution.py:22
  356.2 9.1 %collective-permute-start = (bf16[32,3584]{1,0:T(8,128)(2,1)}, bf16[32,3584]{1,0:T(8,128)(2,1)S(1)}, u32[]{:S(2)}, u32[]{:S(2)}) collective-permute-start(bf16[32,3584]{1,0:T(8,128)(2,1)} %get-tuple-element.282), channel_id=1, source_target_pairs={{8,0},{16,8},{24,16},{32,24},{40,32},{48,40},{56,48},{64,56},{72,6... | collective-permute-start | bytes 688136 | tf_op jit(solution)/shard_map/while/body/eval_jaxpr/ppermute | solution.py:22
  369.8 9.7 %collective-permute-start = (bf16[32,3584]{1,0:T(8,128)(2,1)}, bf16[32,3584]{1,0:T(8,128)(2,1)S(1)}, u32[]{:S(2)}, u32[]{:S(2)}) collective-permute-start(bf16[32,3584]{1,0:T(8,128)(2,1)} %get-tuple-element.282), channel_id=1, source_target_pairs={{8,0},{16,8},{24,16},{32,24},{40,32},{48,40},{56,48},{64,56},{72,6... | collective-permute-start | bytes 688136 | tf_op jit(solution)/shard_map/while/body/eval_jaxpr/ppermute | solution.py:22
  384.0 10.8 %collective-permute-start = (bf16[32,3584]{1,0:T(8,128)(2,1)}, bf16[32,3584]{1,0:T(8,128)(2,1)S(1)}, u32[]{:S(2)}, u32[]{:S(2)}) collective-permute-start(bf16[32,3584]{1,0:T(8,128)(2,1)} %get-tuple-element.282), channel_id=1, source_target_pairs={{8,0},{16,8},{24,16},{32,24},{40,32},{48,40},{56,48},{64,56},{72,6... | collective-permute-start | bytes 688136 | tf_op jit(solution)/shard_map/while/body/eval_jaxpr/ppermute | solution.py:22
  399.3 11.2 %collective-permute-start = (bf16[32,3584]{1,0:T(8,128)(2,1)}, bf16[32,3584]{1,0:T(8,128)(2,1)S(1)}, u32[]{:S(2)}, u32[]{:S(2)}) collective-permute-start(bf16[32,3584]{1,0:T(8,128)(2,1)} %get-tuple-element.282), channel_id=1, source_target_pairs={{8,0},{16,8},{24,16},{32,24},{40,32},{48,40},{56,48},{64,56},{72,6... | collective-permute-start | bytes 688136 | tf_op jit(solution)/shard_map/while/body/eval_jaxpr/ppermute | solution.py:22
  415.0 10.6 %collective-permute-start = (bf16[32,3584]{1,0:T(8,128)(2,1)}, bf16[32,3584]{1,0:T(8,128)(2,1)S(1)}, u32[]{:S(2)}, u32[]{:S(2)}) collective-permute-start(bf16[32,3584]{1,0:T(8,128)(2,1)} %get-tuple-element.282), channel_id=1, source_target_pairs={{8,0},{16,8},{24,16},{32,24},{40,32},{48,40},{56,48},{64,56},{72,6... | collective-permute-start | bytes 688136 | tf_op jit(solution)/shard_map/while/body/eval_jaxpr/ppermute | solution.py:22
  430.1 9.7 %collective-permute-start = (bf16[32,3584]{1,0:T(8,128)(2,1)}, bf16[32,3584]{1,0:T(8,128)(2,1)S(1)}, u32[]{:S(2)}, u32[]{:S(2)}) collective-permute-start(bf16[32,3584]{1,0:T(8,128)(2,1)} %get-tuple-element.282), channel_id=1, source_target_pairs={{8,0},{16,8},{24,16},{32,24},{40,32},{48,40},{56,48},{64,56},{72,6... | collective-permute-start | bytes 688136 | tf_op jit(solution)/shard_map/while/body/eval_jaxpr/ppermute | solution.py:22
  444.3 9.4 %collective-permute-start = (bf16[32,3584]{1,0:T(8,128)(2,1)}, bf16[32,3584]{1,0:T(8,128)(2,1)S(1)}, u32[]{:S(2)}, u32[]{:S(2)}) collective-permute-start(bf16[32,3584]{1,0:T(8,128)(2,1)} %get-tuple-element.282), channel_id=1, source_target_pairs={{8,0},{16,8},{24,16},{32,24},{40,32},{48,40},{56,48},{64,56},{72,6... | collective-permute-start | bytes 688136 | tf_op jit(solution)/shard_map/while/body/eval_jaxpr/ppermute | solution.py:22
  458.2 9.1 %collective-permute-start = (bf16[32,3584]{1,0:T(8,128)(2,1)}, bf16[32,3584]{1,0:T(8,128)(2,1)S(1)}, u32[]{:S(2)}, u32[]{:S(2)}) collective-permute-start(bf16[32,3584]{1,0:T(8,128)(2,1)} %get-tuple-element.282), channel_id=1, source_target_pairs={{8,0},{16,8},{24,16},{32,24},{40,32},{48,40},{56,48},{64,56},{72,6... | collective-permute-start | bytes 688136 | tf_op jit(solution)/shard_map/while/body/eval_jaxpr/ppermute | solution.py:22
  471.8 9.1 %collective-permute-start = (bf16[32,3584]{1,0:T(8,128)(2,1)}, bf16[32,3584]{1,0:T(8,128)(2,1)S(1)}, u32[]{:S(2)}, u32[]{:S(2)}) collective-permute-start(bf16[32,3584]{1,0:T(8,128)(2,1)} %get-tuple-element.282), channel_id=1, source_target_pairs={{8,0},{16,8},{24,16},{32,24},{40,32},{48,40},{56,48},{64,56},{72,6... | collective-permute-start | bytes 688136 | tf_op jit(solution)/shard_map/while/body/eval_jaxpr/ppermute | solution.py:22
  485.4 9.1 %collective-permute-start = (bf16[32,3584]{1,0:T(8,128)(2,1)}, bf16[32,3584]{1,0:T(8,128)(2,1)S(1)}, u32[]{:S(2)}, u32[]{:S(2)}) collective-permute-start(bf16[32,3584]{1,0:T(8,128)(2,1)} %get-tuple-element.282), channel_id=1, source_target_pairs={{8,0},{16,8},{24,16},{32,24},{40,32},{48,40},{56,48},{64,56},{72,6... | collective-permute-start | bytes 688136 | tf_op jit(solution)/shard_map/while/body/eval_jaxpr/ppermute | solution.py:22
  498.9 9.1 %collective-permute-start = (bf16[32,3584]{1,0:T(8,128)(2,1)}, bf16[32,3584]{1,0:T(8,128)(2,1)S(1)}, u32[]{:S(2)}, u32[]{:S(2)}) collective-permute-start(bf16[32,3584]{1,0:T(8,128)(2,1)} %get-tuple-element.282), channel_id=1, source_target_pairs={{8,0},{16,8},{24,16},{32,24},{40,32},{48,40},{56,48},{64,56},{72,6... | collective-permute-start | bytes 688136 | tf_op jit(solution)/shard_map/while/body/eval_jaxpr/ppermute | solution.py:22
  512.5 9.1 %collective-permute-start = (bf16[32,3584]{1,0:T(8,128)(2,1)}, bf16[32,3584]{1,0:T(8,128)(2,1)S(1)}, u32[]{:S(2)}, u32[]{:S(2)}) collective-permute-start(bf16[32,3584]{1,0:T(8,128)(2,1)} %get-tuple-element.282), channel_id=1, source_target_pairs={{8,0},{16,8},{24,16},{32,24},{40,32},{48,40},{56,48},{64,56},{72,6... | collective-permute-start | bytes 688136 | tf_op jit(solution)/shard_map/while/body/eval_jaxpr/ppermute | solution.py:22
  526.1 9.1 %collective-permute-start = (bf16[32,3584]{1,0:T(8,128)(2,1)}, bf16[32,3584]{1,0:T(8,128)(2,1)S(1)}, u32[]{:S(2)}, u32[]{:S(2)}) collective-permute-start(bf16[32,3584]{1,0:T(8,128)(2,1)} %get-tuple-element.282), channel_id=1, source_target_pairs={{8,0},{16,8},{24,16},{32,24},{40,32},{48,40},{56,48},{64,56},{72,6... | collective-permute-start | bytes 688136 | tf_op jit(solution)/shard_map/while/body/eval_jaxpr/ppermute | solution.py:22
  539.7 9.1 %collective-permute-start = (bf16[32,3584]{1,0:T(8,128)(2,1)}, bf16[32,3584]{1,0:T(8,128)(2,1)S(1)}, u32[]{:S(2)}, u32[]{:S(2)}) collective-permute-start(bf16[32,3584]{1,0:T(8,128)(2,1)} %get-tuple-element.282), channel_id=1, source_target_pairs={{8,0},{16,8},{24,16},{32,24},{40,32},{48,40},{56,48},{64,56},{72,6... | collective-permute-start | bytes 688136 | tf_op jit(solution)/shard_map/while/body/eval_jaxpr/ppermute | solution.py:22
  553.3 9.1 %collective-permute-start = (bf16[32,3584]{1,0:T(8,128)(2,1)}, bf16[32,3584]{1,0:T(8,128)(2,1)S(1)}, u32[]{:S(2)}, u32[]{:S(2)}) collective-permute-start(bf16[32,3584]{1,0:T(8,128)(2,1)} %get-tuple-element.282), channel_id=1, source_target_pairs={{8,0},{16,8},{24,16},{32,24},{40,32},{48,40},{56,48},{64,56},{72,6... | collective-permute-start | bytes 688136 | tf_op jit(solution)/shard_map/while/body/eval_jaxpr/ppermute | solution.py:22
  566.9 10.1 %collective-permute-start = (bf16[32,3584]{1,0:T(8,128)(2,1)}, bf16[32,3584]{1,0:T(8,128)(2,1)S(1)}, u32[]{:S(2)}, u32[]{:S(2)}) collective-permute-start(bf16[32,3584]{1,0:T(8,128)(2,1)} %get-tuple-element.282), channel_id=1, source_target_pairs={{8,0},{16,8},{24,16},{32,24},{40,32},{48,40},{56,48},{64,56},{72,6... | collective-permute-start | bytes 688136 | tf_op jit(solution)/shard_map/while/body/eval_jaxpr/ppermute | solution.py:22
  586.8 70.4 %all-to-all-start = ((f32[8,1,448]{2,1,0:T(1,128)}), f32[8,1,448]{2,1,0:T(1,128)S(1)}, u32[]{:S(2)}, u32[]{:S(2)}) async-start(f32[8,1,448]{2,1,0:T(1,128)} %all_to_all.6), calls=%async_computation | async-start | bytes 32768 | tf_op jit(solution)/shard_map/all_to_all | solution.py:241
  634.6 4.4 copy-start.2
  639.0 6.1 copy-start.6
  645.1 1.6 copy-start
  646.6 2.2 copy-start.5

commit v8 on v6

--- a/solution.py
+++ b/solution.py
@@ -32,8 +32,8 @@
 
 def turn_kernel(
     turn_ref, stage_ref,
-    w_hbm, g_hbm, ig_hbm, msg_ref, loss_ref, normed_ref, inv_ref, gain_ref,
-    out_ref, g_out, ig_out,
+    w_hbm, g_hbm, ig_hbm, sum_in, msg_ref, loss_ref, normed_ref, inv_ref, gain_ref,
+    out_ref, g_out, ig_out, sum_out,
     w_v, gn_v, normed_v, loss_v, sems,
     *, group_lanes, head_size, rows_here, groups, seq_rows, feature_count, stage_count, unit_count,
 ):
@@ -77,6 +77,8 @@
             value = value + jnp.where(
                 lane_head == k, stacked[k * rows_here:(k + 1) * rows_here, :], 0.0
             )
+        gain_part = jnp.sum(value * normed_v[:, cols], axis=0, keepdims=True)
+        sum_out[:, cols] = sum_out[:, cols] + jnp.where(active, gain_part, 0.0)
         grad_normed = value * gain_ref[:, cols]
         gn_v[g] = grad_normed
         total = total + jnp.sum(grad_normed * normed_v[:, cols], axis=1, keepdims=True)
@@ -92,8 +94,8 @@
     ig_write.wait()
 
 
-def turn_call(turn, stage, w_split, grad_buffer, input_grads, message, from_loss, normed, inverse,
-              gain, *, head_size, rows_here, stage_count):
+def turn_call(turn, stage, w_split, grad_buffer, input_grads, gain_sum, message, from_loss, normed,
+              inverse, gain, *, head_size, rows_here, stage_count):
     groups, group_heads, unit_count, _, seq_rows = w_split.shape
     feature_count = grad_buffer.shape[1]
     group_lanes = feature_count // groups
@@ -113,6 +115,7 @@
             pl.BlockSpec(memory_space=pl.ANY),
             pl.BlockSpec(memory_space=pltpu.VMEM),
             pl.BlockSpec(memory_space=pl.ANY),
+            pl.BlockSpec(memory_space=pltpu.VMEM),
             pl.BlockSpec((rows_here, feature_count), lambda i, t, s: (0, 0)),
             pl.BlockSpec(memory_space=pl.ANY),
             pl.BlockSpec(memory_space=pl.ANY),
@@ -123,6 +126,7 @@
             pl.BlockSpec((rows_here, feature_count), lambda i, t, s: (0, 0)),
             pl.BlockSpec(memory_space=pltpu.VMEM),
             pl.BlockSpec(memory_space=pl.ANY),
+            pl.BlockSpec(memory_space=pltpu.VMEM),
         ],
         scratch_shapes=[
             pltpu.VMEM((groups, group_heads, rows_here, seq_rows), jnp.bfloat16),
@@ -139,10 +143,12 @@
             jax.ShapeDtypeStruct((rows_here, feature_count), jnp.bfloat16),
             jax.ShapeDtypeStruct(grad_buffer.shape, grad_buffer.dtype),
             jax.ShapeDtypeStruct(input_grads.shape, input_grads.dtype),
-        ],
-        input_output_aliases={3: 1, 4: 2},
+            jax.ShapeDtypeStruct(gain_sum.shape, gain_sum.dtype),
+        ],
+        input_output_aliases={3: 1, 4: 2, 5: 3},
         compiler_params=pltpu.CompilerParams(dimension_semantics=("arbitrary",)),
-    )(turn, stage, w_split, grad_buffer, input_grads, message, from_loss, normed, inverse, gain)
+    )(turn, stage, w_split, grad_buffer, input_grads, gain_sum, message, from_loss, normed, inverse,
+      gain)
 
 
 def on_device(query_acts, key_acts, layer_inputs, grad_out, norm_gains, window_flags):
@@ -196,20 +202,21 @@
     gain_line = gain_row[None, :]
 
     def one_turn(turn_index, carried):
-        message, grad_buffer, input_grads = carried
-        grad_input, grad_buffer, input_grads = turn_call(
+        message, grad_buffer, input_grads, gain_total = carried
+        grad_input, grad_buffer, input_grads, gain_total = turn_call(
             turn_index.astype(jnp.int32).reshape(1), stage, w_split, grad_buffer, input_grads,
-            message, from_loss, normed, inverse, gain_line,
+            gain_total, message, from_loss, normed, inverse, gain_line,
             head_size=head_size, rows_here=rows_here, stage_count=section_count,
         )
-        return (passed_along(grad_input, "pipe", -1), grad_buffer, input_grads)
+        return (passed_along(grad_input, "pipe", -1), grad_buffer, input_grads, gain_total)
 
     initial = (
         jnp.zeros((rows_here, feature_count), jnp.bfloat16),
         jnp.zeros((spare_rows, feature_count), jnp.bfloat16),
         jnp.zeros((spare_rows, feature_count), jnp.bfloat16),
-    )
-    _, grad_buffer, input_grads = lax.fori_loop(
+        jnp.zeros((1, feature_count), jnp.float32),
+    )
+    _, grad_buffer, input_grads, gain_total = lax.fori_loop(
         0, unit_count + section_count - 1, one_turn, initial
     )
     grad_heads = grad_buffer[:seq_rows].reshape(seq_rows, head_count, head_size)
@@ -229,10 +236,7 @@
         * score_scale
     )
     grad_key = grad_key.astype(jnp.bfloat16).reshape(seq_rows, feature_count)
-    grad_value = jnp.einsum(
-        "hji,ihd->jhd", weights_low, grad_heads, preferred_element_type=jnp.float32
-    ).reshape(seq_rows, feature_count)
-    gain_sum = jnp.sum(grad_value * normed, axis=0)
+    gain_sum = gain_total[0]
 
     grad_queries = grad_query.reshape(1, 1, seq_rows, feature_count)
     grad_keys = grad_key.reshape(1, 1, seq_rows, feature_count)

time: 661 us -> 661 us (level)
    unnamed x22 -> x25, local copies, waits for them, and re-layouts: 15.9 us -> 18.7 us
  transfers between devices with their start and end apart: 40 -> 40, of which waited for: 39 -> 39; matrix products, arithmetic and copies ran while one was open for 3% -> 4% of each run, Pallas kernels for 0% -> 0%
where the time goes in v8:
time: 661 us; the launch traced here: 659 us
  starting transfers between devices  279 us (42%)
  Pallas kernels  176 us (27%)
  waiting for transfers between devices  141 us (21%)
  local copies, waits for them, and re-layouts  33 us (5%)
  matrix products  19.5 us (3%)
  other arithmetic  9.25 us (1%)
    ppermute x39, starting transfers between devices, passed_along(): lax.ppermute(value, axis, [(source, source + steps) for source in range(l...  231 us
    pallas_call x39, Pallas kernels, turn_call(): pl.pallas_call(kernel, grid_spec=grid_spec, out_shape=[jax.ShapeDtypeStru...  176 us
    ppermute x39, waiting for transfers between devices, passed_along(): lax.ppermute(value, axis, [(source, source + steps) for source in range(l...  141 us
    all_to_all x1, starting transfers between devices, on_device(): lax.all_to_all(gain_sum.reshape(group_count, feature_count // group_count...  47.8 us
    unnamed x25, local copies, waits for them, and re-layouts  18.7 us
  transfers between devices with their start and end apart: 40, of which 39 were waited for; matrix products, arithmetic and copies ran while one was open for 4% of the time, Pallas kernels for 0%

profile of v8, /device:TPU:15, one launch (start us, length us, event | category | flops | bytes accessed | tf_op | source)
XLA Modules:
  0.0 658.7 jit_solution(9705027366433653694)
XLA Ops:
  25.1 5.2 copy.32
  32.0 548.3 %while.19 = (s32[]{:T(128)}, bf16[32,3584]{1,0:T(8,128)(2,1)S(1)}, bf16[288,3584]{1,0:T(8,128)(2,1)S(1)}, bf16[288,3584]{1,0:T(8,128)(2,1)}, f32[1,3584]{1,0:T(1...) while((s32[]{:T(128)}, bf16[32,3584]{1,0:T(8,128)(2,1)S(1)}, ...), condition=%wide.region_4.5_spmd, body=%wide.region_3.4_spmd.sunk | while | flops 2 | bytes 917661 | solution.py:219
  32.0 4.5 eval_jaxpr.5
  36.5 7.8 %collective-permute-start = (bf16[32,3584]{1,0:T(8,128)(2,1)}, bf16[32,3584]{1,0:T(8,128)(2,1)S(1)}, u32[]{:S(2)}, u32[]{:S(2)}) collective-permute-start(bf16[32,3584]{1,0:T(8,128)(2,1)} %get-tuple-element.310), channel_id=1, source_target_pairs={{8,0},{16,8},{24,16},{32,24},{40,32},{48,40},{56,48},{64,56},{72,6... | collective-permute-start | bytes 688136 | tf_op jit(solution)/shard_map/while/body/eval_jaxpr/ppermute | solution.py:22
  44.3 4.6 collective-permute-done
  48.8 4.5 eval_jaxpr.5
  53.4 6.1 collective-permute-start
  63.1 4.5 eval_jaxpr.5
  67.6 6.1 collective-permute-start
  81.5 5.8 collective-permute-start
  90.6 4.5 eval_jaxpr.5
  95.1 5.8 collective-permute-start
  108.7 5.8 collective-permute-start
  117.8 4.5 eval_jaxpr.5
  122.3 5.8 collective-permute-start
  135.9 5.8 collective-permute-start
  149.5 5.8 collective-permute-start
  163.1 5.8 collective-permute-start
  176.7 5.8 collective-permute-start
  190.2 5.8 collective-permute-start
  204.8 5.8 collective-permute-start
  210.7 5.4 collective-permute-done
  220.5 5.8 collective-permute-start
  226.4 4.9 collective-permute-done
  231.2 4.5 eval_jaxpr.5
  235.8 6.1 collective-permute-start
  250.3 6.1 collective-permute-start
  259.7 4.5 eval_jaxpr.5
  264.2 5.8 collective-permute-start
  277.8 5.8 collective-permute-start
  286.9 4.5 eval_jaxpr.5
  291.4 5.8 collective-permute-start
  305.0 5.8 collective-permute-start
  318.6 5.8 collective-permute-start
  327.7 4.5 eval_jaxpr.5
  332.2 5.8 collective-permute-start
  345.8 5.8 collective-permute-start
  354.9 4.5 eval_jaxpr.5
  359.4 5.8 collective-permute-start
  373.0 5.8 collective-permute-start
  382.7 4.5 eval_jaxpr.5
  387.2 5.8 collective-permute-start
  393.1 5.0 collective-permute-done
  402.6 5.8 collective-permute-start
  408.4 5.3 collective-permute-done
  413.7 4.5 eval_jaxpr.5
  418.2 6.1 collective-permute-start
  428.8 4.5 eval_jaxpr.5
  433.3 6.1 collective-permute-start
  447.4 6.1 collective-permute-start
  456.8 4.5 eval_jaxpr.5
  461.3 5.8 collective-permute-start
  474.9 5.8 collective-permute-start
  488.5 5.8 collective-permute-start
  497.6 4.5 eval_jaxpr.5
  502.1 5.8 collective-permute-start
  515.7 5.8 collective-permute-start
  524.8 4.5 eval_jaxpr.5
  529.3 5.8 collective-permute-start
  542.9 5.8 collective-permute-start
  556.5 5.8 collective-permute-start
  570.1 5.8 collective-permute-start
  581.0 47.8 %all-to-all-start = ((f32[8,1,448]{2,1,0:T(1,128)}), f32[8,1,448]{2,1,0:T(1,128)S(1)}, u32[]{:S(2)}, u32[]{:S(2)}) async-start(f32[8,1,448]{2,1,0:T(1,128)} %all_to_all.6), calls=%async_computation | async-start | bytes 32768 | tf_op jit(solution)/shard_map/all_to_all | solution.py:245
  638.7 6.1 multiply_convert_fusion
  (110 shorter events, 270.0 us)
Async XLA Ops:
  4.3 8.5 %copy-start.4 = (bf16[1,1,256,3584]{2,3,1,0:T(8,128)(2,1)}, bf16[1,1,256,3584]{2,3,1,0:T(8,128)(2,1)S(1)}, u32[]{:S(2)}) copy-start(bf16[1,1,256,3584]{2,3,1,0:T(8,128)(2,1)S(1)} %copy.29) | copy-start | bytes 5505028
  12.8 3.2 copy-start.1
  22.4 2.6 copy-start.2
  30.2 1.8 copy-start.9
  36.5 12.3 %collective-permute-start = (bf16[32,3584]{1,0:T(8,128)(2,1)}, bf16[32,3584]{1,0:T(8,128)(2,1)S(1)}, u32[]{:S(2)}, u32[]{:S(2)}) collective-permute-start(bf16[32,3584]{1,0:T(8,128)(2,1)} %get-tuple-element.310), channel_id=1, source_target_pairs={{8,0},{16,8},{24,16},{32,24},{40,32},{48,40},{56,48},{64,56},{72,6... | collective-permute-start | bytes 688136 | tf_op jit(solution)/shard_map/while/body/eval_jaxpr/ppermute | solution.py:22
  53.4 9.8 %collective-permute-start = (bf16[32,3584]{1,0:T(8,128)(2,1)}, bf16[32,3584]{1,0:T(8,128)(2,1)S(1)}, u32[]{:S(2)}, u32[]{:S(2)}) collective-permute-start(bf16[32,3584]{1,0:T(8,128)(2,1)} %get-tuple-element.310), channel_id=1, source_target_pairs={{8,0},{16,8},{24,16},{32,24},{40,32},{48,40},{56,48},{64,56},{72,6... | collective-permute-start | bytes 688136 | tf_op jit(solution)/shard_map/while/body/eval_jaxpr/ppermute | solution.py:22
  67.6 9.4 %collective-permute-start = (bf16[32,3584]{1,0:T(8,128)(2,1)}, bf16[32,3584]{1,0:T(8,128)(2,1)S(1)}, u32[]{:S(2)}, u32[]{:S(2)}) collective-permute-start(bf16[32,3584]{1,0:T(8,128)(2,1)} %get-tuple-element.310), channel_id=1, source_target_pairs={{8,0},{16,8},{24,16},{32,24},{40,32},{48,40},{56,48},{64,56},{72,6... | collective-permute-start | bytes 688136 | tf_op jit(solution)/shard_map/while/body/eval_jaxpr/ppermute | solution.py:22
  81.5 9.1 %collective-permute-start = (bf16[32,3584]{1,0:T(8,128)(2,1)}, bf16[32,3584]{1,0:T(8,128)(2,1)S(1)}, u32[]{:S(2)}, u32[]{:S(2)}) collective-permute-start(bf16[32,3584]{1,0:T(8,128)(2,1)} %get-tuple-element.310), channel_id=1, source_target_pairs={{8,0},{16,8},{24,16},{32,24},{40,32},{48,40},{56,48},{64,56},{72,6... | collective-permute-start | bytes 688136 | tf_op jit(solution)/shard_map/while/body/eval_jaxpr/ppermute | solution.py:22
  95.1 9.1 %collective-permute-start = (bf16[32,3584]{1,0:T(8,128)(2,1)}, bf16[32,3584]{1,0:T(8,128)(2,1)S(1)}, u32[]{:S(2)}, u32[]{:S(2)}) collective-permute-start(bf16[32,3584]{1,0:T(8,128)(2,1)} %get-tuple-element.310), channel_id=1, source_target_pairs={{8,0},{16,8},{24,16},{32,24},{40,32},{48,40},{56,48},{64,56},{72,6... | collective-permute-start | bytes 688136 | tf_op jit(solution)/shard_map/while/body/eval_jaxpr/ppermute | solution.py:22
  108.7 9.1 %collective-permute-start = (bf16[32,3584]{1,0:T(8,128)(2,1)}, bf16[32,3584]{1,0:T(8,128)(2,1)S(1)}, u32[]{:S(2)}, u32[]{:S(2)}) collective-permute-start(bf16[32,3584]{1,0:T(8,128)(2,1)} %get-tuple-element.310), channel_id=1, source_target_pairs={{8,0},{16,8},{24,16},{32,24},{40,32},{48,40},{56,48},{64,56},{72,6... | collective-permute-start | bytes 688136 | tf_op jit(solution)/shard_map/while/body/eval_jaxpr/ppermute | solution.py:22
  122.3 9.1 %collective-permute-start = (bf16[32,3584]{1,0:T(8,128)(2,1)}, bf16[32,3584]{1,0:T(8,128)(2,1)S(1)}, u32[]{:S(2)}, u32[]{:S(2)}) collective-permute-start(bf16[32,3584]{1,0:T(8,128)(2,1)} %get-tuple-element.310), channel_id=1, source_target_pairs={{8,0},{16,8},{24,16},{32,24},{40,32},{48,40},{56,48},{64,56},{72,6... | collective-permute-start | bytes 688136 | tf_op jit(solution)/shard_map/while/body/eval_jaxpr/ppermute | solution.py:22
  135.9 9.1 %collective-permute-start = (bf16[32,3584]{1,0:T(8,128)(2,1)}, bf16[32,3584]{1,0:T(8,128)(2,1)S(1)}, u32[]{:S(2)}, u32[]{:S(2)}) collective-permute-start(bf16[32,3584]{1,0:T(8,128)(2,1)} %get-tuple-element.310), channel_id=1, source_target_pairs={{8,0},{16,8},{24,16},{32,24},{40,32},{48,40},{56,48},{64,56},{72,6... | collective-permute-start | bytes 688136 | tf_op jit(solution)/shard_map/while/body/eval_jaxpr/ppermute | solution.py:22
  149.5 9.1 %collective-permute-start = (bf16[32,3584]{1,0:T(8,128)(2,1)}, bf16[32,3584]{1,0:T(8,128)(2,1)S(1)}, u32[]{:S(2)}, u32[]{:S(2)}) collective-permute-start(bf16[32,3584]{1,0:T(8,128)(2,1)} %get-tuple-element.310), channel_id=1, source_target_pairs={{8,0},{16,8},{24,16},{32,24},{40,32},{48,40},{56,48},{64,56},{72,6... | collective-permute-start | bytes 688136 | tf_op jit(solution)/shard_map/while/body/eval_jaxpr/ppermute | solution.py:22
  163.1 9.1 %collective-permute-start = (bf16[32,3584]{1,0:T(8,128)(2,1)}, bf16[32,3584]{1,0:T(8,128)(2,1)S(1)}, u32[]{:S(2)}, u32[]{:S(2)}) collective-permute-start(bf16[32,3584]{1,0:T(8,128)(2,1)} %get-tuple-element.310), channel_id=1, source_target_pairs={{8,0},{16,8},{24,16},{32,24},{40,32},{48,40},{56,48},{64,56},{72,6... | collective-permute-start | bytes 688136 | tf_op jit(solution)/shard_map/while/body/eval_jaxpr/ppermute | solution.py:22
  176.7 9.1 %collective-permute-start = (bf16[32,3584]{1,0:T(8,128)(2,1)}, bf16[32,3584]{1,0:T(8,128)(2,1)S(1)}, u32[]{:S(2)}, u32[]{:S(2)}) collective-permute-start(bf16[32,3584]{1,0:T(8,128)(2,1)} %get-tuple-element.310), channel_id=1, source_target_pairs={{8,0},{16,8},{24,16},{32,24},{40,32},{48,40},{56,48},{64,56},{72,6... | collective-permute-start | bytes 688136 | tf_op jit(solution)/shard_map/while/body/eval_jaxpr/ppermute | solution.py:22
  190.2 10.1 %collective-permute-start = (bf16[32,3584]{1,0:T(8,128)(2,1)}, bf16[32,3584]{1,0:T(8,128)(2,1)S(1)}, u32[]{:S(2)}, u32[]{:S(2)}) collective-permute-start(bf16[32,3584]{1,0:T(8,128)(2,1)} %get-tuple-element.310), channel_id=1, source_target_pairs={{8,0},{16,8},{24,16},{32,24},{40,32},{48,40},{56,48},{64,56},{72,6... | collective-permute-start | bytes 688136 | tf_op jit(solution)/shard_map/while/body/eval_jaxpr/ppermute | solution.py:22
  204.8 11.2 %collective-permute-start = (bf16[32,3584]{1,0:T(8,128)(2,1)}, bf16[32,3584]{1,0:T(8,128)(2,1)S(1)}, u32[]{:S(2)}, u32[]{:S(2)}) collective-permute-start(bf16[32,3584]{1,0:T(8,128)(2,1)} %get-tuple-element.310), channel_id=1, source_target_pairs={{8,0},{16,8},{24,16},{32,24},{40,32},{48,40},{56,48},{64,56},{72,6... | collective-permute-start | bytes 688136 | tf_op jit(solution)/shard_map/while/body/eval_jaxpr/ppermute | solution.py:22
  220.5 10.7 %collective-permute-start = (bf16[32,3584]{1,0:T(8,128)(2,1)}, bf16[32,3584]{1,0:T(8,128)(2,1)S(1)}, u32[]{:S(2)}, u32[]{:S(2)}) collective-permute-start(bf16[32,3584]{1,0:T(8,128)(2,1)} %get-tuple-element.310), channel_id=1, source_target_pairs={{8,0},{16,8},{24,16},{32,24},{40,32},{48,40},{56,48},{64,56},{72,6... | collective-permute-start | bytes 688136 | tf_op jit(solution)/shard_map/while/body/eval_jaxpr/ppermute | solution.py:22
  235.8 10.1 %collective-permute-start = (bf16[32,3584]{1,0:T(8,128)(2,1)}, bf16[32,3584]{1,0:T(8,128)(2,1)S(1)}, u32[]{:S(2)}, u32[]{:S(2)}) collective-permute-start(bf16[32,3584]{1,0:T(8,128)(2,1)} %get-tuple-element.310), channel_id=1, source_target_pairs={{8,0},{16,8},{24,16},{32,24},{40,32},{48,40},{56,48},{64,56},{72,6... | collective-permute-start | bytes 688136 | tf_op jit(solution)/shard_map/while/body/eval_jaxpr/ppermute | solution.py:22
  250.3 9.4 %collective-permute-start = (bf16[32,3584]{1,0:T(8,128)(2,1)}, bf16[32,3584]{1,0:T(8,128)(2,1)S(1)}, u32[]{:S(2)}, u32[]{:S(2)}) collective-permute-start(bf16[32,3584]{1,0:T(8,128)(2,1)} %get-tuple-element.310), channel_id=1, source_target_pairs={{8,0},{16,8},{24,16},{32,24},{40,32},{48,40},{56,48},{64,56},{72,6... | collective-permute-start | bytes 688136 | tf_op jit(solution)/shard_map/while/body/eval_jaxpr/ppermute | solution.py:22
  264.2 9.1 %collective-permute-start = (bf16[32,3584]{1,0:T(8,128)(2,1)}, bf16[32,3584]{1,0:T(8,128)(2,1)S(1)}, u32[]{:S(2)}, u32[]{:S(2)}) collective-permute-start(bf16[32,3584]{1,0:T(8,128)(2,1)} %get-tuple-element.310), channel_id=1, source_target_pairs={{8,0},{16,8},{24,16},{32,24},{40,32},{48,40},{56,48},{64,56},{72,6... | collective-permute-start | bytes 688136 | tf_op jit(solution)/shard_map/while/body/eval_jaxpr/ppermute | solution.py:22
  277.8 9.1 %collective-permute-start = (bf16[32,3584]{1,0:T(8,128)(2,1)}, bf16[32,3584]{1,0:T(8,128)(2,1)S(1)}, u32[]{:S(2)}, u32[]{:S(2)}) collective-permute-start(bf16[32,3584]{1,0:T(8,128)(2,1)} %get-tuple-element.310), channel_id=1, source_target_pairs={{8,0},{16,8},{24,16},{32,24},{40,32},{48,40},{56,48},{64,56},{72,6... | collective-permute-start | bytes 688136 | tf_op jit(solution)/shard_map/while/body/eval_jaxpr/ppermute | solution.py:22
  291.4 9.1 %collective-permute-start = (bf16[32,3584]{1,0:T(8,128)(2,1)}, bf16[32,3584]{1,0:T(8,128)(2,1)S(1)}, u32[]{:S(2)}, u32[]{:S(2)}) collective-permute-start(bf16[32,3584]{1,0:T(8,128)(2,1)} %get-tuple-element.310), channel_id=1, source_target_pairs={{8,0},{16,8},{24,16},{32,24},{40,32},{48,40},{56,48},{64,56},{72,6... | collective-permute-start | bytes 688136 | tf_op jit(solution)/shard_map/while/body/eval_jaxpr/ppermute | solution.py:22
  305.0 9.1 %collective-permute-start = (bf16[32,3584]{1,0:T(8,128)(2,1)}, bf16[32,3584]{1,0:T(8,128)(2,1)S(1)}, u32[]{:S(2)}, u32[]{:S(2)}) collective-permute-start(bf16[32,3584]{1,0:T(8,128)(2,1)} %get-tuple-element.310), channel_id=1, source_target_pairs={{8,0},{16,8},{24,16},{32,24},{40,32},{48,40},{56,48},{64,56},{72,6... | collective-permute-start | bytes 688136 | tf_op jit(solution)/shard_map/while/body/eval_jaxpr/ppermute | solution.py:22
  318.6 9.1 %collective-permute-start = (bf16[32,3584]{1,0:T(8,128)(2,1)}, bf16[32,3584]{1,0:T(8,128)(2,1)S(1)}, u32[]{:S(2)}, u32[]{:S(2)}) collective-permute-start(bf16[32,3584]{1,0:T(8,128)(2,1)} %get-tuple-element.310), channel_id=1, source_target_pairs={{8,0},{16,8},{24,16},{32,24},{40,32},{48,40},{56,48},{64,56},{72,6... | collective-permute-start | bytes 688136 | tf_op jit(solution)/shard_map/while/body/eval_jaxpr/ppermute | solution.py:22
  332.2 9.1 %collective-permute-start = (bf16[32,3584]{1,0:T(8,128)(2,1)}, bf16[32,3584]{1,0:T(8,128)(2,1)S(1)}, u32[]{:S(2)}, u32[]{:S(2)}) collective-permute-start(bf16[32,3584]{1,0:T(8,128)(2,1)} %get-tuple-element.310), channel_id=1, source_target_pairs={{8,0},{16,8},{24,16},{32,24},{40,32},{48,40},{56,48},{64,56},{72,6... | collective-permute-start | bytes 688136 | tf_op jit(solution)/shard_map/while/body/eval_jaxpr/ppermute | solution.py:22
  345.8 9.1 %collective-permute-start = (bf16[32,3584]{1,0:T(8,128)(2,1)}, bf16[32,3584]{1,0:T(8,128)(2,1)S(1)}, u32[]{:S(2)}, u32[]{:S(2)}) collective-permute-start(bf16[32,3584]{1,0:T(8,128)(2,1)} %get-tuple-element.310), channel_id=1, source_target_pairs={{8,0},{16,8},{24,16},{32,24},{40,32},{48,40},{56,48},{64,56},{72,6... | collective-permute-start | bytes 688136 | tf_op jit(solution)/shard_map/while/body/eval_jaxpr/ppermute | solution.py:22
  359.4 9.1 %collective-permute-start = (bf16[32,3584]{1,0:T(8,128)(2,1)}, bf16[32,3584]{1,0:T(8,128)(2,1)S(1)}, u32[]{:S(2)}, u32[]{:S(2)}) collective-permute-start(bf16[32,3584]{1,0:T(8,128)(2,1)} %get-tuple-element.310), channel_id=1, source_target_pairs={{8,0},{16,8},{24,16},{32,24},{40,32},{48,40},{56,48},{64,56},{72,6... | collective-permute-start | bytes 688136 | tf_op jit(solution)/shard_map/while/body/eval_jaxpr/ppermute | solution.py:22
  373.0 9.7 %collective-permute-start = (bf16[32,3584]{1,0:T(8,128)(2,1)}, bf16[32,3584]{1,0:T(8,128)(2,1)S(1)}, u32[]{:S(2)}, u32[]{:S(2)}) collective-permute-start(bf16[32,3584]{1,0:T(8,128)(2,1)} %get-tuple-element.310), channel_id=1, source_target_pairs={{8,0},{16,8},{24,16},{32,24},{40,32},{48,40},{56,48},{64,56},{72,6... | collective-permute-start | bytes 688136 | tf_op jit(solution)/shard_map/while/body/eval_jaxpr/ppermute | solution.py:22
  387.2 10.8 %collective-permute-start = (bf16[32,3584]{1,0:T(8,128)(2,1)}, bf16[32,3584]{1,0:T(8,128)(2,1)S(1)}, u32[]{:S(2)}, u32[]{:S(2)}) collective-permute-start(bf16[32,3584]{1,0:T(8,128)(2,1)} %get-tuple-element.310), channel_id=1, source_target_pairs={{8,0},{16,8},{24,16},{32,24},{40,32},{48,40},{56,48},{64,56},{72,6... | collective-permute-start | bytes 688136 | tf_op jit(solution)/shard_map/while/body/eval_jaxpr/ppermute | solution.py:22
  402.6 11.1 %collective-permute-start = (bf16[32,3584]{1,0:T(8,128)(2,1)}, bf16[32,3584]{1,0:T(8,128)(2,1)S(1)}, u32[]{:S(2)}, u32[]{:S(2)}) collective-permute-start(bf16[32,3584]{1,0:T(8,128)(2,1)} %get-tuple-element.310), channel_id=1, source_target_pairs={{8,0},{16,8},{24,16},{32,24},{40,32},{48,40},{56,48},{64,56},{72,6... | collective-permute-start | bytes 688136 | tf_op jit(solution)/shard_map/while/body/eval_jaxpr/ppermute | solution.py:22
  418.2 10.6 %collective-permute-start = (bf16[32,3584]{1,0:T(8,128)(2,1)}, bf16[32,3584]{1,0:T(8,128)(2,1)S(1)}, u32[]{:S(2)}, u32[]{:S(2)}) collective-permute-start(bf16[32,3584]{1,0:T(8,128)(2,1)} %get-tuple-element.310), channel_id=1, source_target_pairs={{8,0},{16,8},{24,16},{32,24},{40,32},{48,40},{56,48},{64,56},{72,6... | collective-permute-start | bytes 688136 | tf_op jit(solution)/shard_map/while/body/eval_jaxpr/ppermute | solution.py:22
  433.3 9.6 %collective-permute-start = (bf16[32,3584]{1,0:T(8,128)(2,1)}, bf16[32,3584]{1,0:T(8,128)(2,1)S(1)}, u32[]{:S(2)}, u32[]{:S(2)}) collective-permute-start(bf16[32,3584]{1,0:T(8,128)(2,1)} %get-tuple-element.310), channel_id=1, source_target_pairs={{8,0},{16,8},{24,16},{32,24},{40,32},{48,40},{56,48},{64,56},{72,6... | collective-permute-start | bytes 688136 | tf_op jit(solution)/shard_map/while/body/eval_jaxpr/ppermute | solution.py:22
  447.4 9.4 %collective-permute-start = (bf16[32,3584]{1,0:T(8,128)(2,1)}, bf16[32,3584]{1,0:T(8,128)(2,1)S(1)}, u32[]{:S(2)}, u32[]{:S(2)}) collective-permute-start(bf16[32,3584]{1,0:T(8,128)(2,1)} %get-tuple-element.310), channel_id=1, source_target_pairs={{8,0},{16,8},{24,16},{32,24},{40,32},{48,40},{56,48},{64,56},{72,6... | collective-permute-start | bytes 688136 | tf_op jit(solution)/shard_map/while/body/eval_jaxpr/ppermute | solution.py:22
  461.3 9.1 %collective-permute-start = (bf16[32,3584]{1,0:T(8,128)(2,1)}, bf16[32,3584]{1,0:T(8,128)(2,1)S(1)}, u32[]{:S(2)}, u32[]{:S(2)}) collective-permute-start(bf16[32,3584]{1,0:T(8,128)(2,1)} %get-tuple-element.310), channel_id=1, source_target_pairs={{8,0},{16,8},{24,16},{32,24},{40,32},{48,40},{56,48},{64,56},{72,6... | collective-permute-start | bytes 688136 | tf_op jit(solution)/shard_map/while/body/eval_jaxpr/ppermute | solution.py:22
  474.9 9.1 %collective-permute-start = (bf16[32,3584]{1,0:T(8,128)(2,1)}, bf16[32,3584]{1,0:T(8,128)(2,1)S(1)}, u32[]{:S(2)}, u32[]{:S(2)}) collective-permute-start(bf16[32,3584]{1,0:T(8,128)(2,1)} %get-tuple-element.310), channel_id=1, source_target_pairs={{8,0},{16,8},{24,16},{32,24},{40,32},{48,40},{56,48},{64,56},{72,6... | collective-permute-start | bytes 688136 | tf_op jit(solution)/shard_map/while/body/eval_jaxpr/ppermute | solution.py:22
  488.5 9.1 %collective-permute-start = (bf16[32,3584]{1,0:T(8,128)(2,1)}, bf16[32,3584]{1,0:T(8,128)(2,1)S(1)}, u32[]{:S(2)}, u32[]{:S(2)}) collective-permute-start(bf16[32,3584]{1,0:T(8,128)(2,1)} %get-tuple-element.310), channel_id=1, source_target_pairs={{8,0},{16,8},{24,16},{32,24},{40,32},{48,40},{56,48},{64,56},{72,6... | collective-permute-start | bytes 688136 | tf_op jit(solution)/shard_map/while/body/eval_jaxpr/ppermute | solution.py:22
  502.1 9.1 %collective-permute-start = (bf16[32,3584]{1,0:T(8,128)(2,1)}, bf16[32,3584]{1,0:T(8,128)(2,1)S(1)}, u32[]{:S(2)}, u32[]{:S(2)}) collective-permute-start(bf16[32,3584]{1,0:T(8,128)(2,1)} %get-tuple-element.310), channel_id=1, source_target_pairs={{8,0},{16,8},{24,16},{32,24},{40,32},{48,40},{56,48},{64,56},{72,6... | collective-permute-start | bytes 688136 | tf_op jit(solution)/shard_map/while/body/eval_jaxpr/ppermute | solution.py:22
  515.7 9.1 %collective-permute-start = (bf16[32,3584]{1,0:T(8,128)(2,1)}, bf16[32,3584]{1,0:T(8,128)(2,1)S(1)}, u32[]{:S(2)}, u32[]{:S(2)}) collective-permute-start(bf16[32,3584]{1,0:T(8,128)(2,1)} %get-tuple-element.310), channel_id=1, source_target_pairs={{8,0},{16,8},{24,16},{32,24},{40,32},{48,40},{56,48},{64,56},{72,6... | collective-permute-start | bytes 688136 | tf_op jit(solution)/shard_map/while/body/eval_jaxpr/ppermute | solution.py:22
  529.3 9.1 %collective-permute-start = (bf16[32,3584]{1,0:T(8,128)(2,1)}, bf16[32,3584]{1,0:T(8,128)(2,1)S(1)}, u32[]{:S(2)}, u32[]{:S(2)}) collective-permute-start(bf16[32,3584]{1,0:T(8,128)(2,1)} %get-tuple-element.310), channel_id=1, source_target_pairs={{8,0},{16,8},{24,16},{32,24},{40,32},{48,40},{56,48},{64,56},{72,6... | collective-permute-start | bytes 688136 | tf_op jit(solution)/shard_map/while/body/eval_jaxpr/ppermute | solution.py:22
  542.9 9.1 %collective-permute-start = (bf16[32,3584]{1,0:T(8,128)(2,1)}, bf16[32,3584]{1,0:T(8,128)(2,1)S(1)}, u32[]{:S(2)}, u32[]{:S(2)}) collective-permute-start(bf16[32,3584]{1,0:T(8,128)(2,1)} %get-tuple-element.310), channel_id=1, source_target_pairs={{8,0},{16,8},{24,16},{32,24},{40,32},{48,40},{56,48},{64,56},{72,6... | collective-permute-start | bytes 688136 | tf_op jit(solution)/shard_map/while/body/eval_jaxpr/ppermute | solution.py:22
  556.5 9.1 %collective-permute-start = (bf16[32,3584]{1,0:T(8,128)(2,1)}, bf16[32,3584]{1,0:T(8,128)(2,1)S(1)}, u32[]{:S(2)}, u32[]{:S(2)}) collective-permute-start(bf16[32,3584]{1,0:T(8,128)(2,1)} %get-tuple-element.310), channel_id=1, source_target_pairs={{8,0},{16,8},{24,16},{32,24},{40,32},{48,40},{56,48},{64,56},{72,6... | collective-permute-start | bytes 688136 | tf_op jit(solution)/shard_map/while/body/eval_jaxpr/ppermute | solution.py:22
  570.1 10.2 %collective-permute-start = (bf16[32,3584]{1,0:T(8,128)(2,1)}, bf16[32,3584]{1,0:T(8,128)(2,1)S(1)}, u32[]{:S(2)}, u32[]{:S(2)}) collective-permute-start(bf16[32,3584]{1,0:T(8,128)(2,1)} %get-tuple-element.310), channel_id=1, source_target_pairs={{8,0},{16,8},{24,16},{32,24},{40,32},{48,40},{56,48},{64,56},{72,6... | collective-permute-start | bytes 688136 | tf_op jit(solution)/shard_map/while/body/eval_jaxpr/ppermute | solution.py:22
  581.0 77.1 %all-to-all-start = ((f32[8,1,448]{2,1,0:T(1,128)}), f32[8,1,448]{2,1,0:T(1,128)S(1)}, u32[]{:S(2)}, u32[]{:S(2)}) async-start(f32[8,1,448]{2,1,0:T(1,128)} %all_to_all.6), calls=%async_computation | async-start | bytes 32768 | tf_op jit(solution)/shard_map/all_to_all | solution.py:245
  630.2 4.0 copy-start.3
  634.2 4.5 copy-start.8
  638.7 6.1 copy-start.6
  644.8 2.7 copy-start
  647.5 2.2 copy-start.5
  649.7 2.1 copy-start.7

commit v9 on v6

--- a/solution.py
+++ b/solution.py
@@ -8,7 +8,7 @@
 from jax.experimental.pallas import tpu as pltpu
 from jax.sharding import PartitionSpec as P
 
-GROUPS = 8
+GROUPS = 16
 WINDOW = 32
 
 

time: 661 us -> 683 us (1.033)
  starting transfers between devices: 279 us -> 332 us
  waiting for transfers between devices: 141 us -> 103 us
  Pallas kernels: 175 us -> 182 us
    ppermute x39 -> x47, starting transfers between devices: 231 us -> 275 us  [passed_along(): lax.ppermute(value, axis, [(source, source + steps) for source in range(l...]
    ppermute x39 -> x47, waiting for transfers between devices: 141 us -> 103 us  [passed_along(): lax.ppermute(value, axis, [(source, source + steps) for source in range(l...]
    all_to_all x1, starting transfers between devices: 47.8 us -> 57.4 us  [on_device(): lax.all_to_all(gain_sum.reshape(group_count, feature_count // group_count...]
    pallas_call x39 -> x47, Pallas kernels: 175 us -> 182 us  [turn_call(): pl.pallas_call(kernel, grid_spec=grid_spec, out_shape=[jax.ShapeDtypeStru...]
  transfers between devices with their start and end apart: 40 -> 48, of which waited for: 39 -> 47; matrix products, arithmetic and copies ran while one was open for 3% -> 3% of each run, Pallas kernels for 0% -> 0%
where the time goes in v9:
time: 683 us; the launch traced here: 680 us
  starting transfers between devices  332 us (49%)
  Pallas kernels  182 us (27%)
  waiting for transfers between devices  103 us (15%)
  local copies, waits for them, and re-layouts  27.9 us (4%)
  matrix products  23 us (3%)
  other arithmetic  10.2 us (1%)
    ppermute x47, starting transfers between devices, passed_along(): lax.ppermute(value, axis, [(source, source + steps) for source in range(l...  275 us
    pallas_call x47, Pallas kernels, turn_call(): pl.pallas_call(kernel, grid_spec=grid_spec, out_shape=[jax.ShapeDtypeStru...  182 us
    ppermute x47, waiting for transfers between devices, passed_along(): lax.ppermute(value, axis, [(source, source + steps) for source in range(l...  103 us
    all_to_all x1, starting transfers between devices, on_device(): lax.all_to_all(gain_sum.reshape(group_count, feature_count // group_count...  57.4 us
    unnamed x22, local copies, waits for them, and re-layouts  15.9 us
  transfers between devices with their start and end apart: 48, of which 47 were waited for; matrix products, arithmetic and copies ran while one was open for 3% of the time, Pallas kernels for 0%

profile of v9, /device:TPU:15, one launch (start us, length us, event | category | flops | bytes accessed | tf_op | source)
XLA Modules:
  0.0 680.5 jit_solution(17565771621374369695)
XLA Ops:
  2.7 4.0 copy.30
  9.6 4.3 copy.28
  13.9 4.2 fusion.7
  28.9 561.1 %while.17 = (s32[]{:T(128)}, bf16[16,3584]{1,0:T(8,128)(2,1)S(1)}, bf16[272,3584]{1,0:T(8,128)(2,1)S(1)}, bf16[272,3584]{1,0:T(8,128)(2,1)}, s32[1]{0:T(128)}, /...) while((s32[]{:T(128)}, bf16[16,3584]{1,0:T(8,128)(2,1)S(1)}, ...), condition=%wide.region_4.5_spmd, body=%wide.region_3.4_spmd.sunk | while | flops 2 | bytes 458901 | solution.py:212
  28.9 3.9 eval_jaxpr.5
  32.8 7.7 %collective-permute-start = (bf16[16,3584]{1,0:T(8,128)(2,1)}, bf16[16,3584]{1,0:T(8,128)(2,1)S(1)}, u32[]{:S(2)}, u32[]{:S(2)}) collective-permute-start(bf16[16,3584]{1,0:T(8,128)(2,1)} %get-tuple-element.282), channel_id=1, source_target_pairs={{8,0},{16,8},{24,16},{32,24},{40,32},{48,40},{56,48},{64,56},{72,6... | collective-permute-start | bytes 344072 | tf_op jit(solution)/shard_map/while/body/eval_jaxpr/ppermute | solution.py:22
  46.6 6.1 collective-permute-start
  54.8 3.9 eval_jaxpr.5
  58.7 5.8 collective-permute-start
  70.4 5.8 collective-permute-start
  82.1 5.8 collective-permute-start
  90.0 3.9 eval_jaxpr.5
  93.9 5.8 collective-permute-start
  105.6 5.8 collective-permute-start
  113.5 3.9 eval_jaxpr.5
  117.4 5.8 collective-permute-start
  129.1 5.8 collective-permute-start
  140.9 5.8 collective-permute-start
  152.6 5.8 collective-permute-start
  165.0 5.8 collective-permute-start
  177.3 6.1 collective-permute-start
  189.4 5.7 collective-permute-start
  201.1 5.7 collective-permute-start
  212.8 5.8 collective-permute-start
  224.6 5.8 collective-permute-start
  236.3 5.8 collective-permute-start
  248.0 5.8 collective-permute-start
  259.8 5.8 collective-permute-start
  271.5 5.8 collective-permute-start
  283.3 5.8 collective-permute-start
  295.1 5.8 collective-permute-start
  308.0 6.1 collective-permute-start
  320.3 6.1 collective-permute-start
  328.5 3.9 eval_jaxpr.5
  332.4 5.8 collective-permute-start
  344.1 5.8 collective-permute-start
  355.8 5.8 collective-permute-start
  363.7 3.9 eval_jaxpr.5
  367.6 5.8 collective-permute-start
  379.3 5.8 collective-permute-start
  391.1 5.8 collective-permute-start
  398.9 3.9 eval_jaxpr.5
  402.8 5.8 collective-permute-start
  414.6 5.8 collective-permute-start
  426.3 5.8 collective-permute-start
  438.5 5.8 collective-permute-start
  451.1 6.1 collective-permute-start
  463.2 5.8 collective-permute-start
  474.9 5.8 collective-permute-start
  486.7 5.8 collective-permute-start
  498.4 5.8 collective-permute-start
  510.1 5.8 collective-permute-start
  518.0 3.9 eval_jaxpr.5
  521.9 5.8 collective-permute-start
  533.6 5.8 collective-permute-start
  545.4 5.8 collective-permute-start
  553.2 3.9 eval_jaxpr.5
  557.1 5.8 collective-permute-start
  568.9 5.8 collective-permute-start
  581.6 5.9 collective-permute-start
  594.2 4.9 fusion.1
  599.8 57.4 %all-to-all-start = ((f32[8,1,448]{2,1,0:T(1,128)}), f32[8,1,448]{2,1,0:T(1,128)S(1)}, u32[]{:S(2)}, u32[]{:S(2)}) async-start(f32[8,1,448]{2,1,0:T(1,128)} %all_to_all.6), calls=%async_computation | async-start | bytes 32768 | tf_op jit(solution)/shard_map/all_to_all | solution.py:241
  657.3 4.4 fusion.2
  661.7 6.1 multiply_convert_fusion
  (130 shorter events, 283.8 us)
Async XLA Ops:
  0.7 6.0 copy-start.8
  9.6 8.5 %copy-start.4 = (bf16[1,1,256,3584]{2,3,1,0:T(8,128)(2,1)}, bf16[1,1,256,3584]{2,3,1,0:T(8,128)(2,1)S(1)}, u32[]{:S(2)}) copy-start(bf16[1,1,256,3584]{2,3,1,0:T(8,128)(2,1)S(1)} %copy.27) | copy-start | bytes 5505028
  18.1 3.2 copy-start.1
  21.3 3.6 copy-start.3
  24.9 4.0 copy-start.7
  32.8 9.8 %collective-permute-start = (bf16[16,3584]{1,0:T(8,128)(2,1)}, bf16[16,3584]{1,0:T(8,128)(2,1)S(1)}, u32[]{:S(2)}, u32[]{:S(2)}) collective-permute-start(bf16[16,3584]{1,0:T(8,128)(2,1)} %get-tuple-element.282), channel_id=1, source_target_pairs={{8,0},{16,8},{24,16},{32,24},{40,32},{48,40},{56,48},{64,56},{72,6... | collective-permute-start | bytes 344072 | tf_op jit(solution)/shard_map/while/body/eval_jaxpr/ppermute | solution.py:22
  46.6 8.2 %collective-permute-start = (bf16[16,3584]{1,0:T(8,128)(2,1)}, bf16[16,3584]{1,0:T(8,128)(2,1)S(1)}, u32[]{:S(2)}, u32[]{:S(2)}) collective-permute-start(bf16[16,3584]{1,0:T(8,128)(2,1)} %get-tuple-element.282), channel_id=1, source_target_pairs={{8,0},{16,8},{24,16},{32,24},{40,32},{48,40},{56,48},{64,56},{72,6... | collective-permute-start | bytes 344072 | tf_op jit(solution)/shard_map/while/body/eval_jaxpr/ppermute | solution.py:22
  58.7 7.9 %collective-permute-start = (bf16[16,3584]{1,0:T(8,128)(2,1)}, bf16[16,3584]{1,0:T(8,128)(2,1)S(1)}, u32[]{:S(2)}, u32[]{:S(2)}) collective-permute-start(bf16[16,3584]{1,0:T(8,128)(2,1)} %get-tuple-element.282), channel_id=1, source_target_pairs={{8,0},{16,8},{24,16},{32,24},{40,32},{48,40},{56,48},{64,56},{72,6... | collective-permute-start | bytes 344072 | tf_op jit(solution)/shard_map/while/body/eval_jaxpr/ppermute | solution.py:22
  70.4 7.9 %collective-permute-start = (bf16[16,3584]{1,0:T(8,128)(2,1)}, bf16[16,3584]{1,0:T(8,128)(2,1)S(1)}, u32[]{:S(2)}, u32[]{:S(2)}) collective-permute-start(bf16[16,3584]{1,0:T(8,128)(2,1)} %get-tuple-element.282), channel_id=1, source_target_pairs={{8,0},{16,8},{24,16},{32,24},{40,32},{48,40},{56,48},{64,56},{72,6... | collective-permute-start | bytes 344072 | tf_op jit(solution)/shard_map/while/body/eval_jaxpr/ppermute | solution.py:22
  82.1 7.9 %collective-permute-start = (bf16[16,3584]{1,0:T(8,128)(2,1)}, bf16[16,3584]{1,0:T(8,128)(2,1)S(1)}, u32[]{:S(2)}, u32[]{:S(2)}) collective-permute-start(bf16[16,3584]{1,0:T(8,128)(2,1)} %get-tuple-element.282), channel_id=1, source_target_pairs={{8,0},{16,8},{24,16},{32,24},{40,32},{48,40},{56,48},{64,56},{72,6... | collective-permute-start | bytes 344072 | tf_op jit(solution)/shard_map/while/body/eval_jaxpr/ppermute | solution.py:22
  93.9 7.9 %collective-permute-start = (bf16[16,3584]{1,0:T(8,128)(2,1)}, bf16[16,3584]{1,0:T(8,128)(2,1)S(1)}, u32[]{:S(2)}, u32[]{:S(2)}) collective-permute-start(bf16[16,3584]{1,0:T(8,128)(2,1)} %get-tuple-element.282), channel_id=1, source_target_pairs={{8,0},{16,8},{24,16},{32,24},{40,32},{48,40},{56,48},{64,56},{72,6... | collective-permute-start | bytes 344072 | tf_op jit(solution)/shard_map/while/body/eval_jaxpr/ppermute | solution.py:22
  105.6 7.9 %collective-permute-start = (bf16[16,3584]{1,0:T(8,128)(2,1)}, bf16[16,3584]{1,0:T(8,128)(2,1)S(1)}, u32[]{:S(2)}, u32[]{:S(2)}) collective-permute-start(bf16[16,3584]{1,0:T(8,128)(2,1)} %get-tuple-element.282), channel_id=1, source_target_pairs={{8,0},{16,8},{24,16},{32,24},{40,32},{48,40},{56,48},{64,56},{72,6... | collective-permute-start | bytes 344072 | tf_op jit(solution)/shard_map/while/body/eval_jaxpr/ppermute | solution.py:22
  117.4 7.9 %collective-permute-start = (bf16[16,3584]{1,0:T(8,128)(2,1)}, bf16[16,3584]{1,0:T(8,128)(2,1)S(1)}, u32[]{:S(2)}, u32[]{:S(2)}) collective-permute-start(bf16[16,3584]{1,0:T(8,128)(2,1)} %get-tuple-element.282), channel_id=1, source_target_pairs={{8,0},{16,8},{24,16},{32,24},{40,32},{48,40},{56,48},{64,56},{72,6... | collective-permute-start | bytes 344072 | tf_op jit(solution)/shard_map/while/body/eval_jaxpr/ppermute | solution.py:22
  129.1 7.9 %collective-permute-start = (bf16[16,3584]{1,0:T(8,128)(2,1)}, bf16[16,3584]{1,0:T(8,128)(2,1)S(1)}, u32[]{:S(2)}, u32[]{:S(2)}) collective-permute-start(bf16[16,3584]{1,0:T(8,128)(2,1)} %get-tuple-element.282), channel_id=1, source_target_pairs={{8,0},{16,8},{24,16},{32,24},{40,32},{48,40},{56,48},{64,56},{72,6... | collective-permute-start | bytes 344072 | tf_op jit(solution)/shard_map/while/body/eval_jaxpr/ppermute | solution.py:22
  140.9 7.9 %collective-permute-start = (bf16[16,3584]{1,0:T(8,128)(2,1)}, bf16[16,3584]{1,0:T(8,128)(2,1)S(1)}, u32[]{:S(2)}, u32[]{:S(2)}) collective-permute-start(bf16[16,3584]{1,0:T(8,128)(2,1)} %get-tuple-element.282), channel_id=1, source_target_pairs={{8,0},{16,8},{24,16},{32,24},{40,32},{48,40},{56,48},{64,56},{72,6... | collective-permute-start | bytes 344072 | tf_op jit(solution)/shard_map/while/body/eval_jaxpr/ppermute | solution.py:22
  152.6 8.5 %collective-permute-start = (bf16[16,3584]{1,0:T(8,128)(2,1)}, bf16[16,3584]{1,0:T(8,128)(2,1)S(1)}, u32[]{:S(2)}, u32[]{:S(2)}) collective-permute-start(bf16[16,3584]{1,0:T(8,128)(2,1)} %get-tuple-element.282), channel_id=1, source_target_pairs={{8,0},{16,8},{24,16},{32,24},{40,32},{48,40},{56,48},{64,56},{72,6... | collective-permute-start | bytes 344072 | tf_op jit(solution)/shard_map/while/body/eval_jaxpr/ppermute | solution.py:22
  165.0 8.4 %collective-permute-start = (bf16[16,3584]{1,0:T(8,128)(2,1)}, bf16[16,3584]{1,0:T(8,128)(2,1)S(1)}, u32[]{:S(2)}, u32[]{:S(2)}) collective-permute-start(bf16[16,3584]{1,0:T(8,128)(2,1)} %get-tuple-element.282), channel_id=1, source_target_pairs={{8,0},{16,8},{24,16},{32,24},{40,32},{48,40},{56,48},{64,56},{72,6... | collective-permute-start | bytes 344072 | tf_op jit(solution)/shard_map/while/body/eval_jaxpr/ppermute | solution.py:22
  177.3 8.2 %collective-permute-start = (bf16[16,3584]{1,0:T(8,128)(2,1)}, bf16[16,3584]{1,0:T(8,128)(2,1)S(1)}, u32[]{:S(2)}, u32[]{:S(2)}) collective-permute-start(bf16[16,3584]{1,0:T(8,128)(2,1)} %get-tuple-element.282), channel_id=1, source_target_pairs={{8,0},{16,8},{24,16},{32,24},{40,32},{48,40},{56,48},{64,56},{72,6... | collective-permute-start | bytes 344072 | tf_op jit(solution)/shard_map/while/body/eval_jaxpr/ppermute | solution.py:22
  189.4 7.8 %collective-permute-start = (bf16[16,3584]{1,0:T(8,128)(2,1)}, bf16[16,3584]{1,0:T(8,128)(2,1)S(1)}, u32[]{:S(2)}, u32[]{:S(2)}) collective-permute-start(bf16[16,3584]{1,0:T(8,128)(2,1)} %get-tuple-element.282), channel_id=1, source_target_pairs={{8,0},{16,8},{24,16},{32,24},{40,32},{48,40},{56,48},{64,56},{72,6... | collective-permute-start | bytes 344072 | tf_op jit(solution)/shard_map/while/body/eval_jaxpr/ppermute | solution.py:22
  201.1 7.8 %collective-permute-start = (bf16[16,3584]{1,0:T(8,128)(2,1)}, bf16[16,3584]{1,0:T(8,128)(2,1)S(1)}, u32[]{:S(2)}, u32[]{:S(2)}) collective-permute-start(bf16[16,3584]{1,0:T(8,128)(2,1)} %get-tuple-element.282), channel_id=1, source_target_pairs={{8,0},{16,8},{24,16},{32,24},{40,32},{48,40},{56,48},{64,56},{72,6... | collective-permute-start | bytes 344072 | tf_op jit(solution)/shard_map/while/body/eval_jaxpr/ppermute | solution.py:22
  212.8 7.9 %collective-permute-start = (bf16[16,3584]{1,0:T(8,128)(2,1)}, bf16[16,3584]{1,0:T(8,128)(2,1)S(1)}, u32[]{:S(2)}, u32[]{:S(2)}) collective-permute-start(bf16[16,3584]{1,0:T(8,128)(2,1)} %get-tuple-element.282), channel_id=1, source_target_pairs={{8,0},{16,8},{24,16},{32,24},{40,32},{48,40},{56,48},{64,56},{72,6... | collective-permute-start | bytes 344072 | tf_op jit(solution)/shard_map/while/body/eval_jaxpr/ppermute | solution.py:22
  224.6 7.9 %collective-permute-start = (bf16[16,3584]{1,0:T(8,128)(2,1)}, bf16[16,3584]{1,0:T(8,128)(2,1)S(1)}, u32[]{:S(2)}, u32[]{:S(2)}) collective-permute-start(bf16[16,3584]{1,0:T(8,128)(2,1)} %get-tuple-element.282), channel_id=1, source_target_pairs={{8,0},{16,8},{24,16},{32,24},{40,32},{48,40},{56,48},{64,56},{72,6... | collective-permute-start | bytes 344072 | tf_op jit(solution)/shard_map/while/body/eval_jaxpr/ppermute | solution.py:22
  236.3 7.9 %collective-permute-start = (bf16[16,3584]{1,0:T(8,128)(2,1)}, bf16[16,3584]{1,0:T(8,128)(2,1)S(1)}, u32[]{:S(2)}, u32[]{:S(2)}) collective-permute-start(bf16[16,3584]{1,0:T(8,128)(2,1)} %get-tuple-element.282), channel_id=1, source_target_pairs={{8,0},{16,8},{24,16},{32,24},{40,32},{48,40},{56,48},{64,56},{72,6... | collective-permute-start | bytes 344072 | tf_op jit(solution)/shard_map/while/body/eval_jaxpr/ppermute | solution.py:22
  248.0 7.9 %collective-permute-start = (bf16[16,3584]{1,0:T(8,128)(2,1)}, bf16[16,3584]{1,0:T(8,128)(2,1)S(1)}, u32[]{:S(2)}, u32[]{:S(2)}) collective-permute-start(bf16[16,3584]{1,0:T(8,128)(2,1)} %get-tuple-element.282), channel_id=1, source_target_pairs={{8,0},{16,8},{24,16},{32,24},{40,32},{48,40},{56,48},{64,56},{72,6... | collective-permute-start | bytes 344072 | tf_op jit(solution)/shard_map/while/body/eval_jaxpr/ppermute | solution.py:22
  259.8 7.9 %collective-permute-start = (bf16[16,3584]{1,0:T(8,128)(2,1)}, bf16[16,3584]{1,0:T(8,128)(2,1)S(1)}, u32[]{:S(2)}, u32[]{:S(2)}) collective-permute-start(bf16[16,3584]{1,0:T(8,128)(2,1)} %get-tuple-element.282), channel_id=1, source_target_pairs={{8,0},{16,8},{24,16},{32,24},{40,32},{48,40},{56,48},{64,56},{72,6... | collective-permute-start | bytes 344072 | tf_op jit(solution)/shard_map/while/body/eval_jaxpr/ppermute | solution.py:22
  271.5 7.9 %collective-permute-start = (bf16[16,3584]{1,0:T(8,128)(2,1)}, bf16[16,3584]{1,0:T(8,128)(2,1)S(1)}, u32[]{:S(2)}, u32[]{:S(2)}) collective-permute-start(bf16[16,3584]{1,0:T(8,128)(2,1)} %get-tuple-element.282), channel_id=1, source_target_pairs={{8,0},{16,8},{24,16},{32,24},{40,32},{48,40},{56,48},{64,56},{72,6... | collective-permute-start | bytes 344072 | tf_op jit(solution)/shard_map/while/body/eval_jaxpr/ppermute | solution.py:22
  283.3 8.0 %collective-permute-start = (bf16[16,3584]{1,0:T(8,128)(2,1)}, bf16[16,3584]{1,0:T(8,128)(2,1)S(1)}, u32[]{:S(2)}, u32[]{:S(2)}) collective-permute-start(bf16[16,3584]{1,0:T(8,128)(2,1)} %get-tuple-element.282), channel_id=1, source_target_pairs={{8,0},{16,8},{24,16},{32,24},{40,32},{48,40},{56,48},{64,56},{72,6... | collective-permute-start | bytes 344072 | tf_op jit(solution)/shard_map/while/body/eval_jaxpr/ppermute | solution.py:22
  295.1 9.0 %collective-permute-start = (bf16[16,3584]{1,0:T(8,128)(2,1)}, bf16[16,3584]{1,0:T(8,128)(2,1)S(1)}, u32[]{:S(2)}, u32[]{:S(2)}) collective-permute-start(bf16[16,3584]{1,0:T(8,128)(2,1)} %get-tuple-element.282), channel_id=1, source_target_pairs={{8,0},{16,8},{24,16},{32,24},{40,32},{48,40},{56,48},{64,56},{72,6... | collective-permute-start | bytes 344072 | tf_op jit(solution)/shard_map/while/body/eval_jaxpr/ppermute | solution.py:22
  308.0 8.4 %collective-permute-start = (bf16[16,3584]{1,0:T(8,128)(2,1)}, bf16[16,3584]{1,0:T(8,128)(2,1)S(1)}, u32[]{:S(2)}, u32[]{:S(2)}) collective-permute-start(bf16[16,3584]{1,0:T(8,128)(2,1)} %get-tuple-element.282), channel_id=1, source_target_pairs={{8,0},{16,8},{24,16},{32,24},{40,32},{48,40},{56,48},{64,56},{72,6... | collective-permute-start | bytes 344072 | tf_op jit(solution)/shard_map/while/body/eval_jaxpr/ppermute | solution.py:22
  320.3 8.2 %collective-permute-start = (bf16[16,3584]{1,0:T(8,128)(2,1)}, bf16[16,3584]{1,0:T(8,128)(2,1)S(1)}, u32[]{:S(2)}, u32[]{:S(2)}) collective-permute-start(bf16[16,3584]{1,0:T(8,128)(2,1)} %get-tuple-element.282), channel_id=1, source_target_pairs={{8,0},{16,8},{24,16},{32,24},{40,32},{48,40},{56,48},{64,56},{72,6... | collective-permute-start | bytes 344072 | tf_op jit(solution)/shard_map/while/body/eval_jaxpr/ppermute | solution.py:22
  332.4 7.9 %collective-permute-start = (bf16[16,3584]{1,0:T(8,128)(2,1)}, bf16[16,3584]{1,0:T(8,128)(2,1)S(1)}, u32[]{:S(2)}, u32[]{:S(2)}) collective-permute-start(bf16[16,3584]{1,0:T(8,128)(2,1)} %get-tuple-element.282), channel_id=1, source_target_pairs={{8,0},{16,8},{24,16},{32,24},{40,32},{48,40},{56,48},{64,56},{72,6... | collective-permute-start | bytes 344072 | tf_op jit(solution)/shard_map/while/body/eval_jaxpr/ppermute | solution.py:22
  344.1 7.9 %collective-permute-start = (bf16[16,3584]{1,0:T(8,128)(2,1)}, bf16[16,3584]{1,0:T(8,128)(2,1)S(1)}, u32[]{:S(2)}, u32[]{:S(2)}) collective-permute-start(bf16[16,3584]{1,0:T(8,128)(2,1)} %get-tuple-element.282), channel_id=1, source_target_pairs={{8,0},{16,8},{24,16},{32,24},{40,32},{48,40},{56,48},{64,56},{72,6... | collective-permute-start | bytes 344072 | tf_op jit(solution)/shard_map/while/body/eval_jaxpr/ppermute | solution.py:22
  355.8 7.9 %collective-permute-start = (bf16[16,3584]{1,0:T(8,128)(2,1)}, bf16[16,3584]{1,0:T(8,128)(2,1)S(1)}, u32[]{:S(2)}, u32[]{:S(2)}) collective-permute-start(bf16[16,3584]{1,0:T(8,128)(2,1)} %get-tuple-element.282), channel_id=1, source_target_pairs={{8,0},{16,8},{24,16},{32,24},{40,32},{48,40},{56,48},{64,56},{72,6... | collective-permute-start | bytes 344072 | tf_op jit(solution)/shard_map/while/body/eval_jaxpr/ppermute | solution.py:22
  367.6 7.9 %collective-permute-start = (bf16[16,3584]{1,0:T(8,128)(2,1)}, bf16[16,3584]{1,0:T(8,128)(2,1)S(1)}, u32[]{:S(2)}, u32[]{:S(2)}) collective-permute-start(bf16[16,3584]{1,0:T(8,128)(2,1)} %get-tuple-element.282), channel_id=1, source_target_pairs={{8,0},{16,8},{24,16},{32,24},{40,32},{48,40},{56,48},{64,56},{72,6... | collective-permute-start | bytes 344072 | tf_op jit(solution)/shard_map/while/body/eval_jaxpr/ppermute | solution.py:22
  379.3 7.9 %collective-permute-start = (bf16[16,3584]{1,0:T(8,128)(2,1)}, bf16[16,3584]{1,0:T(8,128)(2,1)S(1)}, u32[]{:S(2)}, u32[]{:S(2)}) collective-permute-start(bf16[16,3584]{1,0:T(8,128)(2,1)} %get-tuple-element.282), channel_id=1, source_target_pairs={{8,0},{16,8},{24,16},{32,24},{40,32},{48,40},{56,48},{64,56},{72,6... | collective-permute-start | bytes 344072 | tf_op jit(solution)/shard_map/while/body/eval_jaxpr/ppermute | solution.py:22
  391.1 7.9 %collective-permute-start = (bf16[16,3584]{1,0:T(8,128)(2,1)}, bf16[16,3584]{1,0:T(8,128)(2,1)S(1)}, u32[]{:S(2)}, u32[]{:S(2)}) collective-permute-start(bf16[16,3584]{1,0:T(8,128)(2,1)} %get-tuple-element.282), channel_id=1, source_target_pairs={{8,0},{16,8},{24,16},{32,24},{40,32},{48,40},{56,48},{64,56},{72,6... | collective-permute-start | bytes 344072 | tf_op jit(solution)/shard_map/while/body/eval_jaxpr/ppermute | solution.py:22
  402.8 7.9 %collective-permute-start = (bf16[16,3584]{1,0:T(8,128)(2,1)}, bf16[16,3584]{1,0:T(8,128)(2,1)S(1)}, u32[]{:S(2)}, u32[]{:S(2)}) collective-permute-start(bf16[16,3584]{1,0:T(8,128)(2,1)} %get-tuple-element.282), channel_id=1, source_target_pairs={{8,0},{16,8},{24,16},{32,24},{40,32},{48,40},{56,48},{64,56},{72,6... | collective-permute-start | bytes 344072 | tf_op jit(solution)/shard_map/while/body/eval_jaxpr/ppermute | solution.py:22
  414.6 7.9 %collective-permute-start = (bf16[16,3584]{1,0:T(8,128)(2,1)}, bf16[16,3584]{1,0:T(8,128)(2,1)S(1)}, u32[]{:S(2)}, u32[]{:S(2)}) collective-permute-start(bf16[16,3584]{1,0:T(8,128)(2,1)} %get-tuple-element.282), channel_id=1, source_target_pairs={{8,0},{16,8},{24,16},{32,24},{40,32},{48,40},{56,48},{64,56},{72,6... | collective-permute-start | bytes 344072 | tf_op jit(solution)/shard_map/while/body/eval_jaxpr/ppermute | solution.py:22
  426.3 8.3 %collective-permute-start = (bf16[16,3584]{1,0:T(8,128)(2,1)}, bf16[16,3584]{1,0:T(8,128)(2,1)S(1)}, u32[]{:S(2)}, u32[]{:S(2)}) collective-permute-start(bf16[16,3584]{1,0:T(8,128)(2,1)} %get-tuple-element.282), channel_id=1, source_target_pairs={{8,0},{16,8},{24,16},{32,24},{40,32},{48,40},{56,48},{64,56},{72,6... | collective-permute-start | bytes 344072 | tf_op jit(solution)/shard_map/while/body/eval_jaxpr/ppermute | solution.py:22
  438.5 8.7 %collective-permute-start = (bf16[16,3584]{1,0:T(8,128)(2,1)}, bf16[16,3584]{1,0:T(8,128)(2,1)S(1)}, u32[]{:S(2)}, u32[]{:S(2)}) collective-permute-start(bf16[16,3584]{1,0:T(8,128)(2,1)} %get-tuple-element.282), channel_id=1, source_target_pairs={{8,0},{16,8},{24,16},{32,24},{40,32},{48,40},{56,48},{64,56},{72,6... | collective-permute-start | bytes 344072 | tf_op jit(solution)/shard_map/while/body/eval_jaxpr/ppermute | solution.py:22
  451.1 8.2 %collective-permute-start = (bf16[16,3584]{1,0:T(8,128)(2,1)}, bf16[16,3584]{1,0:T(8,128)(2,1)S(1)}, u32[]{:S(2)}, u32[]{:S(2)}) collective-permute-start(bf16[16,3584]{1,0:T(8,128)(2,1)} %get-tuple-element.282), channel_id=1, source_target_pairs={{8,0},{16,8},{24,16},{32,24},{40,32},{48,40},{56,48},{64,56},{72,6... | collective-permute-start | bytes 344072 | tf_op jit(solution)/shard_map/while/body/eval_jaxpr/ppermute | solution.py:22
  463.2 7.9 %collective-permute-start = (bf16[16,3584]{1,0:T(8,128)(2,1)}, bf16[16,3584]{1,0:T(8,128)(2,1)S(1)}, u32[]{:S(2)}, u32[]{:S(2)}) collective-permute-start(bf16[16,3584]{1,0:T(8,128)(2,1)} %get-tuple-element.282), channel_id=1, source_target_pairs={{8,0},{16,8},{24,16},{32,24},{40,32},{48,40},{56,48},{64,56},{72,6... | collective-permute-start | bytes 344072 | tf_op jit(solution)/shard_map/while/body/eval_jaxpr/ppermute | solution.py:22
  474.9 7.9 %collective-permute-start = (bf16[16,3584]{1,0:T(8,128)(2,1)}, bf16[16,3584]{1,0:T(8,128)(2,1)S(1)}, u32[]{:S(2)}, u32[]{:S(2)}) collective-permute-start(bf16[16,3584]{1,0:T(8,128)(2,1)} %get-tuple-element.282), channel_id=1, source_target_pairs={{8,0},{16,8},{24,16},{32,24},{40,32},{48,40},{56,48},{64,56},{72,6... | collective-permute-start | bytes 344072 | tf_op jit(solution)/shard_map/while/body/eval_jaxpr/ppermute | solution.py:22
  486.7 7.9 %collective-permute-start = (bf16[16,3584]{1,0:T(8,128)(2,1)}, bf16[16,3584]{1,0:T(8,128)(2,1)S(1)}, u32[]{:S(2)}, u32[]{:S(2)}) collective-permute-start(bf16[16,3584]{1,0:T(8,128)(2,1)} %get-tuple-element.282), channel_id=1, source_target_pairs={{8,0},{16,8},{24,16},{32,24},{40,32},{48,40},{56,48},{64,56},{72,6... | collective-permute-start | bytes 344072 | tf_op jit(solution)/shard_map/while/body/eval_jaxpr/ppermute | solution.py:22
  498.4 7.9 %collective-permute-start = (bf16[16,3584]{1,0:T(8,128)(2,1)}, bf16[16,3584]{1,0:T(8,128)(2,1)S(1)}, u32[]{:S(2)}, u32[]{:S(2)}) collective-permute-start(bf16[16,3584]{1,0:T(8,128)(2,1)} %get-tuple-element.282), channel_id=1, source_target_pairs={{8,0},{16,8},{24,16},{32,24},{40,32},{48,40},{56,48},{64,56},{72,6... | collective-permute-start | bytes 344072 | tf_op jit(solution)/shard_map/while/body/eval_jaxpr/ppermute | solution.py:22
  510.1 7.9 %collective-permute-start = (bf16[16,3584]{1,0:T(8,128)(2,1)}, bf16[16,3584]{1,0:T(8,128)(2,1)S(1)}, u32[]{:S(2)}, u32[]{:S(2)}) collective-permute-start(bf16[16,3584]{1,0:T(8,128)(2,1)} %get-tuple-element.282), channel_id=1, source_target_pairs={{8,0},{16,8},{24,16},{32,24},{40,32},{48,40},{56,48},{64,56},{72,6... | collective-permute-start | bytes 344072 | tf_op jit(solution)/shard_map/while/body/eval_jaxpr/ppermute | solution.py:22
  521.9 7.9 %collective-permute-start = (bf16[16,3584]{1,0:T(8,128)(2,1)}, bf16[16,3584]{1,0:T(8,128)(2,1)S(1)}, u32[]{:S(2)}, u32[]{:S(2)}) collective-permute-start(bf16[16,3584]{1,0:T(8,128)(2,1)} %get-tuple-element.282), channel_id=1, source_target_pairs={{8,0},{16,8},{24,16},{32,24},{40,32},{48,40},{56,48},{64,56},{72,6... | collective-permute-start | bytes 344072 | tf_op jit(solution)/shard_map/while/body/eval_jaxpr/ppermute | solution.py:22
  533.6 7.9 %collective-permute-start = (bf16[16,3584]{1,0:T(8,128)(2,1)}, bf16[16,3584]{1,0:T(8,128)(2,1)S(1)}, u32[]{:S(2)}, u32[]{:S(2)}) collective-permute-start(bf16[16,3584]{1,0:T(8,128)(2,1)} %get-tuple-element.282), channel_id=1, source_target_pairs={{8,0},{16,8},{24,16},{32,24},{40,32},{48,40},{56,48},{64,56},{72,6... | collective-permute-start | bytes 344072 | tf_op jit(solution)/shard_map/while/body/eval_jaxpr/ppermute | solution.py:22
  545.4 7.9 %collective-permute-start = (bf16[16,3584]{1,0:T(8,128)(2,1)}, bf16[16,3584]{1,0:T(8,128)(2,1)S(1)}, u32[]{:S(2)}, u32[]{:S(2)}) collective-permute-start(bf16[16,3584]{1,0:T(8,128)(2,1)} %get-tuple-element.282), channel_id=1, source_target_pairs={{8,0},{16,8},{24,16},{32,24},{40,32},{48,40},{56,48},{64,56},{72,6... | collective-permute-start | bytes 344072 | tf_op jit(solution)/shard_map/while/body/eval_jaxpr/ppermute | solution.py:22
  557.1 7.9 %collective-permute-start = (bf16[16,3584]{1,0:T(8,128)(2,1)}, bf16[16,3584]{1,0:T(8,128)(2,1)S(1)}, u32[]{:S(2)}, u32[]{:S(2)}) collective-permute-start(bf16[16,3584]{1,0:T(8,128)(2,1)} %get-tuple-element.282), channel_id=1, source_target_pairs={{8,0},{16,8},{24,16},{32,24},{40,32},{48,40},{56,48},{64,56},{72,6... | collective-permute-start | bytes 344072 | tf_op jit(solution)/shard_map/while/body/eval_jaxpr/ppermute | solution.py:22
  568.9 8.9 %collective-permute-start = (bf16[16,3584]{1,0:T(8,128)(2,1)}, bf16[16,3584]{1,0:T(8,128)(2,1)S(1)}, u32[]{:S(2)}, u32[]{:S(2)}) collective-permute-start(bf16[16,3584]{1,0:T(8,128)(2,1)} %get-tuple-element.282), channel_id=1, source_target_pairs={{8,0},{16,8},{24,16},{32,24},{40,32},{48,40},{56,48},{64,56},{72,6... | collective-permute-start | bytes 344072 | tf_op jit(solution)/shard_map/while/body/eval_jaxpr/ppermute | solution.py:22
  581.6 8.4 %collective-permute-start = (bf16[16,3584]{1,0:T(8,128)(2,1)}, bf16[16,3584]{1,0:T(8,128)(2,1)S(1)}, u32[]{:S(2)}, u32[]{:S(2)}) collective-permute-start(bf16[16,3584]{1,0:T(8,128)(2,1)} %get-tuple-element.282), channel_id=1, source_target_pairs={{8,0},{16,8},{24,16},{32,24},{40,32},{48,40},{56,48},{64,56},{72,6... | collective-permute-start | bytes 344072 | tf_op jit(solution)/shard_map/while/body/eval_jaxpr/ppermute | solution.py:22
  599.8 80.1 %all-to-all-start = ((f32[8,1,448]{2,1,0:T(1,128)}), f32[8,1,448]{2,1,0:T(1,128)S(1)}, u32[]{:S(2)}, u32[]{:S(2)}) async-start(f32[8,1,448]{2,1,0:T(1,128)} %all_to_all.6), calls=%async_computation | async-start | bytes 32768 | tf_op jit(solution)/shard_map/all_to_all | solution.py:241
  657.3 4.4 copy-start.2
  661.7 6.1 copy-start.6
  667.8 1.5 copy-start
  669.3 2.2 copy-start.5

commit v10 on v6

--- a/solution.py
+++ b/solution.py
@@ -67,16 +67,11 @@
     for g in range(groups):
         cols = slice(g * group_lanes, (g + 1) * group_lanes)
         w_copies[g].wait()
-        stacked = jnp.dot(
-            w_v[g].reshape(group_heads * rows_here, seq_rows),
-            g_out[pl.ds(0, seq_rows), cols],
-            preferred_element_type=jnp.float32,
-        )
+        group_rows = g_out[pl.ds(0, seq_rows), cols]
         value = jnp.zeros((rows_here, group_lanes), jnp.float32)
         for k in range(group_heads):
-            value = value + jnp.where(
-                lane_head == k, stacked[k * rows_here:(k + 1) * rows_here, :], 0.0
-            )
+            head_part = jnp.dot(w_v[g, k], group_rows, preferred_element_type=jnp.float32)
+            value = value + jnp.where(lane_head == k, head_part, 0.0)
         grad_normed = value * gain_ref[:, cols]
         gn_v[g] = grad_normed
         total = total + jnp.sum(grad_normed * normed_v[:, cols], axis=1, keepdims=True)

time: 661 us -> 713 us (1.079)
  Pallas kernels: 175 us -> 228 us
    pallas_call x39, Pallas kernels: 175 us -> 228 us  [turn_call(): pl.pallas_call(kernel, grid_spec=grid_spec, out_shape=[jax.ShapeDtypeStru...]
where the time goes in v10:
time: 713 us; the launch traced here: 710 us
  starting transfers between devices  279 us (39%)
  Pallas kernels  228 us (32%)
  waiting for transfers between devices  140 us (20%)
  local copies, waits for them, and re-layouts  28 us (4%)
  matrix products  23 us (3%)
  other arithmetic  10.2 us (1%)
    ppermute x39, starting transfers between devices, passed_along(): lax.ppermute(value, axis, [(source, source + steps) for source in range(l...  231 us
    pallas_call x39, Pallas kernels, turn_call(): pl.pallas_call(kernel, grid_spec=grid_spec, out_shape=[jax.ShapeDtypeStru...  228 us
    ppermute x39, waiting for transfers between devices, passed_along(): lax.ppermute(value, axis, [(source, source + steps) for source in range(l...  140 us
    all_to_all x1, starting transfers between devices, on_device(): lax.all_to_all(gain_sum.reshape(group_count, feature_count // group_count...  47.8 us
    unnamed x22, local copies, waits for them, and re-layouts  15.9 us
  transfers between devices with their start and end apart: 40, of which 39 were waited for; matrix products, arithmetic and copies ran while one was open for 3% of the time, Pallas kernels for 0%

profile of v10, /device:TPU:15, one launch (start us, length us, event | category | flops | bytes accessed | tf_op | source)
XLA Modules:
  0.0 709.9 jit_solution(15579210428898567867)
XLA Ops:
  29.0 600.0 %while.17 = (s32[]{:T(128)}, bf16[32,3584]{1,0:T(8,128)(2,1)S(1)}, bf16[288,3584]{1,0:T(8,128)(2,1)S(1)}, bf16[288,3584]{1,0:T(8,128)(2,1)}, s32[1]{0:T(128)}, /...) while((s32[]{:T(128)}, bf16[32,3584]{1,0:T(8,128)(2,1)S(1)}, ...), condition=%wide.region_4.5_spmd, body=%wide.region_3.4_spmd.sunk | while | flops 2 | bytes 917653 | solution.py:207
  29.0 5.9 eval_jaxpr.5
  34.9 7.7 %collective-permute-start = (bf16[32,3584]{1,0:T(8,128)(2,1)}, bf16[32,3584]{1,0:T(8,128)(2,1)S(1)}, u32[]{:S(2)}, u32[]{:S(2)}) collective-permute-start(bf16[32,3584]{1,0:T(8,128)(2,1)} %get-tuple-element.282), channel_id=1, source_target_pairs={{8,0},{16,8},{24,16},{32,24},{40,32},{48,40},{56,48},{64,56},{72,6... | collective-permute-start | bytes 688136 | tf_op jit(solution)/shard_map/while/body/eval_jaxpr/ppermute | solution.py:22
  47.2 5.9 eval_jaxpr.5
  53.1 6.1 collective-permute-start
  62.8 5.9 eval_jaxpr.5
  68.7 6.1 collective-permute-start
  78.1 5.9 eval_jaxpr.5
  93.0 5.9 eval_jaxpr.5
  98.9 5.8 collective-permute-start
  108.0 5.9 eval_jaxpr.5
  113.9 5.8 collective-permute-start
  122.9 5.9 eval_jaxpr.5
  137.9 5.8 eval_jaxpr.5
  143.7 5.8 collective-permute-start
  152.8 5.8 eval_jaxpr.5
  158.7 5.8 collective-permute-start
  167.8 5.8 eval_jaxpr.5
  173.6 5.8 collective-permute-start
  182.7 5.8 eval_jaxpr.5
  188.6 5.8 collective-permute-start
  197.7 5.8 eval_jaxpr.5
  212.6 5.8 eval_jaxpr.5
  228.3 5.8 eval_jaxpr.5
  245.1 5.9 eval_jaxpr.5
  262.0 5.9 eval_jaxpr.5
  267.8 6.1 collective-permute-start
  278.2 5.9 eval_jaxpr.5
  284.1 6.1 collective-permute-start
  293.4 5.9 eval_jaxpr.5
  299.3 6.2 collective-permute-start
  308.7 5.9 eval_jaxpr.5
  323.7 5.9 eval_jaxpr.5
  329.6 5.8 collective-permute-start
  338.7 5.9 eval_jaxpr.5
  353.6 5.9 eval_jaxpr.5
  368.6 5.9 eval_jaxpr.5
  374.4 5.8 collective-permute-start
  383.5 5.9 eval_jaxpr.5
  398.5 5.9 eval_jaxpr.5
  404.3 5.8 collective-permute-start
  413.4 5.9 eval_jaxpr.5
  428.4 5.9 eval_jaxpr.5
  443.3 5.9 eval_jaxpr.5
  449.2 5.8 collective-permute-start
  459.4 5.9 eval_jaxpr.5
  476.5 5.9 eval_jaxpr.5
  482.4 5.8 collective-permute-start
  493.1 5.9 eval_jaxpr.5
  499.0 6.1 collective-permute-start
  509.1 5.9 eval_jaxpr.5
  514.9 6.1 collective-permute-start
  524.3 5.9 eval_jaxpr.5
  539.3 5.9 eval_jaxpr.5
  545.1 5.8 collective-permute-start
  554.2 5.9 eval_jaxpr.5
  569.2 5.9 eval_jaxpr.5
  575.0 5.8 collective-permute-start
  584.1 5.9 eval_jaxpr.5
  599.1 5.9 eval_jaxpr.5
  614.0 5.9 eval_jaxpr.5
  619.9 5.8 collective-permute-start
  638.8 47.8 %all-to-all-start = ((f32[8,1,448]{2,1,0:T(1,128)}), f32[8,1,448]{2,1,0:T(1,128)S(1)}, u32[]{:S(2)}, u32[]{:S(2)}) async-start(f32[8,1,448]{2,1,0:T(1,128)} %all_to_all.6), calls=%async_computation | async-start | bytes 32768 | tf_op jit(solution)/shard_map/all_to_all | solution.py:236
  691.1 6.1 multiply_convert_fusion
  (106 shorter events, 293.9 us)
Async XLA Ops:
  0.7 6.0 copy-start.8
  9.6 8.5 %copy-start.4 = (bf16[1,1,256,3584]{2,3,1,0:T(8,128)(2,1)}, bf16[1,1,256,3584]{2,3,1,0:T(8,128)(2,1)S(1)}, u32[]{:S(2)}) copy-start(bf16[1,1,256,3584]{2,3,1,0:T(8,128)(2,1)S(1)} %copy.27) | copy-start | bytes 5505028
  18.1 3.2 copy-start.1
  21.3 3.6 copy-start.3
  24.9 4.1 copy-start.7
  34.9 12.3 %collective-permute-start = (bf16[32,3584]{1,0:T(8,128)(2,1)}, bf16[32,3584]{1,0:T(8,128)(2,1)S(1)}, u32[]{:S(2)}, u32[]{:S(2)}) collective-permute-start(bf16[32,3584]{1,0:T(8,128)(2,1)} %get-tuple-element.282), channel_id=1, source_target_pairs={{8,0},{16,8},{24,16},{32,24},{40,32},{48,40},{56,48},{64,56},{72,6... | collective-permute-start | bytes 688136 | tf_op jit(solution)/shard_map/while/body/eval_jaxpr/ppermute | solution.py:22
  53.1 9.8 %collective-permute-start = (bf16[32,3584]{1,0:T(8,128)(2,1)}, bf16[32,3584]{1,0:T(8,128)(2,1)S(1)}, u32[]{:S(2)}, u32[]{:S(2)}) collective-permute-start(bf16[32,3584]{1,0:T(8,128)(2,1)} %get-tuple-element.282), channel_id=1, source_target_pairs={{8,0},{16,8},{24,16},{32,24},{40,32},{48,40},{56,48},{64,56},{72,6... | collective-permute-start | bytes 688136 | tf_op jit(solution)/shard_map/while/body/eval_jaxpr/ppermute | solution.py:22
  68.7 9.4 %collective-permute-start = (bf16[32,3584]{1,0:T(8,128)(2,1)}, bf16[32,3584]{1,0:T(8,128)(2,1)S(1)}, u32[]{:S(2)}, u32[]{:S(2)}) collective-permute-start(bf16[32,3584]{1,0:T(8,128)(2,1)} %get-tuple-element.282), channel_id=1, source_target_pairs={{8,0},{16,8},{24,16},{32,24},{40,32},{48,40},{56,48},{64,56},{72,6... | collective-permute-start | bytes 688136 | tf_op jit(solution)/shard_map/while/body/eval_jaxpr/ppermute | solution.py:22
  84.0 9.1 %collective-permute-start = (bf16[32,3584]{1,0:T(8,128)(2,1)}, bf16[32,3584]{1,0:T(8,128)(2,1)S(1)}, u32[]{:S(2)}, u32[]{:S(2)}) collective-permute-start(bf16[32,3584]{1,0:T(8,128)(2,1)} %get-tuple-element.282), channel_id=1, source_target_pairs={{8,0},{16,8},{24,16},{32,24},{40,32},{48,40},{56,48},{64,56},{72,6... | collective-permute-start | bytes 688136 | tf_op jit(solution)/shard_map/while/body/eval_jaxpr/ppermute | solution.py:22
  98.9 9.1 %collective-permute-start = (bf16[32,3584]{1,0:T(8,128)(2,1)}, bf16[32,3584]{1,0:T(8,128)(2,1)S(1)}, u32[]{:S(2)}, u32[]{:S(2)}) collective-permute-start(bf16[32,3584]{1,0:T(8,128)(2,1)} %get-tuple-element.282), channel_id=1, source_target_pairs={{8,0},{16,8},{24,16},{32,24},{40,32},{48,40},{56,48},{64,56},{72,6... | collective-permute-start | bytes 688136 | tf_op jit(solution)/shard_map/while/body/eval_jaxpr/ppermute | solution.py:22
  113.9 9.1 %collective-permute-start = (bf16[32,3584]{1,0:T(8,128)(2,1)}, bf16[32,3584]{1,0:T(8,128)(2,1)S(1)}, u32[]{:S(2)}, u32[]{:S(2)}) collective-permute-start(bf16[32,3584]{1,0:T(8,128)(2,1)} %get-tuple-element.282), channel_id=1, source_target_pairs={{8,0},{16,8},{24,16},{32,24},{40,32},{48,40},{56,48},{64,56},{72,6... | collective-permute-start | bytes 688136 | tf_op jit(solution)/shard_map/while/body/eval_jaxpr/ppermute | solution.py:22
  128.8 9.1 %collective-permute-start = (bf16[32,3584]{1,0:T(8,128)(2,1)}, bf16[32,3584]{1,0:T(8,128)(2,1)S(1)}, u32[]{:S(2)}, u32[]{:S(2)}) collective-permute-start(bf16[32,3584]{1,0:T(8,128)(2,1)} %get-tuple-element.282), channel_id=1, source_target_pairs={{8,0},{16,8},{24,16},{32,24},{40,32},{48,40},{56,48},{64,56},{72,6... | collective-permute-start | bytes 688136 | tf_op jit(solution)/shard_map/while/body/eval_jaxpr/ppermute | solution.py:22
  143.7 9.1 %collective-permute-start = (bf16[32,3584]{1,0:T(8,128)(2,1)}, bf16[32,3584]{1,0:T(8,128)(2,1)S(1)}, u32[]{:S(2)}, u32[]{:S(2)}) collective-permute-start(bf16[32,3584]{1,0:T(8,128)(2,1)} %get-tuple-element.282), channel_id=1, source_target_pairs={{8,0},{16,8},{24,16},{32,24},{40,32},{48,40},{56,48},{64,56},{72,6... | collective-permute-start | bytes 688136 | tf_op jit(solution)/shard_map/while/body/eval_jaxpr/ppermute | solution.py:22
  158.7 9.1 %collective-permute-start = (bf16[32,3584]{1,0:T(8,128)(2,1)}, bf16[32,3584]{1,0:T(8,128)(2,1)S(1)}, u32[]{:S(2)}, u32[]{:S(2)}) collective-permute-start(bf16[32,3584]{1,0:T(8,128)(2,1)} %get-tuple-element.282), channel_id=1, source_target_pairs={{8,0},{16,8},{24,16},{32,24},{40,32},{48,40},{56,48},{64,56},{72,6... | collective-permute-start | bytes 688136 | tf_op jit(solution)/shard_map/while/body/eval_jaxpr/ppermute | solution.py:22
  173.6 9.1 %collective-permute-start = (bf16[32,3584]{1,0:T(8,128)(2,1)}, bf16[32,3584]{1,0:T(8,128)(2,1)S(1)}, u32[]{:S(2)}, u32[]{:S(2)}) collective-permute-start(bf16[32,3584]{1,0:T(8,128)(2,1)} %get-tuple-element.282), channel_id=1, source_target_pairs={{8,0},{16,8},{24,16},{32,24},{40,32},{48,40},{56,48},{64,56},{72,6... | collective-permute-start | bytes 688136 | tf_op jit(solution)/shard_map/while/body/eval_jaxpr/ppermute | solution.py:22
  188.6 9.1 %collective-permute-start = (bf16[32,3584]{1,0:T(8,128)(2,1)}, bf16[32,3584]{1,0:T(8,128)(2,1)S(1)}, u32[]{:S(2)}, u32[]{:S(2)}) collective-permute-start(bf16[32,3584]{1,0:T(8,128)(2,1)} %get-tuple-element.282), channel_id=1, source_target_pairs={{8,0},{16,8},{24,16},{32,24},{40,32},{48,40},{56,48},{64,56},{72,6... | collective-permute-start | bytes 688136 | tf_op jit(solution)/shard_map/while/body/eval_jaxpr/ppermute | solution.py:22
  203.5 9.1 %collective-permute-start = (bf16[32,3584]{1,0:T(8,128)(2,1)}, bf16[32,3584]{1,0:T(8,128)(2,1)S(1)}, u32[]{:S(2)}, u32[]{:S(2)}) collective-permute-start(bf16[32,3584]{1,0:T(8,128)(2,1)} %get-tuple-element.282), channel_id=1, source_target_pairs={{8,0},{16,8},{24,16},{32,24},{40,32},{48,40},{56,48},{64,56},{72,6... | collective-permute-start | bytes 688136 | tf_op jit(solution)/shard_map/while/body/eval_jaxpr/ppermute | solution.py:22
  218.4 9.9 %collective-permute-start = (bf16[32,3584]{1,0:T(8,128)(2,1)}, bf16[32,3584]{1,0:T(8,128)(2,1)S(1)}, u32[]{:S(2)}, u32[]{:S(2)}) collective-permute-start(bf16[32,3584]{1,0:T(8,128)(2,1)} %get-tuple-element.282), channel_id=1, source_target_pairs={{8,0},{16,8},{24,16},{32,24},{40,32},{48,40},{56,48},{64,56},{72,6... | collective-permute-start | bytes 688136 | tf_op jit(solution)/shard_map/while/body/eval_jaxpr/ppermute | solution.py:22
  234.2 11.0 %collective-permute-start = (bf16[32,3584]{1,0:T(8,128)(2,1)}, bf16[32,3584]{1,0:T(8,128)(2,1)S(1)}, u32[]{:S(2)}, u32[]{:S(2)}) collective-permute-start(bf16[32,3584]{1,0:T(8,128)(2,1)} %get-tuple-element.282), channel_id=1, source_target_pairs={{8,0},{16,8},{24,16},{32,24},{40,32},{48,40},{56,48},{64,56},{72,6... | collective-permute-start | bytes 688136 | tf_op jit(solution)/shard_map/while/body/eval_jaxpr/ppermute | solution.py:22
  251.0 11.0 %collective-permute-start = (bf16[32,3584]{1,0:T(8,128)(2,1)}, bf16[32,3584]{1,0:T(8,128)(2,1)S(1)}, u32[]{:S(2)}, u32[]{:S(2)}) collective-permute-start(bf16[32,3584]{1,0:T(8,128)(2,1)} %get-tuple-element.282), channel_id=1, source_target_pairs={{8,0},{16,8},{24,16},{32,24},{40,32},{48,40},{56,48},{64,56},{72,6... | collective-permute-start | bytes 688136 | tf_op jit(solution)/shard_map/while/body/eval_jaxpr/ppermute | solution.py:22
  267.8 10.4 %collective-permute-start = (bf16[32,3584]{1,0:T(8,128)(2,1)}, bf16[32,3584]{1,0:T(8,128)(2,1)S(1)}, u32[]{:S(2)}, u32[]{:S(2)}) collective-permute-start(bf16[32,3584]{1,0:T(8,128)(2,1)} %get-tuple-element.282), channel_id=1, source_target_pairs={{8,0},{16,8},{24,16},{32,24},{40,32},{48,40},{56,48},{64,56},{72,6... | collective-permute-start | bytes 688136 | tf_op jit(solution)/shard_map/while/body/eval_jaxpr/ppermute | solution.py:22
  284.1 9.4 %collective-permute-start = (bf16[32,3584]{1,0:T(8,128)(2,1)}, bf16[32,3584]{1,0:T(8,128)(2,1)S(1)}, u32[]{:S(2)}, u32[]{:S(2)}) collective-permute-start(bf16[32,3584]{1,0:T(8,128)(2,1)} %get-tuple-element.282), channel_id=1, source_target_pairs={{8,0},{16,8},{24,16},{32,24},{40,32},{48,40},{56,48},{64,56},{72,6... | collective-permute-start | bytes 688136 | tf_op jit(solution)/shard_map/while/body/eval_jaxpr/ppermute | solution.py:22
  299.3 9.4 %collective-permute-start = (bf16[32,3584]{1,0:T(8,128)(2,1)}, bf16[32,3584]{1,0:T(8,128)(2,1)S(1)}, u32[]{:S(2)}, u32[]{:S(2)}) collective-permute-start(bf16[32,3584]{1,0:T(8,128)(2,1)} %get-tuple-element.282), channel_id=1, source_target_pairs={{8,0},{16,8},{24,16},{32,24},{40,32},{48,40},{56,48},{64,56},{72,6... | collective-permute-start | bytes 688136 | tf_op jit(solution)/shard_map/while/body/eval_jaxpr/ppermute | solution.py:22
  314.6 9.1 %collective-permute-start = (bf16[32,3584]{1,0:T(8,128)(2,1)}, bf16[32,3584]{1,0:T(8,128)(2,1)S(1)}, u32[]{:S(2)}, u32[]{:S(2)}) collective-permute-start(bf16[32,3584]{1,0:T(8,128)(2,1)} %get-tuple-element.282), channel_id=1, source_target_pairs={{8,0},{16,8},{24,16},{32,24},{40,32},{48,40},{56,48},{64,56},{72,6... | collective-permute-start | bytes 688136 | tf_op jit(solution)/shard_map/while/body/eval_jaxpr/ppermute | solution.py:22
  329.6 9.1 %collective-permute-start = (bf16[32,3584]{1,0:T(8,128)(2,1)}, bf16[32,3584]{1,0:T(8,128)(2,1)S(1)}, u32[]{:S(2)}, u32[]{:S(2)}) collective-permute-start(bf16[32,3584]{1,0:T(8,128)(2,1)} %get-tuple-element.282), channel_id=1, source_target_pairs={{8,0},{16,8},{24,16},{32,24},{40,32},{48,40},{56,48},{64,56},{72,6... | collective-permute-start | bytes 688136 | tf_op jit(solution)/shard_map/while/body/eval_jaxpr/ppermute | solution.py:22
  344.5 9.1 %collective-permute-start = (bf16[32,3584]{1,0:T(8,128)(2,1)}, bf16[32,3584]{1,0:T(8,128)(2,1)S(1)}, u32[]{:S(2)}, u32[]{:S(2)}) collective-permute-start(bf16[32,3584]{1,0:T(8,128)(2,1)} %get-tuple-element.282), channel_id=1, source_target_pairs={{8,0},{16,8},{24,16},{32,24},{40,32},{48,40},{56,48},{64,56},{72,6... | collective-permute-start | bytes 688136 | tf_op jit(solution)/shard_map/while/body/eval_jaxpr/ppermute | solution.py:22
  359.5 9.1 %collective-permute-start = (bf16[32,3584]{1,0:T(8,128)(2,1)}, bf16[32,3584]{1,0:T(8,128)(2,1)S(1)}, u32[]{:S(2)}, u32[]{:S(2)}) collective-permute-start(bf16[32,3584]{1,0:T(8,128)(2,1)} %get-tuple-element.282), channel_id=1, source_target_pairs={{8,0},{16,8},{24,16},{32,24},{40,32},{48,40},{56,48},{64,56},{72,6... | collective-permute-start | bytes 688136 | tf_op jit(solution)/shard_map/while/body/eval_jaxpr/ppermute | solution.py:22
  374.4 9.1 %collective-permute-start = (bf16[32,3584]{1,0:T(8,128)(2,1)}, bf16[32,3584]{1,0:T(8,128)(2,1)S(1)}, u32[]{:S(2)}, u32[]{:S(2)}) collective-permute-start(bf16[32,3584]{1,0:T(8,128)(2,1)} %get-tuple-element.282), channel_id=1, source_target_pairs={{8,0},{16,8},{24,16},{32,24},{40,32},{48,40},{56,48},{64,56},{72,6... | collective-permute-start | bytes 688136 | tf_op jit(solution)/shard_map/while/body/eval_jaxpr/ppermute | solution.py:22
  389.4 9.1 %collective-permute-start = (bf16[32,3584]{1,0:T(8,128)(2,1)}, bf16[32,3584]{1,0:T(8,128)(2,1)S(1)}, u32[]{:S(2)}, u32[]{:S(2)}) collective-permute-start(bf16[32,3584]{1,0:T(8,128)(2,1)} %get-tuple-element.282), channel_id=1, source_target_pairs={{8,0},{16,8},{24,16},{32,24},{40,32},{48,40},{56,48},{64,56},{72,6... | collective-permute-start | bytes 688136 | tf_op jit(solution)/shard_map/while/body/eval_jaxpr/ppermute | solution.py:22
  404.3 9.1 %collective-permute-start = (bf16[32,3584]{1,0:T(8,128)(2,1)}, bf16[32,3584]{1,0:T(8,128)(2,1)S(1)}, u32[]{:S(2)}, u32[]{:S(2)}) collective-permute-start(bf16[32,3584]{1,0:T(8,128)(2,1)} %get-tuple-element.282), channel_id=1, source_target_pairs={{8,0},{16,8},{24,16},{32,24},{40,32},{48,40},{56,48},{64,56},{72,6... | collective-permute-start | bytes 688136 | tf_op jit(solution)/shard_map/while/body/eval_jaxpr/ppermute | solution.py:22
  419.3 9.1 %collective-permute-start = (bf16[32,3584]{1,0:T(8,128)(2,1)}, bf16[32,3584]{1,0:T(8,128)(2,1)S(1)}, u32[]{:S(2)}, u32[]{:S(2)}) collective-permute-start(bf16[32,3584]{1,0:T(8,128)(2,1)} %get-tuple-element.282), channel_id=1, source_target_pairs={{8,0},{16,8},{24,16},{32,24},{40,32},{48,40},{56,48},{64,56},{72,6... | collective-permute-start | bytes 688136 | tf_op jit(solution)/shard_map/while/body/eval_jaxpr/ppermute | solution.py:22
  434.2 9.1 %collective-permute-start = (bf16[32,3584]{1,0:T(8,128)(2,1)}, bf16[32,3584]{1,0:T(8,128)(2,1)S(1)}, u32[]{:S(2)}, u32[]{:S(2)}) collective-permute-start(bf16[32,3584]{1,0:T(8,128)(2,1)} %get-tuple-element.282), channel_id=1, source_target_pairs={{8,0},{16,8},{24,16},{32,24},{40,32},{48,40},{56,48},{64,56},{72,6... | collective-permute-start | bytes 688136 | tf_op jit(solution)/shard_map/while/body/eval_jaxpr/ppermute | solution.py:22
  449.2 10.2 %collective-permute-start = (bf16[32,3584]{1,0:T(8,128)(2,1)}, bf16[32,3584]{1,0:T(8,128)(2,1)S(1)}, u32[]{:S(2)}, u32[]{:S(2)}) collective-permute-start(bf16[32,3584]{1,0:T(8,128)(2,1)} %get-tuple-element.282), channel_id=1, source_target_pairs={{8,0},{16,8},{24,16},{32,24},{40,32},{48,40},{56,48},{64,56},{72,6... | collective-permute-start | bytes 688136 | tf_op jit(solution)/shard_map/while/body/eval_jaxpr/ppermute | solution.py:22
  465.2 11.3 %collective-permute-start = (bf16[32,3584]{1,0:T(8,128)(2,1)}, bf16[32,3584]{1,0:T(8,128)(2,1)S(1)}, u32[]{:S(2)}, u32[]{:S(2)}) collective-permute-start(bf16[32,3584]{1,0:T(8,128)(2,1)} %get-tuple-element.282), channel_id=1, source_target_pairs={{8,0},{16,8},{24,16},{32,24},{40,32},{48,40},{56,48},{64,56},{72,6... | collective-permute-start | bytes 688136 | tf_op jit(solution)/shard_map/while/body/eval_jaxpr/ppermute | solution.py:22
  482.4 10.7 %collective-permute-start = (bf16[32,3584]{1,0:T(8,128)(2,1)}, bf16[32,3584]{1,0:T(8,128)(2,1)S(1)}, u32[]{:S(2)}, u32[]{:S(2)}) collective-permute-start(bf16[32,3584]{1,0:T(8,128)(2,1)} %get-tuple-element.282), channel_id=1, source_target_pairs={{8,0},{16,8},{24,16},{32,24},{40,32},{48,40},{56,48},{64,56},{72,6... | collective-permute-start | bytes 688136 | tf_op jit(solution)/shard_map/while/body/eval_jaxpr/ppermute | solution.py:22
  499.0 10.1 %collective-permute-start = (bf16[32,3584]{1,0:T(8,128)(2,1)}, bf16[32,3584]{1,0:T(8,128)(2,1)S(1)}, u32[]{:S(2)}, u32[]{:S(2)}) collective-permute-start(bf16[32,3584]{1,0:T(8,128)(2,1)} %get-tuple-element.282), channel_id=1, source_target_pairs={{8,0},{16,8},{24,16},{32,24},{40,32},{48,40},{56,48},{64,56},{72,6... | collective-permute-start | bytes 688136 | tf_op jit(solution)/shard_map/while/body/eval_jaxpr/ppermute | solution.py:22
  514.9 9.4 %collective-permute-start = (bf16[32,3584]{1,0:T(8,128)(2,1)}, bf16[32,3584]{1,0:T(8,128)(2,1)S(1)}, u32[]{:S(2)}, u32[]{:S(2)}) collective-permute-start(bf16[32,3584]{1,0:T(8,128)(2,1)} %get-tuple-element.282), channel_id=1, source_target_pairs={{8,0},{16,8},{24,16},{32,24},{40,32},{48,40},{56,48},{64,56},{72,6... | collective-permute-start | bytes 688136 | tf_op jit(solution)/shard_map/while/body/eval_jaxpr/ppermute | solution.py:22
  530.2 9.1 %collective-permute-start = (bf16[32,3584]{1,0:T(8,128)(2,1)}, bf16[32,3584]{1,0:T(8,128)(2,1)S(1)}, u32[]{:S(2)}, u32[]{:S(2)}) collective-permute-start(bf16[32,3584]{1,0:T(8,128)(2,1)} %get-tuple-element.282), channel_id=1, source_target_pairs={{8,0},{16,8},{24,16},{32,24},{40,32},{48,40},{56,48},{64,56},{72,6... | collective-permute-start | bytes 688136 | tf_op jit(solution)/shard_map/while/body/eval_jaxpr/ppermute | solution.py:22
  545.1 9.1 %collective-permute-start = (bf16[32,3584]{1,0:T(8,128)(2,1)}, bf16[32,3584]{1,0:T(8,128)(2,1)S(1)}, u32[]{:S(2)}, u32[]{:S(2)}) collective-permute-start(bf16[32,3584]{1,0:T(8,128)(2,1)} %get-tuple-element.282), channel_id=1, source_target_pairs={{8,0},{16,8},{24,16},{32,24},{40,32},{48,40},{56,48},{64,56},{72,6... | collective-permute-start | bytes 688136 | tf_op jit(solution)/shard_map/while/body/eval_jaxpr/ppermute | solution.py:22
  560.1 9.1 %collective-permute-start = (bf16[32,3584]{1,0:T(8,128)(2,1)}, bf16[32,3584]{1,0:T(8,128)(2,1)S(1)}, u32[]{:S(2)}, u32[]{:S(2)}) collective-permute-start(bf16[32,3584]{1,0:T(8,128)(2,1)} %get-tuple-element.282), channel_id=1, source_target_pairs={{8,0},{16,8},{24,16},{32,24},{40,32},{48,40},{56,48},{64,56},{72,6... | collective-permute-start | bytes 688136 | tf_op jit(solution)/shard_map/while/body/eval_jaxpr/ppermute | solution.py:22
  575.0 9.1 %collective-permute-start = (bf16[32,3584]{1,0:T(8,128)(2,1)}, bf16[32,3584]{1,0:T(8,128)(2,1)S(1)}, u32[]{:S(2)}, u32[]{:S(2)}) collective-permute-start(bf16[32,3584]{1,0:T(8,128)(2,1)} %get-tuple-element.282), channel_id=1, source_target_pairs={{8,0},{16,8},{24,16},{32,24},{40,32},{48,40},{56,48},{64,56},{72,6... | collective-permute-start | bytes 688136 | tf_op jit(solution)/shard_map/while/body/eval_jaxpr/ppermute | solution.py:22
  590.0 9.1 %collective-permute-start = (bf16[32,3584]{1,0:T(8,128)(2,1)}, bf16[32,3584]{1,0:T(8,128)(2,1)S(1)}, u32[]{:S(2)}, u32[]{:S(2)}) collective-permute-start(bf16[32,3584]{1,0:T(8,128)(2,1)} %get-tuple-element.282), channel_id=1, source_target_pairs={{8,0},{16,8},{24,16},{32,24},{40,32},{48,40},{56,48},{64,56},{72,6... | collective-permute-start | bytes 688136 | tf_op jit(solution)/shard_map/while/body/eval_jaxpr/ppermute | solution.py:22
  604.9 9.1 %collective-permute-start = (bf16[32,3584]{1,0:T(8,128)(2,1)}, bf16[32,3584]{1,0:T(8,128)(2,1)S(1)}, u32[]{:S(2)}, u32[]{:S(2)}) collective-permute-start(bf16[32,3584]{1,0:T(8,128)(2,1)} %get-tuple-element.282), channel_id=1, source_target_pairs={{8,0},{16,8},{24,16},{32,24},{40,32},{48,40},{56,48},{64,56},{72,6... | collective-permute-start | bytes 688136 | tf_op jit(solution)/shard_map/while/body/eval_jaxpr/ppermute | solution.py:22
  619.9 9.1 %collective-permute-start = (bf16[32,3584]{1,0:T(8,128)(2,1)}, bf16[32,3584]{1,0:T(8,128)(2,1)S(1)}, u32[]{:S(2)}, u32[]{:S(2)}) collective-permute-start(bf16[32,3584]{1,0:T(8,128)(2,1)} %get-tuple-element.282), channel_id=1, source_target_pairs={{8,0},{16,8},{24,16},{32,24},{40,32},{48,40},{56,48},{64,56},{72,6... | collective-permute-start | bytes 688136 | tf_op jit(solution)/shard_map/while/body/eval_jaxpr/ppermute | solution.py:22
  638.8 70.5 %all-to-all-start = ((f32[8,1,448]{2,1,0:T(1,128)}), f32[8,1,448]{2,1,0:T(1,128)S(1)}, u32[]{:S(2)}, u32[]{:S(2)}) async-start(f32[8,1,448]{2,1,0:T(1,128)} %all_to_all.6), calls=%async_computation | async-start | bytes 32768 | tf_op jit(solution)/shard_map/all_to_all | solution.py:236
  686.7 4.4 copy-start.2
  691.1 6.1 copy-start.6
  697.2 1.6 copy-start
  698.7 2.2 copy-start.5
